TPU v7x, 512 devices: a whole 4x4x16 slice. The times are simulated.
512 devices in a mesh: cfg: 2 (over core), grp: 4 (over y), seq: 64 (over x, z).
Axes of the slice: x: 4, y: 4, z: 16, core: 2. Of those that a mesh axis runs over, the one named last changes fastest.
Arguments:
- query: bfloat16 [2, 4, 2, 128, 2432], P('cfg', 'grp', None, 'seq'), may hold values from -150 to 150
- keys: bfloat16 [2, 4, 2, 128, 2432], P('cfg', 'grp', None, 'seq'), may hold values from -5.5 to 5.5
- values: bfloat16 [2, 4, 2, 128, 2432], P('cfg', 'grp', None, 'seq'), may hold values from -5 to 5
- hidden: bfloat16 [2, 4, 2, 128, 2432], P('cfg', 'grp', None, 'seq'), may hold values from -23 to 23
- latent: float32 [4, 2, 128, 64], P('grp', None, 'seq', 'cfg'), may hold values from -6 to 6
- deal: int32 [4, 2], replicated, may hold values from 0 to 5, as said below
- lengths: int32 [4, 2], replicated, may hold values from 64 to 128, as said below
- w_out: bfloat16 [2432, 2432], P(('cfg', 'seq')), may hold values from -0.125 to 0.125
- attn_gate: float32 [2, 6, 2432], P('cfg'), may hold values from 0.25 to 1.75
- modulation: float32 [2, 6, 2, 2432], P('cfg'), may hold values from -3 to 3
- w_final: bfloat16 [2432, 64], replicated, may hold values from -0.125 to 0.125
- guide: float32 [6], replicated, may hold values from 2 to 7
- step_size: float32 [6], replicated, may hold values from 0.15 to 0.5
Outputs:
- latent_next: float32 [4, 2, 128, 64], P('grp', None, 'seq', 'cfg')
Inputs may be any that keep to these rules, and one draw needn't show every extreme that they name: `deal`: column 0 of row g names the whole item of group g, column 1 the item split between groups g and g xor 1 (equal in both rows); every one of the 6 items is named by exactly one column-0 entry or one pair of column-1 entries. `lengths`: in each column some group has all 128 slots live.
All inputs are finite; a program needn't handle non-finite values.
Results may differ from a plain program's by a relative error of at most 0.0049.
Values may be sent and summed in bfloat16 or wider, within the bound.
No kernel may reach another device: no remote copies, remote signals or barrier semaphores. Data moves between devices by JAX's collectives and lax.ppermute only.
A program may use at most 128 MiB of HBM per device.

v0:
```python
import jax
import jax.numpy as jnp
from jax import lax
from jax.sharding import PartitionSpec as P

D = 2432
HEADS = 38
HD = 64


NORM_EPS = 1e-06


def from_partner(x, axis, apart):
    return lax.ppermute(x, axis, [(i, i ^ 1 << apart) for i in range(lax.axis_size(axis))])


def attend(queries, keys_all, values_all, live_keys):
    row_count = queries.shape[0]
    query_heads = queries.reshape(row_count, HEADS, HD)
    key_heads = keys_all.reshape(-1, HEADS, HD)
    value_heads = values_all.reshape(-1, HEADS, HD)
    scores = jnp.einsum(
        "shd,khd->hsk", query_heads, key_heads, preferred_element_type=jnp.float32
    ) * HD ** (-0.5)
    scores = jnp.where(live_keys[None, None, :], scores, -jnp.inf)
    peak_score = jnp.max(scores, axis=2, keepdims=True)
    raw_weights = jnp.exp(scores - peak_score)
    row_total = jnp.sum(raw_weights, axis=2, keepdims=True)
    weights = raw_weights.astype(jnp.bfloat16)
    mixed_out = (
        jnp.einsum("hsk,khd->hsd", weights, value_heads, preferred_element_type=jnp.float32)
        / row_total
    )
    return jnp.transpose(mixed_out, (1, 0, 2)).reshape(row_count, HEADS * HD)


def shards(
    query,
    keys,
    values,
    hidden,
    latent,
    deal,
    lengths,
    w_out,
    attn_gate,
    modulation,
    w_final,
    guide,
    step_size,
):
    group_id = lax.axis_index("grp")
    branch = lax.axis_index("cfg")
    partner = jnp.bitwise_xor(group_id, 1)
    own_lengths = lax.dynamic_index_in_dim(lengths, group_id, 0, keepdims=False)
    pair_lengths = lax.dynamic_index_in_dim(lengths, partner, 0, keepdims=False)
    item_ids = lax.dynamic_index_in_dim(deal, group_id, 0, keepdims=False)
    resident_key_rows = keys[0, 0]
    local_values = values[0, 0]
    shard_rows = resident_key_rows.shape[1]
    far_keys, far_values = from_partner((resident_key_rows[1], local_values[1]), "grp", 0)
    combined_key_rows, joint_values = (
        lax.all_gather(
            jnp.concatenate([resident_key_rows, far_keys[None]], 0), "seq", axis=1, tiled=True
        ),
        lax.all_gather(
            jnp.concatenate([local_values, far_values[None]], 0), "seq", axis=1, tiled=True
        ),
    )
    group_keys, group_values = (combined_key_rows[:2], joint_values[:2])
    pair_keys, pair_values = (combined_key_rows[2], joint_values[2])
    slot_total = group_keys.shape[1]
    slot_ids = jnp.arange(slot_total)
    live_home = slot_ids < own_lengths[0]
    live_own = slot_ids < own_lengths[1]
    live_pair = slot_ids < pair_lengths[1]
    local_query = query[0, 0]
    local_output_rows = attend(local_query[0], group_keys[0], group_values[0], live_home)
    shared = attend(
        local_query[1],
        jnp.concatenate([group_keys[1], pair_keys], 0),
        jnp.concatenate([group_values[1], pair_values], 0),
        jnp.concatenate([live_own, live_pair], 0),
    )
    attn_rows = (
        jnp.stack([local_output_rows, shared]).astype(jnp.bfloat16).reshape(2 * shard_rows, D)
    )
    projected = jnp.dot(
        attn_rows,
        lax.all_gather(w_out, ("cfg", "seq"), axis=0, tiled=True),
        preferred_element_type=jnp.float32,
    )
    projected = projected.reshape(2, shard_rows, D)
    item_count = guide.shape[0]
    indicator_mask = (jnp.arange(item_count)[None, :] == item_ids[:, None]).astype(jnp.float32)
    gate_now = jnp.einsum(
        "ri,id->rd", indicator_mask, attn_gate[0], precision=lax.Precision.HIGHEST
    )
    stream = hidden[0, 0].astype(jnp.float32) + gate_now[:, None, :] * projected
    row_mean = jnp.mean(stream, axis=2, keepdims=True)
    centred = stream - row_mean
    row_var = jnp.mean(centred * centred, axis=2, keepdims=True)
    normed = centred * lax.rsqrt(row_var + NORM_EPS)
    selected_entries = jnp.einsum(
        "ub,bkg->ukg", indicator_mask, modulation[0], precision=lax.Precision.HIGHEST
    )
    shaped = (
        normed * (1.0 + selected_entries[:, 1][:, None, :]) + selected_entries[:, 0][:, None, :]
    ).astype(jnp.bfloat16)
    velocity = jnp.einsum("rsd,dc->rsc", shaped, w_final, preferred_element_type=jnp.float32)
    row_slots = lax.axis_index("seq") * shard_rows + jnp.arange(shard_rows)
    live_rows = jnp.stack([row_slots < own_lengths[0], row_slots < own_lengths[1]])
    velocity = jnp.where(live_rows[:, :, None], velocity, jnp.float32(0.0))
    weight_now = jnp.sum(indicator_mask * guide[None, :], axis=1)[:, None, None]
    step_now = jnp.sum(indicator_mask * step_size[None, :], axis=1)[:, None, None]
    latent_part = latent[0]
    part_width = latent_part.shape[2]
    outgoing_velocity = lax.dynamic_slice_in_dim(velocity, (1 - branch) * part_width, part_width, 2)
    own_velocity = lax.dynamic_slice_in_dim(velocity, branch * part_width, part_width, 2)
    other_velocity = from_partner(outgoing_velocity, "cfg", 0)
    is_conditional = branch == 0
    cond_velocity = jnp.where(is_conditional, own_velocity, other_velocity)
    uncond_velocity = jnp.where(is_conditional, other_velocity, own_velocity)
    guided = uncond_velocity + weight_now * (cond_velocity - uncond_velocity)
    updated = latent_part - step_now * guided
    return updated[None]


def solution(mesh):
    placed = (
        P("cfg", "grp", None, "seq", None),
        P("cfg", "grp", None, "seq", None),
        P("cfg", "grp", None, "seq", None),
        P("cfg", "grp", None, "seq", None),
        P("grp", None, "seq", "cfg"),
        P(),
        P(),
        P(("cfg", "seq"), None),
        P("cfg", None, None),
        P("cfg", None, None, None),
        P(),
        P(),
        P(),
    )
    return jax.shard_map(
        shards, mesh=mesh, in_specs=placed, out_specs=P("grp", None, "seq", "cfg"), check_vma=False
    )
```

profile of v0, /device:TPU:1, one launch (start us, length us, event | category | flops | bytes accessed | tf_op | source)
XLA Modules:
  0.0 488.3 jit_solution(13304708734672202299)
XLA Ops:
  6.5 0.8 slice_bitcast_fusion.1
  7.3 4.0 collective-permute-start.1
  11.3 0.7 copy.77
  13.1 0.7 slice_bitcast_fusion.2
  13.8 3.4 collective-permute-start
  17.2 0.7 copy.78
  19.0 0.7 all-gather.9.cloned.1.call-update
  19.7 0.7 fusion.67
  20.5 0.8 constant_dynamic-slice_fusion.2
  21.9 0.9 fusion.57
  23.4 0.7 iota_compare_fusion.5
  24.1 1.3 iota_compare_fusion.3
  25.4 1.3 fusion.58
  26.8 1.0 fusion.34
  27.8 1.2 fusion.32
  29.0 122.6 %all-gather.7.cloned.1.call-done = bf16[3,128,2432]{2,0,1:T(4,128)(2,1)} async-done(((bf16[3,2,2432]{2,0,1:T(4,128)(2,1)}), bf16[3,128,2432]{2,0,1:T(4,128)(2,1)}) %all-gather.7.cloned.1.call-update) | async-done | bytes 1867792 | tf_op jit(solution)/shard_map/all_gather | solution.py:67
  151.6 7.6 %fusion.66 = (bf16[1,128,2432]{2,0,1:T(2,128)(2,1)S(1)}, bf16[1,128,2432]{2,0,1:T(2,128)(2,1)}, bf16[1,128,2432]{2,0,1:T(2,128)(2,1)S(1)}) fusion(bf16[3,128,2432]{2,0,1:T(4,128)(2,1)} %all-gather.7.cloned.1.call-done), kind=kLoop, calls=%fused_computation.84 | loop fusion | bytes 3735552 | tf_op jit(solution)/shard_map/slice | solution.py:79
  159.2 2.7 copy.57
  162.0 2.1 copy.56
  164.0 127.7 %all-gather.5.cloned.1.call-done = bf16[3,128,2432]{2,0,1:T(4,128)(2,1)} async-done(((bf16[3,2,2432]{2,0,1:T(4,128)(2,1)}), bf16[3,128,2432]{2,0,1:T(4,128)(2,1)}) %all-gather.5.cloned.1.call-update) | async-done | bytes 1867792 | tf_op jit(solution)/shard_map/all_gather | solution.py:64
  291.8 8.0 %fusion.65 = (bf16[1,128,2432]{2,0,1:T(2,128)(2,1)S(1)}, bf16[1,128,2432]{2,0,1:T(2,128)(2,1)}, bf16[1,128,2432]{2,0,1:T(2,128)(2,1)}) fusion(bf16[3,128,2432]{2,0,1:T(4,128)(2,1)} %all-gather.5.cloned.1.call-done), kind=kLoop, calls=%fused_computation.83 | loop fusion | bytes 3735552 | tf_op jit(solution)/shard_map/slice | solution.py:79
  299.8 3.6 copy.54
  303.4 3.6 copy.53
  306.9 1.7 fusion.69
  309.4 1.4 copy.51
  310.9 1.4 copy.47
  313.4 141.1 %all-gather.9.cloned.1.call-done = bf16[128,19,2432]{2,1,0:T(8,128)(2,1)} async-done(((bf16[1,19,2432]{2,1,0:T(8,128)(2,1)}), bf16[128,19,2432]{2,1,0:T(8,128)(2,1)}) %all-gather.9.cloned.1.call-update) | async-done | bytes 11829264 | tf_op jit(solution)/shard_map/all_gather | solution.py:91
  454.5 16.7 %reshape.76 = bf16[2432,2432,1]{1,0,2:T(8,128)(2,1)} reshape(bf16[128,19,2432]{2,1,0:T(8,128)(2,1)} %all-gather.9.cloned.1.call-done) | data formatting | bytes 23658496
  471.3 6.2 %fusion.71 = (f32[2,2]{1,0:T(2,128)S(1)}, f32[2,2,2432]{2,1,0:T(2,128)S(1)}) fusion(bf16[2432,2432,1]{1,0,2:T(8,128)(2,1)} %reshape.76, bf16[1,2,2432]{2,1,0:T(2,128)(2,1)S(1)} %stack_reshape.9, bf16[1,2,2432]{2,1,0:T(2,128)(2,1)S(1)} %stack_reshape.8, f32[2,2432]{1,0:T(2,128)S(1)} %fusion.34, bf16[1,1,2,2,2432]{4,3,2,1,0:T(2,128)(2,1)S(1)} %copy-done.2), kind=kOutput, calls=%fused_computation.89 | convolution fusion | flops 47394812 | bytes 11926544 | tf_op jit(solution)/shard_map/dot_general | solution.py:89
  478.1 2.2 collective-permute-start.2
  480.4 0.7 collective-permute-done.2
  481.1 0.7 fusion.55
  (45 shorter events, 6.1 us)
Async XLA Ops:
  6.5 471.2 %copy-start = (bf16[2432,64]{0,1:T(8,128)(2,1)S(1)}, bf16[2432,64]{0,1:T(8,128)(2,1)}, u32[]{:S(2)}) copy-start(bf16[2432,64]{0,1:T(8,128)(2,1)} %param.23) | copy-start | bytes 933892
  6.5 145.1 %all-gather.7.cloned.1.call-start = ((), (), s32[]{:S(2)}) async-start(), calls=%async_computation.1 | async-start | bytes 2529280 | tf_op jit(solution)/shard_map/all_gather | solution.py:67
  7.3 5.1 %collective-permute-start.1 = (bf16[2,2432]{1,0:T(2,128)(2,1)S(1)}, bf16[2,2432]{1,0:T(2,128)(2,1)S(1)}, u32[]{:S(2)}, u32[]{:S(2)}) collective-permute-start(bf16[2,2432]{1,0:T(2,128)(2,1)S(1)} %slice_bitcast_fusion.1), channel_id=1, source_target_pairs={{0,64},{64,0},{128,192},{192,128},{1,65},{65,1},{129,193},{193,129... | collective-permute-start | bytes 29192 | tf_op jit(solution)/shard_map/ppermute | solution.py:15
  13.1 278.7 %all-gather.5.cloned.1.call-start = ((), (), s32[]{:S(2)}) async-start(), calls=%async_computation | async-start | bytes 2529280 | tf_op jit(solution)/shard_map/all_gather | solution.py:64
  13.8 4.4 collective-permute-start
  18.9 435.6 %all-gather.9.cloned.1.call-start = ((), (), s32[]{:S(2)}) async-start(), calls=%async_computation.2 | async-start | bytes 15058944 | tf_op jit(solution)/shard_map/all_gather | solution.py:91
  306.9 1.9 copy-start.1
  313.4 157.8 %copy-start.2 = (bf16[1,1,2,2,2432]{4,3,2,1,0:T(2,128)(2,1)S(1)}, bf16[1,1,2,2,2432]{4,3,2,1,0:T(2,128)(2,1)}, u32[]{:S(2)}) copy-start(bf16[1,1,2,2,2432]{4,3,2,1,0:T(2,128)(2,1)} %param.16) | copy-start | bytes 58372
  471.2 9.0 %copy-start.4 = (f32[6]{0:T(128)S(1)}, f32[6]{0:T(128)}, u32[]{:S(2)}) copy-start(f32[6]{0:T(128)} %param.25) | copy-start | bytes 76
  471.2 9.0 %copy-start.5 = (f32[6]{0:T(128)S(1)}, f32[6]{0:T(128)}, u32[]{:S(2)}) copy-start(f32[6]{0:T(128)} %param.24) | copy-start | bytes 76
  471.2 9.9 %copy-start.3 = (f32[1,2,2,32]{3,2,1,0:T(2,128)S(1)}, f32[1,2,2,32]{3,2,1,0:T(2,128)}, u32[]{:S(2)}) copy-start(f32[1,2,2,32]{3,2,1,0:T(2,128)} %param.17) | copy-start | bytes 1540
  478.1 3.1 collective-permute-start.2
Sparse Core Ops, SparseCore 0:
  13.2 138.4 all-gather.6
  154.6 137.1 all-gather.4
  294.8 159.6 all-gather.8
where the time goes:
time: 490 us; the launch traced here: 488 us
  waiting for transfers between devices  393 us (80%)
  local copies, waits for them, and re-layouts  54.1 us (11%)
  between operations  13.3 us (3%)
  matrix products  11.7 us (2%)
  starting transfers between devices  9.63 us (2%)
  other arithmetic  6.06 us (1%)
    all_gather x1, waiting for transfers between devices, shards(): lax.all_gather(w_out, ('cfg', 'seq'), axis=0, tiled=True)  141 us
    all_gather x1, waiting for transfers between devices, shards(): lax.all_gather(jnp.concatenate([resident_key_rows, far_keys[None]], 0), '...  128 us
    all_gather x1, waiting for transfers between devices, shards(): lax.all_gather(jnp.concatenate([local_values, far_values[None]], 0), 'seq...  123 us
    unnamed x15, local copies, waits for them, and re-layouts  18.2 us
  transfers between devices with their start and end apart: 6, of which 6 were waited for; matrix products, arithmetic and copies ran while one was open for 9% of the time, Pallas kernels for 0%

commit v1 on v0

--- a/solution.py
+++ b/solution.py
@@ -15,24 +15,19 @@
     return lax.ppermute(x, axis, [(i, i ^ 1 << apart) for i in range(lax.axis_size(axis))])
 
 
-def attend(queries, keys_all, values_all, live_keys):
-    row_count = queries.shape[0]
-    query_heads = queries.reshape(row_count, HEADS, HD)
-    key_heads = keys_all.reshape(-1, HEADS, HD)
-    value_heads = values_all.reshape(-1, HEADS, HD)
+def head_attend(queries, keys_all, values_all, live_keys):
     scores = jnp.einsum(
-        "shd,khd->hsk", query_heads, key_heads, preferred_element_type=jnp.float32
+        "sd,kd->sk", queries, keys_all, preferred_element_type=jnp.float32
     ) * HD ** (-0.5)
-    scores = jnp.where(live_keys[None, None, :], scores, -jnp.inf)
-    peak_score = jnp.max(scores, axis=2, keepdims=True)
+    scores = jnp.where(live_keys[None, :], scores, -jnp.inf)
+    peak_score = jnp.max(scores, axis=1, keepdims=True)
     raw_weights = jnp.exp(scores - peak_score)
-    row_total = jnp.sum(raw_weights, axis=2, keepdims=True)
+    row_total = jnp.sum(raw_weights, axis=1, keepdims=True)
     weights = raw_weights.astype(jnp.bfloat16)
-    mixed_out = (
-        jnp.einsum("hsk,khd->hsd", weights, value_heads, preferred_element_type=jnp.float32)
+    return (
+        jnp.einsum("sk,kd->sd", weights, values_all, preferred_element_type=jnp.float32)
         / row_total
     )
-    return jnp.transpose(mixed_out, (1, 0, 2)).reshape(row_count, HEADS * HD)
 
 
 def shards(
@@ -50,48 +45,69 @@
     guide,
     step_size,
 ):
+    nseq = lax.axis_size("seq")
     group_id = lax.axis_index("grp")
     branch = lax.axis_index("cfg")
     partner = jnp.bitwise_xor(group_id, 1)
     own_lengths = lax.dynamic_index_in_dim(lengths, group_id, 0, keepdims=False)
     pair_lengths = lax.dynamic_index_in_dim(lengths, partner, 0, keepdims=False)
     item_ids = lax.dynamic_index_in_dim(deal, group_id, 0, keepdims=False)
+    local_query = query[0, 0]
     resident_key_rows = keys[0, 0]
     local_values = values[0, 0]
     shard_rows = resident_key_rows.shape[1]
+    slot_total = nseq * shard_rows
     far_keys, far_values = from_partner((resident_key_rows[1], local_values[1]), "grp", 0)
-    combined_key_rows, joint_values = (
-        lax.all_gather(
-            jnp.concatenate([resident_key_rows, far_keys[None]], 0), "seq", axis=1, tiled=True
-        ),
-        lax.all_gather(
-            jnp.concatenate([local_values, far_values[None]], 0), "seq", axis=1, tiled=True
-        ),
+
+    def to_heads(x):
+        n = x.shape[0]
+        x = x.reshape(n, shard_rows, HEADS, HD).transpose(2, 0, 1, 3)
+        return jnp.pad(x, ((0, nseq - HEADS), (0, 0), (0, 0), (0, 0)))
+
+    packed = jnp.concatenate(
+        [
+            to_heads(local_query),
+            to_heads(jnp.concatenate([resident_key_rows, far_keys[None]], 0)),
+            to_heads(jnp.concatenate([local_values, far_values[None]], 0)),
+        ],
+        axis=1,
     )
-    group_keys, group_values = (combined_key_rows[:2], joint_values[:2])
-    pair_keys, pair_values = (combined_key_rows[2], joint_values[2])
-    slot_total = group_keys.shape[1]
+    head_rows = lax.all_to_all(packed, "seq", 0, 0, tiled=True)
+    head_rows = head_rows.transpose(1, 0, 2, 3).reshape(8, slot_total, HD)
+    head_q, head_k, head_v = head_rows[0:2], head_rows[2:5], head_rows[5:8]
     slot_ids = jnp.arange(slot_total)
     live_home = slot_ids < own_lengths[0]
     live_own = slot_ids < own_lengths[1]
     live_pair = slot_ids < pair_lengths[1]
-    local_query = query[0, 0]
-    local_output_rows = attend(local_query[0], group_keys[0], group_values[0], live_home)
-    shared = attend(
-        local_query[1],
-        jnp.concatenate([group_keys[1], pair_keys], 0),
-        jnp.concatenate([group_values[1], pair_values], 0),
+    home_out = head_attend(head_q[0], head_k[0], head_v[0], live_home)
+    shared_out = head_attend(
+        head_q[1],
+        jnp.concatenate([head_k[1], head_k[2]], 0),
+        jnp.concatenate([head_v[1], head_v[2]], 0),
         jnp.concatenate([live_own, live_pair], 0),
     )
-    attn_rows = (
-        jnp.stack([local_output_rows, shared]).astype(jnp.bfloat16).reshape(2 * shard_rows, D)
+    head_attn = jnp.stack([home_out, shared_out]).astype(jnp.bfloat16)
+
+    every_head = lax.all_to_all(
+        jnp.broadcast_to(head_attn[None], (nseq,) + head_attn.shape), "seq", 0, 0, tiled=True
     )
-    projected = jnp.dot(
-        attn_rows,
-        lax.all_gather(w_out, ("cfg", "seq"), axis=0, tiled=True),
-        preferred_element_type=jnp.float32,
+    attn_rows = every_head[:HEADS].transpose(1, 2, 0, 3).reshape(2 * slot_total, D)
+
+    block_rows = w_out.shape[0]
+    col_width = D // nseq
+    w_parts = w_out.reshape(block_rows, nseq, col_width).transpose(1, 0, 2)
+    w_half = lax.all_to_all(w_parts, "seq", 0, 0, tiled=True).reshape(nseq * block_rows, col_width)
+    w_other = from_partner(w_half, "cfg", 0)
+    w_cols = jnp.where(
+        branch == 0,
+        jnp.concatenate([w_half, w_other], 0),
+        jnp.concatenate([w_other, w_half], 0),
     )
-    projected = projected.reshape(2, shard_rows, D)
+    projected_cols = jnp.dot(attn_rows, w_cols, preferred_element_type=jnp.float32)
+    projected_parts = projected_cols.reshape(2, nseq, shard_rows, col_width).transpose(1, 0, 2, 3)
+    projected = lax.all_to_all(projected_parts, "seq", 0, 0, tiled=True)
+    projected = projected.transpose(1, 2, 0, 3).reshape(2, shard_rows, D)
+
     item_count = guide.shape[0]
     indicator_mask = (jnp.arange(item_count)[None, :] == item_ids[:, None]).astype(jnp.float32)
     gate_now = jnp.einsum(

time: 490 us -> 214 us (0.44)
  waiting for transfers between devices: 393 us -> 122 us
  starting transfers between devices: 9.63 us -> 59.3 us
  local copies, waits for them, and re-layouts: 54.1 us -> 22.5 us
  between operations: 13.3 us -> 0.4 us
  matrix products: 11.7 us -> 3.63 us
    all_gather x3 -> x0, waiting for transfers between devices: 391 us -> none  [the longest x1 141 us: shards(): lax.all_gather(w_out, ('cfg', 'seq'), axis=0, tiled=True)]
    all_to_all x0 -> x4, waiting for transfers between devices: none -> 121 us  [the longest x1 84.4 us: shards(): lax.all_to_all(jnp.broadcast_to(head_attn[None], (nseq,) + head_attn.shap...]
    all_to_all x0 -> x4, starting transfers between devices: none -> 43.1 us  [the longest x1 18.4 us: shards(): head_rows = lax.all_to_all(packed, 'seq', 0, 0, tiled=True)]
    slice x9 -> x1, local copies, waits for them, and re-layouts: 31.1 us -> 0.18 us  [shards(): home_out = head_attend(head_q[0], head_k[0], head_v[0], live_home)]
    unnamed x15 -> x20, local copies, waits for them, and re-layouts: 18.2 us -> 3.53 us
    ppermute x3 -> x4, starting transfers between devices: 9.55 us -> 16.2 us  [from_partner(): lax.ppermute(x, axis, [(i, i ^ 1 << apart) for i in range(lax.axis_size(a...]
    dot_general x5, matrix products: 9.25 us -> 2.89 us  [the longest x1 2.01 us: shards(): jnp.dot(attn_rows, w_cols, preferred_element_type=jnp.float32)]
    transpose x0 -> x5, local copies, waits for them, and re-layouts: none -> 5.21 us  [the longest x2 4.85 us: shards(): every_head[:HEADS].transpose(1, 2, 0, 3).reshape(2 * slot_total, D)]
  transfers between devices with their start and end apart: 6 -> 8, of which waited for: 6 -> 6; matrix products, arithmetic and copies ran while one was open for 9% -> 7% of each run, Pallas kernels for 0% -> 0%
where the time goes in v1:
time: 214 us; the launch traced here: 213 us
  waiting for transfers between devices  122 us (57%)
  starting transfers between devices  59.3 us (28%)
  local copies, waits for them, and re-layouts  22.5 us (11%)
  other arithmetic  5.45 us (3%)
  matrix products  3.63 us (2%)
    all_to_all x1, waiting for transfers between devices, shards(): lax.all_to_all(jnp.broadcast_to(head_attn[None], (nseq,) + head_attn.shap...  84.4 us
    all_to_all x1, starting transfers between devices, shards(): head_rows = lax.all_to_all(packed, 'seq', 0, 0, tiled=True)  18.4 us
    ppermute x4, starting transfers between devices, from_partner(): lax.ppermute(x, axis, [(i, i ^ 1 << apart) for i in range(lax.axis_size(a...  16.2 us
    all_to_all x1, waiting for transfers between devices, shards(): projected = lax.all_to_all(projected_parts, 'seq', 0, 0, tiled=True)  12.9 us
    all_to_all x1, starting transfers between devices, shards(): projected = lax.all_to_all(projected_parts, 'seq', 0, 0, tiled=True)  12.4 us
    all_to_all x1, waiting for transfers between devices, shards(): lax.all_to_all(w_parts, 'seq', 0, 0, tiled=True)  12.2 us
    all_to_all x1, waiting for transfers between devices, shards(): head_rows = lax.all_to_all(packed, 'seq', 0, 0, tiled=True)  11.5 us
    all_to_all x1, starting transfers between devices, shards(): lax.all_to_all(w_parts, 'seq', 0, 0, tiled=True)  7.14 us
  transfers between devices with their start and end apart: 8, of which 6 were waited for; matrix products, arithmetic and copies ran while one was open for 7% of the time, Pallas kernels for 0%

profile of v1, /device:TPU:1, one launch (start us, length us, event | category | flops | bytes accessed | tf_op | source)
XLA Modules:
  0.0 213.3 jit_solution(10987646264702426462)
XLA Ops:
  0.0 0.8 slice_bitcast_fusion.3
  0.8 4.0 %collective-permute-start = (bf16[2,2432]{1,0:T(2,128)(2,1)S(1)}, bf16[2,2432]{1,0:T(2,128)(2,1)S(1)}, u32[]{:S(2)}, u32[]{:S(2)}) collective-permute-start(bf16[2,2432]{1,0:T(2,128)(2,1)S(1)} %slice_bitcast_fusion.3), channel_id=1, source_target_pairs={{0,64},{64,0},{128,192},{192,128},{1,65},{65,1},{129,193},{193,129... | collective-permute-start | bytes 29192 | tf_op jit(solution)/shard_map/ppermute | solution.py:15
  4.8 0.7 slice_bitcast_fusion.2
  5.5 1.9 collective-permute-start.1
  7.4 0.9 constant_dynamic-slice_fusion.2
  8.4 0.8 concatenate.39
  9.2 0.8 concatenate.42
  10.1 0.8 reshape_squeeze.3
  11.4 1.6 reshape.117
  13.3 1.0 reshape.127
  14.9 0.8 reshape.125
  15.7 18.4 %all-to-all-start = ((bf16[64,2,512]{2,1,0:T(2,128)(2,1)}), bf16[64,2,512]{2,1,0:T(2,128)(2,1)S(1)}, u32[]{:S(2)}, u32[]{:S(2)}) async-start(bf16[64,2,512]{2,1,0:T(2,128)(2,1)} %reshape.125), calls=%async_computation | async-start | bytes 262144 | tf_op jit(solution)/shard_map/all_to_all | solution.py:75
  34.7 0.6 iota_compare_fusion.9
  36.0 0.7 iota_compare_fusion.7
  36.7 11.5 %all-to-all-done = bf16[64,2,512]{2,1,0:T(2,128)(2,1)S(1)} async-done(((bf16[64,2,512]{2,1,0:T(2,128)(2,1)}), bf16[64,2,512]{2,1,0:T(2,128)(2,1)S(1)}, u32[]{:S(2)}, u32[]{:S(2)}) %all-to-all-start) | async-done | bytes 131104 | tf_op jit(solution)/shard_map/all_to_all | solution.py:75
  48.1 7.1 %all-to-all-start.2 = ((bf16[64,2,361]{2,1,0:T(2,128)(2,1)}), bf16[64,2,361]{2,1,0:T(2,128)(2,1)S(1)}, u32[]{:S(2)}, u32[]{:S(2)}) async-start(bf16[64,2,361]{2,1,0:T(2,128)(2,1)} %reshape.127), calls=%async_computation.2 | async-start | bytes 196608 | tf_op jit(solution)/shard_map/all_to_all | solution.py:99
  56.9 12.2 %all-to-all-done.2 = bf16[64,2,361]{2,1,0:T(2,128)(2,1)S(1)} async-done(((bf16[64,2,361]{2,1,0:T(2,128)(2,1)}), bf16[64,2,361]{2,1,0:T(2,128)(2,1)S(1)}, u32[]{:S(2)}, u32[]{:S(2)}) %all-to-all-start.2) | async-done | bytes 92448 | tf_op jit(solution)/shard_map/all_to_all | solution.py:99
  69.1 1.9 broadcast_in_dim.45
  71.0 5.1 %all-to-all-start.1 = ((bf16[64,2,128,64]{2,3,1,0:T(8,128)(2,1)}), bf16[64,2,128,64]{2,3,1,0:T(8,128)(2,1)S(1)}, u32[]{:S(2)}, u32[]{:S(2)}) async-start(bf16[64,2,128,64]{2,3,1,0:T(8,128)(2,1)} %broadcast_in_dim.45), calls=%async_computation.1 | async-start | bytes 4194304 | tf_op jit(solution)/shard_map/all_to_all | solution.py:91
  77.2 4.9 %collective-permute-start.2 = (bf16[1216,38]{1,0:T(8,128)(2,1)S(1)}, bf16[1216,38]{1,0:T(8,128)(2,1)S(1)}, u32[]{:S(2)}, u32[]{:S(2)}) collective-permute-start(bf16[1216,38]{1,0:T(8,128)(2,1)S(1)} %reshape.118), channel_id=1, source_target_pairs={{0,256},{256,0},{1,257},{257,1},{2,258},{258,2},{3,259},{259,3},{4... | collective-permute-start | bytes 277256 | tf_op jit(solution)/shard_map/ppermute | solution.py:15
  83.5 84.4 %all-to-all-done.1 = bf16[64,2,128,64]{2,3,1,0:T(8,128)(2,1)S(1)} async-done(((bf16[64,2,128,64]{2,3,1,0:T(8,128)(2,1)}), bf16[64,2,128,64]{2,3,1,0:T(8,128)(2,1)S(1)}, u32[]{:S(2)}, u32[]{:S(2)}) %all-to-all-start.1) | async-done | bytes 2097184 | tf_op jit(solution)/shard_map/all_to_all | solution.py:91
  167.9 1.1 slice_bitcast_fusion
  169.0 3.7 %copy.32 = bf16[2,128,38,64]{3,2,1,0:T(8,128)(2,1)S(1)} copy(bf16[2,128,38,64]{1,3,0,2:T(8,128)(2,1)} %slice_bitcast_fusion) | data formatting | bytes 2490368 | tf_op jit(solution)/shard_map/transpose | solution.py:94
  172.8 2.4 %dot_general.31 = bf16[2,64,2,2432]{3,2,1,0:T(2,128)(2,1)} reshape(bf16[2,128,38,64]{3,2,1,0:T(8,128)(2,1)S(1)} %copy.32) | data formatting | bytes 2490368 | tf_op jit(solution)/shard_map/dot_general | solution.py:106
  175.1 2.0 fusion.3
  177.3 0.8 reshape.129
  178.2 12.4 %all-to-all-start.3 = ((f32[64,1,152]{2,1,0:T(1,128)}), f32[64,1,152]{2,1,0:T(1,128)S(1)}, u32[]{:S(2)}, u32[]{:S(2)}) async-start(f32[64,1,152]{2,1,0:T(1,128)} %reshape.129), calls=%async_computation.3 | async-start | bytes 131072 | tf_op jit(solution)/shard_map/all_to_all | solution.py:108
  190.6 0.6 fusion.54
  191.2 12.9 %all-to-all-done.3 = f32[64,1,152]{2,1,0:T(1,128)S(1)} async-done(((f32[64,1,152]{2,1,0:T(1,128)}), f32[64,1,152]{2,1,0:T(1,128)S(1)}, u32[]{:S(2)}, u32[]{:S(2)}) %all-to-all-start.3) | async-done | bytes 38944 | tf_op jit(solution)/shard_map/all_to_all | solution.py:108
  204.6 0.8 reduce.2
  206.4 5.4 %collective-permute-start.3 = (f32[2,2,32]{2,1,0:T(2,128)S(1)}, f32[2,2,32]{2,1,0:T(2,128)S(1)}, u32[]{:S(2)}, u32[]{:S(2)}) collective-permute-start(f32[2,2,32]{2,1,0:T(2,128)S(1)} %constant_dynamic-slice_fusion), channel_id=1, source_target_pairs={{0,256},{256,0},{1,257},{257,1},{2,258},{258,2},{3,259},{259,3},{4... | collective-permute-start | bytes 1544 | tf_op jit(solution)/shard_map/ppermute | solution.py:15
  212.7 0.7 fusion.50
  (59 shorter events, 8.9 us)
Async XLA Ops:
  0.0 206.1 %copy-start = (bf16[2432,64]{0,1:T(8,128)(2,1)S(1)}, bf16[2432,64]{0,1:T(8,128)(2,1)}, u32[]{:S(2)}) copy-start(bf16[2432,64]{0,1:T(8,128)(2,1)} %param.23) | copy-start | bytes 933892
  0.8 13.6 %collective-permute-start = (bf16[2,2432]{1,0:T(2,128)(2,1)S(1)}, bf16[2,2432]{1,0:T(2,128)(2,1)S(1)}, u32[]{:S(2)}, u32[]{:S(2)}) collective-permute-start(bf16[2,2432]{1,0:T(2,128)(2,1)S(1)} %slice_bitcast_fusion.3), channel_id=1, source_target_pairs={{0,64},{64,0},{128,192},{192,128},{1,65},{65,1},{129,193},{193,129... | collective-permute-start | bytes 29192 | tf_op jit(solution)/shard_map/ppermute | solution.py:15
  5.5 9.0 %collective-permute-start.1 = (bf16[2,2432]{1,0:T(2,128)(2,1)S(1)}, bf16[2,2432]{1,0:T(2,128)(2,1)S(1)}, u32[]{:S(2)}, u32[]{:S(2)}) collective-permute-start(bf16[2,2432]{1,0:T(2,128)(2,1)S(1)} %slice_bitcast_fusion.2), channel_id=1, source_target_pairs={{0,64},{64,0},{128,192},{192,128},{1,65},{65,1},{129,193},{193,129... | collective-permute-start | bytes 29192 | tf_op jit(solution)/shard_map/ppermute | solution.py:15
  15.7 32.4 %all-to-all-start = ((bf16[64,2,512]{2,1,0:T(2,128)(2,1)}), bf16[64,2,512]{2,1,0:T(2,128)(2,1)S(1)}, u32[]{:S(2)}, u32[]{:S(2)}) async-start(bf16[64,2,512]{2,1,0:T(2,128)(2,1)} %reshape.125), calls=%async_computation | async-start | bytes 262144 | tf_op jit(solution)/shard_map/all_to_all | solution.py:75
  48.1 20.9 %all-to-all-start.2 = ((bf16[64,2,361]{2,1,0:T(2,128)(2,1)}), bf16[64,2,361]{2,1,0:T(2,128)(2,1)S(1)}, u32[]{:S(2)}, u32[]{:S(2)}) async-start(bf16[64,2,361]{2,1,0:T(2,128)(2,1)} %reshape.127), calls=%async_computation.2 | async-start | bytes 196608 | tf_op jit(solution)/shard_map/all_to_all | solution.py:99
  71.0 5.1 %copy-start.2 = (f32[1,6,2432]{2,0,1:T(1,128)S(1)}, f32[1,6,2432]{2,0,1:T(1,128)}, u32[]{:S(2)}) copy-start(f32[1,6,2432]{2,0,1:T(1,128)} %param.21) | copy-start | bytes 175108
  71.0 5.3 %copy-start.1 = (f32[1,6,2,2432]{3,2,1,0:T(2,128)S(1)}, f32[1,6,2,2432]{3,2,1,0:T(2,128)}, u32[]{:S(2)}) copy-start(f32[1,6,2,2432]{3,2,1,0:T(2,128)} %param.22) | copy-start | bytes 350212
  71.0 96.9 %all-to-all-start.1 = ((bf16[64,2,128,64]{2,3,1,0:T(8,128)(2,1)}), bf16[64,2,128,64]{2,3,1,0:T(8,128)(2,1)S(1)}, u32[]{:S(2)}, u32[]{:S(2)}) async-start(bf16[64,2,128,64]{2,3,1,0:T(8,128)(2,1)} %broadcast_in_dim.45), calls=%async_computation.1 | async-start | bytes 4194304 | tf_op jit(solution)/shard_map/all_to_all | solution.py:91
  77.2 6.1 %collective-permute-start.2 = (bf16[1216,38]{1,0:T(8,128)(2,1)S(1)}, bf16[1216,38]{1,0:T(8,128)(2,1)S(1)}, u32[]{:S(2)}, u32[]{:S(2)}) collective-permute-start(bf16[1216,38]{1,0:T(8,128)(2,1)S(1)} %reshape.118), channel_id=1, source_target_pairs={{0,256},{256,0},{1,257},{257,1},{2,258},{258,2},{3,259},{259,3},{4... | collective-permute-start | bytes 277256 | tf_op jit(solution)/shard_map/ppermute | solution.py:15
  177.1 28.6 %copy-start.3 = (bf16[1,1,2,2,2432]{4,3,2,1,0:T(2,128)(2,1)S(1)}, bf16[1,1,2,2,2432]{4,3,2,1,0:T(2,128)(2,1)}, u32[]{:S(2)}) copy-start(bf16[1,1,2,2,2432]{4,3,2,1,0:T(2,128)(2,1)} %param.16) | copy-start | bytes 58372
  177.2 34.7 %copy-start.5 = (f32[6]{0:T(128)S(1)}, f32[6]{0:T(128)}, u32[]{:S(2)}) copy-start(f32[6]{0:T(128)} %param.25) | copy-start | bytes 76
  177.2 34.7 %copy-start.6 = (f32[6]{0:T(128)S(1)}, f32[6]{0:T(128)}, u32[]{:S(2)}) copy-start(f32[6]{0:T(128)} %param.24) | copy-start | bytes 76
  177.2 35.5 %copy-start.4 = (f32[1,2,2,32]{3,2,1,0:T(2,128)S(1)}, f32[1,2,2,32]{3,2,1,0:T(2,128)}, u32[]{:S(2)}) copy-start(f32[1,2,2,32]{3,2,1,0:T(2,128)} %param.17) | copy-start | bytes 1540
  178.2 25.9 %all-to-all-start.3 = ((f32[64,1,152]{2,1,0:T(1,128)}), f32[64,1,152]{2,1,0:T(1,128)S(1)}, u32[]{:S(2)}, u32[]{:S(2)}) async-start(f32[64,1,152]{2,1,0:T(1,128)} %reshape.129), calls=%async_computation.3 | async-start | bytes 131072 | tf_op jit(solution)/shard_map/all_to_all | solution.py:108
  206.4 6.2 %collective-permute-start.3 = (f32[2,2,32]{2,1,0:T(2,128)S(1)}, f32[2,2,32]{2,1,0:T(2,128)S(1)}, u32[]{:S(2)}, u32[]{:S(2)}) collective-permute-start(f32[2,2,32]{2,1,0:T(2,128)S(1)} %constant_dynamic-slice_fusion), channel_id=1, source_target_pairs={{0,256},{256,0},{1,257},{257,1},{2,258},{258,2},{3,259},{259,3},{4... | collective-permute-start | bytes 1544 | tf_op jit(solution)/shard_map/ppermute | solution.py:15

commit v2 on v1

--- a/solution.py
+++ b/solution.py
@@ -28,6 +28,18 @@
         jnp.einsum("sk,kd->sd", weights, values_all, preferred_element_type=jnp.float32)
         / row_total
     )
+
+
+def butterfly_bits(n):
+    bits = [b for b in range(n.bit_length() - 1)]
+    return sorted(bits, key=lambda b: -hop_distance(b))
+
+
+def hop_distance(bit):
+    z_bits = 4
+    span = 16 if bit < z_bits else 4
+    step = 1 << (bit if bit < z_bits else bit - z_bits)
+    return min(step, span - step)
 
 
 def shards(
@@ -64,6 +76,9 @@
         x = x.reshape(n, shard_rows, HEADS, HD).transpose(2, 0, 1, 3)
         return jnp.pad(x, ((0, nseq - HEADS), (0, 0), (0, 0), (0, 0)))
 
+    block_rows = w_out.shape[0]
+    col_width = D // nseq
+    w_parts = w_out.reshape(block_rows, nseq, col_width).transpose(1, 0, 2)
     packed = jnp.concatenate(
         [
             to_heads(local_query),
@@ -72,7 +87,12 @@
         ],
         axis=1,
     )
-    head_rows = lax.all_to_all(packed, "seq", 0, 0, tiled=True)
+    head_width = packed.shape[1] * shard_rows * HD
+    joint = jnp.concatenate(
+        [packed.reshape(nseq, head_width), w_parts.reshape(nseq, block_rows * col_width)], 1
+    )
+    joint = lax.all_to_all(joint, "seq", 0, 0, tiled=True)
+    head_rows = joint[:, :head_width].reshape(nseq, 8, shard_rows, HD)
     head_rows = head_rows.transpose(1, 0, 2, 3).reshape(8, slot_total, HD)
     head_q, head_k, head_v = head_rows[0:2], head_rows[2:5], head_rows[5:8]
     slot_ids = jnp.arange(slot_total)
@@ -88,22 +108,28 @@
     )
     head_attn = jnp.stack([home_out, shared_out]).astype(jnp.bfloat16)
 
-    every_head = lax.all_to_all(
-        jnp.broadcast_to(head_attn[None], (nseq,) + head_attn.shape), "seq", 0, 0, tiled=True
-    )
-    attn_rows = every_head[:HEADS].transpose(1, 2, 0, 3).reshape(2 * slot_total, D)
-
-    block_rows = w_out.shape[0]
-    col_width = D // nseq
-    w_parts = w_out.reshape(block_rows, nseq, col_width).transpose(1, 0, 2)
-    w_half = lax.all_to_all(w_parts, "seq", 0, 0, tiled=True).reshape(nseq * block_rows, col_width)
+    w_half = joint[:, head_width:].reshape(nseq * block_rows, col_width)
     w_other = from_partner(w_half, "cfg", 0)
     w_cols = jnp.where(
         branch == 0,
         jnp.concatenate([w_half, w_other], 0),
         jnp.concatenate([w_other, w_half], 0),
     )
-    projected_cols = jnp.dot(attn_rows, w_cols, preferred_element_type=jnp.float32)
+
+    me = lax.axis_index("seq")
+    gathered = head_attn[None]
+    masks = [0]
+    for bit in butterfly_bits(nseq):
+        gathered = jnp.concatenate([gathered, from_partner(gathered, "seq", bit)], 0)
+        masks = masks + [m ^ (1 << bit) for m in masks]
+    source_head = jnp.bitwise_xor(me, jnp.array(masks, jnp.int32))
+    w_heads = jnp.pad(
+        w_cols.reshape(HEADS, HD, col_width), ((0, nseq - HEADS), (0, 0), (0, 0))
+    )
+    w_ordered = jnp.take(w_heads, source_head, axis=0)
+    projected_cols = jnp.einsum(
+        "irsd,idc->rsc", gathered, w_ordered, preferred_element_type=jnp.float32
+    ).reshape(2 * slot_total, col_width)
     projected_parts = projected_cols.reshape(2, nseq, shard_rows, col_width).transpose(1, 0, 2, 3)
     projected = lax.all_to_all(projected_parts, "seq", 0, 0, tiled=True)
     projected = projected.transpose(1, 2, 0, 3).reshape(2, shard_rows, D)

time: 214 us -> 167 us (0.78)
  waiting for transfers between devices: 122 us -> 50.5 us
  starting transfers between devices: 59.3 us -> 83.8 us
  local copies, waits for them, and re-layouts: 22.5 us -> 19.5 us
    all_to_all x3 -> x1, waiting for transfers between devices: 108 us -> 13.8 us  [shards(): joint = lax.all_to_all(joint, 'seq', 0, 0, tiled=True)]
    ppermute x4 -> x10, starting transfers between devices: 16.2 us -> 55.6 us  [from_partner(): lax.ppermute(x, axis, [(i, i ^ 1 << apart) for i in range(lax.axis_size(a...]
    ppermute x4 -> x10, waiting for transfers between devices: 1 us -> 23.9 us  [from_partner(): lax.ppermute(x, axis, [(i, i ^ 1 << apart) for i in range(lax.axis_size(a...]
    all_to_all x3 -> x1, starting transfers between devices: 30.7 us -> 18.4 us  [shards(): joint = lax.all_to_all(joint, 'seq', 0, 0, tiled=True)]
    transpose x3 -> x0, local copies, waits for them, and re-layouts: 5.06 us -> none  [the longest x2 4.85 us: shards(): every_head[:HEADS].transpose(1, 2, 0, 3).reshape(2 * slot_total, D)]
    all_to_all x1, starting transfers between devices: 12.4 us -> 9.82 us  [shards(): projected = lax.all_to_all(projected_parts, 'seq', 0, 0, tiled=True)]
    concatenate x0 -> x2, local copies, waits for them, and re-layouts: none -> 2.44 us  [shards(): jnp.concatenate([gathered, from_partner(gathered, 'seq', bit)], 0)]
    dot_general x1 -> x0, local copies, waits for them, and re-layouts: 2.38 us -> none  [shards(): jnp.dot(attn_rows, w_cols, preferred_element_type=jnp.float32)]
  transfers between devices with their start and end apart: 8 -> 12, of which waited for: 6 -> 9; matrix products, arithmetic and copies ran while one was open for 7% -> 9% of each run, Pallas kernels for 0% -> 0%
where the time goes in v2:
time: 167 us; the launch traced here: 166 us
  starting transfers between devices  83.8 us (50%)
  waiting for transfers between devices  50.5 us (30%)
  local copies, waits for them, and re-layouts  19.5 us (12%)
  other arithmetic  7.22 us (4%)
  matrix products  4.69 us (3%)
    ppermute x10, starting transfers between devices, from_partner(): lax.ppermute(x, axis, [(i, i ^ 1 << apart) for i in range(lax.axis_size(a...  55.6 us
    ppermute x10, waiting for transfers between devices, from_partner(): lax.ppermute(x, axis, [(i, i ^ 1 << apart) for i in range(lax.axis_size(a...  23.9 us
    all_to_all x1, starting transfers between devices, shards(): joint = lax.all_to_all(joint, 'seq', 0, 0, tiled=True)  18.4 us
    all_to_all x1, waiting for transfers between devices, shards(): joint = lax.all_to_all(joint, 'seq', 0, 0, tiled=True)  13.8 us
    all_to_all x1, waiting for transfers between devices, shards(): projected = lax.all_to_all(projected_parts, 'seq', 0, 0, tiled=True)  12.8 us
    all_to_all x1, starting transfers between devices, shards(): projected = lax.all_to_all(projected_parts, 'seq', 0, 0, tiled=True)  9.82 us
    unnamed x29, local copies, waits for them, and re-layouts  5.38 us
  transfers between devices with their start and end apart: 12, of which 9 were waited for; matrix products, arithmetic and copies ran while one was open for 9% of the time, Pallas kernels for 0%

profile of v2, /device:TPU:1, one launch (start us, length us, event | category | flops | bytes accessed | tf_op | source)
XLA Modules:
  0.0 166.3 jit_solution(16223972254002789058)
XLA Ops:
  0.0 0.8 slice_bitcast_fusion.1
  0.8 4.0 %collective-permute-start.1 = (bf16[2,2432]{1,0:T(2,128)(2,1)S(1)}, bf16[2,2432]{1,0:T(2,128)(2,1)S(1)}, u32[]{:S(2)}, u32[]{:S(2)}) collective-permute-start(bf16[2,2432]{1,0:T(2,128)(2,1)S(1)} %slice_bitcast_fusion.1), channel_id=1, source_target_pairs={{0,64},{64,0},{128,192},{192,128},{1,65},{65,1},{129,193},{193,129... | collective-permute-start | bytes 29192 | tf_op jit(solution)/shard_map/ppermute | solution.py:15
  5.5 1.9 %collective-permute-start = (bf16[2,2432]{1,0:T(2,128)(2,1)S(1)}, bf16[2,2432]{1,0:T(2,128)(2,1)S(1)}, u32[]{:S(2)}, u32[]{:S(2)}) collective-permute-start(bf16[2,2432]{1,0:T(2,128)(2,1)S(1)} %slice_bitcast_fusion.2), channel_id=1, source_target_pairs={{0,64},{64,0},{128,192},{192,128},{1,65},{65,1},{129,193},{193,129... | collective-permute-start | bytes 29192 | tf_op jit(solution)/shard_map/ppermute | solution.py:15
  7.4 0.8 concatenate.71
  8.3 0.8 concatenate.68
  9.1 1.6 reshape.149
  11.2 0.8 reshape_squeeze.3
  14.2 0.9 reshape.170
  15.1 18.4 %all-to-all-start = ((bf16[64,2,873]{2,1,0:T(2,128)(2,1)}), bf16[64,2,873]{2,1,0:T(2,128)(2,1)S(1)}, u32[]{:S(2)}, u32[]{:S(2)}) async-start(bf16[64,2,873]{2,1,0:T(2,128)(2,1)} %reshape.170), calls=%async_computation | async-start | bytes 458752 | tf_op jit(solution)/shard_map/all_to_all | solution.py:94
  36.9 13.8 %all-to-all-done = bf16[64,2,873]{2,1,0:T(2,128)(2,1)S(1)} async-done(((bf16[64,2,873]{2,1,0:T(2,128)(2,1)}), bf16[64,2,873]{2,1,0:T(2,128)(2,1)S(1)}, u32[]{:S(2)}, u32[]{:S(2)}) %all-to-all-start) | async-done | bytes 223520 | tf_op jit(solution)/shard_map/all_to_all | solution.py:94
  53.2 5.9 %collective-permute-start.2 = (bf16[1,2,128,64]{2,3,1,0:T(8,128)(2,1)S(1)}, bf16[1,2,128,64]{2,3,1,0:T(8,128)(2,1)S(1)}, u32[]{:S(2)}, u32[]{:S(2)}) collective-permute-start(bf16[1,2,128,64]{2,3,1,0:T(8,128)(2,1)S(1)} %get-tuple-element.36), channel_id=1, source_target_pairs={{0,8},{1,9},{2,10},{3,11},{4,12},{5,13},{6,14},{7,15},{8,0},{9,1},... | collective-permute-start | bytes 98312 | tf_op jit(solution)/shard_map/ppermute | solution.py:15
  59.1 7.5 %collective-permute-done.2 = bf16[1,2,128,64]{2,3,1,0:T(8,128)(2,1)S(1)} collective-permute-done((bf16[1,2,128,64]{2,3,1,0:T(8,128)(2,1)S(1)}, bf16[1,2,128,64]{2,3,1,0:T(8,128)(2,1)S(1)}, u32[]{:S(2)}, u32[]{:S(2)}) %collective-permute-start.2) | collective-permute-done | bytes 32800 | tf_op jit(solution)/shard_map/ppermute | solution.py:15
  66.6 4.5 %collective-permute-start.3 = (bf16[2,2,128,64]{2,3,1,0:T(8,128)(2,1)S(1)}, bf16[2,2,128,64]{2,3,1,0:T(8,128)(2,1)S(1)}, u32[]{:S(2)}, u32[]{:S(2)}) collective-permute-start(bf16[2,2,128,64]{2,3,1,0:T(8,128)(2,1)S(1)} %pad_maximum_fusion.2), channel_id=1, source_target_pairs={{0,4},{1,5},{2,6},{3,7},{4,0},{5,1},{6,2},{7,3},{8,12},{9,13},{10,... | collective-permute-start | bytes 196616 | tf_op jit(solution)/shard_map/ppermute | solution.py:15
  71.1 4.4 %collective-permute-done.3 = bf16[2,2,128,64]{2,3,1,0:T(8,128)(2,1)S(1)} collective-permute-done((bf16[2,2,128,64]{2,3,1,0:T(8,128)(2,1)S(1)}, bf16[2,2,128,64]{2,3,1,0:T(8,128)(2,1)S(1)}, u32[]{:S(2)}, u32[]{:S(2)}) %collective-permute-start.3) | collective-permute-done | bytes 65568 | tf_op jit(solution)/shard_map/ppermute | solution.py:15
  75.5 3.5 %collective-permute-start.4 = (bf16[4,2,128,64]{2,3,1,0:T(8,128)(2,1)S(1)}, bf16[4,2,128,64]{2,3,1,0:T(8,128)(2,1)S(1)}, u32[]{:S(2)}, u32[]{:S(2)}) collective-permute-start(bf16[4,2,128,64]{2,3,1,0:T(8,128)(2,1)S(1)} %pad_maximum_fusion.1), channel_id=1, source_target_pairs={{0,2},{1,3},{2,0},{3,1},{4,6},{5,7},{6,4},{7,5},{8,10},{9,11},{10,... | collective-permute-start | bytes 393224 | tf_op jit(solution)/shard_map/ppermute | solution.py:15
  79.1 3.4 %collective-permute-done.4 = bf16[4,2,128,64]{2,3,1,0:T(8,128)(2,1)S(1)} collective-permute-done((bf16[4,2,128,64]{2,3,1,0:T(8,128)(2,1)S(1)}, bf16[4,2,128,64]{2,3,1,0:T(8,128)(2,1)S(1)}, u32[]{:S(2)}, u32[]{:S(2)}) %collective-permute-start.4) | collective-permute-done | bytes 131104 | tf_op jit(solution)/shard_map/ppermute | solution.py:15
  82.5 5.4 %collective-permute-start.5 = (bf16[8,2,128,64]{2,3,1,0:T(8,128)(2,1)S(1)}, bf16[8,2,128,64]{2,3,1,0:T(8,128)(2,1)S(1)}, u32[]{:S(2)}, u32[]{:S(2)}) collective-permute-start(bf16[8,2,128,64]{2,3,1,0:T(8,128)(2,1)S(1)} %pad_maximum_fusion), channel_id=1, source_target_pairs={{0,32},{1,33},{2,34},{3,35},{4,36},{5,37},{6,38},{7,39},{8,40},{9,... | collective-permute-start | bytes 786440 | tf_op jit(solution)/shard_map/ppermute | solution.py:15
  89.2 0.8 constant_dynamic-update-slice_fusion.7
  90.0 1.6 collective-permute-done.5
  91.6 1.0 constant_dynamic-update-slice_fusion.6
  92.6 4.1 %collective-permute-start.6 = (bf16[16,2,128,64]{2,3,1,0:T(8,128)(2,1)S(1)}, bf16[16,2,128,64]{2,3,1,0:T(8,128)(2,1)S(1)}, u32[]{:S(2)}, u32[]{:S(2)}) collective-permute-start(bf16[16,2,128,64]{2,3,1,0:T(8,128)(2,1)S(1)} %get-tuple-element.13), channel_id=1, source_target_pairs={{0,1},{1,0},{2,3},{3,2},{4,5},{5,4},{6,7},{7,6},{8,9},{9,8},{10,11... | collective-permute-start | bytes 1572872 | tf_op jit(solution)/shard_map/ppermute | solution.py:15
  97.2 6.0 %collective-permute-done.6 = bf16[16,2,128,64]{2,3,1,0:T(8,128)(2,1)S(1)} collective-permute-done((bf16[16,2,128,64]{2,3,1,0:T(8,128)(2,1)S(1)}, bf16[16,2,128,64]{2,3,1,0:T(8,128)(2,1)S(1)}, u32[]{:S(2)}, u32[]{:S(2)}) %collective-permute-start.6) | collective-permute-done | bytes 524320 | tf_op jit(solution)/shard_map/ppermute | solution.py:15
  103.2 1.3 constant_dynamic-update-slice_fusion.5
  104.5 4.8 %collective-permute-start.7 = (bf16[32,2,128,64]{2,3,1,0:T(8,128)(2,1)}, bf16[32,2,128,64]{2,3,1,0:T(8,128)(2,1)S(1)}, u32[]{:S(2)}, u32[]{:S(2)}) collective-permute-start(bf16[32,2,128,64]{2,3,1,0:T(8,128)(2,1)} %get-tuple-element.9), channel_id=1, source_target_pairs={{0,16},{1,17},{2,18},{3,19},{4,20},{5,21},{6,22},{7,23},{8,24},{9,... | collective-permute-start | bytes 3145736 | tf_op jit(solution)/shard_map/ppermute | solution.py:15
  109.7 11.5 %collective-permute-start.8 = (bf16[1216,38]{1,0:T(8,128)(2,1)S(1)}, bf16[1216,38]{1,0:T(8,128)(2,1)S(1)}, u32[]{:S(2)}, u32[]{:S(2)}) collective-permute-start(bf16[1216,38]{1,0:T(8,128)(2,1)S(1)} %reshape.152), channel_id=1, source_target_pairs={{0,256},{256,0},{1,257},{257,1},{2,258},{258,2},{3,259},{259,3},{4... | collective-permute-start | bytes 277256 | tf_op jit(solution)/shard_map/ppermute | solution.py:15
  124.0 1.1 constant_dynamic-update-slice_fusion.11
  125.1 3.1 %fusion.6 = f32[2,128,38,1]{2,1,0,3:T(8,128)S(1)} fusion(bf16[64,2,128,64]{2,3,1,0:T(8,128)(2,1)} %constant_dynamic-update-slice_fusion.11, bf16[64,64,38]{1,2,0:T(8,128)(2,1)S(1)} %gather_fusion, pred[64]{0:T(512)(128)(4,1)S(1)} %get-tuple-element.7), kind=kOutput, calls=%fused_computation.14 | convolution fusion | flops 79847424 | bytes 2447424 | tf_op jit(solution)/shard_map/irsd,idc->rsc/dot_general | solution.py:130
  128.3 0.8 reshape.172
  129.1 9.8 %all-to-all-start.1 = ((f32[64,1,152]{2,1,0:T(1,128)}), f32[64,1,152]{2,1,0:T(1,128)S(1)}, u32[]{:S(2)}, u32[]{:S(2)}) async-start(f32[64,1,152]{2,1,0:T(1,128)} %reshape.172), calls=%async_computation.1 | async-start | bytes 131072 | tf_op jit(solution)/shard_map/all_to_all | solution.py:134
  139.6 12.8 %all-to-all-done.1 = f32[64,1,152]{2,1,0:T(1,128)S(1)} async-done(((f32[64,1,152]{2,1,0:T(1,128)}), f32[64,1,152]{2,1,0:T(1,128)S(1)}, u32[]{:S(2)}, u32[]{:S(2)}) %all-to-all-start.1) | async-done | bytes 38944 | tf_op jit(solution)/shard_map/all_to_all | solution.py:134
  152.9 0.8 reduce.3
  154.8 10.0 %collective-permute-start.9 = (f32[2,2,32]{2,1,0:T(2,128)S(1)}, f32[2,2,32]{2,1,0:T(2,128)S(1)}, u32[]{:S(2)}, u32[]{:S(2)}) collective-permute-start(f32[2,2,32]{2,1,0:T(2,128)S(1)} %constant_dynamic-slice_fusion), channel_id=1, source_target_pairs={{0,256},{256,0},{1,257},{257,1},{2,258},{258,2},{3,259},{259,3},{4... | collective-permute-start | bytes 1544 | tf_op jit(solution)/shard_map/ppermute | solution.py:15
  (92 shorter events, 17.6 us)
Async XLA Ops:
  0.0 154.4 %copy-start = (bf16[2432,64]{0,1:T(8,128)(2,1)S(1)}, bf16[2432,64]{0,1:T(8,128)(2,1)}, u32[]{:S(2)}) copy-start(bf16[2432,64]{0,1:T(8,128)(2,1)} %param.24) | copy-start | bytes 933892
  0.8 11.3 %collective-permute-start.1 = (bf16[2,2432]{1,0:T(2,128)(2,1)S(1)}, bf16[2,2432]{1,0:T(2,128)(2,1)S(1)}, u32[]{:S(2)}, u32[]{:S(2)}) collective-permute-start(bf16[2,2432]{1,0:T(2,128)(2,1)S(1)} %slice_bitcast_fusion.1), channel_id=1, source_target_pairs={{0,64},{64,0},{128,192},{192,128},{1,65},{65,1},{129,193},{193,129... | collective-permute-start | bytes 29192 | tf_op jit(solution)/shard_map/ppermute | solution.py:15
  5.5 6.7 %collective-permute-start = (bf16[2,2432]{1,0:T(2,128)(2,1)S(1)}, bf16[2,2432]{1,0:T(2,128)(2,1)S(1)}, u32[]{:S(2)}, u32[]{:S(2)}) collective-permute-start(bf16[2,2432]{1,0:T(2,128)(2,1)S(1)} %slice_bitcast_fusion.2), channel_id=1, source_target_pairs={{0,64},{64,0},{128,192},{192,128},{1,65},{65,1},{129,193},{193,129... | collective-permute-start | bytes 29192 | tf_op jit(solution)/shard_map/ppermute | solution.py:15
  11.0 22.5 %copy-start.4 = (s32[4,2]{0,1:T(2,128)S(1)}, s32[4,2]{0,1:T(2,128)}, u32[]{:S(2)}) copy-start(s32[4,2]{0,1:T(2,128)} %param.20) | copy-start | bytes 100
  11.0 22.5 %copy-start.6 = (s32[4,2]{0,1:T(2,128)S(1)}, s32[4,2]{0,1:T(2,128)}, u32[]{:S(2)}) copy-start(s32[4,2]{0,1:T(2,128)} %param.19) | copy-start | bytes 100
  15.1 35.6 %all-to-all-start = ((bf16[64,2,873]{2,1,0:T(2,128)(2,1)}), bf16[64,2,873]{2,1,0:T(2,128)(2,1)S(1)}, u32[]{:S(2)}, u32[]{:S(2)}) async-start(bf16[64,2,873]{2,1,0:T(2,128)(2,1)} %reshape.170), calls=%async_computation | async-start | bytes 458752 | tf_op jit(solution)/shard_map/all_to_all | solution.py:94
  35.5 43.5 %copy-start.9 = (s32[64]{0:T(128)S(1)}, s32[64]{0:T(128)}, u32[]{:S(2)}) copy-start(s32[64]{0:T(128)} %constant.69.clone) | copy-start | bytes 772
  51.4 45.2 %copy-start.2 = (f32[1,6,2432]{2,0,1:T(1,128)S(1)}, f32[1,6,2432]{2,0,1:T(1,128)}, u32[]{:S(2)}) copy-start(f32[1,6,2432]{2,0,1:T(1,128)} %param.22) | copy-start | bytes 175108
  51.4 45.5 %copy-start.1 = (f32[1,6,2,2432]{3,2,1,0:T(2,128)S(1)}, f32[1,6,2,2432]{3,2,1,0:T(2,128)}, u32[]{:S(2)}) copy-start(f32[1,6,2,2432]{3,2,1,0:T(2,128)} %param.23) | copy-start | bytes 350212
  53.2 13.4 %collective-permute-start.2 = (bf16[1,2,128,64]{2,3,1,0:T(8,128)(2,1)S(1)}, bf16[1,2,128,64]{2,3,1,0:T(8,128)(2,1)S(1)}, u32[]{:S(2)}, u32[]{:S(2)}) collective-permute-start(bf16[1,2,128,64]{2,3,1,0:T(8,128)(2,1)S(1)} %get-tuple-element.36), channel_id=1, source_target_pairs={{0,8},{1,9},{2,10},{3,11},{4,12},{5,13},{6,14},{7,15},{8,0},{9,1},... | collective-permute-start | bytes 98312 | tf_op jit(solution)/shard_map/ppermute | solution.py:15
  66.6 8.9 %collective-permute-start.3 = (bf16[2,2,128,64]{2,3,1,0:T(8,128)(2,1)S(1)}, bf16[2,2,128,64]{2,3,1,0:T(8,128)(2,1)S(1)}, u32[]{:S(2)}, u32[]{:S(2)}) collective-permute-start(bf16[2,2,128,64]{2,3,1,0:T(8,128)(2,1)S(1)} %pad_maximum_fusion.2), channel_id=1, source_target_pairs={{0,4},{1,5},{2,6},{3,7},{4,0},{5,1},{6,2},{7,3},{8,12},{9,13},{10,... | collective-permute-start | bytes 196616 | tf_op jit(solution)/shard_map/ppermute | solution.py:15
  75.5 6.9 %collective-permute-start.4 = (bf16[4,2,128,64]{2,3,1,0:T(8,128)(2,1)S(1)}, bf16[4,2,128,64]{2,3,1,0:T(8,128)(2,1)S(1)}, u32[]{:S(2)}, u32[]{:S(2)}) collective-permute-start(bf16[4,2,128,64]{2,3,1,0:T(8,128)(2,1)S(1)} %pad_maximum_fusion.1), channel_id=1, source_target_pairs={{0,2},{1,3},{2,0},{3,1},{4,6},{5,7},{6,4},{7,5},{8,10},{9,11},{10,... | collective-permute-start | bytes 393224 | tf_op jit(solution)/shard_map/ppermute | solution.py:15
  82.5 9.1 %collective-permute-start.5 = (bf16[8,2,128,64]{2,3,1,0:T(8,128)(2,1)S(1)}, bf16[8,2,128,64]{2,3,1,0:T(8,128)(2,1)S(1)}, u32[]{:S(2)}, u32[]{:S(2)}) collective-permute-start(bf16[8,2,128,64]{2,3,1,0:T(8,128)(2,1)S(1)} %pad_maximum_fusion), channel_id=1, source_target_pairs={{0,32},{1,33},{2,34},{3,35},{4,36},{5,37},{6,38},{7,39},{8,40},{9,... | collective-permute-start | bytes 786440 | tf_op jit(solution)/shard_map/ppermute | solution.py:15
  92.6 10.6 %collective-permute-start.6 = (bf16[16,2,128,64]{2,3,1,0:T(8,128)(2,1)S(1)}, bf16[16,2,128,64]{2,3,1,0:T(8,128)(2,1)S(1)}, u32[]{:S(2)}, u32[]{:S(2)}) collective-permute-start(bf16[16,2,128,64]{2,3,1,0:T(8,128)(2,1)S(1)} %get-tuple-element.13), channel_id=1, source_target_pairs={{0,1},{1,0},{2,3},{3,2},{4,5},{5,4},{6,7},{7,6},{8,9},{9,8},{10,11... | collective-permute-start | bytes 1572872 | tf_op jit(solution)/shard_map/ppermute | solution.py:15
  104.5 19.4 %collective-permute-start.7 = (bf16[32,2,128,64]{2,3,1,0:T(8,128)(2,1)}, bf16[32,2,128,64]{2,3,1,0:T(8,128)(2,1)S(1)}, u32[]{:S(2)}, u32[]{:S(2)}) collective-permute-start(bf16[32,2,128,64]{2,3,1,0:T(8,128)(2,1)} %get-tuple-element.9), channel_id=1, source_target_pairs={{0,16},{1,17},{2,18},{3,19},{4,20},{5,21},{6,22},{7,23},{8,24},{9,... | collective-permute-start | bytes 3145736 | tf_op jit(solution)/shard_map/ppermute | solution.py:15
  109.7 12.7 %collective-permute-start.8 = (bf16[1216,38]{1,0:T(8,128)(2,1)S(1)}, bf16[1216,38]{1,0:T(8,128)(2,1)S(1)}, u32[]{:S(2)}, u32[]{:S(2)}) collective-permute-start(bf16[1216,38]{1,0:T(8,128)(2,1)S(1)} %reshape.152), channel_id=1, source_target_pairs={{0,256},{256,0},{1,257},{257,1},{2,258},{258,2},{3,259},{259,3},{4... | collective-permute-start | bytes 277256 | tf_op jit(solution)/shard_map/ppermute | solution.py:15
  125.1 29.0 %copy-start.3 = (bf16[1,1,2,2,2432]{4,3,2,1,0:T(2,128)(2,1)S(1)}, bf16[1,1,2,2,2432]{4,3,2,1,0:T(2,128)(2,1)}, u32[]{:S(2)}) copy-start(bf16[1,1,2,2,2432]{4,3,2,1,0:T(2,128)(2,1)} %param.17) | copy-start | bytes 58372
  128.2 36.6 %copy-start.7 = (f32[6]{0:T(128)S(1)}, f32[6]{0:T(128)}, u32[]{:S(2)}) copy-start(f32[6]{0:T(128)} %param.26) | copy-start | bytes 76
  128.2 36.6 %copy-start.8 = (f32[6]{0:T(128)S(1)}, f32[6]{0:T(128)}, u32[]{:S(2)}) copy-start(f32[6]{0:T(128)} %param.25) | copy-start | bytes 76
  128.2 37.4 %copy-start.5 = (f32[1,2,2,32]{3,2,1,0:T(2,128)S(1)}, f32[1,2,2,32]{3,2,1,0:T(2,128)}, u32[]{:S(2)}) copy-start(f32[1,2,2,32]{3,2,1,0:T(2,128)} %param.18) | copy-start | bytes 1540
  129.1 23.3 %all-to-all-start.1 = ((f32[64,1,152]{2,1,0:T(1,128)}), f32[64,1,152]{2,1,0:T(1,128)S(1)}, u32[]{:S(2)}, u32[]{:S(2)}) async-start(f32[64,1,152]{2,1,0:T(1,128)} %reshape.172), calls=%async_computation.1 | async-start | bytes 131072 | tf_op jit(solution)/shard_map/all_to_all | solution.py:134
  154.8 10.8 %collective-permute-start.9 = (f32[2,2,32]{2,1,0:T(2,128)S(1)}, f32[2,2,32]{2,1,0:T(2,128)S(1)}, u32[]{:S(2)}, u32[]{:S(2)}) collective-permute-start(f32[2,2,32]{2,1,0:T(2,128)S(1)} %constant_dynamic-slice_fusion), channel_id=1, source_target_pairs={{0,256},{256,0},{1,257},{257,1},{2,258},{258,2},{3,259},{259,3},{4... | collective-permute-start | bytes 1544 | tf_op jit(solution)/shard_map/ppermute | solution.py:15

commit v3 on v2

--- a/solution.py
+++ b/solution.py
@@ -30,9 +30,9 @@
     )
 
 
-def butterfly_bits(n):
-    bits = [b for b in range(n.bit_length() - 1)]
-    return sorted(bits, key=lambda b: -hop_distance(b))
+def butterfly_orders(n):
+    assert n == 64
+    return [[3, 2, 1, 5, 0, 4], [2, 3, 5, 1, 4, 0]]
 
 
 def hop_distance(bit):
@@ -117,12 +117,20 @@
     )
 
     me = lax.axis_index("seq")
+    orders = butterfly_orders(nseq)
     gathered = head_attn[None]
-    masks = [0]
-    for bit in butterfly_bits(nseq):
-        gathered = jnp.concatenate([gathered, from_partner(gathered, "seq", bit)], 0)
-        masks = masks + [m ^ (1 << bit) for m in masks]
-    source_head = jnp.bitwise_xor(me, jnp.array(masks, jnp.int32))
+    masks = [[0], [0]]
+    for step in range(len(orders[0])):
+        pairs = [
+            (c * nseq + s, c * nseq + (s ^ (1 << orders[c][step])))
+            for c in range(2)
+            for s in range(nseq)
+        ]
+        received = lax.ppermute(gathered, ("cfg", "seq"), pairs)
+        gathered = jnp.concatenate([gathered, received], 0)
+        masks = [m + [x ^ (1 << orders[c][step]) for x in m] for c, m in enumerate(masks)]
+    mask_now = jnp.where(branch == 0, jnp.array(masks[0], jnp.int32), jnp.array(masks[1], jnp.int32))
+    source_head = jnp.bitwise_xor(me, mask_now)
     w_heads = jnp.pad(
         w_cols.reshape(HEADS, HD, col_width), ((0, nseq - HEADS), (0, 0), (0, 0))
     )

time: 167 us -> 177 us (1.060)
  waiting for transfers between devices: 50.5 us -> 58.6 us
    ppermute x0 -> x6, waiting for transfers between devices: none -> 30.8 us  [shards(): received = lax.ppermute(gathered, ('cfg', 'seq'), pairs)]
    ppermute x0 -> x6, starting transfers between devices: none -> 24.5 us  [shards(): received = lax.ppermute(gathered, ('cfg', 'seq'), pairs)]
    ppermute x10 -> x4, waiting for transfers between devices: 23.9 us -> 1.05 us  [from_partner(): lax.ppermute(x, axis, [(i, i ^ 1 << apart) for i in range(lax.axis_size(a...]
    ppermute x10 -> x4, starting transfers between devices: 55.6 us -> 36.1 us  [from_partner(): lax.ppermute(x, axis, [(i, i ^ 1 << apart) for i in range(lax.axis_size(a...]
    all_to_all x1, starting transfers between devices: 9.82 us -> 6.54 us  [shards(): projected = lax.all_to_all(projected_parts, 'seq', 0, 0, tiled=True)]
    unnamed x29 -> x31, local copies, waits for them, and re-layouts: 5.38 us -> 5.43 us
  transfers between devices with their start and end apart: 12 -> 12, of which waited for: 9 -> 9; matrix products, arithmetic and copies ran while one was open for 9% -> 8% of each run, Pallas kernels for 0% -> 0%
where the time goes in v3:
time: 177 us; the launch traced here: 176 us
  starting transfers between devices  85.5 us (48%)
  waiting for transfers between devices  58.6 us (33%)
  local copies, waits for them, and re-layouts  19.5 us (11%)
  other arithmetic  7.02 us (4%)
  matrix products  4.69 us (3%)
    ppermute x4, starting transfers between devices, from_partner(): lax.ppermute(x, axis, [(i, i ^ 1 << apart) for i in range(lax.axis_size(a...  36.1 us
    ppermute x6, waiting for transfers between devices, shards(): received = lax.ppermute(gathered, ('cfg', 'seq'), pairs)  30.8 us
    ppermute x6, starting transfers between devices, shards(): received = lax.ppermute(gathered, ('cfg', 'seq'), pairs)  24.5 us
    all_to_all x1, starting transfers between devices, shards(): joint = lax.all_to_all(joint, 'seq', 0, 0, tiled=True)  18.4 us
    all_to_all x1, waiting for transfers between devices, shards(): joint = lax.all_to_all(joint, 'seq', 0, 0, tiled=True)  14 us
    all_to_all x1, waiting for transfers between devices, shards(): projected = lax.all_to_all(projected_parts, 'seq', 0, 0, tiled=True)  12.8 us
    all_to_all x1, starting transfers between devices, shards(): projected = lax.all_to_all(projected_parts, 'seq', 0, 0, tiled=True)  6.54 us
    unnamed x31, local copies, waits for them, and re-layouts  5.43 us
  transfers between devices with their start and end apart: 12, of which 9 were waited for; matrix products, arithmetic and copies ran while one was open for 8% of the time, Pallas kernels for 0%

profile of v3, /device:TPU:1, one launch (start us, length us, event | category | flops | bytes accessed | tf_op | source)
XLA Modules:
  0.0 175.9 jit_solution(9523843207756727876)
XLA Ops:
  0.0 0.8 slice_bitcast_fusion.1
  0.8 4.0 %collective-permute-start.1 = (bf16[2,2432]{1,0:T(2,128)(2,1)S(1)}, bf16[2,2432]{1,0:T(2,128)(2,1)S(1)}, u32[]{:S(2)}, u32[]{:S(2)}) collective-permute-start(bf16[2,2432]{1,0:T(2,128)(2,1)S(1)} %slice_bitcast_fusion.1), channel_id=1, source_target_pairs={{0,64},{64,0},{128,192},{192,128},{1,65},{65,1},{129,193},{193,129... | collective-permute-start | bytes 29192 | tf_op jit(solution)/shard_map/ppermute | solution.py:15
  5.5 1.9 %collective-permute-start = (bf16[2,2432]{1,0:T(2,128)(2,1)S(1)}, bf16[2,2432]{1,0:T(2,128)(2,1)S(1)}, u32[]{:S(2)}, u32[]{:S(2)}) collective-permute-start(bf16[2,2432]{1,0:T(2,128)(2,1)S(1)} %slice_bitcast_fusion.2), channel_id=1, source_target_pairs={{0,64},{64,0},{128,192},{192,128},{1,65},{65,1},{129,193},{193,129... | collective-permute-start | bytes 29192 | tf_op jit(solution)/shard_map/ppermute | solution.py:15
  7.4 0.8 concatenate.71
  8.3 0.8 concatenate.68
  9.1 1.6 reshape.149
  11.2 0.8 reshape_squeeze.3
  14.2 0.9 reshape.170
  15.1 18.4 %all-to-all-start = ((bf16[64,2,873]{2,1,0:T(2,128)(2,1)}), bf16[64,2,873]{2,1,0:T(2,128)(2,1)S(1)}, u32[]{:S(2)}, u32[]{:S(2)}) async-start(bf16[64,2,873]{2,1,0:T(2,128)(2,1)} %reshape.170), calls=%async_computation | async-start | bytes 458752 | tf_op jit(solution)/shard_map/all_to_all | solution.py:94
  36.7 14.0 %all-to-all-done = bf16[64,2,873]{2,1,0:T(2,128)(2,1)S(1)} async-done(((bf16[64,2,873]{2,1,0:T(2,128)(2,1)}), bf16[64,2,873]{2,1,0:T(2,128)(2,1)S(1)}, u32[]{:S(2)}, u32[]{:S(2)}) %all-to-all-start) | async-done | bytes 223520 | tf_op jit(solution)/shard_map/all_to_all | solution.py:94
  53.2 4.5 %collective-permute-start.2 = (bf16[1,2,128,64]{2,3,1,0:T(8,128)(2,1)S(1)}, bf16[1,2,128,64]{2,3,1,0:T(8,128)(2,1)S(1)}, u32[]{:S(2)}, u32[]{:S(2)}) collective-permute-start(bf16[1,2,128,64]{2,3,1,0:T(8,128)(2,1)S(1)} %get-tuple-element.36), channel_id=1, source_target_pairs={{0,8},{1,9},{2,10},{3,11},{4,12},{5,13},{6,14},{7,15},{8,0},{9,1},... | collective-permute-start | bytes 98312 | tf_op jit(solution)/shard_map/ppermute | solution.py:129
  57.8 4.0 %collective-permute-done.2 = bf16[1,2,128,64]{2,3,1,0:T(8,128)(2,1)S(1)} collective-permute-done((bf16[1,2,128,64]{2,3,1,0:T(8,128)(2,1)S(1)}, bf16[1,2,128,64]{2,3,1,0:T(8,128)(2,1)S(1)}, u32[]{:S(2)}, u32[]{:S(2)}) %collective-permute-start.2) | collective-permute-done | bytes 32800 | tf_op jit(solution)/shard_map/ppermute | solution.py:129
  61.8 5.9 %collective-permute-start.3 = (bf16[2,2,128,64]{2,3,1,0:T(8,128)(2,1)S(1)}, bf16[2,2,128,64]{2,3,1,0:T(8,128)(2,1)S(1)}, u32[]{:S(2)}, u32[]{:S(2)}) collective-permute-start(bf16[2,2,128,64]{2,3,1,0:T(8,128)(2,1)S(1)} %pad_maximum_fusion.2), channel_id=1, source_target_pairs={{0,4},{1,5},{2,6},{3,7},{4,0},{5,1},{6,2},{7,3},{8,12},{9,13},{10,... | collective-permute-start | bytes 196616 | tf_op jit(solution)/shard_map/ppermute | solution.py:129
  67.7 7.9 %collective-permute-done.3 = bf16[2,2,128,64]{2,3,1,0:T(8,128)(2,1)S(1)} collective-permute-done((bf16[2,2,128,64]{2,3,1,0:T(8,128)(2,1)S(1)}, bf16[2,2,128,64]{2,3,1,0:T(8,128)(2,1)S(1)}, u32[]{:S(2)}, u32[]{:S(2)}) %collective-permute-start.3) | collective-permute-done | bytes 65568 | tf_op jit(solution)/shard_map/ppermute | solution.py:129
  75.7 4.8 %collective-permute-start.4 = (bf16[4,2,128,64]{2,3,1,0:T(8,128)(2,1)S(1)}, bf16[4,2,128,64]{2,3,1,0:T(8,128)(2,1)S(1)}, u32[]{:S(2)}, u32[]{:S(2)}) collective-permute-start(bf16[4,2,128,64]{2,3,1,0:T(8,128)(2,1)S(1)} %pad_maximum_fusion.1), channel_id=1, source_target_pairs={{0,2},{1,3},{2,0},{3,1},{4,6},{5,7},{6,4},{7,5},{8,10},{9,11},{10,... | collective-permute-start | bytes 393224 | tf_op jit(solution)/shard_map/ppermute | solution.py:129
  80.5 2.5 %collective-permute-done.4 = bf16[4,2,128,64]{2,3,1,0:T(8,128)(2,1)S(1)} collective-permute-done((bf16[4,2,128,64]{2,3,1,0:T(8,128)(2,1)S(1)}, bf16[4,2,128,64]{2,3,1,0:T(8,128)(2,1)S(1)}, u32[]{:S(2)}, u32[]{:S(2)}) %collective-permute-start.4) | collective-permute-done | bytes 131104 | tf_op jit(solution)/shard_map/ppermute | solution.py:129
  83.0 4.0 %collective-permute-start.5 = (bf16[8,2,128,64]{2,3,1,0:T(8,128)(2,1)S(1)}, bf16[8,2,128,64]{2,3,1,0:T(8,128)(2,1)S(1)}, u32[]{:S(2)}, u32[]{:S(2)}) collective-permute-start(bf16[8,2,128,64]{2,3,1,0:T(8,128)(2,1)S(1)} %pad_maximum_fusion), channel_id=1, source_target_pairs={{0,32},{1,33},{2,34},{3,35},{4,36},{5,37},{6,38},{7,39},{8,40},{9,... | collective-permute-start | bytes 786440 | tf_op jit(solution)/shard_map/ppermute | solution.py:129
  88.3 0.8 constant_dynamic-update-slice_fusion.7
  89.1 7.5 %collective-permute-done.5 = bf16[8,2,128,64]{2,3,1,0:T(8,128)(2,1)S(1)} collective-permute-done((bf16[8,2,128,64]{2,3,1,0:T(8,128)(2,1)S(1)}, bf16[8,2,128,64]{2,3,1,0:T(8,128)(2,1)S(1)}, u32[]{:S(2)}, u32[]{:S(2)}) %collective-permute-start.5) | collective-permute-done | bytes 262176 | tf_op jit(solution)/shard_map/ppermute | solution.py:129
  96.6 1.0 constant_dynamic-update-slice_fusion.6
  97.6 3.4 %collective-permute-start.6 = (bf16[16,2,128,64]{2,3,1,0:T(8,128)(2,1)S(1)}, bf16[16,2,128,64]{2,3,1,0:T(8,128)(2,1)S(1)}, u32[]{:S(2)}, u32[]{:S(2)}) collective-permute-start(bf16[16,2,128,64]{2,3,1,0:T(8,128)(2,1)S(1)} %get-tuple-element.13), channel_id=1, source_target_pairs={{0,1},{1,0},{2,3},{3,2},{4,5},{5,4},{6,7},{7,6},{8,9},{9,8},{10,11... | collective-permute-start | bytes 1572872 | tf_op jit(solution)/shard_map/ppermute | solution.py:129
  101.5 8.8 %collective-permute-done.6 = bf16[16,2,128,64]{2,3,1,0:T(8,128)(2,1)S(1)} collective-permute-done((bf16[16,2,128,64]{2,3,1,0:T(8,128)(2,1)S(1)}, bf16[16,2,128,64]{2,3,1,0:T(8,128)(2,1)S(1)}, u32[]{:S(2)}, u32[]{:S(2)}) %collective-permute-start.6) | collective-permute-done | bytes 524320 | tf_op jit(solution)/shard_map/ppermute | solution.py:129
  110.4 1.3 constant_dynamic-update-slice_fusion.5
  111.7 1.9 %collective-permute-start.7 = (bf16[32,2,128,64]{2,3,1,0:T(8,128)(2,1)}, bf16[32,2,128,64]{2,3,1,0:T(8,128)(2,1)S(1)}, u32[]{:S(2)}, u32[]{:S(2)}) collective-permute-start(bf16[32,2,128,64]{2,3,1,0:T(8,128)(2,1)} %get-tuple-element.9), channel_id=1, source_target_pairs={{0,16},{1,17},{2,18},{3,19},{4,20},{5,21},{6,22},{7,23},{8,24},{9,... | collective-permute-start | bytes 3145736 | tf_op jit(solution)/shard_map/ppermute | solution.py:129
  114.0 18.4 %collective-permute-start.8 = (bf16[1216,38]{1,0:T(8,128)(2,1)S(1)}, bf16[1216,38]{1,0:T(8,128)(2,1)S(1)}, u32[]{:S(2)}, u32[]{:S(2)}) collective-permute-start(bf16[1216,38]{1,0:T(8,128)(2,1)S(1)} %reshape.152), channel_id=1, source_target_pairs={{0,256},{256,0},{1,257},{257,1},{2,258},{258,2},{3,259},{259,3},{4... | collective-permute-start | bytes 277256 | tf_op jit(solution)/shard_map/ppermute | solution.py:15
  135.1 1.1 constant_dynamic-update-slice_fusion.11
  136.3 3.1 %fusion.6 = f32[2,128,38,1]{2,1,0,3:T(8,128)S(1)} fusion(bf16[64,2,128,64]{2,3,1,0:T(8,128)(2,1)} %constant_dynamic-update-slice_fusion.11, bf16[64,64,38]{1,2,0:T(8,128)(2,1)S(1)} %gather_fusion, pred[64]{0:T(512)(128)(4,1)S(1)} %get-tuple-element.7), kind=kOutput, calls=%fused_computation.14 | convolution fusion | flops 79847424 | bytes 2447424 | tf_op jit(solution)/shard_map/irsd,idc->rsc/dot_general | solution.py:138
  139.4 0.8 reshape.172
  140.3 6.5 %all-to-all-start.1 = ((f32[64,1,152]{2,1,0:T(1,128)}), f32[64,1,152]{2,1,0:T(1,128)S(1)}, u32[]{:S(2)}, u32[]{:S(2)}) async-start(f32[64,1,152]{2,1,0:T(1,128)} %reshape.172), calls=%async_computation.1 | async-start | bytes 131072 | tf_op jit(solution)/shard_map/all_to_all | solution.py:142
  147.5 12.8 %all-to-all-done.1 = f32[64,1,152]{2,1,0:T(1,128)S(1)} async-done(((f32[64,1,152]{2,1,0:T(1,128)}), f32[64,1,152]{2,1,0:T(1,128)S(1)}, u32[]{:S(2)}, u32[]{:S(2)}) %all-to-all-start.1) | async-done | bytes 38944 | tf_op jit(solution)/shard_map/all_to_all | solution.py:142
  160.8 0.8 reduce.3
  162.7 11.8 %collective-permute-start.9 = (f32[2,2,32]{2,1,0:T(2,128)S(1)}, f32[2,2,32]{2,1,0:T(2,128)S(1)}, u32[]{:S(2)}, u32[]{:S(2)}) collective-permute-start(f32[2,2,32]{2,1,0:T(2,128)S(1)} %constant_dynamic-slice_fusion), channel_id=1, source_target_pairs={{0,256},{256,0},{1,257},{257,1},{2,258},{258,2},{3,259},{259,3},{4... | collective-permute-start | bytes 1544 | tf_op jit(solution)/shard_map/ppermute | solution.py:15
  (94 shorter events, 17.5 us)
Async XLA Ops:
  0.0 162.3 %copy-start = (bf16[2432,64]{0,1:T(8,128)(2,1)S(1)}, bf16[2432,64]{0,1:T(8,128)(2,1)}, u32[]{:S(2)}) copy-start(bf16[2432,64]{0,1:T(8,128)(2,1)} %param.25) | copy-start | bytes 933892
  0.8 11.3 %collective-permute-start.1 = (bf16[2,2432]{1,0:T(2,128)(2,1)S(1)}, bf16[2,2432]{1,0:T(2,128)(2,1)S(1)}, u32[]{:S(2)}, u32[]{:S(2)}) collective-permute-start(bf16[2,2432]{1,0:T(2,128)(2,1)S(1)} %slice_bitcast_fusion.1), channel_id=1, source_target_pairs={{0,64},{64,0},{128,192},{192,128},{1,65},{65,1},{129,193},{193,129... | collective-permute-start | bytes 29192 | tf_op jit(solution)/shard_map/ppermute | solution.py:15
  5.5 6.7 %collective-permute-start = (bf16[2,2432]{1,0:T(2,128)(2,1)S(1)}, bf16[2,2432]{1,0:T(2,128)(2,1)S(1)}, u32[]{:S(2)}, u32[]{:S(2)}) collective-permute-start(bf16[2,2432]{1,0:T(2,128)(2,1)S(1)} %slice_bitcast_fusion.2), channel_id=1, source_target_pairs={{0,64},{64,0},{128,192},{192,128},{1,65},{65,1},{129,193},{193,129... | collective-permute-start | bytes 29192 | tf_op jit(solution)/shard_map/ppermute | solution.py:15
  11.0 22.5 %copy-start.4 = (s32[4,2]{0,1:T(2,128)S(1)}, s32[4,2]{0,1:T(2,128)}, u32[]{:S(2)}) copy-start(s32[4,2]{0,1:T(2,128)} %param.21) | copy-start | bytes 100
  11.0 22.5 %copy-start.6 = (s32[4,2]{0,1:T(2,128)S(1)}, s32[4,2]{0,1:T(2,128)}, u32[]{:S(2)}) copy-start(s32[4,2]{0,1:T(2,128)} %param.20) | copy-start | bytes 100
  15.1 35.6 %all-to-all-start = ((bf16[64,2,873]{2,1,0:T(2,128)(2,1)}), bf16[64,2,873]{2,1,0:T(2,128)(2,1)S(1)}, u32[]{:S(2)}, u32[]{:S(2)}) async-start(bf16[64,2,873]{2,1,0:T(2,128)(2,1)} %reshape.170), calls=%async_computation | async-start | bytes 458752 | tf_op jit(solution)/shard_map/all_to_all | solution.py:94
  35.4 45.0 %copy-start.9 = (s32[64]{0:T(128)S(1)}, s32[64]{0:T(128)}, u32[]{:S(2)}) copy-start(s32[64]{0:T(128)} %constant.71.clone) | copy-start | bytes 772
  35.4 45.0 %copy-start.10 = (s32[64]{0:T(128)S(1)}, s32[64]{0:T(128)}, u32[]{:S(2)}) copy-start(s32[64]{0:T(128)} %constant.72.clone) | copy-start | bytes 772
  51.4 49.6 %copy-start.2 = (f32[1,6,2432]{2,0,1:T(1,128)S(1)}, f32[1,6,2432]{2,0,1:T(1,128)}, u32[]{:S(2)}) copy-start(f32[1,6,2432]{2,0,1:T(1,128)} %param.23) | copy-start | bytes 175108
  51.4 49.8 %copy-start.1 = (f32[1,6,2,2432]{3,2,1,0:T(2,128)S(1)}, f32[1,6,2,2432]{3,2,1,0:T(2,128)}, u32[]{:S(2)}) copy-start(f32[1,6,2,2432]{3,2,1,0:T(2,128)} %param.24) | copy-start | bytes 350212
  53.2 8.6 %collective-permute-start.2 = (bf16[1,2,128,64]{2,3,1,0:T(8,128)(2,1)S(1)}, bf16[1,2,128,64]{2,3,1,0:T(8,128)(2,1)S(1)}, u32[]{:S(2)}, u32[]{:S(2)}) collective-permute-start(bf16[1,2,128,64]{2,3,1,0:T(8,128)(2,1)S(1)} %get-tuple-element.36), channel_id=1, source_target_pairs={{0,8},{1,9},{2,10},{3,11},{4,12},{5,13},{6,14},{7,15},{8,0},{9,1},... | collective-permute-start | bytes 98312 | tf_op jit(solution)/shard_map/ppermute | solution.py:129
  61.8 13.8 %collective-permute-start.3 = (bf16[2,2,128,64]{2,3,1,0:T(8,128)(2,1)S(1)}, bf16[2,2,128,64]{2,3,1,0:T(8,128)(2,1)S(1)}, u32[]{:S(2)}, u32[]{:S(2)}) collective-permute-start(bf16[2,2,128,64]{2,3,1,0:T(8,128)(2,1)S(1)} %pad_maximum_fusion.2), channel_id=1, source_target_pairs={{0,4},{1,5},{2,6},{3,7},{4,0},{5,1},{6,2},{7,3},{8,12},{9,13},{10,... | collective-permute-start | bytes 196616 | tf_op jit(solution)/shard_map/ppermute | solution.py:129
  75.7 7.3 %collective-permute-start.4 = (bf16[4,2,128,64]{2,3,1,0:T(8,128)(2,1)S(1)}, bf16[4,2,128,64]{2,3,1,0:T(8,128)(2,1)S(1)}, u32[]{:S(2)}, u32[]{:S(2)}) collective-permute-start(bf16[4,2,128,64]{2,3,1,0:T(8,128)(2,1)S(1)} %pad_maximum_fusion.1), channel_id=1, source_target_pairs={{0,2},{1,3},{2,0},{3,1},{4,6},{5,7},{6,4},{7,5},{8,10},{9,11},{10,... | collective-permute-start | bytes 393224 | tf_op jit(solution)/shard_map/ppermute | solution.py:129
  83.0 13.6 %collective-permute-start.5 = (bf16[8,2,128,64]{2,3,1,0:T(8,128)(2,1)S(1)}, bf16[8,2,128,64]{2,3,1,0:T(8,128)(2,1)S(1)}, u32[]{:S(2)}, u32[]{:S(2)}) collective-permute-start(bf16[8,2,128,64]{2,3,1,0:T(8,128)(2,1)S(1)} %pad_maximum_fusion), channel_id=1, source_target_pairs={{0,32},{1,33},{2,34},{3,35},{4,36},{5,37},{6,38},{7,39},{8,40},{9,... | collective-permute-start | bytes 786440 | tf_op jit(solution)/shard_map/ppermute | solution.py:129
  97.6 12.8 %collective-permute-start.6 = (bf16[16,2,128,64]{2,3,1,0:T(8,128)(2,1)S(1)}, bf16[16,2,128,64]{2,3,1,0:T(8,128)(2,1)S(1)}, u32[]{:S(2)}, u32[]{:S(2)}) collective-permute-start(bf16[16,2,128,64]{2,3,1,0:T(8,128)(2,1)S(1)} %get-tuple-element.13), channel_id=1, source_target_pairs={{0,1},{1,0},{2,3},{3,2},{4,5},{5,4},{6,7},{7,6},{8,9},{9,8},{10,11... | collective-permute-start | bytes 1572872 | tf_op jit(solution)/shard_map/ppermute | solution.py:129
  111.7 23.4 %collective-permute-start.7 = (bf16[32,2,128,64]{2,3,1,0:T(8,128)(2,1)}, bf16[32,2,128,64]{2,3,1,0:T(8,128)(2,1)S(1)}, u32[]{:S(2)}, u32[]{:S(2)}) collective-permute-start(bf16[32,2,128,64]{2,3,1,0:T(8,128)(2,1)} %get-tuple-element.9), channel_id=1, source_target_pairs={{0,16},{1,17},{2,18},{3,19},{4,20},{5,21},{6,22},{7,23},{8,24},{9,... | collective-permute-start | bytes 3145736 | tf_op jit(solution)/shard_map/ppermute | solution.py:129
  114.0 19.6 %collective-permute-start.8 = (bf16[1216,38]{1,0:T(8,128)(2,1)S(1)}, bf16[1216,38]{1,0:T(8,128)(2,1)S(1)}, u32[]{:S(2)}, u32[]{:S(2)}) collective-permute-start(bf16[1216,38]{1,0:T(8,128)(2,1)S(1)} %reshape.152), channel_id=1, source_target_pairs={{0,256},{256,0},{1,257},{257,1},{2,258},{258,2},{3,259},{259,3},{4... | collective-permute-start | bytes 277256 | tf_op jit(solution)/shard_map/ppermute | solution.py:15
  136.3 25.7 %copy-start.3 = (bf16[1,1,2,2,2432]{4,3,2,1,0:T(2,128)(2,1)S(1)}, bf16[1,1,2,2,2432]{4,3,2,1,0:T(2,128)(2,1)}, u32[]{:S(2)}) copy-start(bf16[1,1,2,2,2432]{4,3,2,1,0:T(2,128)(2,1)} %param.18) | copy-start | bytes 58372
  139.3 35.1 %copy-start.7 = (f32[6]{0:T(128)S(1)}, f32[6]{0:T(128)}, u32[]{:S(2)}) copy-start(f32[6]{0:T(128)} %param.27) | copy-start | bytes 76
  139.4 35.1 %copy-start.8 = (f32[6]{0:T(128)S(1)}, f32[6]{0:T(128)}, u32[]{:S(2)}) copy-start(f32[6]{0:T(128)} %param.26) | copy-start | bytes 76
  139.4 35.9 %copy-start.5 = (f32[1,2,2,32]{3,2,1,0:T(2,128)S(1)}, f32[1,2,2,32]{3,2,1,0:T(2,128)}, u32[]{:S(2)}) copy-start(f32[1,2,2,32]{3,2,1,0:T(2,128)} %param.19) | copy-start | bytes 1540
  140.3 20.1 %all-to-all-start.1 = ((f32[64,1,152]{2,1,0:T(1,128)}), f32[64,1,152]{2,1,0:T(1,128)S(1)}, u32[]{:S(2)}, u32[]{:S(2)}) async-start(f32[64,1,152]{2,1,0:T(1,128)} %reshape.172), calls=%async_computation.1 | async-start | bytes 131072 | tf_op jit(solution)/shard_map/all_to_all | solution.py:142
  162.7 12.6 %collective-permute-start.9 = (f32[2,2,32]{2,1,0:T(2,128)S(1)}, f32[2,2,32]{2,1,0:T(2,128)S(1)}, u32[]{:S(2)}, u32[]{:S(2)}) collective-permute-start(f32[2,2,32]{2,1,0:T(2,128)S(1)} %constant_dynamic-slice_fusion), channel_id=1, source_target_pairs={{0,256},{256,0},{1,257},{257,1},{2,258},{258,2},{3,259},{259,3},{4... | collective-permute-start | bytes 1544 | tf_op jit(solution)/shard_map/ppermute | solution.py:15

commit v4 on v2

--- a/solution.py
+++ b/solution.py
@@ -30,16 +30,9 @@
     )
 
 
-def butterfly_bits(n):
-    bits = [b for b in range(n.bit_length() - 1)]
-    return sorted(bits, key=lambda b: -hop_distance(b))
-
-
-def hop_distance(bit):
-    z_bits = 4
-    span = 16 if bit < z_bits else 4
-    step = 1 << (bit if bit < z_bits else bit - z_bits)
-    return min(step, span - step)
+def radix4_digits(n):
+    assert n == 64
+    return [2, 0, 4]
 
 
 def shards(
@@ -119,9 +112,15 @@
     me = lax.axis_index("seq")
     gathered = head_attn[None]
     masks = [0]
-    for bit in butterfly_bits(nseq):
-        gathered = jnp.concatenate([gathered, from_partner(gathered, "seq", bit)], 0)
-        masks = masks + [m ^ (1 << bit) for m in masks]
+    for low_bit in radix4_digits(nseq):
+        parts = [gathered]
+        grown = list(masks)
+        for digit in (1, 2, 3):
+            shift = digit << low_bit
+            parts.append(lax.ppermute(gathered, "seq", [(i, i ^ shift) for i in range(nseq)]))
+            grown += [m ^ shift for m in masks]
+        gathered = jnp.concatenate(parts, 0)
+        masks = grown
     source_head = jnp.bitwise_xor(me, jnp.array(masks, jnp.int32))
     w_heads = jnp.pad(
         w_cols.reshape(HEADS, HD, col_width), ((0, nseq - HEADS), (0, 0), (0, 0))

time: 167 us -> 170 us (1.018)
  starting transfers between devices: 83.8 us -> 79.9 us
  waiting for transfers between devices: 50.5 us -> 54.3 us
  local copies, waits for them, and re-layouts: 19.5 us -> 21.4 us
    ppermute x10 -> x4, starting transfers between devices: 55.6 us -> 17.2 us  [from_partner(): lax.ppermute(x, axis, [(i, i ^ 1 << apart) for i in range(lax.axis_size(a...]
    ppermute x0 -> x9, starting transfers between devices: none -> 36.4 us  [shards(): lax.ppermute(gathered, 'seq', [(i, i ^ shift) for i in range(nseq)])]
    ppermute x0 -> x9, waiting for transfers between devices: none -> 24 us  [shards(): lax.ppermute(gathered, 'seq', [(i, i ^ shift) for i in range(nseq)])]
    ppermute x10 -> x4, waiting for transfers between devices: 23.9 us -> 0.6 us  [from_partner(): lax.ppermute(x, axis, [(i, i ^ 1 << apart) for i in range(lax.axis_size(a...]
    all_to_all x1, waiting for transfers between devices: 13.8 us -> 16.9 us  [shards(): joint = lax.all_to_all(joint, 'seq', 0, 0, tiled=True)]
    all_to_all x1, starting transfers between devices: 9.82 us -> 7.72 us  [shards(): projected = lax.all_to_all(projected_parts, 'seq', 0, 0, tiled=True)]
    unnamed x29 -> x26, local copies, waits for them, and re-layouts: 5.38 us -> 7.43 us
  transfers between devices with their start and end apart: 12 -> 15, of which waited for: 9 -> 8; matrix products, arithmetic and copies ran while one was open for 9% -> 12% of each run, Pallas kernels for 0% -> 0%
where the time goes in v4:
time: 170 us; the launch traced here: 169 us
  starting transfers between devices  79.9 us (47%)
  waiting for transfers between devices  54.3 us (32%)
  local copies, waits for them, and re-layouts  21.4 us (13%)
  other arithmetic  7.27 us (4%)
  matrix products  5.59 us (3%)
    ppermute x9, starting transfers between devices, shards(): lax.ppermute(gathered, 'seq', [(i, i ^ shift) for i in range(nseq)])  36.4 us
    ppermute x9, waiting for transfers between devices, shards(): lax.ppermute(gathered, 'seq', [(i, i ^ shift) for i in range(nseq)])  24 us
    all_to_all x1, starting transfers between devices, shards(): joint = lax.all_to_all(joint, 'seq', 0, 0, tiled=True)  18.6 us
    ppermute x4, starting transfers between devices, from_partner(): lax.ppermute(x, axis, [(i, i ^ 1 << apart) for i in range(lax.axis_size(a...  17.2 us
    all_to_all x1, waiting for transfers between devices, shards(): joint = lax.all_to_all(joint, 'seq', 0, 0, tiled=True)  16.9 us
    all_to_all x1, waiting for transfers between devices, shards(): projected = lax.all_to_all(projected_parts, 'seq', 0, 0, tiled=True)  12.8 us
    all_to_all x1, starting transfers between devices, shards(): projected = lax.all_to_all(projected_parts, 'seq', 0, 0, tiled=True)  7.72 us
    unnamed x26, local copies, waits for them, and re-layouts  7.43 us
  transfers between devices with their start and end apart: 15, of which 8 were waited for; matrix products, arithmetic and copies ran while one was open for 12% of the time, Pallas kernels for 0%

profile of v4, /device:TPU:1, one launch (start us, length us, event | category | flops | bytes accessed | tf_op | source)
XLA Modules:
  0.0 169.1 jit_solution(1276811708649228686)
XLA Ops:
  0.8 4.0 %collective-permute-start.1 = (bf16[2,2432]{1,0:T(2,128)(2,1)S(1)}, bf16[2,2432]{1,0:T(2,128)(2,1)S(1)}, u32[]{:S(2)}, u32[]{:S(2)}) collective-permute-start(bf16[2,2432]{1,0:T(2,128)(2,1)S(1)} %slice_bitcast_fusion.1), channel_id=1, source_target_pairs={{0,64},{64,0},{128,192},{192,128},{1,65},{65,1},{129,193},{193,129... | collective-permute-start | bytes 29192 | tf_op jit(solution)/shard_map/ppermute | solution.py:15
  5.5 1.9 %collective-permute-start = (bf16[2,2432]{1,0:T(2,128)(2,1)S(1)}, bf16[2,2432]{1,0:T(2,128)(2,1)S(1)}, u32[]{:S(2)}, u32[]{:S(2)}) collective-permute-start(bf16[2,2432]{1,0:T(2,128)(2,1)S(1)} %slice_bitcast_fusion.2), channel_id=1, source_target_pairs={{0,64},{64,0},{128,192},{192,128},{1,65},{65,1},{129,193},{193,129... | collective-permute-start | bytes 29192 | tf_op jit(solution)/shard_map/ppermute | solution.py:15
  7.4 0.9 constant_dynamic-slice_fusion.2
  11.5 1.2 fusion.18
  12.7 0.8 concatenate.59
  13.6 0.8 concatenate.56
  14.4 1.6 reshape.149
  16.5 0.8 reshape_squeeze.3
  19.4 0.9 reshape.170
  20.3 18.6 %all-to-all-start = ((bf16[64,2,873]{2,1,0:T(2,128)(2,1)}), bf16[64,2,873]{2,1,0:T(2,128)(2,1)S(1)}, u32[]{:S(2)}, u32[]{:S(2)}) async-start(bf16[64,2,873]{2,1,0:T(2,128)(2,1)} %reshape.170), calls=%async_computation | async-start | bytes 458752 | tf_op jit(solution)/shard_map/all_to_all | solution.py:87
  39.2 16.9 %all-to-all-done = bf16[64,2,873]{2,1,0:T(2,128)(2,1)S(1)} async-done(((bf16[64,2,873]{2,1,0:T(2,128)(2,1)}), bf16[64,2,873]{2,1,0:T(2,128)(2,1)S(1)}, u32[]{:S(2)}, u32[]{:S(2)}) %all-to-all-start) | async-done | bytes 223520 | tf_op jit(solution)/shard_map/all_to_all | solution.py:87
  58.6 4.5 %collective-permute-start.2 = (bf16[1,2,128,64]{2,3,1,0:T(8,128)(2,1)S(1)}, bf16[1,2,128,64]{2,3,1,0:T(8,128)(2,1)S(1)}, u32[]{:S(2)}, u32[]{:S(2)}) collective-permute-start(bf16[1,2,128,64]{2,3,1,0:T(8,128)(2,1)S(1)} %get-tuple-element.33), channel_id=1, source_target_pairs={{0,4},{1,5},{2,6},{3,7},{4,0},{5,1},{6,2},{7,3},{8,12},{9,13},{10,... | collective-permute-start | bytes 98312 | tf_op jit(solution)/shard_map/ppermute | solution.py:120
  63.2 7.1 %collective-permute-start.3 = (bf16[1,2,128,64]{2,3,1,0:T(8,128)(2,1)S(1)}, bf16[1,2,128,64]{2,3,1,0:T(8,128)(2,1)S(1)}, u32[]{:S(2)}, u32[]{:S(2)}) collective-permute-start(bf16[1,2,128,64]{2,3,1,0:T(8,128)(2,1)S(1)} %get-tuple-element.33), channel_id=1, source_target_pairs={{0,8},{1,9},{2,10},{3,11},{4,12},{5,13},{6,14},{7,15},{8,0},{9,1},... | collective-permute-start | bytes 98312 | tf_op jit(solution)/shard_map/ppermute | solution.py:120
  70.3 4.6 %collective-permute-start.4 = (bf16[1,2,128,64]{2,3,1,0:T(8,128)(2,1)S(1)}, bf16[1,2,128,64]{2,3,1,0:T(8,128)(2,1)S(1)}, u32[]{:S(2)}, u32[]{:S(2)}) collective-permute-start(bf16[1,2,128,64]{2,3,1,0:T(8,128)(2,1)S(1)} %get-tuple-element.33), channel_id=1, source_target_pairs={{0,12},{1,13},{2,14},{3,15},{4,8},{5,9},{6,10},{7,11},{8,4},{9,5},... | collective-permute-start | bytes 98312 | tf_op jit(solution)/shard_map/ppermute | solution.py:120
  74.9 1.7 collective-permute-done.3
  76.6 2.9 %collective-permute-done.4 = bf16[1,2,128,64]{2,3,1,0:T(8,128)(2,1)S(1)} collective-permute-done((bf16[1,2,128,64]{2,3,1,0:T(8,128)(2,1)S(1)}, bf16[1,2,128,64]{2,3,1,0:T(8,128)(2,1)S(1)}, u32[]{:S(2)}, u32[]{:S(2)}) %collective-permute-start.4) | collective-permute-done | bytes 32800 | tf_op jit(solution)/shard_map/ppermute | solution.py:120
  79.5 1.9 %collective-permute-start.5 = (bf16[4,2,128,64]{2,3,1,0:T(8,128)(2,1)S(1)}, bf16[4,2,128,64]{2,3,1,0:T(8,128)(2,1)S(1)}, u32[]{:S(2)}, u32[]{:S(2)}) collective-permute-start(bf16[4,2,128,64]{2,3,1,0:T(8,128)(2,1)S(1)} %pad_maximum_fusion), channel_id=1, source_target_pairs={{0,1},{1,0},{2,3},{3,2},{4,5},{5,4},{6,7},{7,6},{8,9},{9,8},{10,11... | collective-permute-start | bytes 393224 | tf_op jit(solution)/shard_map/ppermute | solution.py:120
  81.4 3.6 %collective-permute-start.6 = (bf16[4,2,128,64]{2,3,1,0:T(8,128)(2,1)S(1)}, bf16[4,2,128,64]{2,3,1,0:T(8,128)(2,1)S(1)}, u32[]{:S(2)}, u32[]{:S(2)}) collective-permute-start(bf16[4,2,128,64]{2,3,1,0:T(8,128)(2,1)S(1)} %pad_maximum_fusion), channel_id=1, source_target_pairs={{0,2},{1,3},{2,0},{3,1},{4,6},{5,7},{6,4},{7,5},{8,10},{9,11},{10,... | collective-permute-start | bytes 393224 | tf_op jit(solution)/shard_map/ppermute | solution.py:120
  85.0 3.8 %collective-permute-start.7 = (bf16[4,2,128,64]{2,3,1,0:T(8,128)(2,1)S(1)}, bf16[4,2,128,64]{2,3,1,0:T(8,128)(2,1)S(1)}, u32[]{:S(2)}, u32[]{:S(2)}) collective-permute-start(bf16[4,2,128,64]{2,3,1,0:T(8,128)(2,1)S(1)} %pad_maximum_fusion), channel_id=1, source_target_pairs={{0,3},{1,2},{2,1},{3,0},{4,7},{5,6},{6,5},{7,4},{8,11},{9,10},{10,... | collective-permute-start | bytes 393224 | tf_op jit(solution)/shard_map/ppermute | solution.py:120
  93.8 3.3 %collective-permute-start.8 = (bf16[16,2,128,64]{2,3,1,0:T(8,128)(2,1)}, bf16[16,2,128,64]{2,3,1,0:T(8,128)(2,1)S(1)}, u32[]{:S(2)}, u32[]{:S(2)}) collective-permute-start(bf16[16,2,128,64]{2,3,1,0:T(8,128)(2,1)} %get-tuple-element.17), channel_id=1, source_target_pairs={{0,16},{1,17},{2,18},{3,19},{4,20},{5,21},{6,22},{7,23},{8,24},{9,... | collective-permute-start | bytes 1572872 | tf_op jit(solution)/shard_map/ppermute | solution.py:120
  97.5 7.4 %collective-permute-start.11 = (bf16[1216,38]{1,0:T(8,128)(2,1)S(1)}, bf16[1216,38]{1,0:T(8,128)(2,1)S(1)}, u32[]{:S(2)}, u32[]{:S(2)}) collective-permute-start(bf16[1216,38]{1,0:T(8,128)(2,1)S(1)} %reshape.152), channel_id=1, source_target_pairs={{0,256},{256,0},{1,257},{257,1},{2,258},{258,2},{3,259},{259,3},{4... | collective-permute-start | bytes 277256 | tf_op jit(solution)/shard_map/ppermute | solution.py:15
  104.9 5.0 %collective-permute-start.9 = (bf16[16,2,128,64]{2,3,1,0:T(8,128)(2,1)}, bf16[16,2,128,64]{2,3,1,0:T(8,128)(2,1)S(1)}, u32[]{:S(2)}, u32[]{:S(2)}) collective-permute-start(bf16[16,2,128,64]{2,3,1,0:T(8,128)(2,1)} %get-tuple-element.17), channel_id=1, source_target_pairs={{0,32},{1,33},{2,34},{3,35},{4,36},{5,37},{6,38},{7,39},{8,40},{9,... | collective-permute-start | bytes 1572872 | tf_op jit(solution)/shard_map/ppermute | solution.py:120
  110.9 2.7 %collective-permute-start.10 = (bf16[16,2,128,64]{2,3,1,0:T(8,128)(2,1)}, bf16[16,2,128,64]{2,3,1,0:T(8,128)(2,1)S(1)}, u32[]{:S(2)}, u32[]{:S(2)}) collective-permute-start(bf16[16,2,128,64]{2,3,1,0:T(8,128)(2,1)} %get-tuple-element.17), channel_id=1, source_target_pairs={{0,48},{1,49},{2,50},{3,51},{4,52},{5,53},{6,54},{7,55},{8,56},{9,... | collective-permute-start | bytes 1572872 | tf_op jit(solution)/shard_map/ppermute | solution.py:120
  115.0 0.8 constant_dynamic-update-slice_fusion.9
  115.8 6.7 %collective-permute-done.9 = bf16[16,2,128,64]{2,3,1,0:T(8,128)(2,1)S(1)} collective-permute-done((bf16[16,2,128,64]{2,3,1,0:T(8,128)(2,1)}, bf16[16,2,128,64]{2,3,1,0:T(8,128)(2,1)S(1)}, u32[]{:S(2)}, u32[]{:S(2)}) %collective-permute-start.9) | collective-permute-done | bytes 524320 | tf_op jit(solution)/shard_map/ppermute | solution.py:120
  122.5 0.8 constant_dynamic-update-slice_fusion.8
  123.4 11.9 %collective-permute-done.10 = bf16[16,2,128,64]{2,3,1,0:T(8,128)(2,1)S(1)} collective-permute-done((bf16[16,2,128,64]{2,3,1,0:T(8,128)(2,1)}, bf16[16,2,128,64]{2,3,1,0:T(8,128)(2,1)S(1)}, u32[]{:S(2)}, u32[]{:S(2)}) %collective-permute-start.10) | collective-permute-done | bytes 524320 | tf_op jit(solution)/shard_map/ppermute | solution.py:120
  135.3 0.8 constant_dynamic-update-slice_fusion.7
  136.1 3.1 %fusion.6 = f32[2,128,38,1]{2,1,0,3:T(8,128)S(1)} fusion(bf16[64,2,128,64]{2,3,1,0:T(8,128)(2,1)} %constant_dynamic-update-slice_fusion.7, bf16[64,64,38]{1,2,0:T(8,128)(2,1)S(1)} %gather_fusion, pred[64]{0:T(512)(128)(4,1)S(1)} %get-tuple-element.7), kind=kOutput, calls=%fused_computation.14 | convolution fusion | flops 79847424 | bytes 2447424 | tf_op jit(solution)/shard_map/irsd,idc->rsc/dot_general | solution.py:129
  140.1 7.7 %all-to-all-start.1 = ((f32[64,1,152]{2,1,0:T(1,128)}), f32[64,1,152]{2,1,0:T(1,128)S(1)}, u32[]{:S(2)}, u32[]{:S(2)}) async-start(f32[64,1,152]{2,1,0:T(1,128)} %reshape.172), calls=%async_computation.1 | async-start | bytes 131072 | tf_op jit(solution)/shard_map/all_to_all | solution.py:133
  148.5 12.8 %all-to-all-done.1 = f32[64,1,152]{2,1,0:T(1,128)S(1)} async-done(((f32[64,1,152]{2,1,0:T(1,128)}), f32[64,1,152]{2,1,0:T(1,128)S(1)}, u32[]{:S(2)}, u32[]{:S(2)}) %all-to-all-start.1) | async-done | bytes 38944 | tf_op jit(solution)/shard_map/all_to_all | solution.py:133
  163.7 3.9 %collective-permute-start.12 = (f32[2,2,32]{2,1,0:T(2,128)S(1)}, f32[2,2,32]{2,1,0:T(2,128)S(1)}, u32[]{:S(2)}, u32[]{:S(2)}) collective-permute-start(f32[2,2,32]{2,1,0:T(2,128)S(1)} %constant_dynamic-slice_fusion), channel_id=1, source_target_pairs={{0,256},{256,0},{1,257},{257,1},{2,258},{258,2},{3,259},{259,3},{4... | collective-permute-start | bytes 1544 | tf_op jit(solution)/shard_map/ppermute | solution.py:15
  (93 shorter events, 22.9 us)
Async XLA Ops:
  0.0 163.4 %copy-start = (bf16[2432,64]{0,1:T(8,128)(2,1)S(1)}, bf16[2432,64]{0,1:T(8,128)(2,1)}, u32[]{:S(2)}) copy-start(bf16[2432,64]{0,1:T(8,128)(2,1)} %param.24) | copy-start | bytes 933892
  0.8 16.6 %collective-permute-start.1 = (bf16[2,2432]{1,0:T(2,128)(2,1)S(1)}, bf16[2,2432]{1,0:T(2,128)(2,1)S(1)}, u32[]{:S(2)}, u32[]{:S(2)}) collective-permute-start(bf16[2,2432]{1,0:T(2,128)(2,1)S(1)} %slice_bitcast_fusion.1), channel_id=1, source_target_pairs={{0,64},{64,0},{128,192},{192,128},{1,65},{65,1},{129,193},{193,129... | collective-permute-start | bytes 29192 | tf_op jit(solution)/shard_map/ppermute | solution.py:15
  5.5 12.0 %collective-permute-start = (bf16[2,2432]{1,0:T(2,128)(2,1)S(1)}, bf16[2,2432]{1,0:T(2,128)(2,1)S(1)}, u32[]{:S(2)}, u32[]{:S(2)}) collective-permute-start(bf16[2,2432]{1,0:T(2,128)(2,1)S(1)} %slice_bitcast_fusion.2), channel_id=1, source_target_pairs={{0,64},{64,0},{128,192},{192,128},{1,65},{65,1},{129,193},{193,129... | collective-permute-start | bytes 29192 | tf_op jit(solution)/shard_map/ppermute | solution.py:15
  16.3 22.7 %copy-start.1 = (f32[1,6,2432]{2,0,1:T(1,128)S(1)}, f32[1,6,2432]{2,0,1:T(1,128)}, u32[]{:S(2)}) copy-start(f32[1,6,2432]{2,0,1:T(1,128)} %param.22) | copy-start | bytes 175108
  20.3 54.5 %copy-start.6 = (s32[64]{0:T(128)S(1)}, s32[64]{0:T(128)}, u32[]{:S(2)}) copy-start(s32[64]{0:T(128)} %constant.69.clone) | copy-start | bytes 772
  20.3 35.7 %all-to-all-start = ((bf16[64,2,873]{2,1,0:T(2,128)(2,1)}), bf16[64,2,873]{2,1,0:T(2,128)(2,1)S(1)}, u32[]{:S(2)}, u32[]{:S(2)}) async-start(bf16[64,2,873]{2,1,0:T(2,128)(2,1)} %reshape.170), calls=%async_computation | async-start | bytes 458752 | tf_op jit(solution)/shard_map/all_to_all | solution.py:87
  58.6 16.2 %collective-permute-start.2 = (bf16[1,2,128,64]{2,3,1,0:T(8,128)(2,1)S(1)}, bf16[1,2,128,64]{2,3,1,0:T(8,128)(2,1)S(1)}, u32[]{:S(2)}, u32[]{:S(2)}) collective-permute-start(bf16[1,2,128,64]{2,3,1,0:T(8,128)(2,1)S(1)} %get-tuple-element.33), channel_id=1, source_target_pairs={{0,4},{1,5},{2,6},{3,7},{4,0},{5,1},{6,2},{7,3},{8,12},{9,13},{10,... | collective-permute-start | bytes 98312 | tf_op jit(solution)/shard_map/ppermute | solution.py:120
  63.2 13.4 %collective-permute-start.3 = (bf16[1,2,128,64]{2,3,1,0:T(8,128)(2,1)S(1)}, bf16[1,2,128,64]{2,3,1,0:T(8,128)(2,1)S(1)}, u32[]{:S(2)}, u32[]{:S(2)}) collective-permute-start(bf16[1,2,128,64]{2,3,1,0:T(8,128)(2,1)S(1)} %get-tuple-element.33), channel_id=1, source_target_pairs={{0,8},{1,9},{2,10},{3,11},{4,12},{5,13},{6,14},{7,15},{8,0},{9,1},... | collective-permute-start | bytes 98312 | tf_op jit(solution)/shard_map/ppermute | solution.py:120
  70.3 9.2 %collective-permute-start.4 = (bf16[1,2,128,64]{2,3,1,0:T(8,128)(2,1)S(1)}, bf16[1,2,128,64]{2,3,1,0:T(8,128)(2,1)S(1)}, u32[]{:S(2)}, u32[]{:S(2)}) collective-permute-start(bf16[1,2,128,64]{2,3,1,0:T(8,128)(2,1)S(1)} %get-tuple-element.33), channel_id=1, source_target_pairs={{0,12},{1,13},{2,14},{3,15},{4,8},{5,9},{6,10},{7,11},{8,4},{9,5},... | collective-permute-start | bytes 98312 | tf_op jit(solution)/shard_map/ppermute | solution.py:120
  79.5 11.2 %collective-permute-start.5 = (bf16[4,2,128,64]{2,3,1,0:T(8,128)(2,1)S(1)}, bf16[4,2,128,64]{2,3,1,0:T(8,128)(2,1)S(1)}, u32[]{:S(2)}, u32[]{:S(2)}) collective-permute-start(bf16[4,2,128,64]{2,3,1,0:T(8,128)(2,1)S(1)} %pad_maximum_fusion), channel_id=1, source_target_pairs={{0,1},{1,0},{2,3},{3,2},{4,5},{5,4},{6,7},{7,6},{8,9},{9,8},{10,11... | collective-permute-start | bytes 393224 | tf_op jit(solution)/shard_map/ppermute | solution.py:120
  81.4 10.1 %collective-permute-start.6 = (bf16[4,2,128,64]{2,3,1,0:T(8,128)(2,1)S(1)}, bf16[4,2,128,64]{2,3,1,0:T(8,128)(2,1)S(1)}, u32[]{:S(2)}, u32[]{:S(2)}) collective-permute-start(bf16[4,2,128,64]{2,3,1,0:T(8,128)(2,1)S(1)} %pad_maximum_fusion), channel_id=1, source_target_pairs={{0,2},{1,3},{2,0},{3,1},{4,6},{5,7},{6,4},{7,5},{8,10},{9,11},{10,... | collective-permute-start | bytes 393224 | tf_op jit(solution)/shard_map/ppermute | solution.py:120
  85.0 8.1 %collective-permute-start.7 = (bf16[4,2,128,64]{2,3,1,0:T(8,128)(2,1)S(1)}, bf16[4,2,128,64]{2,3,1,0:T(8,128)(2,1)S(1)}, u32[]{:S(2)}, u32[]{:S(2)}) collective-permute-start(bf16[4,2,128,64]{2,3,1,0:T(8,128)(2,1)S(1)} %pad_maximum_fusion), channel_id=1, source_target_pairs={{0,3},{1,2},{2,1},{3,0},{4,7},{5,6},{6,5},{7,4},{8,11},{9,10},{10,... | collective-permute-start | bytes 393224 | tf_op jit(solution)/shard_map/ppermute | solution.py:120
  93.8 21.2 %collective-permute-start.8 = (bf16[16,2,128,64]{2,3,1,0:T(8,128)(2,1)}, bf16[16,2,128,64]{2,3,1,0:T(8,128)(2,1)S(1)}, u32[]{:S(2)}, u32[]{:S(2)}) collective-permute-start(bf16[16,2,128,64]{2,3,1,0:T(8,128)(2,1)} %get-tuple-element.17), channel_id=1, source_target_pairs={{0,16},{1,17},{2,18},{3,19},{4,20},{5,21},{6,22},{7,23},{8,24},{9,... | collective-permute-start | bytes 1572872 | tf_op jit(solution)/shard_map/ppermute | solution.py:120
  97.5 13.2 %collective-permute-start.11 = (bf16[1216,38]{1,0:T(8,128)(2,1)S(1)}, bf16[1216,38]{1,0:T(8,128)(2,1)S(1)}, u32[]{:S(2)}, u32[]{:S(2)}) collective-permute-start(bf16[1216,38]{1,0:T(8,128)(2,1)S(1)} %reshape.152), channel_id=1, source_target_pairs={{0,256},{256,0},{1,257},{257,1},{2,258},{258,2},{3,259},{259,3},{4... | collective-permute-start | bytes 277256 | tf_op jit(solution)/shard_map/ppermute | solution.py:15
  104.9 17.7 %collective-permute-start.9 = (bf16[16,2,128,64]{2,3,1,0:T(8,128)(2,1)}, bf16[16,2,128,64]{2,3,1,0:T(8,128)(2,1)S(1)}, u32[]{:S(2)}, u32[]{:S(2)}) collective-permute-start(bf16[16,2,128,64]{2,3,1,0:T(8,128)(2,1)} %get-tuple-element.17), channel_id=1, source_target_pairs={{0,32},{1,33},{2,34},{3,35},{4,36},{5,37},{6,38},{7,39},{8,40},{9,... | collective-permute-start | bytes 1572872 | tf_op jit(solution)/shard_map/ppermute | solution.py:120
  110.9 24.4 %collective-permute-start.10 = (bf16[16,2,128,64]{2,3,1,0:T(8,128)(2,1)}, bf16[16,2,128,64]{2,3,1,0:T(8,128)(2,1)S(1)}, u32[]{:S(2)}, u32[]{:S(2)}) collective-permute-start(bf16[16,2,128,64]{2,3,1,0:T(8,128)(2,1)} %get-tuple-element.17), channel_id=1, source_target_pairs={{0,48},{1,49},{2,50},{3,51},{4,52},{5,53},{6,54},{7,55},{8,56},{9,... | collective-permute-start | bytes 1572872 | tf_op jit(solution)/shard_map/ppermute | solution.py:120
  136.1 26.9 %copy-start.2 = (bf16[1,1,2,2,2432]{4,3,2,1,0:T(2,128)(2,1)S(1)}, bf16[1,1,2,2,2432]{4,3,2,1,0:T(2,128)(2,1)}, u32[]{:S(2)}) copy-start(bf16[1,1,2,2,2432]{4,3,2,1,0:T(2,128)(2,1)} %param.17) | copy-start | bytes 58372
  139.2 28.5 %copy-start.4 = (f32[6]{0:T(128)S(1)}, f32[6]{0:T(128)}, u32[]{:S(2)}) copy-start(f32[6]{0:T(128)} %param.26) | copy-start | bytes 76
  139.2 28.5 %copy-start.5 = (f32[6]{0:T(128)S(1)}, f32[6]{0:T(128)}, u32[]{:S(2)}) copy-start(f32[6]{0:T(128)} %param.25) | copy-start | bytes 76
  139.2 29.2 %copy-start.3 = (f32[1,2,2,32]{3,2,1,0:T(2,128)S(1)}, f32[1,2,2,32]{3,2,1,0:T(2,128)}, u32[]{:S(2)}) copy-start(f32[1,2,2,32]{3,2,1,0:T(2,128)} %param.18) | copy-start | bytes 1540
  140.1 21.2 %all-to-all-start.1 = ((f32[64,1,152]{2,1,0:T(1,128)}), f32[64,1,152]{2,1,0:T(1,128)S(1)}, u32[]{:S(2)}, u32[]{:S(2)}) async-start(f32[64,1,152]{2,1,0:T(1,128)} %reshape.172), calls=%async_computation.1 | async-start | bytes 131072 | tf_op jit(solution)/shard_map/all_to_all | solution.py:133
  163.7 4.7 %collective-permute-start.12 = (f32[2,2,32]{2,1,0:T(2,128)S(1)}, f32[2,2,32]{2,1,0:T(2,128)S(1)}, u32[]{:S(2)}, u32[]{:S(2)}) collective-permute-start(f32[2,2,32]{2,1,0:T(2,128)S(1)} %constant_dynamic-slice_fusion), channel_id=1, source_target_pairs={{0,256},{256,0},{1,257},{257,1},{2,258},{258,2},{3,259},{259,3},{4... | collective-permute-start | bytes 1544 | tf_op jit(solution)/shard_map/ppermute | solution.py:15

commit v5 on v4

--- a/solution.py
+++ b/solution.py
@@ -30,9 +30,19 @@
     )
 
 
-def radix4_digits(n):
+def plane_heads(n):
     assert n == 64
-    return [2, 0, 4]
+    return -(-HEADS // 4)
+
+
+def head_placement(n):
+    used = plane_heads(n)
+    table = []
+    for j in range(n):
+        x, z = divmod(j, 16)
+        head = x * used + z
+        table.append(head if z < used and head < HEADS else HEADS)
+    return table
 
 
 def shards(
@@ -64,10 +74,13 @@
     slot_total = nseq * shard_rows
     far_keys, far_values = from_partner((resident_key_rows[1], local_values[1]), "grp", 0)
 
+    head_table = head_placement(nseq)
+
     def to_heads(x):
         n = x.shape[0]
         x = x.reshape(n, shard_rows, HEADS, HD).transpose(2, 0, 1, 3)
-        return jnp.pad(x, ((0, nseq - HEADS), (0, 0), (0, 0), (0, 0)))
+        x = jnp.pad(x, ((0, 1), (0, 0), (0, 0), (0, 0)))
+        return jnp.take(x, jnp.array(head_table, jnp.int32), axis=0)
 
     block_rows = w_out.shape[0]
     col_width = D // nseq
@@ -112,7 +125,7 @@
     me = lax.axis_index("seq")
     gathered = head_attn[None]
     masks = [0]
-    for low_bit in radix4_digits(nseq):
+    for low_bit in (2, 0):
         parts = [gathered]
         grown = list(masks)
         for digit in (1, 2, 3):
@@ -121,10 +134,22 @@
             grown += [m ^ shift for m in masks]
         gathered = jnp.concatenate(parts, 0)
         masks = grown
-    source_head = jnp.bitwise_xor(me, jnp.array(masks, jnp.int32))
-    w_heads = jnp.pad(
-        w_cols.reshape(HEADS, HD, col_width), ((0, nseq - HEADS), (0, 0), (0, 0))
-    )
+    plane = len(masks)
+    inverse = [masks.index(z) for z in range(plane)]
+    my_z = me % plane
+    my_x = me // plane
+    by_z = jnp.take(gathered, jnp.take(jnp.array(inverse, jnp.int32), jnp.bitwise_xor(my_z, jnp.arange(plane))), axis=0)
+    used = plane_heads(nseq)
+    outgoing = by_z[:used]
+    parts = [by_z]
+    sources = [my_x * plane + jnp.arange(plane)]
+    for digit in (1, 2, 3):
+        shift = digit * plane
+        parts.append(lax.ppermute(outgoing, "seq", [(i, i ^ shift) for i in range(nseq)]))
+        sources.append(jnp.bitwise_xor(my_x, digit) * plane + jnp.arange(used))
+    gathered = jnp.concatenate(parts, 0)
+    source_head = jnp.take(jnp.array(head_table, jnp.int32), jnp.concatenate(sources))
+    w_heads = jnp.pad(w_cols.reshape(HEADS, HD, col_width), ((0, 1), (0, 0), (0, 0)))
     w_ordered = jnp.take(w_heads, source_head, axis=0)
     projected_cols = jnp.einsum(
         "irsd,idc->rsc", gathered, w_ordered, preferred_element_type=jnp.float32

time: 170 us -> 154 us (0.906)
  waiting for transfers between devices: 54.3 us -> 44.1 us
  local copies, waits for them, and re-layouts: 21.4 us -> 16.1 us
  matrix products: 5.59 us -> 2.73 us
  starting transfers between devices: 79.9 us -> 81.9 us
    ppermute x9 -> x6, waiting for transfers between devices: 24 us -> 4.36 us  [shards(): lax.ppermute(gathered, 'seq', [(i, i ^ shift) for i in range(nseq)])]
    ppermute x0 -> x3, starting transfers between devices: none -> 11.6 us  [shards(): lax.ppermute(outgoing, 'seq', [(i, i ^ shift) for i in range(nseq)])]
    ppermute x9 -> x6, starting transfers between devices: 36.4 us -> 25.5 us  [shards(): lax.ppermute(gathered, 'seq', [(i, i ^ shift) for i in range(nseq)])]
    ppermute x0 -> x3, waiting for transfers between devices: none -> 9.22 us  [shards(): lax.ppermute(outgoing, 'seq', [(i, i ^ shift) for i in range(nseq)])]
    gather x0 -> x6, local copies, waits for them, and re-layouts: none -> 5.04 us  [the longest x3 2.26 us: to_heads(): return jnp.take(x, jnp.array(head_table, jnp.int32), axis=0)]
    unnamed x26 -> x38, local copies, waits for them, and re-layouts: 7.43 us -> 2.42 us
    dot_general x1, matrix products: 3.06 us -> 1.11 us  [shards(): jnp.einsum('irsd,idc->rsc', gathered, w_ordered, preferred_element_type=j...]
  transfers between devices with their start and end apart: 15 -> 15, of which waited for: 8 -> 6; matrix products, arithmetic and copies ran while one was open for 12% -> 9% of each run, Pallas kernels for 0% -> 0%
where the time goes in v5:
time: 154 us; the launch traced here: 153 us
  starting transfers between devices  81.9 us (53%)
  waiting for transfers between devices  44.1 us (29%)
  local copies, waits for them, and re-layouts  16.1 us (10%)
  other arithmetic  7.3 us (5%)
  matrix products  2.73 us (2%)
    ppermute x6, starting transfers between devices, shards(): lax.ppermute(gathered, 'seq', [(i, i ^ shift) for i in range(nseq)])  25.5 us
    all_to_all x1, starting transfers between devices, shards(): joint = lax.all_to_all(joint, 'seq', 0, 0, tiled=True)  18.4 us
    ppermute x4, starting transfers between devices, from_partner(): lax.ppermute(x, axis, [(i, i ^ 1 << apart) for i in range(lax.axis_size(a...  17.6 us
    all_to_all x1, waiting for transfers between devices, shards(): joint = lax.all_to_all(joint, 'seq', 0, 0, tiled=True)  17 us
    all_to_all x1, waiting for transfers between devices, shards(): projected = lax.all_to_all(projected_parts, 'seq', 0, 0, tiled=True)  12.9 us
    ppermute x3, starting transfers between devices, shards(): lax.ppermute(outgoing, 'seq', [(i, i ^ shift) for i in range(nseq)])  11.6 us
    ppermute x3, waiting for transfers between devices, shards(): lax.ppermute(outgoing, 'seq', [(i, i ^ shift) for i in range(nseq)])  9.22 us
    all_to_all x1, starting transfers between devices, shards(): projected = lax.all_to_all(projected_parts, 'seq', 0, 0, tiled=True)  8.9 us
  transfers between devices with their start and end apart: 15, of which 6 were waited for; matrix products, arithmetic and copies ran while one was open for 9% of the time, Pallas kernels for 0%

profile of v5, /device:TPU:1, one launch (start us, length us, event | category | flops | bytes accessed | tf_op | source)
XLA Modules:
  0.0 153.1 jit_solution(16999238056224374079)
XLA Ops:
  0.0 0.8 slice_bitcast_fusion.2
  0.8 4.0 %collective-permute-start = (bf16[2,2432]{1,0:T(2,128)(2,1)S(1)}, bf16[2,2432]{1,0:T(2,128)(2,1)S(1)}, u32[]{:S(2)}, u32[]{:S(2)}) collective-permute-start(bf16[2,2432]{1,0:T(2,128)(2,1)S(1)} %slice_bitcast_fusion.2), channel_id=1, source_target_pairs={{0,64},{64,0},{128,192},{192,128},{1,65},{65,1},{129,193},{193,129... | collective-permute-start | bytes 29192 | tf_op jit(solution)/shard_map/ppermute | solution.py:15
  4.8 0.7 slice_bitcast_fusion.1
  5.5 1.9 %collective-permute-start.1 = (bf16[2,2432]{1,0:T(2,128)(2,1)S(1)}, bf16[2,2432]{1,0:T(2,128)(2,1)S(1)}, u32[]{:S(2)}, u32[]{:S(2)}) collective-permute-start(bf16[2,2432]{1,0:T(2,128)(2,1)S(1)} %slice_bitcast_fusion.1), channel_id=1, source_target_pairs={{0,64},{64,0},{128,192},{192,128},{1,65},{65,1},{129,193},{193,129... | collective-permute-start | bytes 29192 | tf_op jit(solution)/shard_map/ppermute | solution.py:15
  7.5 1.4 gather_fusion
  9.2 0.8 gather_fusion.3
  14.3 0.8 reshape.406
  15.6 0.7 gather_fusion.1
  16.6 0.8 gather_fusion.5
  17.7 0.8 gather_fusion.6
  20.4 0.9 reshape.478
  21.3 18.4 %all-to-all-start = ((bf16[64,2,873]{2,1,0:T(2,128)(2,1)}), bf16[64,2,873]{2,1,0:T(2,128)(2,1)S(1)}, u32[]{:S(2)}, u32[]{:S(2)}) async-start(bf16[64,2,873]{2,1,0:T(2,128)(2,1)} %reshape.478), calls=%async_computation | async-start | bytes 458752 | tf_op jit(solution)/shard_map/all_to_all | solution.py:100
  39.9 17.0 %all-to-all-done = bf16[64,2,873]{2,1,0:T(2,128)(2,1)S(1)} async-done(((bf16[64,2,873]{2,1,0:T(2,128)(2,1)}), bf16[64,2,873]{2,1,0:T(2,128)(2,1)S(1)}, u32[]{:S(2)}, u32[]{:S(2)}) %all-to-all-start) | async-done | bytes 223520 | tf_op jit(solution)/shard_map/all_to_all | solution.py:100
  58.8 4.5 %collective-permute-start.2 = (bf16[1,2,128,64]{2,3,1,0:T(8,128)(2,1)S(1)}, bf16[1,2,128,64]{2,3,1,0:T(8,128)(2,1)S(1)}, u32[]{:S(2)}, u32[]{:S(2)}) collective-permute-start(bf16[1,2,128,64]{2,3,1,0:T(8,128)(2,1)S(1)} %get-tuple-element.18), channel_id=1, source_target_pairs={{0,4},{1,5},{2,6},{3,7},{4,0},{5,1},{6,2},{7,3},{8,12},{9,13},{10,... | collective-permute-start | bytes 98312 | tf_op jit(solution)/shard_map/ppermute | solution.py:133
  63.4 7.1 %collective-permute-start.3 = (bf16[1,2,128,64]{2,3,1,0:T(8,128)(2,1)S(1)}, bf16[1,2,128,64]{2,3,1,0:T(8,128)(2,1)S(1)}, u32[]{:S(2)}, u32[]{:S(2)}) collective-permute-start(bf16[1,2,128,64]{2,3,1,0:T(8,128)(2,1)S(1)} %get-tuple-element.18), channel_id=1, source_target_pairs={{0,8},{1,9},{2,10},{3,11},{4,12},{5,13},{6,14},{7,15},{8,0},{9,1},... | collective-permute-start | bytes 98312 | tf_op jit(solution)/shard_map/ppermute | solution.py:133
  70.5 4.6 %collective-permute-start.4 = (bf16[1,2,128,64]{2,3,1,0:T(8,128)(2,1)S(1)}, bf16[1,2,128,64]{2,3,1,0:T(8,128)(2,1)S(1)}, u32[]{:S(2)}, u32[]{:S(2)}) collective-permute-start(bf16[1,2,128,64]{2,3,1,0:T(8,128)(2,1)S(1)} %get-tuple-element.18), channel_id=1, source_target_pairs={{0,12},{1,13},{2,14},{3,15},{4,8},{5,9},{6,10},{7,11},{8,4},{9,5},... | collective-permute-start | bytes 98312 | tf_op jit(solution)/shard_map/ppermute | solution.py:133
  76.1 6.2 %collective-permute-start.11 = (bf16[1216,38]{1,0:T(8,128)(2,1)S(1)}, bf16[1216,38]{1,0:T(8,128)(2,1)S(1)}, u32[]{:S(2)}, u32[]{:S(2)}) collective-permute-start(bf16[1216,38]{1,0:T(8,128)(2,1)S(1)} %reshape.409), channel_id=1, source_target_pairs={{0,256},{256,0},{1,257},{257,1},{2,258},{258,2},{3,259},{259,3},{4... | collective-permute-start | bytes 277256 | tf_op jit(solution)/shard_map/ppermute | solution.py:15
  82.5 2.5 %collective-permute-start.5 = (bf16[4,2,128,64]{2,3,1,0:T(8,128)(2,1)S(1)}, bf16[4,2,128,64]{2,3,1,0:T(8,128)(2,1)S(1)}, u32[]{:S(2)}, u32[]{:S(2)}) collective-permute-start(bf16[4,2,128,64]{2,3,1,0:T(8,128)(2,1)S(1)} %pad_maximum_fusion.1), channel_id=1, source_target_pairs={{0,1},{1,0},{2,3},{3,2},{4,5},{5,4},{6,7},{7,6},{8,9},{9,8},{10,11... | collective-permute-start | bytes 393224 | tf_op jit(solution)/shard_map/ppermute | solution.py:133
  85.0 3.0 %collective-permute-start.6 = (bf16[4,2,128,64]{2,3,1,0:T(8,128)(2,1)S(1)}, bf16[4,2,128,64]{2,3,1,0:T(8,128)(2,1)S(1)}, u32[]{:S(2)}, u32[]{:S(2)}) collective-permute-start(bf16[4,2,128,64]{2,3,1,0:T(8,128)(2,1)S(1)} %pad_maximum_fusion.1), channel_id=1, source_target_pairs={{0,2},{1,3},{2,0},{3,1},{4,6},{5,7},{6,4},{7,5},{8,10},{9,11},{10,... | collective-permute-start | bytes 393224 | tf_op jit(solution)/shard_map/ppermute | solution.py:133
  88.1 3.7 %collective-permute-start.7 = (bf16[4,2,128,64]{2,3,1,0:T(8,128)(2,1)S(1)}, bf16[4,2,128,64]{2,3,1,0:T(8,128)(2,1)S(1)}, u32[]{:S(2)}, u32[]{:S(2)}) collective-permute-start(bf16[4,2,128,64]{2,3,1,0:T(8,128)(2,1)S(1)} %pad_maximum_fusion.1), channel_id=1, source_target_pairs={{0,3},{1,2},{2,1},{3,0},{4,7},{5,6},{6,5},{7,4},{8,11},{9,10},{10,... | collective-permute-start | bytes 393224 | tf_op jit(solution)/shard_map/ppermute | solution.py:133
  92.0 4.3 %collective-permute-done.6 = bf16[4,2,128,64]{2,3,1,0:T(8,128)(2,1)S(1)} collective-permute-done((bf16[4,2,128,64]{2,3,1,0:T(8,128)(2,1)S(1)}, bf16[4,2,128,64]{2,3,1,0:T(8,128)(2,1)S(1)}, u32[]{:S(2)}, u32[]{:S(2)}) %collective-permute-start.6) | collective-permute-done | bytes 131104 | tf_op jit(solution)/shard_map/ppermute | solution.py:133
  97.3 6.5 %collective-permute-start.10 = (bf16[10,2,128,64]{2,3,1,0:T(8,128)(2,1)S(1)}, bf16[10,2,128,64]{2,3,1,0:T(8,128)(2,1)S(1)}, u32[]{:S(2)}, u32[]{:S(2)}) collective-permute-start(bf16[10,2,128,64]{2,3,1,0:T(8,128)(2,1)S(1)} %slice.124), channel_id=1, source_target_pairs={{0,48},{1,49},{2,50},{3,51},{4,52},{5,53},{6,54},{7,55},{8,56},{9,... | collective-permute-start | bytes 983048 | tf_op jit(solution)/shard_map/ppermute | solution.py:148
  103.8 1.9 %collective-permute-start.8 = (bf16[10,2,128,64]{2,3,1,0:T(8,128)(2,1)S(1)}, bf16[10,2,128,64]{2,3,1,0:T(8,128)(2,1)S(1)}, u32[]{:S(2)}, u32[]{:S(2)}) collective-permute-start(bf16[10,2,128,64]{2,3,1,0:T(8,128)(2,1)S(1)} %slice.124), channel_id=1, source_target_pairs={{0,16},{1,17},{2,18},{3,19},{4,20},{5,21},{6,22},{7,23},{8,24},{9,... | collective-permute-start | bytes 983048 | tf_op jit(solution)/shard_map/ppermute | solution.py:148
  105.7 3.1 %collective-permute-start.9 = (bf16[10,2,128,64]{2,3,1,0:T(8,128)(2,1)S(1)}, bf16[10,2,128,64]{2,3,1,0:T(8,128)(2,1)S(1)}, u32[]{:S(2)}, u32[]{:S(2)}) collective-permute-start(bf16[10,2,128,64]{2,3,1,0:T(8,128)(2,1)S(1)} %slice.124), channel_id=1, source_target_pairs={{0,32},{1,33},{2,34},{3,35},{4,36},{5,37},{6,38},{7,39},{8,40},{9,... | collective-permute-start | bytes 983048 | tf_op jit(solution)/shard_map/ppermute | solution.py:148
  110.1 3.1 %collective-permute-done.8 = bf16[10,2,128,64]{2,3,1,0:T(8,128)(2,1)S(1)} collective-permute-done((bf16[10,2,128,64]{2,3,1,0:T(8,128)(2,1)S(1)}, bf16[10,2,128,64]{2,3,1,0:T(8,128)(2,1)S(1)}, u32[]{:S(2)}, u32[]{:S(2)}) %collective-permute-start.8) | collective-permute-done | bytes 327712 | tf_op jit(solution)/shard_map/ppermute | solution.py:148
  113.2 6.1 %collective-permute-done.9 = bf16[10,2,128,64]{2,3,1,0:T(8,128)(2,1)S(1)} collective-permute-done((bf16[10,2,128,64]{2,3,1,0:T(8,128)(2,1)S(1)}, bf16[10,2,128,64]{2,3,1,0:T(8,128)(2,1)S(1)}, u32[]{:S(2)}, u32[]{:S(2)}) %collective-permute-start.9) | collective-permute-done | bytes 327712 | tf_op jit(solution)/shard_map/ppermute | solution.py:148
  119.3 1.1 fusion
  120.5 0.8 reshape.480
  121.3 8.9 %all-to-all-start.1 = ((f32[64,1,152]{2,1,0:T(1,128)}), f32[64,1,152]{2,1,0:T(1,128)S(1)}, u32[]{:S(2)}, u32[]{:S(2)}) async-start(f32[64,1,152]{2,1,0:T(1,128)} %reshape.480), calls=%async_computation.1 | async-start | bytes 131072 | tf_op jit(solution)/shard_map/all_to_all | solution.py:158
  130.9 12.9 %all-to-all-done.1 = f32[64,1,152]{2,1,0:T(1,128)S(1)} async-done(((f32[64,1,152]{2,1,0:T(1,128)}), f32[64,1,152]{2,1,0:T(1,128)S(1)}, u32[]{:S(2)}, u32[]{:S(2)}) %all-to-all-start.1) | async-done | bytes 38944 | tf_op jit(solution)/shard_map/all_to_all | solution.py:158
  144.3 0.8 reduce.3
  146.2 5.5 %collective-permute-start.12 = (f32[2,2,32]{2,1,0:T(2,128)S(1)}, f32[2,2,32]{2,1,0:T(2,128)S(1)}, u32[]{:S(2)}, u32[]{:S(2)}) collective-permute-start(f32[2,2,32]{2,1,0:T(2,128)S(1)} %constant_dynamic-slice_fusion), channel_id=1, source_target_pairs={{0,256},{256,0},{1,257},{257,1},{2,258},{258,2},{3,259},{259,3},{4... | collective-permute-start | bytes 1544 | tf_op jit(solution)/shard_map/ppermute | solution.py:15
  (134 shorter events, 16.4 us)
Async XLA Ops:
  0.0 145.8 %copy-start = (bf16[2432,64]{0,1:T(8,128)(2,1)S(1)}, bf16[2432,64]{0,1:T(8,128)(2,1)}, u32[]{:S(2)}) copy-start(bf16[2432,64]{0,1:T(8,128)(2,1)} %param.30) | copy-start | bytes 933892
  0.0 9.1 %copy-start.1 = (s32[64]{0:T(128)S(1)}, s32[64]{0:T(128)}, u32[]{:S(2)}) copy-start(s32[64]{0:T(128)} %constant.157.clone) | copy-start | bytes 772
  0.8 15.5 %collective-permute-start = (bf16[2,2432]{1,0:T(2,128)(2,1)S(1)}, bf16[2,2432]{1,0:T(2,128)(2,1)S(1)}, u32[]{:S(2)}, u32[]{:S(2)}) collective-permute-start(bf16[2,2432]{1,0:T(2,128)(2,1)S(1)} %slice_bitcast_fusion.2), channel_id=1, source_target_pairs={{0,64},{64,0},{128,192},{192,128},{1,65},{65,1},{129,193},{193,129... | collective-permute-start | bytes 29192 | tf_op jit(solution)/shard_map/ppermute | solution.py:15
  5.5 11.9 %collective-permute-start.1 = (bf16[2,2432]{1,0:T(2,128)(2,1)S(1)}, bf16[2,2432]{1,0:T(2,128)(2,1)S(1)}, u32[]{:S(2)}, u32[]{:S(2)}) collective-permute-start(bf16[2,2432]{1,0:T(2,128)(2,1)S(1)} %slice_bitcast_fusion.1), channel_id=1, source_target_pairs={{0,64},{64,0},{128,192},{192,128},{1,65},{65,1},{129,193},{193,129... | collective-permute-start | bytes 29192 | tf_op jit(solution)/shard_map/ppermute | solution.py:15
  7.5 2.5 %copy-start.9 = (s32[4,2]{0,1:T(2,128)S(1)}, s32[4,2]{0,1:T(2,128)}, u32[]{:S(2)}) copy-start(s32[4,2]{0,1:T(2,128)} %param.26) | copy-start | bytes 100
  7.5 2.5 %copy-start.11 = (s32[4,2]{0,1:T(2,128)S(1)}, s32[4,2]{0,1:T(2,128)}, u32[]{:S(2)}) copy-start(s32[4,2]{0,1:T(2,128)} %param.25) | copy-start | bytes 100
  7.5 5.7 %copy-start.4 = (f32[1,6,2432]{2,0,1:T(1,128)S(1)}, f32[1,6,2432]{2,0,1:T(1,128)}, u32[]{:S(2)}) copy-start(f32[1,6,2432]{2,0,1:T(1,128)} %param.28) | copy-start | bytes 175108
  7.5 5.9 %copy-start.2 = (f32[1,6,2,2432]{3,2,1,0:T(2,128)S(1)}, f32[1,6,2,2432]{3,2,1,0:T(2,128)}, u32[]{:S(2)}) copy-start(f32[1,6,2,2432]{3,2,1,0:T(2,128)} %param.29) | copy-start | bytes 350212
  8.9 4.9 %copy-start.6 = (bf16[1,1,2,2,2432]{4,3,2,1,0:T(2,128)(2,1)S(1)}, bf16[1,1,2,2,2432]{4,3,2,1,0:T(2,128)(2,1)}, u32[]{:S(2)}) copy-start(bf16[1,1,2,2,2432]{4,3,2,1,0:T(2,128)(2,1)} %param.21) | copy-start | bytes 58372
  8.9 5.0 %copy-start.7 = (bf16[1,1,2,2,2432]{4,3,2,1,0:T(2,128)(2,1)S(1)}, bf16[1,1,2,2,2432]{4,3,2,1,0:T(2,128)(2,1)}, u32[]{:S(2)}) copy-start(bf16[1,1,2,2,2432]{4,3,2,1,0:T(2,128)(2,1)} %param.22) | copy-start | bytes 58372
  9.1 4.9 %copy-start.8 = (bf16[1,1,2,2,2432]{4,3,2,1,0:T(2,128)(2,1)S(1)}, bf16[1,1,2,2,2432]{4,3,2,1,0:T(2,128)(2,1)}, u32[]{:S(2)}) copy-start(bf16[1,1,2,2,2432]{4,3,2,1,0:T(2,128)(2,1)} %param.20) | copy-start | bytes 58372
  9.2 5.1 %copy-start.3 = (bf16[19,2432]{1,0:T(8,128)(2,1)S(1)}, bf16[19,2432]{1,0:T(8,128)(2,1)}, u32[]{:S(2)}) copy-start(bf16[19,2432]{1,0:T(8,128)(2,1)} %param.27) | copy-start | bytes 277252
  21.3 35.6 %all-to-all-start = ((bf16[64,2,873]{2,1,0:T(2,128)(2,1)}), bf16[64,2,873]{2,1,0:T(2,128)(2,1)S(1)}, u32[]{:S(2)}, u32[]{:S(2)}) async-start(bf16[64,2,873]{2,1,0:T(2,128)(2,1)} %reshape.478), calls=%async_computation | async-start | bytes 458752 | tf_op jit(solution)/shard_map/all_to_all | solution.py:100
  58.8 23.6 %collective-permute-start.2 = (bf16[1,2,128,64]{2,3,1,0:T(8,128)(2,1)S(1)}, bf16[1,2,128,64]{2,3,1,0:T(8,128)(2,1)S(1)}, u32[]{:S(2)}, u32[]{:S(2)}) collective-permute-start(bf16[1,2,128,64]{2,3,1,0:T(8,128)(2,1)S(1)} %get-tuple-element.18), channel_id=1, source_target_pairs={{0,4},{1,5},{2,6},{3,7},{4,0},{5,1},{6,2},{7,3},{8,12},{9,13},{10,... | collective-permute-start | bytes 98312 | tf_op jit(solution)/shard_map/ppermute | solution.py:133
  63.4 19.1 %collective-permute-start.3 = (bf16[1,2,128,64]{2,3,1,0:T(8,128)(2,1)S(1)}, bf16[1,2,128,64]{2,3,1,0:T(8,128)(2,1)S(1)}, u32[]{:S(2)}, u32[]{:S(2)}) collective-permute-start(bf16[1,2,128,64]{2,3,1,0:T(8,128)(2,1)S(1)} %get-tuple-element.18), channel_id=1, source_target_pairs={{0,8},{1,9},{2,10},{3,11},{4,12},{5,13},{6,14},{7,15},{8,0},{9,1},... | collective-permute-start | bytes 98312 | tf_op jit(solution)/shard_map/ppermute | solution.py:133
  70.5 12.0 %collective-permute-start.4 = (bf16[1,2,128,64]{2,3,1,0:T(8,128)(2,1)S(1)}, bf16[1,2,128,64]{2,3,1,0:T(8,128)(2,1)S(1)}, u32[]{:S(2)}, u32[]{:S(2)}) collective-permute-start(bf16[1,2,128,64]{2,3,1,0:T(8,128)(2,1)S(1)} %get-tuple-element.18), channel_id=1, source_target_pairs={{0,12},{1,13},{2,14},{3,15},{4,8},{5,9},{6,10},{7,11},{8,4},{9,5},... | collective-permute-start | bytes 98312 | tf_op jit(solution)/shard_map/ppermute | solution.py:133
  76.1 15.8 %collective-permute-start.11 = (bf16[1216,38]{1,0:T(8,128)(2,1)S(1)}, bf16[1216,38]{1,0:T(8,128)(2,1)S(1)}, u32[]{:S(2)}, u32[]{:S(2)}) collective-permute-start(bf16[1216,38]{1,0:T(8,128)(2,1)S(1)} %reshape.409), channel_id=1, source_target_pairs={{0,256},{256,0},{1,257},{257,1},{2,258},{258,2},{3,259},{259,3},{4... | collective-permute-start | bytes 277256 | tf_op jit(solution)/shard_map/ppermute | solution.py:15
  82.5 9.5 %collective-permute-start.5 = (bf16[4,2,128,64]{2,3,1,0:T(8,128)(2,1)S(1)}, bf16[4,2,128,64]{2,3,1,0:T(8,128)(2,1)S(1)}, u32[]{:S(2)}, u32[]{:S(2)}) collective-permute-start(bf16[4,2,128,64]{2,3,1,0:T(8,128)(2,1)S(1)} %pad_maximum_fusion.1), channel_id=1, source_target_pairs={{0,1},{1,0},{2,3},{3,2},{4,5},{5,4},{6,7},{7,6},{8,9},{9,8},{10,11... | collective-permute-start | bytes 393224 | tf_op jit(solution)/shard_map/ppermute | solution.py:133
  85.0 11.4 %collective-permute-start.6 = (bf16[4,2,128,64]{2,3,1,0:T(8,128)(2,1)S(1)}, bf16[4,2,128,64]{2,3,1,0:T(8,128)(2,1)S(1)}, u32[]{:S(2)}, u32[]{:S(2)}) collective-permute-start(bf16[4,2,128,64]{2,3,1,0:T(8,128)(2,1)S(1)} %pad_maximum_fusion.1), channel_id=1, source_target_pairs={{0,2},{1,3},{2,0},{3,1},{4,6},{5,7},{6,4},{7,5},{8,10},{9,11},{10,... | collective-permute-start | bytes 393224 | tf_op jit(solution)/shard_map/ppermute | solution.py:133
  88.1 8.3 %collective-permute-start.7 = (bf16[4,2,128,64]{2,3,1,0:T(8,128)(2,1)S(1)}, bf16[4,2,128,64]{2,3,1,0:T(8,128)(2,1)S(1)}, u32[]{:S(2)}, u32[]{:S(2)}) collective-permute-start(bf16[4,2,128,64]{2,3,1,0:T(8,128)(2,1)S(1)} %pad_maximum_fusion.1), channel_id=1, source_target_pairs={{0,3},{1,2},{2,1},{3,0},{4,7},{5,6},{6,5},{7,4},{8,11},{9,10},{10,... | collective-permute-start | bytes 393224 | tf_op jit(solution)/shard_map/ppermute | solution.py:133
  97.3 12.8 %collective-permute-start.10 = (bf16[10,2,128,64]{2,3,1,0:T(8,128)(2,1)S(1)}, bf16[10,2,128,64]{2,3,1,0:T(8,128)(2,1)S(1)}, u32[]{:S(2)}, u32[]{:S(2)}) collective-permute-start(bf16[10,2,128,64]{2,3,1,0:T(8,128)(2,1)S(1)} %slice.124), channel_id=1, source_target_pairs={{0,48},{1,49},{2,50},{3,51},{4,52},{5,53},{6,54},{7,55},{8,56},{9,... | collective-permute-start | bytes 983048 | tf_op jit(solution)/shard_map/ppermute | solution.py:148
  103.8 9.4 %collective-permute-start.8 = (bf16[10,2,128,64]{2,3,1,0:T(8,128)(2,1)S(1)}, bf16[10,2,128,64]{2,3,1,0:T(8,128)(2,1)S(1)}, u32[]{:S(2)}, u32[]{:S(2)}) collective-permute-start(bf16[10,2,128,64]{2,3,1,0:T(8,128)(2,1)S(1)} %slice.124), channel_id=1, source_target_pairs={{0,16},{1,17},{2,18},{3,19},{4,20},{5,21},{6,22},{7,23},{8,24},{9,... | collective-permute-start | bytes 983048 | tf_op jit(solution)/shard_map/ppermute | solution.py:148
  105.7 13.6 %collective-permute-start.9 = (bf16[10,2,128,64]{2,3,1,0:T(8,128)(2,1)S(1)}, bf16[10,2,128,64]{2,3,1,0:T(8,128)(2,1)S(1)}, u32[]{:S(2)}, u32[]{:S(2)}) collective-permute-start(bf16[10,2,128,64]{2,3,1,0:T(8,128)(2,1)S(1)} %slice.124), channel_id=1, source_target_pairs={{0,32},{1,33},{2,34},{3,35},{4,36},{5,37},{6,38},{7,39},{8,40},{9,... | collective-permute-start | bytes 983048 | tf_op jit(solution)/shard_map/ppermute | solution.py:148
  120.5 25.0 %copy-start.5 = (bf16[1,1,2,2,2432]{4,3,2,1,0:T(2,128)(2,1)S(1)}, bf16[1,1,2,2,2432]{4,3,2,1,0:T(2,128)(2,1)}, u32[]{:S(2)}) copy-start(bf16[1,1,2,2,2432]{4,3,2,1,0:T(2,128)(2,1)} %param.23) | copy-start | bytes 58372
  121.3 22.4 %all-to-all-start.1 = ((f32[64,1,152]{2,1,0:T(1,128)}), f32[64,1,152]{2,1,0:T(1,128)S(1)}, u32[]{:S(2)}, u32[]{:S(2)}) async-start(f32[64,1,152]{2,1,0:T(1,128)} %reshape.480), calls=%async_computation.1 | async-start | bytes 131072 | tf_op jit(solution)/shard_map/all_to_all | solution.py:158
  145.3 6.4 %copy-start.12 = (f32[6]{0:T(128)S(1)}, f32[6]{0:T(128)}, u32[]{:S(2)}) copy-start(f32[6]{0:T(128)} %param.32) | copy-start | bytes 76
  145.3 6.4 %copy-start.13 = (f32[6]{0:T(128)S(1)}, f32[6]{0:T(128)}, u32[]{:S(2)}) copy-start(f32[6]{0:T(128)} %param.31) | copy-start | bytes 76
  145.3 7.1 %copy-start.10 = (f32[1,2,2,32]{3,2,1,0:T(2,128)S(1)}, f32[1,2,2,32]{3,2,1,0:T(2,128)}, u32[]{:S(2)}) copy-start(f32[1,2,2,32]{3,2,1,0:T(2,128)} %param.24) | copy-start | bytes 1540
  146.2 6.3 %collective-permute-start.12 = (f32[2,2,32]{2,1,0:T(2,128)S(1)}, f32[2,2,32]{2,1,0:T(2,128)S(1)}, u32[]{:S(2)}, u32[]{:S(2)}) collective-permute-start(f32[2,2,32]{2,1,0:T(2,128)S(1)} %constant_dynamic-slice_fusion), channel_id=1, source_target_pairs={{0,256},{256,0},{1,257},{257,1},{2,258},{258,2},{3,259},{259,3},{4... | collective-permute-start | bytes 1544 | tf_op jit(solution)/shard_map/ppermute | solution.py:15

commit v6 on v5

--- a/solution.py
+++ b/solution.py
@@ -28,6 +28,19 @@
         jnp.einsum("sk,kd->sd", weights, values_all, preferred_element_type=jnp.float32)
         / row_total
     )
+
+
+def projection_split(n):
+    regions, chunks = [], []
+    for j in range(n):
+        x, z = divmod(j, 16)
+        regions.append(x % 2)
+        chunks.append((x // 2) * 16 + z)
+    return regions, chunks
+
+
+def owner_of(region_of, chunk_of, region, chunk):
+    return [j for j in range(len(region_of)) if region_of[j] == region and chunk_of[j] == chunk][0]
 
 
 def plane_heads(n):
@@ -83,8 +96,11 @@
         return jnp.take(x, jnp.array(head_table, jnp.int32), axis=0)
 
     block_rows = w_out.shape[0]
-    col_width = D // nseq
-    w_parts = w_out.reshape(block_rows, nseq, col_width).transpose(1, 0, 2)
+    region_of, chunk_of = projection_split(nseq)
+    chunks = max(chunk_of) + 1
+    col_width = D // chunks
+    w_parts = w_out.reshape(block_rows, chunks, col_width).transpose(1, 0, 2)
+    w_parts = jnp.take(w_parts, jnp.array(chunk_of, jnp.int32), axis=0)
     packed = jnp.concatenate(
         [
             to_heads(local_query),
@@ -140,11 +156,12 @@
     my_x = me // plane
     by_z = jnp.take(gathered, jnp.take(jnp.array(inverse, jnp.int32), jnp.bitwise_xor(my_z, jnp.arange(plane))), axis=0)
     used = plane_heads(nseq)
-    outgoing = by_z[:used]
-    parts = [by_z]
+    my_region = my_x % 2
+    parts = [lax.dynamic_index_in_dim(by_z, my_region, 1, keepdims=False)]
     sources = [my_x * plane + jnp.arange(plane)]
     for digit in (1, 2, 3):
         shift = digit * plane
+        outgoing = lax.dynamic_index_in_dim(by_z[:used], (my_x ^ digit) % 2, 1, keepdims=False)
         parts.append(lax.ppermute(outgoing, "seq", [(i, i ^ shift) for i in range(nseq)]))
         sources.append(jnp.bitwise_xor(my_x, digit) * plane + jnp.arange(used))
     gathered = jnp.concatenate(parts, 0)
@@ -152,11 +169,16 @@
     w_heads = jnp.pad(w_cols.reshape(HEADS, HD, col_width), ((0, 1), (0, 0), (0, 0)))
     w_ordered = jnp.take(w_heads, source_head, axis=0)
     projected_cols = jnp.einsum(
-        "irsd,idc->rsc", gathered, w_ordered, preferred_element_type=jnp.float32
-    ).reshape(2 * slot_total, col_width)
-    projected_parts = projected_cols.reshape(2, nseq, shard_rows, col_width).transpose(1, 0, 2, 3)
-    projected = lax.all_to_all(projected_parts, "seq", 0, 0, tiled=True)
-    projected = projected.transpose(1, 2, 0, 3).reshape(2, shard_rows, D)
+        "isd,idc->sc", gathered, w_ordered, preferred_element_type=jnp.float32
+    )
+    projected_parts = projected_cols.reshape(nseq, shard_rows, col_width)
+    received = lax.all_to_all(projected_parts, "seq", 0, 0, tiled=True)
+    by_region = []
+    for region in range(2):
+        owners = [owner_of(region_of, chunk_of, region, c) for c in range(chunks)]
+        picked = jnp.take(received, jnp.array(owners, jnp.int32), axis=0)
+        by_region.append(picked.transpose(1, 0, 2).reshape(shard_rows, D))
+    projected = jnp.stack(by_region)
 
     item_count = guide.shape[0]
     indicator_mask = (jnp.arange(item_count)[None, :] == item_ids[:, None]).astype(jnp.float32)

time: 154 us -> 153 us (level)
  starting transfers between devices: 81.9 us -> 78.9 us
    ppermute x3, waiting for transfers between devices: 9.22 us -> 4.13 us  [shards(): lax.ppermute(outgoing, 'seq', [(i, i ^ shift) for i in range(nseq)])]
    all_to_all x1, waiting for transfers between devices: 17 us -> 20.4 us  [shards(): joint = lax.all_to_all(joint, 'seq', 0, 0, tiled=True)]
    ppermute x3, starting transfers between devices: 11.6 us -> 9.34 us  [shards(): lax.ppermute(outgoing, 'seq', [(i, i ^ shift) for i in range(nseq)])]
    gather x0 -> x4, local copies, waits for them, and re-layouts: none -> 2.09 us  [the longest x2 1.22 us: shards(): picked = jnp.take(received, jnp.array(owners, jnp.int32), axis=0)]
    ppermute x6, waiting for transfers between devices: 4.36 us -> 6.21 us  [shards(): lax.ppermute(gathered, 'seq', [(i, i ^ shift) for i in range(nseq)])]
  transfers between devices with their start and end apart: 15 -> 15, of which waited for: 6 -> 6; matrix products, arithmetic and copies ran while one was open for 9% -> 11% of each run, Pallas kernels for 0% -> 0%
where the time goes in v6:
time: 153 us; the launch traced here: 152 us
  starting transfers between devices  78.9 us (52%)
  waiting for transfers between devices  44.8 us (29%)
  local copies, waits for them, and re-layouts  16.6 us (11%)
  other arithmetic  7.95 us (5%)
  matrix products  2.77 us (2%)
    ppermute x6, starting transfers between devices, shards(): lax.ppermute(gathered, 'seq', [(i, i ^ shift) for i in range(nseq)])  25.5 us
    all_to_all x1, waiting for transfers between devices, shards(): joint = lax.all_to_all(joint, 'seq', 0, 0, tiled=True)  20.4 us
    all_to_all x1, starting transfers between devices, shards(): joint = lax.all_to_all(joint, 'seq', 0, 0, tiled=True)  18.4 us
    ppermute x4, starting transfers between devices, from_partner(): lax.ppermute(x, axis, [(i, i ^ 1 << apart) for i in range(lax.axis_size(a...  17.9 us
    all_to_all x1, waiting for transfers between devices, shards(): received = lax.all_to_all(projected_parts, 'seq', 0, 0, tiled=True)  13.5 us
    ppermute x3, starting transfers between devices, shards(): lax.ppermute(outgoing, 'seq', [(i, i ^ shift) for i in range(nseq)])  9.34 us
    all_to_all x1, starting transfers between devices, shards(): received = lax.all_to_all(projected_parts, 'seq', 0, 0, tiled=True)  7.77 us
    ppermute x6, waiting for transfers between devices, shards(): lax.ppermute(gathered, 'seq', [(i, i ^ shift) for i in range(nseq)])  6.21 us
  transfers between devices with their start and end apart: 15, of which 6 were waited for; matrix products, arithmetic and copies ran while one was open for 11% of the time, Pallas kernels for 0%

profile of v6, /device:TPU:1, one launch (start us, length us, event | category | flops | bytes accessed | tf_op | source)
XLA Modules:
  0.0 152.1 jit_solution(13525615753442447131)
XLA Ops:
  0.0 0.8 slice_bitcast_fusion.1
  0.8 4.0 %collective-permute-start.1 = (bf16[2,2432]{1,0:T(2,128)(2,1)S(1)}, bf16[2,2432]{1,0:T(2,128)(2,1)S(1)}, u32[]{:S(2)}, u32[]{:S(2)}) collective-permute-start(bf16[2,2432]{1,0:T(2,128)(2,1)S(1)} %slice_bitcast_fusion.1), channel_id=1, source_target_pairs={{0,64},{64,0},{128,192},{192,128},{1,65},{65,1},{129,193},{193,129... | collective-permute-start | bytes 29192 | tf_op jit(solution)/shard_map/ppermute | solution.py:15
  4.8 0.7 slice_bitcast_fusion.2
  5.5 1.9 %collective-permute-start = (bf16[2,2432]{1,0:T(2,128)(2,1)S(1)}, bf16[2,2432]{1,0:T(2,128)(2,1)S(1)}, u32[]{:S(2)}, u32[]{:S(2)}) collective-permute-start(bf16[2,2432]{1,0:T(2,128)(2,1)S(1)} %slice_bitcast_fusion.2), channel_id=1, source_target_pairs={{0,64},{64,0},{128,192},{192,128},{1,65},{65,1},{129,193},{193,129... | collective-permute-start | bytes 29192 | tf_op jit(solution)/shard_map/ppermute | solution.py:15
  8.2 1.3 gather_fusion
  9.6 0.9 constant_dynamic-slice_fusion.3
  14.2 0.8 gather_fusion.4
  17.8 0.7 gather_fusion.1
  18.9 0.8 gather_fusion.7
  20.0 0.8 gather_fusion.6
  21.9 0.8 reduce.2
  22.8 1.1 reshape.512
  23.8 18.4 %all-to-all-start = ((bf16[64,2,1234]{2,1,0:T(2,128)(2,1)}), bf16[64,2,1234]{2,1,0:T(2,128)(2,1)S(1)}, u32[]{:S(2)}, u32[]{:S(2)}) async-start(bf16[64,2,1234]{2,1,0:T(2,128)(2,1)} %reshape.512), calls=%async_computation | async-start | bytes 655360 | tf_op jit(solution)/shard_map/all_to_all | solution.py:116
  42.9 20.4 %all-to-all-done = bf16[64,2,1234]{2,1,0:T(2,128)(2,1)S(1)} async-done(((bf16[64,2,1234]{2,1,0:T(2,128)(2,1)}), bf16[64,2,1234]{2,1,0:T(2,128)(2,1)S(1)}, u32[]{:S(2)}, u32[]{:S(2)}) %all-to-all-start) | async-done | bytes 315936 | tf_op jit(solution)/shard_map/all_to_all | solution.py:116
  65.4 4.6 %collective-permute-start.2 = (bf16[1,2,128,64]{2,3,1,0:T(8,128)(2,1)S(1)}, bf16[1,2,128,64]{2,3,1,0:T(8,128)(2,1)S(1)}, u32[]{:S(2)}, u32[]{:S(2)}) collective-permute-start(bf16[1,2,128,64]{2,3,1,0:T(8,128)(2,1)S(1)} %get-tuple-element.24), channel_id=1, source_target_pairs={{0,4},{1,5},{2,6},{3,7},{4,0},{5,1},{6,2},{7,3},{8,12},{9,13},{10,... | collective-permute-start | bytes 98312 | tf_op jit(solution)/shard_map/ppermute | solution.py:149
  70.0 7.5 %collective-permute-start.3 = (bf16[1,2,128,64]{2,3,1,0:T(8,128)(2,1)S(1)}, bf16[1,2,128,64]{2,3,1,0:T(8,128)(2,1)S(1)}, u32[]{:S(2)}, u32[]{:S(2)}) collective-permute-start(bf16[1,2,128,64]{2,3,1,0:T(8,128)(2,1)S(1)} %get-tuple-element.24), channel_id=1, source_target_pairs={{0,8},{1,9},{2,10},{3,11},{4,12},{5,13},{6,14},{7,15},{8,0},{9,1},... | collective-permute-start | bytes 98312 | tf_op jit(solution)/shard_map/ppermute | solution.py:149
  77.5 4.1 %collective-permute-start.4 = (bf16[1,2,128,64]{2,3,1,0:T(8,128)(2,1)S(1)}, bf16[1,2,128,64]{2,3,1,0:T(8,128)(2,1)S(1)}, u32[]{:S(2)}, u32[]{:S(2)}) collective-permute-start(bf16[1,2,128,64]{2,3,1,0:T(8,128)(2,1)S(1)} %get-tuple-element.24), channel_id=1, source_target_pairs={{0,12},{1,13},{2,14},{3,15},{4,8},{5,9},{6,10},{7,11},{8,4},{9,5},... | collective-permute-start | bytes 98312 | tf_op jit(solution)/shard_map/ppermute | solution.py:149
  82.8 6.4 %collective-permute-start.11 = (bf16[1216,76]{1,0:T(8,128)(2,1)S(1)}, bf16[1216,76]{1,0:T(8,128)(2,1)S(1)}, u32[]{:S(2)}, u32[]{:S(2)}) collective-permute-start(bf16[1216,76]{1,0:T(8,128)(2,1)S(1)} %reshape.417), channel_id=1, source_target_pairs={{0,256},{256,0},{1,257},{257,1},{2,258},{258,2},{3,259},{259,3},{4... | collective-permute-start | bytes 554504 | tf_op jit(solution)/shard_map/ppermute | solution.py:15
  89.2 2.5 %collective-permute-start.5 = (bf16[4,2,128,64]{2,3,1,0:T(8,128)(2,1)S(1)}, bf16[4,2,128,64]{2,3,1,0:T(8,128)(2,1)S(1)}, u32[]{:S(2)}, u32[]{:S(2)}) collective-permute-start(bf16[4,2,128,64]{2,3,1,0:T(8,128)(2,1)S(1)} %pad_maximum_fusion.1), channel_id=1, source_target_pairs={{0,1},{1,0},{2,3},{3,2},{4,5},{5,4},{6,7},{7,6},{8,9},{9,8},{10,11... | collective-permute-start | bytes 393224 | tf_op jit(solution)/shard_map/ppermute | solution.py:149
  91.7 2.8 %collective-permute-start.6 = (bf16[4,2,128,64]{2,3,1,0:T(8,128)(2,1)S(1)}, bf16[4,2,128,64]{2,3,1,0:T(8,128)(2,1)S(1)}, u32[]{:S(2)}, u32[]{:S(2)}) collective-permute-start(bf16[4,2,128,64]{2,3,1,0:T(8,128)(2,1)S(1)} %pad_maximum_fusion.1), channel_id=1, source_target_pairs={{0,2},{1,3},{2,0},{3,1},{4,6},{5,7},{6,4},{7,5},{8,10},{9,11},{10,... | collective-permute-start | bytes 393224 | tf_op jit(solution)/shard_map/ppermute | solution.py:149
  94.6 4.0 %collective-permute-start.7 = (bf16[4,2,128,64]{2,3,1,0:T(8,128)(2,1)S(1)}, bf16[4,2,128,64]{2,3,1,0:T(8,128)(2,1)S(1)}, u32[]{:S(2)}, u32[]{:S(2)}) collective-permute-start(bf16[4,2,128,64]{2,3,1,0:T(8,128)(2,1)S(1)} %pad_maximum_fusion.1), channel_id=1, source_target_pairs={{0,3},{1,2},{2,1},{3,0},{4,7},{5,6},{6,5},{7,4},{8,11},{9,10},{10,... | collective-permute-start | bytes 393224 | tf_op jit(solution)/shard_map/ppermute | solution.py:149
  98.6 6.2 %collective-permute-done.6 = bf16[4,2,128,64]{2,3,1,0:T(8,128)(2,1)S(1)} collective-permute-done((bf16[4,2,128,64]{2,3,1,0:T(8,128)(2,1)S(1)}, bf16[4,2,128,64]{2,3,1,0:T(8,128)(2,1)S(1)}, u32[]{:S(2)}, u32[]{:S(2)}) %collective-permute-start.6) | collective-permute-done | bytes 131104 | tf_op jit(solution)/shard_map/ppermute | solution.py:149
  105.7 4.9 %collective-permute-start.10 = (bf16[10,128,64]{1,2,0:T(8,128)(2,1)S(1)}, bf16[10,128,64]{1,2,0:T(8,128)(2,1)S(1)}, u32[]{:S(2)}, u32[]{:S(2)}) collective-permute-start(bf16[10,128,64]{1,2,0:T(8,128)(2,1)S(1)} %get-tuple-element.12), channel_id=1, source_target_pairs={{0,48},{1,49},{2,50},{3,51},{4,52},{5,53},{6,54},{7,55},{8,56},{9,... | collective-permute-start | bytes 491528 | tf_op jit(solution)/shard_map/ppermute | solution.py:165
  110.7 1.9 %collective-permute-start.9 = (bf16[10,128,64]{1,2,0:T(8,128)(2,1)S(1)}, bf16[10,128,64]{1,2,0:T(8,128)(2,1)S(1)}, u32[]{:S(2)}, u32[]{:S(2)}) collective-permute-start(bf16[10,128,64]{1,2,0:T(8,128)(2,1)S(1)} %get-tuple-element.13), channel_id=1, source_target_pairs={{0,32},{1,33},{2,34},{3,35},{4,36},{5,37},{6,38},{7,39},{8,40},{9,... | collective-permute-start | bytes 491528 | tf_op jit(solution)/shard_map/ppermute | solution.py:165
  112.6 2.5 %collective-permute-start.8 = (bf16[10,128,64]{1,2,0:T(8,128)(2,1)S(1)}, bf16[10,128,64]{1,2,0:T(8,128)(2,1)S(1)}, u32[]{:S(2)}, u32[]{:S(2)}) collective-permute-start(bf16[10,128,64]{1,2,0:T(8,128)(2,1)S(1)} %get-tuple-element.11), channel_id=1, source_target_pairs={{0,16},{1,17},{2,18},{3,19},{4,20},{5,21},{6,22},{7,23},{8,24},{9,... | collective-permute-start | bytes 491528 | tf_op jit(solution)/shard_map/ppermute | solution.py:165
  115.6 0.7 gather_fusion.5
  116.3 1.9 %collective-permute-done.9 = bf16[10,128,64]{1,2,0:T(8,128)(2,1)S(1)} collective-permute-done((bf16[10,128,64]{1,2,0:T(8,128)(2,1)S(1)}, bf16[10,128,64]{1,2,0:T(8,128)(2,1)S(1)}, u32[]{:S(2)}, u32[]{:S(2)}) %collective-permute-start.9) | collective-permute-done | bytes 163872 | tf_op jit(solution)/shard_map/ppermute | solution.py:165
  118.2 2.2 %collective-permute-done.8 = bf16[10,128,64]{1,2,0:T(8,128)(2,1)S(1)} collective-permute-done((bf16[10,128,64]{1,2,0:T(8,128)(2,1)S(1)}, bf16[10,128,64]{1,2,0:T(8,128)(2,1)S(1)}, u32[]{:S(2)}, u32[]{:S(2)}) %collective-permute-start.8) | collective-permute-done | bytes 163872 | tf_op jit(solution)/shard_map/ppermute | solution.py:165
  120.5 1.1 fusion.6
  121.6 7.8 %all-to-all-start.1 = ((f32[64,2,76]{2,1,0:T(2,128)}), f32[64,2,76]{2,1,0:T(2,128)S(1)}, u32[]{:S(2)}, u32[]{:S(2)}) async-start(f32[64,2,76]{2,1,0:T(2,128)} %bitcast.39), calls=%async_computation.1 | async-start | bytes 131072 | tf_op jit(solution)/shard_map/all_to_all | solution.py:175
  129.4 13.5 %all-to-all-done.1 = f32[64,2,76]{2,1,0:T(2,128)S(1)} async-done(((f32[64,2,76]{2,1,0:T(2,128)}), f32[64,2,76]{2,1,0:T(2,128)S(1)}, u32[]{:S(2)}, u32[]{:S(2)}) %all-to-all-start.1) | async-done | bytes 38944 | tf_op jit(solution)/shard_map/all_to_all | solution.py:175
  145.1 5.6 %collective-permute-start.12 = (f32[2,2,32]{2,1,0:T(2,128)S(1)}, f32[2,2,32]{2,1,0:T(2,128)S(1)}, u32[]{:S(2)}, u32[]{:S(2)}) collective-permute-start(f32[2,2,32]{2,1,0:T(2,128)S(1)} %constant_dynamic-slice_fusion), channel_id=1, source_target_pairs={{0,256},{256,0},{1,257},{257,1},{2,258},{258,2},{3,259},{259,3},{4... | collective-permute-start | bytes 1544 | tf_op jit(solution)/shard_map/ppermute | solution.py:15
  (133 shorter events, 17.5 us)
Async XLA Ops:
  0.0 144.7 %copy-start = (bf16[2432,64]{0,1:T(8,128)(2,1)S(1)}, bf16[2432,64]{0,1:T(8,128)(2,1)}, u32[]{:S(2)}) copy-start(bf16[2432,64]{0,1:T(8,128)(2,1)} %param.35) | copy-start | bytes 933892
  0.0 14.2 %copy-start.1 = (s32[64]{0:T(128)S(1)}, s32[64]{0:T(128)}, u32[]{:S(2)}) copy-start(s32[64]{0:T(128)} %constant.218.clone) | copy-start | bytes 772
  0.0 15.8 %copy-start.5 = (bf16[1,1,2,2,2432]{4,3,2,1,0:T(2,128)(2,1)S(1)}, bf16[1,1,2,2,2432]{4,3,2,1,0:T(2,128)(2,1)}, u32[]{:S(2)}) copy-start(bf16[1,1,2,2,2432]{4,3,2,1,0:T(2,128)(2,1)} %param.27) | copy-start | bytes 58372
  0.0 15.9 %copy-start.6 = (bf16[1,1,2,2,2432]{4,3,2,1,0:T(2,128)(2,1)S(1)}, bf16[1,1,2,2,2432]{4,3,2,1,0:T(2,128)(2,1)}, u32[]{:S(2)}) copy-start(bf16[1,1,2,2,2432]{4,3,2,1,0:T(2,128)(2,1)} %param.26) | copy-start | bytes 58372
  0.0 16.0 %copy-start.3 = (bf16[19,2432]{1,0:T(8,128)(2,1)S(1)}, bf16[19,2432]{1,0:T(8,128)(2,1)}, u32[]{:S(2)}) copy-start(bf16[19,2432]{1,0:T(8,128)(2,1)} %param.32) | copy-start | bytes 277252
  0.8 17.8 %collective-permute-start.1 = (bf16[2,2432]{1,0:T(2,128)(2,1)S(1)}, bf16[2,2432]{1,0:T(2,128)(2,1)S(1)}, u32[]{:S(2)}, u32[]{:S(2)}) collective-permute-start(bf16[2,2432]{1,0:T(2,128)(2,1)S(1)} %slice_bitcast_fusion.1), channel_id=1, source_target_pairs={{0,64},{64,0},{128,192},{192,128},{1,65},{65,1},{129,193},{193,129... | collective-permute-start | bytes 29192 | tf_op jit(solution)/shard_map/ppermute | solution.py:15
  5.5 14.1 %collective-permute-start = (bf16[2,2432]{1,0:T(2,128)(2,1)S(1)}, bf16[2,2432]{1,0:T(2,128)(2,1)S(1)}, u32[]{:S(2)}, u32[]{:S(2)}) collective-permute-start(bf16[2,2432]{1,0:T(2,128)(2,1)S(1)} %slice_bitcast_fusion.2), channel_id=1, source_target_pairs={{0,64},{64,0},{128,192},{192,128},{1,65},{65,1},{129,193},{193,129... | collective-permute-start | bytes 29192 | tf_op jit(solution)/shard_map/ppermute | solution.py:15
  16.6 1.0 copy-start.8
  22.7 19.6 %copy-start.4 = (f32[1,6,2432]{2,0,1:T(1,128)S(1)}, f32[1,6,2432]{2,0,1:T(1,128)}, u32[]{:S(2)}) copy-start(f32[1,6,2432]{2,0,1:T(1,128)} %param.33) | copy-start | bytes 175108
  22.7 19.8 %copy-start.2 = (f32[1,6,2,2432]{3,2,1,0:T(2,128)S(1)}, f32[1,6,2,2432]{3,2,1,0:T(2,128)}, u32[]{:S(2)}) copy-start(f32[1,6,2,2432]{3,2,1,0:T(2,128)} %param.34) | copy-start | bytes 350212
  23.8 39.5 %all-to-all-start = ((bf16[64,2,1234]{2,1,0:T(2,128)(2,1)}), bf16[64,2,1234]{2,1,0:T(2,128)(2,1)S(1)}, u32[]{:S(2)}, u32[]{:S(2)}) async-start(bf16[64,2,1234]{2,1,0:T(2,128)(2,1)} %reshape.512), calls=%async_computation | async-start | bytes 655360 | tf_op jit(solution)/shard_map/all_to_all | solution.py:116
  65.4 23.7 %collective-permute-start.2 = (bf16[1,2,128,64]{2,3,1,0:T(8,128)(2,1)S(1)}, bf16[1,2,128,64]{2,3,1,0:T(8,128)(2,1)S(1)}, u32[]{:S(2)}, u32[]{:S(2)}) collective-permute-start(bf16[1,2,128,64]{2,3,1,0:T(8,128)(2,1)S(1)} %get-tuple-element.24), channel_id=1, source_target_pairs={{0,4},{1,5},{2,6},{3,7},{4,0},{5,1},{6,2},{7,3},{8,12},{9,13},{10,... | collective-permute-start | bytes 98312 | tf_op jit(solution)/shard_map/ppermute | solution.py:149
  70.0 19.2 %collective-permute-start.3 = (bf16[1,2,128,64]{2,3,1,0:T(8,128)(2,1)S(1)}, bf16[1,2,128,64]{2,3,1,0:T(8,128)(2,1)S(1)}, u32[]{:S(2)}, u32[]{:S(2)}) collective-permute-start(bf16[1,2,128,64]{2,3,1,0:T(8,128)(2,1)S(1)} %get-tuple-element.24), channel_id=1, source_target_pairs={{0,8},{1,9},{2,10},{3,11},{4,12},{5,13},{6,14},{7,15},{8,0},{9,1},... | collective-permute-start | bytes 98312 | tf_op jit(solution)/shard_map/ppermute | solution.py:149
  77.5 11.7 %collective-permute-start.4 = (bf16[1,2,128,64]{2,3,1,0:T(8,128)(2,1)S(1)}, bf16[1,2,128,64]{2,3,1,0:T(8,128)(2,1)S(1)}, u32[]{:S(2)}, u32[]{:S(2)}) collective-permute-start(bf16[1,2,128,64]{2,3,1,0:T(8,128)(2,1)S(1)} %get-tuple-element.24), channel_id=1, source_target_pairs={{0,12},{1,13},{2,14},{3,15},{4,8},{5,9},{6,10},{7,11},{8,4},{9,5},... | collective-permute-start | bytes 98312 | tf_op jit(solution)/shard_map/ppermute | solution.py:149
  82.8 32.4 %collective-permute-start.11 = (bf16[1216,76]{1,0:T(8,128)(2,1)S(1)}, bf16[1216,76]{1,0:T(8,128)(2,1)S(1)}, u32[]{:S(2)}, u32[]{:S(2)}) collective-permute-start(bf16[1216,76]{1,0:T(8,128)(2,1)S(1)} %reshape.417), channel_id=1, source_target_pairs={{0,256},{256,0},{1,257},{257,1},{2,258},{258,2},{3,259},{259,3},{4... | collective-permute-start | bytes 554504 | tf_op jit(solution)/shard_map/ppermute | solution.py:15
  89.2 9.3 %collective-permute-start.5 = (bf16[4,2,128,64]{2,3,1,0:T(8,128)(2,1)S(1)}, bf16[4,2,128,64]{2,3,1,0:T(8,128)(2,1)S(1)}, u32[]{:S(2)}, u32[]{:S(2)}) collective-permute-start(bf16[4,2,128,64]{2,3,1,0:T(8,128)(2,1)S(1)} %pad_maximum_fusion.1), channel_id=1, source_target_pairs={{0,1},{1,0},{2,3},{3,2},{4,5},{5,4},{6,7},{7,6},{8,9},{9,8},{10,11... | collective-permute-start | bytes 393224 | tf_op jit(solution)/shard_map/ppermute | solution.py:149
  91.7 13.1 %collective-permute-start.6 = (bf16[4,2,128,64]{2,3,1,0:T(8,128)(2,1)S(1)}, bf16[4,2,128,64]{2,3,1,0:T(8,128)(2,1)S(1)}, u32[]{:S(2)}, u32[]{:S(2)}) collective-permute-start(bf16[4,2,128,64]{2,3,1,0:T(8,128)(2,1)S(1)} %pad_maximum_fusion.1), channel_id=1, source_target_pairs={{0,2},{1,3},{2,0},{3,1},{4,6},{5,7},{6,4},{7,5},{8,10},{9,11},{10,... | collective-permute-start | bytes 393224 | tf_op jit(solution)/shard_map/ppermute | solution.py:149
  94.6 10.3 %collective-permute-start.7 = (bf16[4,2,128,64]{2,3,1,0:T(8,128)(2,1)S(1)}, bf16[4,2,128,64]{2,3,1,0:T(8,128)(2,1)S(1)}, u32[]{:S(2)}, u32[]{:S(2)}) collective-permute-start(bf16[4,2,128,64]{2,3,1,0:T(8,128)(2,1)S(1)} %pad_maximum_fusion.1), channel_id=1, source_target_pairs={{0,3},{1,2},{2,1},{3,0},{4,7},{5,6},{6,5},{7,4},{8,11},{9,10},{10,... | collective-permute-start | bytes 393224 | tf_op jit(solution)/shard_map/ppermute | solution.py:149
  105.7 10.6 %collective-permute-start.10 = (bf16[10,128,64]{1,2,0:T(8,128)(2,1)S(1)}, bf16[10,128,64]{1,2,0:T(8,128)(2,1)S(1)}, u32[]{:S(2)}, u32[]{:S(2)}) collective-permute-start(bf16[10,128,64]{1,2,0:T(8,128)(2,1)S(1)} %get-tuple-element.12), channel_id=1, source_target_pairs={{0,48},{1,49},{2,50},{3,51},{4,52},{5,53},{6,54},{7,55},{8,56},{9,... | collective-permute-start | bytes 491528 | tf_op jit(solution)/shard_map/ppermute | solution.py:165
  110.7 7.6 %collective-permute-start.9 = (bf16[10,128,64]{1,2,0:T(8,128)(2,1)S(1)}, bf16[10,128,64]{1,2,0:T(8,128)(2,1)S(1)}, u32[]{:S(2)}, u32[]{:S(2)}) collective-permute-start(bf16[10,128,64]{1,2,0:T(8,128)(2,1)S(1)} %get-tuple-element.13), channel_id=1, source_target_pairs={{0,32},{1,33},{2,34},{3,35},{4,36},{5,37},{6,38},{7,39},{8,40},{9,... | collective-permute-start | bytes 491528 | tf_op jit(solution)/shard_map/ppermute | solution.py:165
  112.6 7.8 %collective-permute-start.8 = (bf16[10,128,64]{1,2,0:T(8,128)(2,1)S(1)}, bf16[10,128,64]{1,2,0:T(8,128)(2,1)S(1)}, u32[]{:S(2)}, u32[]{:S(2)}) collective-permute-start(bf16[10,128,64]{1,2,0:T(8,128)(2,1)S(1)} %get-tuple-element.11), channel_id=1, source_target_pairs={{0,16},{1,17},{2,18},{3,19},{4,20},{5,21},{6,22},{7,23},{8,24},{9,... | collective-permute-start | bytes 491528 | tf_op jit(solution)/shard_map/ppermute | solution.py:165
  116.3 13.1 %copy-start.12 = (s32[32]{0:T(128)S(1)}, s32[32]{0:T(128)}, u32[]{:S(2)}) copy-start(s32[32]{0:T(128)} %constant.295) | copy-start | bytes 388
  116.3 13.1 %copy-start.13 = (s32[32]{0:T(128)S(1)}, s32[32]{0:T(128)}, u32[]{:S(2)}) copy-start(s32[32]{0:T(128)} %constant.294) | copy-start | bytes 388
  116.3 28.1 %copy-start.7 = (bf16[1,1,2,2,2432]{4,3,2,1,0:T(2,128)(2,1)S(1)}, bf16[1,1,2,2,2432]{4,3,2,1,0:T(2,128)(2,1)}, u32[]{:S(2)}) copy-start(bf16[1,1,2,2,2432]{4,3,2,1,0:T(2,128)(2,1)} %param.28) | copy-start | bytes 58372
  121.6 29.1 %copy-start.10 = (f32[6]{0:T(128)S(1)}, f32[6]{0:T(128)}, u32[]{:S(2)}) copy-start(f32[6]{0:T(128)} %param.37) | copy-start | bytes 76
  121.6 29.1 %copy-start.11 = (f32[6]{0:T(128)S(1)}, f32[6]{0:T(128)}, u32[]{:S(2)}) copy-start(f32[6]{0:T(128)} %param.36) | copy-start | bytes 76
  121.6 29.9 %copy-start.9 = (f32[1,2,2,32]{3,2,1,0:T(2,128)S(1)}, f32[1,2,2,32]{3,2,1,0:T(2,128)}, u32[]{:S(2)}) copy-start(f32[1,2,2,32]{3,2,1,0:T(2,128)} %param.29) | copy-start | bytes 1540
  121.6 21.3 %all-to-all-start.1 = ((f32[64,2,76]{2,1,0:T(2,128)}), f32[64,2,76]{2,1,0:T(2,128)S(1)}, u32[]{:S(2)}, u32[]{:S(2)}) async-start(f32[64,2,76]{2,1,0:T(2,128)} %bitcast.39), calls=%async_computation.1 | async-start | bytes 131072 | tf_op jit(solution)/shard_map/all_to_all | solution.py:175
  145.1 6.4 %collective-permute-start.12 = (f32[2,2,32]{2,1,0:T(2,128)S(1)}, f32[2,2,32]{2,1,0:T(2,128)S(1)}, u32[]{:S(2)}, u32[]{:S(2)}) collective-permute-start(f32[2,2,32]{2,1,0:T(2,128)S(1)} %constant_dynamic-slice_fusion), channel_id=1, source_target_pairs={{0,256},{256,0},{1,257},{257,1},{2,258},{258,2},{3,259},{259,3},{4... | collective-permute-start | bytes 1544 | tf_op jit(solution)/shard_map/ppermute | solution.py:15

commit v7 on v6

--- a/solution.py
+++ b/solution.py
@@ -89,25 +89,29 @@
 
     head_table = head_placement(nseq)
 
+    used = plane_heads(nseq)
+    planes = nseq // 16
+
     def to_heads(x):
         n = x.shape[0]
         x = x.reshape(n, shard_rows, HEADS, HD).transpose(2, 0, 1, 3)
-        x = jnp.pad(x, ((0, 1), (0, 0), (0, 0), (0, 0)))
-        return jnp.take(x, jnp.array(head_table, jnp.int32), axis=0)
-
-    block_rows = w_out.shape[0]
+        x = jnp.pad(x, ((0, planes * used - HEADS), (0, 0), (0, 0), (0, 0)))
+        x = x.reshape(planes, used, n, shard_rows, HD)
+        x = jnp.pad(x, ((0, 0), (0, 16 - used), (0, 0), (0, 0), (0, 0)))
+        return x.reshape(nseq, n, shard_rows, HD)
+
     region_of, chunk_of = projection_split(nseq)
     chunks = max(chunk_of) + 1
+    block_rows = w_out.shape[0]
     col_width = D // chunks
     w_parts = w_out.reshape(block_rows, chunks, col_width).transpose(1, 0, 2)
-    w_parts = jnp.take(w_parts, jnp.array(chunk_of, jnp.int32), axis=0)
-    packed = jnp.concatenate(
-        [
-            to_heads(local_query),
-            to_heads(jnp.concatenate([resident_key_rows, far_keys[None]], 0)),
-            to_heads(jnp.concatenate([local_values, far_values[None]], 0)),
-        ],
-        axis=1,
+    w_parts = w_parts.reshape(planes // 2, 1, 16, block_rows, col_width)
+    w_parts = jnp.broadcast_to(w_parts, (planes // 2, 2, 16, block_rows, col_width))
+    w_parts = w_parts.reshape(nseq, block_rows, col_width)
+    packed = to_heads(
+        jnp.concatenate(
+            [local_query, resident_key_rows, far_keys[None], local_values, far_values[None]], 0
+        )
     )
     head_width = packed.shape[1] * shard_rows * HD
     joint = jnp.concatenate(
@@ -155,7 +159,6 @@
     my_z = me % plane
     my_x = me // plane
     by_z = jnp.take(gathered, jnp.take(jnp.array(inverse, jnp.int32), jnp.bitwise_xor(my_z, jnp.arange(plane))), axis=0)
-    used = plane_heads(nseq)
     my_region = my_x % 2
     parts = [lax.dynamic_index_in_dim(by_z, my_region, 1, keepdims=False)]
     sources = [my_x * plane + jnp.arange(plane)]

time: 153 us -> 149 us (0.974)
  local copies, waits for them, and re-layouts: 16.6 us -> 14.7 us
  other arithmetic: 7.95 us -> 6.09 us
    gather x5 -> x0, local copies, waits for them, and re-layouts: 3.13 us -> none  [the longest x3 2.26 us: to_heads(): return jnp.take(x, jnp.array(head_table, jnp.int32), axis=0)]
  transfers between devices with their start and end apart: 15 -> 15, of which waited for: 6 -> 6; matrix products, arithmetic and copies ran while one was open for 11% -> 9% of each run, Pallas kernels for 0% -> 0%
where the time goes in v7:
time: 149 us; the launch traced here: 148 us
  starting transfers between devices  78.9 us (53%)
  waiting for transfers between devices  44.8 us (30%)
  local copies, waits for them, and re-layouts  14.7 us (10%)
  other arithmetic  6.09 us (4%)
  matrix products  2.77 us (2%)
    ppermute x6, starting transfers between devices, shards(): lax.ppermute(gathered, 'seq', [(i, i ^ shift) for i in range(nseq)])  25.5 us
    all_to_all x1, waiting for transfers between devices, shards(): joint = lax.all_to_all(joint, 'seq', 0, 0, tiled=True)  20.4 us
    all_to_all x1, starting transfers between devices, shards(): joint = lax.all_to_all(joint, 'seq', 0, 0, tiled=True)  18.4 us
    ppermute x4, starting transfers between devices, from_partner(): lax.ppermute(x, axis, [(i, i ^ 1 << apart) for i in range(lax.axis_size(a...  17.9 us
    all_to_all x1, waiting for transfers between devices, shards(): received = lax.all_to_all(projected_parts, 'seq', 0, 0, tiled=True)  13.5 us
    ppermute x3, starting transfers between devices, shards(): lax.ppermute(outgoing, 'seq', [(i, i ^ shift) for i in range(nseq)])  9.32 us
    all_to_all x1, starting transfers between devices, shards(): received = lax.all_to_all(projected_parts, 'seq', 0, 0, tiled=True)  7.84 us
    ppermute x6, waiting for transfers between devices, shards(): lax.ppermute(gathered, 'seq', [(i, i ^ shift) for i in range(nseq)])  6.23 us
  transfers between devices with their start and end apart: 15, of which 6 were waited for; matrix products, arithmetic and copies ran while one was open for 9% of the time, Pallas kernels for 0%

profile of v7, /device:TPU:1, one launch (start us, length us, event | category | flops | bytes accessed | tf_op | source)
XLA Modules:
  0.0 148.3 jit_solution(15145913563074589655)
XLA Ops:
  0.0 0.8 slice_bitcast_fusion.2
  0.8 4.0 %collective-permute-start = (bf16[2,2432]{1,0:T(2,128)(2,1)S(1)}, bf16[2,2432]{1,0:T(2,128)(2,1)S(1)}, u32[]{:S(2)}, u32[]{:S(2)}) collective-permute-start(bf16[2,2432]{1,0:T(2,128)(2,1)S(1)} %slice_bitcast_fusion.2), channel_id=1, source_target_pairs={{0,64},{64,0},{128,192},{192,128},{1,65},{65,1},{129,193},{193,129... | collective-permute-start | bytes 29192 | tf_op jit(solution)/shard_map/ppermute | solution.py:15
  4.8 0.7 slice_bitcast_fusion.1
  5.5 1.9 %collective-permute-start.1 = (bf16[2,2432]{1,0:T(2,128)(2,1)S(1)}, bf16[2,2432]{1,0:T(2,128)(2,1)S(1)}, u32[]{:S(2)}, u32[]{:S(2)}) collective-permute-start(bf16[2,2432]{1,0:T(2,128)(2,1)S(1)} %slice_bitcast_fusion.1), channel_id=1, source_target_pairs={{0,64},{64,0},{128,192},{192,128},{1,65},{65,1},{129,193},{193,129... | collective-permute-start | bytes 29192 | tf_op jit(solution)/shard_map/ppermute | solution.py:15
  7.4 0.8 concatenate.97
  8.5 1.3 gather_fusion
  9.9 0.8 concatenate.96
  14.0 0.8 gather_fusion.2
  14.9 0.7 fusion.48
  18.0 0.8 reduce.2
  18.9 1.1 reshape.462
  19.9 18.4 %all-to-all-start = ((bf16[64,2,1234]{2,1,0:T(2,128)(2,1)}), bf16[64,2,1234]{2,1,0:T(2,128)(2,1)S(1)}, u32[]{:S(2)}, u32[]{:S(2)}) async-start(bf16[64,2,1234]{2,1,0:T(2,128)(2,1)} %reshape.462), calls=%async_computation | async-start | bytes 655360 | tf_op jit(solution)/shard_map/all_to_all | solution.py:120
  39.0 20.4 %all-to-all-done = bf16[64,2,1234]{2,1,0:T(2,128)(2,1)S(1)} async-done(((bf16[64,2,1234]{2,1,0:T(2,128)(2,1)}), bf16[64,2,1234]{2,1,0:T(2,128)(2,1)S(1)}, u32[]{:S(2)}, u32[]{:S(2)}) %all-to-all-start) | async-done | bytes 315936 | tf_op jit(solution)/shard_map/all_to_all | solution.py:120
  61.6 4.6 %collective-permute-start.2 = (bf16[1,2,128,64]{2,3,1,0:T(8,128)(2,1)S(1)}, bf16[1,2,128,64]{2,3,1,0:T(8,128)(2,1)S(1)}, u32[]{:S(2)}, u32[]{:S(2)}) collective-permute-start(bf16[1,2,128,64]{2,3,1,0:T(8,128)(2,1)S(1)} %get-tuple-element.23), channel_id=1, source_target_pairs={{0,4},{1,5},{2,6},{3,7},{4,0},{5,1},{6,2},{7,3},{8,12},{9,13},{10,... | collective-permute-start | bytes 98312 | tf_op jit(solution)/shard_map/ppermute | solution.py:153
  66.1 7.5 %collective-permute-start.3 = (bf16[1,2,128,64]{2,3,1,0:T(8,128)(2,1)S(1)}, bf16[1,2,128,64]{2,3,1,0:T(8,128)(2,1)S(1)}, u32[]{:S(2)}, u32[]{:S(2)}) collective-permute-start(bf16[1,2,128,64]{2,3,1,0:T(8,128)(2,1)S(1)} %get-tuple-element.23), channel_id=1, source_target_pairs={{0,8},{1,9},{2,10},{3,11},{4,12},{5,13},{6,14},{7,15},{8,0},{9,1},... | collective-permute-start | bytes 98312 | tf_op jit(solution)/shard_map/ppermute | solution.py:153
  73.6 4.1 %collective-permute-start.4 = (bf16[1,2,128,64]{2,3,1,0:T(8,128)(2,1)S(1)}, bf16[1,2,128,64]{2,3,1,0:T(8,128)(2,1)S(1)}, u32[]{:S(2)}, u32[]{:S(2)}) collective-permute-start(bf16[1,2,128,64]{2,3,1,0:T(8,128)(2,1)S(1)} %get-tuple-element.23), channel_id=1, source_target_pairs={{0,12},{1,13},{2,14},{3,15},{4,8},{5,9},{6,10},{7,11},{8,4},{9,5},... | collective-permute-start | bytes 98312 | tf_op jit(solution)/shard_map/ppermute | solution.py:153
  78.9 6.4 %collective-permute-start.11 = (bf16[1216,76]{1,0:T(8,128)(2,1)S(1)}, bf16[1216,76]{1,0:T(8,128)(2,1)S(1)}, u32[]{:S(2)}, u32[]{:S(2)}) collective-permute-start(bf16[1216,76]{1,0:T(8,128)(2,1)S(1)} %reshape.403), channel_id=1, source_target_pairs={{0,256},{256,0},{1,257},{257,1},{2,258},{258,2},{3,259},{259,3},{4... | collective-permute-start | bytes 554504 | tf_op jit(solution)/shard_map/ppermute | solution.py:15
  85.4 2.5 %collective-permute-start.5 = (bf16[4,2,128,64]{2,3,1,0:T(8,128)(2,1)S(1)}, bf16[4,2,128,64]{2,3,1,0:T(8,128)(2,1)S(1)}, u32[]{:S(2)}, u32[]{:S(2)}) collective-permute-start(bf16[4,2,128,64]{2,3,1,0:T(8,128)(2,1)S(1)} %pad_maximum_fusion), channel_id=1, source_target_pairs={{0,1},{1,0},{2,3},{3,2},{4,5},{5,4},{6,7},{7,6},{8,9},{9,8},{10,11... | collective-permute-start | bytes 393224 | tf_op jit(solution)/shard_map/ppermute | solution.py:153
  87.9 2.8 %collective-permute-start.6 = (bf16[4,2,128,64]{2,3,1,0:T(8,128)(2,1)S(1)}, bf16[4,2,128,64]{2,3,1,0:T(8,128)(2,1)S(1)}, u32[]{:S(2)}, u32[]{:S(2)}) collective-permute-start(bf16[4,2,128,64]{2,3,1,0:T(8,128)(2,1)S(1)} %pad_maximum_fusion), channel_id=1, source_target_pairs={{0,2},{1,3},{2,0},{3,1},{4,6},{5,7},{6,4},{7,5},{8,10},{9,11},{10,... | collective-permute-start | bytes 393224 | tf_op jit(solution)/shard_map/ppermute | solution.py:153
  90.7 4.0 %collective-permute-start.7 = (bf16[4,2,128,64]{2,3,1,0:T(8,128)(2,1)S(1)}, bf16[4,2,128,64]{2,3,1,0:T(8,128)(2,1)S(1)}, u32[]{:S(2)}, u32[]{:S(2)}) collective-permute-start(bf16[4,2,128,64]{2,3,1,0:T(8,128)(2,1)S(1)} %pad_maximum_fusion), channel_id=1, source_target_pairs={{0,3},{1,2},{2,1},{3,0},{4,7},{5,6},{6,5},{7,4},{8,11},{9,10},{10,... | collective-permute-start | bytes 393224 | tf_op jit(solution)/shard_map/ppermute | solution.py:153
  94.8 6.2 %collective-permute-done.6 = bf16[4,2,128,64]{2,3,1,0:T(8,128)(2,1)S(1)} collective-permute-done((bf16[4,2,128,64]{2,3,1,0:T(8,128)(2,1)S(1)}, bf16[4,2,128,64]{2,3,1,0:T(8,128)(2,1)S(1)}, u32[]{:S(2)}, u32[]{:S(2)}) %collective-permute-start.6) | collective-permute-done | bytes 131104 | tf_op jit(solution)/shard_map/ppermute | solution.py:153
  101.9 4.9 %collective-permute-start.10 = (bf16[10,128,64]{1,2,0:T(8,128)(2,1)S(1)}, bf16[10,128,64]{1,2,0:T(8,128)(2,1)S(1)}, u32[]{:S(2)}, u32[]{:S(2)}) collective-permute-start(bf16[10,128,64]{1,2,0:T(8,128)(2,1)S(1)} %get-tuple-element.11), channel_id=1, source_target_pairs={{0,48},{1,49},{2,50},{3,51},{4,52},{5,53},{6,54},{7,55},{8,56},{9,... | collective-permute-start | bytes 491528 | tf_op jit(solution)/shard_map/ppermute | solution.py:168
  106.8 2.1 %collective-permute-start.9 = (bf16[10,128,64]{1,2,0:T(8,128)(2,1)S(1)}, bf16[10,128,64]{1,2,0:T(8,128)(2,1)S(1)}, u32[]{:S(2)}, u32[]{:S(2)}) collective-permute-start(bf16[10,128,64]{1,2,0:T(8,128)(2,1)S(1)} %get-tuple-element.12), channel_id=1, source_target_pairs={{0,32},{1,33},{2,34},{3,35},{4,36},{5,37},{6,38},{7,39},{8,40},{9,... | collective-permute-start | bytes 491528 | tf_op jit(solution)/shard_map/ppermute | solution.py:168
  109.0 2.3 %collective-permute-start.8 = (bf16[10,128,64]{1,2,0:T(8,128)(2,1)S(1)}, bf16[10,128,64]{1,2,0:T(8,128)(2,1)S(1)}, u32[]{:S(2)}, u32[]{:S(2)}) collective-permute-start(bf16[10,128,64]{1,2,0:T(8,128)(2,1)S(1)} %get-tuple-element.10), channel_id=1, source_target_pairs={{0,16},{1,17},{2,18},{3,19},{4,20},{5,21},{6,22},{7,23},{8,24},{9,... | collective-permute-start | bytes 491528 | tf_op jit(solution)/shard_map/ppermute | solution.py:168
  111.7 0.7 gather_fusion.3
  112.5 1.9 %collective-permute-done.9 = bf16[10,128,64]{1,2,0:T(8,128)(2,1)S(1)} collective-permute-done((bf16[10,128,64]{1,2,0:T(8,128)(2,1)S(1)}, bf16[10,128,64]{1,2,0:T(8,128)(2,1)S(1)}, u32[]{:S(2)}, u32[]{:S(2)}) %collective-permute-start.9) | collective-permute-done | bytes 163872 | tf_op jit(solution)/shard_map/ppermute | solution.py:168
  114.4 2.2 %collective-permute-done.8 = bf16[10,128,64]{1,2,0:T(8,128)(2,1)S(1)} collective-permute-done((bf16[10,128,64]{1,2,0:T(8,128)(2,1)S(1)}, bf16[10,128,64]{1,2,0:T(8,128)(2,1)S(1)}, u32[]{:S(2)}, u32[]{:S(2)}) %collective-permute-start.8) | collective-permute-done | bytes 163872 | tf_op jit(solution)/shard_map/ppermute | solution.py:168
  116.6 1.1 fusion.6
  117.7 7.8 %all-to-all-start.1 = ((f32[64,2,76]{2,1,0:T(2,128)}), f32[64,2,76]{2,1,0:T(2,128)S(1)}, u32[]{:S(2)}, u32[]{:S(2)}) async-start(f32[64,2,76]{2,1,0:T(2,128)} %bitcast.39), calls=%async_computation.1 | async-start | bytes 131072 | tf_op jit(solution)/shard_map/all_to_all | solution.py:178
  125.6 13.5 %all-to-all-done.1 = f32[64,2,76]{2,1,0:T(2,128)S(1)} async-done(((f32[64,2,76]{2,1,0:T(2,128)}), f32[64,2,76]{2,1,0:T(2,128)S(1)}, u32[]{:S(2)}, u32[]{:S(2)}) %all-to-all-start.1) | async-done | bytes 38944 | tf_op jit(solution)/shard_map/all_to_all | solution.py:178
  141.3 5.6 %collective-permute-start.12 = (f32[2,2,32]{2,1,0:T(2,128)S(1)}, f32[2,2,32]{2,1,0:T(2,128)S(1)}, u32[]{:S(2)}, u32[]{:S(2)}) collective-permute-start(f32[2,2,32]{2,1,0:T(2,128)S(1)} %constant_dynamic-slice_fusion.1), channel_id=1, source_target_pairs={{0,256},{256,0},{1,257},{257,1},{2,258},{258,2},{3,259},{259,3},{4... | collective-permute-start | bytes 1544 | tf_op jit(solution)/shard_map/ppermute | solution.py:15
  147.6 0.7 fusion.43
  (127 shorter events, 13.9 us)
Async XLA Ops:
  0.0 140.9 %copy-start = (bf16[2432,64]{0,1:T(8,128)(2,1)S(1)}, bf16[2432,64]{0,1:T(8,128)(2,1)}, u32[]{:S(2)}) copy-start(bf16[2432,64]{0,1:T(8,128)(2,1)} %param.29) | copy-start | bytes 933892
  0.0 14.0 %copy-start.1 = (s32[64]{0:T(128)S(1)}, s32[64]{0:T(128)}, u32[]{:S(2)}) copy-start(s32[64]{0:T(128)} %constant.181.clone) | copy-start | bytes 772
  0.0 10.8 %copy-start.7 = (s32[4,2]{0,1:T(2,128)S(1)}, s32[4,2]{0,1:T(2,128)}, u32[]{:S(2)}) copy-start(s32[4,2]{0,1:T(2,128)} %param.25) | copy-start | bytes 100
  0.0 10.8 %copy-start.9 = (s32[4,2]{0,1:T(2,128)S(1)}, s32[4,2]{0,1:T(2,128)}, u32[]{:S(2)}) copy-start(s32[4,2]{0,1:T(2,128)} %param.24) | copy-start | bytes 100
  0.8 14.8 %copy-start.5 = (bf16[1,1,2,2,2432]{4,3,2,1,0:T(2,128)(2,1)S(1)}, bf16[1,1,2,2,2432]{4,3,2,1,0:T(2,128)(2,1)}, u32[]{:S(2)}) copy-start(bf16[1,1,2,2,2432]{4,3,2,1,0:T(2,128)(2,1)} %param.21) | copy-start | bytes 58372
  0.8 15.8 %collective-permute-start = (bf16[2,2432]{1,0:T(2,128)(2,1)S(1)}, bf16[2,2432]{1,0:T(2,128)(2,1)S(1)}, u32[]{:S(2)}, u32[]{:S(2)}) collective-permute-start(bf16[2,2432]{1,0:T(2,128)(2,1)S(1)} %slice_bitcast_fusion.2), channel_id=1, source_target_pairs={{0,64},{64,0},{128,192},{192,128},{1,65},{65,1},{129,193},{193,129... | collective-permute-start | bytes 29192 | tf_op jit(solution)/shard_map/ppermute | solution.py:15
  5.5 11.2 %collective-permute-start.1 = (bf16[2,2432]{1,0:T(2,128)(2,1)S(1)}, bf16[2,2432]{1,0:T(2,128)(2,1)S(1)}, u32[]{:S(2)}, u32[]{:S(2)}) collective-permute-start(bf16[2,2432]{1,0:T(2,128)(2,1)S(1)} %slice_bitcast_fusion.1), channel_id=1, source_target_pairs={{0,64},{64,0},{128,192},{192,128},{1,65},{65,1},{129,193},{193,129... | collective-permute-start | bytes 29192 | tf_op jit(solution)/shard_map/ppermute | solution.py:15
  8.3 7.4 %copy-start.3 = (bf16[19,2432]{1,0:T(8,128)(2,1)S(1)}, bf16[19,2432]{1,0:T(8,128)(2,1)}, u32[]{:S(2)}) copy-start(bf16[19,2432]{1,0:T(8,128)(2,1)} %param.26) | copy-start | bytes 277252
  18.8 19.6 %copy-start.4 = (f32[1,6,2432]{2,0,1:T(1,128)S(1)}, f32[1,6,2432]{2,0,1:T(1,128)}, u32[]{:S(2)}) copy-start(f32[1,6,2432]{2,0,1:T(1,128)} %param.27) | copy-start | bytes 175108
  18.8 19.8 %copy-start.2 = (f32[1,6,2,2432]{3,2,1,0:T(2,128)S(1)}, f32[1,6,2,2432]{3,2,1,0:T(2,128)}, u32[]{:S(2)}) copy-start(f32[1,6,2,2432]{3,2,1,0:T(2,128)} %param.28) | copy-start | bytes 350212
  19.9 39.5 %all-to-all-start = ((bf16[64,2,1234]{2,1,0:T(2,128)(2,1)}), bf16[64,2,1234]{2,1,0:T(2,128)(2,1)S(1)}, u32[]{:S(2)}, u32[]{:S(2)}) async-start(bf16[64,2,1234]{2,1,0:T(2,128)(2,1)} %reshape.462), calls=%async_computation | async-start | bytes 655360 | tf_op jit(solution)/shard_map/all_to_all | solution.py:120
  61.6 23.8 %collective-permute-start.2 = (bf16[1,2,128,64]{2,3,1,0:T(8,128)(2,1)S(1)}, bf16[1,2,128,64]{2,3,1,0:T(8,128)(2,1)S(1)}, u32[]{:S(2)}, u32[]{:S(2)}) collective-permute-start(bf16[1,2,128,64]{2,3,1,0:T(8,128)(2,1)S(1)} %get-tuple-element.23), channel_id=1, source_target_pairs={{0,4},{1,5},{2,6},{3,7},{4,0},{5,1},{6,2},{7,3},{8,12},{9,13},{10,... | collective-permute-start | bytes 98312 | tf_op jit(solution)/shard_map/ppermute | solution.py:153
  66.1 19.2 %collective-permute-start.3 = (bf16[1,2,128,64]{2,3,1,0:T(8,128)(2,1)S(1)}, bf16[1,2,128,64]{2,3,1,0:T(8,128)(2,1)S(1)}, u32[]{:S(2)}, u32[]{:S(2)}) collective-permute-start(bf16[1,2,128,64]{2,3,1,0:T(8,128)(2,1)S(1)} %get-tuple-element.23), channel_id=1, source_target_pairs={{0,8},{1,9},{2,10},{3,11},{4,12},{5,13},{6,14},{7,15},{8,0},{9,1},... | collective-permute-start | bytes 98312 | tf_op jit(solution)/shard_map/ppermute | solution.py:153
  73.6 11.8 %collective-permute-start.4 = (bf16[1,2,128,64]{2,3,1,0:T(8,128)(2,1)S(1)}, bf16[1,2,128,64]{2,3,1,0:T(8,128)(2,1)S(1)}, u32[]{:S(2)}, u32[]{:S(2)}) collective-permute-start(bf16[1,2,128,64]{2,3,1,0:T(8,128)(2,1)S(1)} %get-tuple-element.23), channel_id=1, source_target_pairs={{0,12},{1,13},{2,14},{3,15},{4,8},{5,9},{6,10},{7,11},{8,4},{9,5},... | collective-permute-start | bytes 98312 | tf_op jit(solution)/shard_map/ppermute | solution.py:153
  78.9 32.4 %collective-permute-start.11 = (bf16[1216,76]{1,0:T(8,128)(2,1)S(1)}, bf16[1216,76]{1,0:T(8,128)(2,1)S(1)}, u32[]{:S(2)}, u32[]{:S(2)}) collective-permute-start(bf16[1216,76]{1,0:T(8,128)(2,1)S(1)} %reshape.403), channel_id=1, source_target_pairs={{0,256},{256,0},{1,257},{257,1},{2,258},{258,2},{3,259},{259,3},{4... | collective-permute-start | bytes 554504 | tf_op jit(solution)/shard_map/ppermute | solution.py:15
  85.4 9.3 %collective-permute-start.5 = (bf16[4,2,128,64]{2,3,1,0:T(8,128)(2,1)S(1)}, bf16[4,2,128,64]{2,3,1,0:T(8,128)(2,1)S(1)}, u32[]{:S(2)}, u32[]{:S(2)}) collective-permute-start(bf16[4,2,128,64]{2,3,1,0:T(8,128)(2,1)S(1)} %pad_maximum_fusion), channel_id=1, source_target_pairs={{0,1},{1,0},{2,3},{3,2},{4,5},{5,4},{6,7},{7,6},{8,9},{9,8},{10,11... | collective-permute-start | bytes 393224 | tf_op jit(solution)/shard_map/ppermute | solution.py:153
  87.9 13.1 %collective-permute-start.6 = (bf16[4,2,128,64]{2,3,1,0:T(8,128)(2,1)S(1)}, bf16[4,2,128,64]{2,3,1,0:T(8,128)(2,1)S(1)}, u32[]{:S(2)}, u32[]{:S(2)}) collective-permute-start(bf16[4,2,128,64]{2,3,1,0:T(8,128)(2,1)S(1)} %pad_maximum_fusion), channel_id=1, source_target_pairs={{0,2},{1,3},{2,0},{3,1},{4,6},{5,7},{6,4},{7,5},{8,10},{9,11},{10,... | collective-permute-start | bytes 393224 | tf_op jit(solution)/shard_map/ppermute | solution.py:153
  90.7 10.3 %collective-permute-start.7 = (bf16[4,2,128,64]{2,3,1,0:T(8,128)(2,1)S(1)}, bf16[4,2,128,64]{2,3,1,0:T(8,128)(2,1)S(1)}, u32[]{:S(2)}, u32[]{:S(2)}) collective-permute-start(bf16[4,2,128,64]{2,3,1,0:T(8,128)(2,1)S(1)} %pad_maximum_fusion), channel_id=1, source_target_pairs={{0,3},{1,2},{2,1},{3,0},{4,7},{5,6},{6,5},{7,4},{8,11},{9,10},{10,... | collective-permute-start | bytes 393224 | tf_op jit(solution)/shard_map/ppermute | solution.py:153
  101.9 10.6 %collective-permute-start.10 = (bf16[10,128,64]{1,2,0:T(8,128)(2,1)S(1)}, bf16[10,128,64]{1,2,0:T(8,128)(2,1)S(1)}, u32[]{:S(2)}, u32[]{:S(2)}) collective-permute-start(bf16[10,128,64]{1,2,0:T(8,128)(2,1)S(1)} %get-tuple-element.11), channel_id=1, source_target_pairs={{0,48},{1,49},{2,50},{3,51},{4,52},{5,53},{6,54},{7,55},{8,56},{9,... | collective-permute-start | bytes 491528 | tf_op jit(solution)/shard_map/ppermute | solution.py:168
  106.8 7.6 %collective-permute-start.9 = (bf16[10,128,64]{1,2,0:T(8,128)(2,1)S(1)}, bf16[10,128,64]{1,2,0:T(8,128)(2,1)S(1)}, u32[]{:S(2)}, u32[]{:S(2)}) collective-permute-start(bf16[10,128,64]{1,2,0:T(8,128)(2,1)S(1)} %get-tuple-element.12), channel_id=1, source_target_pairs={{0,32},{1,33},{2,34},{3,35},{4,36},{5,37},{6,38},{7,39},{8,40},{9,... | collective-permute-start | bytes 491528 | tf_op jit(solution)/shard_map/ppermute | solution.py:168
  109.0 7.6 %collective-permute-start.8 = (bf16[10,128,64]{1,2,0:T(8,128)(2,1)S(1)}, bf16[10,128,64]{1,2,0:T(8,128)(2,1)S(1)}, u32[]{:S(2)}, u32[]{:S(2)}) collective-permute-start(bf16[10,128,64]{1,2,0:T(8,128)(2,1)S(1)} %get-tuple-element.10), channel_id=1, source_target_pairs={{0,16},{1,17},{2,18},{3,19},{4,20},{5,21},{6,22},{7,23},{8,24},{9,... | collective-permute-start | bytes 491528 | tf_op jit(solution)/shard_map/ppermute | solution.py:168
  112.4 13.2 %copy-start.12 = (s32[32]{0:T(128)S(1)}, s32[32]{0:T(128)}, u32[]{:S(2)}) copy-start(s32[32]{0:T(128)} %constant.217) | copy-start | bytes 388
  112.4 13.2 %copy-start.13 = (s32[32]{0:T(128)S(1)}, s32[32]{0:T(128)}, u32[]{:S(2)}) copy-start(s32[32]{0:T(128)} %constant.216) | copy-start | bytes 388
  112.5 28.1 %copy-start.6 = (bf16[1,1,2,2,2432]{4,3,2,1,0:T(2,128)(2,1)S(1)}, bf16[1,1,2,2,2432]{4,3,2,1,0:T(2,128)(2,1)}, u32[]{:S(2)}) copy-start(bf16[1,1,2,2,2432]{4,3,2,1,0:T(2,128)(2,1)} %param.22) | copy-start | bytes 58372
  117.7 29.1 %copy-start.10 = (f32[6]{0:T(128)S(1)}, f32[6]{0:T(128)}, u32[]{:S(2)}) copy-start(f32[6]{0:T(128)} %param.31) | copy-start | bytes 76
  117.7 29.1 %copy-start.11 = (f32[6]{0:T(128)S(1)}, f32[6]{0:T(128)}, u32[]{:S(2)}) copy-start(f32[6]{0:T(128)} %param.30) | copy-start | bytes 76
  117.7 29.9 %copy-start.8 = (f32[1,2,2,32]{3,2,1,0:T(2,128)S(1)}, f32[1,2,2,32]{3,2,1,0:T(2,128)}, u32[]{:S(2)}) copy-start(f32[1,2,2,32]{3,2,1,0:T(2,128)} %param.23) | copy-start | bytes 1540
  117.7 21.4 %all-to-all-start.1 = ((f32[64,2,76]{2,1,0:T(2,128)}), f32[64,2,76]{2,1,0:T(2,128)S(1)}, u32[]{:S(2)}, u32[]{:S(2)}) async-start(f32[64,2,76]{2,1,0:T(2,128)} %bitcast.39), calls=%async_computation.1 | async-start | bytes 131072 | tf_op jit(solution)/shard_map/all_to_all | solution.py:178
  141.3 6.4 %collective-permute-start.12 = (f32[2,2,32]{2,1,0:T(2,128)S(1)}, f32[2,2,32]{2,1,0:T(2,128)S(1)}, u32[]{:S(2)}, u32[]{:S(2)}) collective-permute-start(f32[2,2,32]{2,1,0:T(2,128)S(1)} %constant_dynamic-slice_fusion.1), channel_id=1, source_target_pairs={{0,256},{256,0},{1,257},{257,1},{2,258},{258,2},{3,259},{259,3},{4... | collective-permute-start | bytes 1544 | tf_op jit(solution)/shard_map/ppermute | solution.py:15

commit v8 on v7

--- a/solution.py
+++ b/solution.py
@@ -113,12 +113,7 @@
             [local_query, resident_key_rows, far_keys[None], local_values, far_values[None]], 0
         )
     )
-    head_width = packed.shape[1] * shard_rows * HD
-    joint = jnp.concatenate(
-        [packed.reshape(nseq, head_width), w_parts.reshape(nseq, block_rows * col_width)], 1
-    )
-    joint = lax.all_to_all(joint, "seq", 0, 0, tiled=True)
-    head_rows = joint[:, :head_width].reshape(nseq, 8, shard_rows, HD)
+    head_rows = lax.all_to_all(packed, "seq", 0, 0, tiled=True)
     head_rows = head_rows.transpose(1, 0, 2, 3).reshape(8, slot_total, HD)
     head_q, head_k, head_v = head_rows[0:2], head_rows[2:5], head_rows[5:8]
     slot_ids = jnp.arange(slot_total)
@@ -134,7 +129,8 @@
     )
     head_attn = jnp.stack([home_out, shared_out]).astype(jnp.bfloat16)
 
-    w_half = joint[:, head_width:].reshape(nseq * block_rows, col_width)
+    w_parts, _ = lax.optimization_barrier((w_parts, head_attn))
+    w_half = lax.all_to_all(w_parts, "seq", 0, 0, tiled=True).reshape(nseq * block_rows, col_width)
     w_other = from_partner(w_half, "cfg", 0)
     w_cols = jnp.where(
         branch == 0,

time: 149 us -> 157 us (1.054)
  starting transfers between devices: 78.9 us -> 91.1 us
  waiting for transfers between devices: 44.8 us -> 41.5 us
    all_to_all x1 -> x2, starting transfers between devices: 18.4 us -> 25.6 us  [the longest x1 18.4 us: shards(): head_rows = lax.all_to_all(packed, 'seq', 0, 0, tiled=True)]
    all_to_all x1 -> x2, waiting for transfers between devices: 20.4 us -> 13.9 us  [the longest x1 13.9 us: shards(): head_rows = lax.all_to_all(packed, 'seq', 0, 0, tiled=True)]
    all_to_all x1, starting transfers between devices: 7.84 us -> 12.5 us  [shards(): received = lax.all_to_all(projected_parts, 'seq', 0, 0, tiled=True)]
    ppermute x6, waiting for transfers between devices: 6.23 us -> 9.1 us  [shards(): lax.ppermute(gathered, 'seq', [(i, i ^ shift) for i in range(nseq)])]
  transfers between devices with their start and end apart: 15 -> 16, of which waited for: 6 -> 8; matrix products, arithmetic and copies ran while one was open for 9% -> 10% of each run, Pallas kernels for 0% -> 0%
where the time goes in v8:
time: 157 us; the launch traced here: 156 us
  starting transfers between devices  91.1 us (58%)
  waiting for transfers between devices  41.5 us (26%)
  local copies, waits for them, and re-layouts  14.4 us (9%)
  other arithmetic  5.27 us (3%)
  matrix products  2.78 us (2%)
    ppermute x6, starting transfers between devices, shards(): lax.ppermute(gathered, 'seq', [(i, i ^ shift) for i in range(nseq)])  25.5 us
    all_to_all x1, starting transfers between devices, shards(): head_rows = lax.all_to_all(packed, 'seq', 0, 0, tiled=True)  18.4 us
    ppermute x4, starting transfers between devices, from_partner(): lax.ppermute(x, axis, [(i, i ^ 1 << apart) for i in range(lax.axis_size(a...  18 us
    all_to_all x1, waiting for transfers between devices, shards(): head_rows = lax.all_to_all(packed, 'seq', 0, 0, tiled=True)  13.9 us
    all_to_all x1, waiting for transfers between devices, shards(): received = lax.all_to_all(projected_parts, 'seq', 0, 0, tiled=True)  13.5 us
    all_to_all x1, starting transfers between devices, shards(): received = lax.all_to_all(projected_parts, 'seq', 0, 0, tiled=True)  12.5 us
    ppermute x3, starting transfers between devices, shards(): lax.ppermute(outgoing, 'seq', [(i, i ^ shift) for i in range(nseq)])  9.62 us
    ppermute x6, waiting for transfers between devices, shards(): lax.ppermute(gathered, 'seq', [(i, i ^ shift) for i in range(nseq)])  9.1 us
  transfers between devices with their start and end apart: 16, of which 8 were waited for; matrix products, arithmetic and copies ran while one was open for 10% of the time, Pallas kernels for 0%

profile of v8, /device:TPU:1, one launch (start us, length us, event | category | flops | bytes accessed | tf_op | source)
XLA Modules:
  0.0 156.0 jit_solution(10808456895026118304)
XLA Ops:
  0.0 0.8 slice_bitcast_fusion.2
  0.8 4.0 %collective-permute-start = (bf16[2,2432]{1,0:T(2,128)(2,1)S(1)}, bf16[2,2432]{1,0:T(2,128)(2,1)S(1)}, u32[]{:S(2)}, u32[]{:S(2)}) collective-permute-start(bf16[2,2432]{1,0:T(2,128)(2,1)S(1)} %slice_bitcast_fusion.2), channel_id=1, source_target_pairs={{0,64},{64,0},{128,192},{192,128},{1,65},{65,1},{129,193},{193,129... | collective-permute-start | bytes 29192 | tf_op jit(solution)/shard_map/ppermute | solution.py:15
  4.8 0.7 slice_bitcast_fusion.1
  5.5 1.9 %collective-permute-start.1 = (bf16[2,2432]{1,0:T(2,128)(2,1)S(1)}, bf16[2,2432]{1,0:T(2,128)(2,1)S(1)}, u32[]{:S(2)}, u32[]{:S(2)}) collective-permute-start(bf16[2,2432]{1,0:T(2,128)(2,1)S(1)} %slice_bitcast_fusion.1), channel_id=1, source_target_pairs={{0,64},{64,0},{128,192},{192,128},{1,65},{65,1},{129,193},{193,129... | collective-permute-start | bytes 29192 | tf_op jit(solution)/shard_map/ppermute | solution.py:15
  7.5 0.9 concatenate.94
  8.6 1.4 gather_fusion
  10.0 0.9 constant_dynamic-slice_fusion.3
  14.2 0.8 gather_fusion.2
  17.1 1.1 reshape.466
  18.9 0.8 reshape.464
  19.7 18.4 %all-to-all-start = ((bf16[64,2,512]{2,1,0:T(2,128)(2,1)}), bf16[64,2,512]{2,1,0:T(2,128)(2,1)S(1)}, u32[]{:S(2)}, u32[]{:S(2)}) async-start(bf16[64,2,512]{2,1,0:T(2,128)(2,1)} %reshape.464), calls=%async_computation | async-start | bytes 262144 | tf_op jit(solution)/shard_map/all_to_all | solution.py:116
  38.2 13.9 %all-to-all-done = bf16[64,2,512]{2,1,0:T(2,128)(2,1)S(1)} async-done(((bf16[64,2,512]{2,1,0:T(2,128)(2,1)}), bf16[64,2,512]{2,1,0:T(2,128)(2,1)S(1)}, u32[]{:S(2)}, u32[]{:S(2)}) %all-to-all-start) | async-done | bytes 131104 | tf_op jit(solution)/shard_map/all_to_all | solution.py:116
  52.1 7.1 %all-to-all-start.1 = ((bf16[64,2,722]{2,1,0:T(2,128)(2,1)}), bf16[64,2,722]{2,1,0:T(2,128)(2,1)S(1)}, u32[]{:S(2)}, u32[]{:S(2)}) async-start(bf16[64,2,722]{2,1,0:T(2,128)(2,1)} %reshape.466), calls=%async_computation.1 | async-start | bytes 393216 | tf_op jit(solution)/shard_map/all_to_all | solution.py:133
  60.8 6.8 %collective-permute-start.2 = (bf16[1,2,128,64]{2,3,1,0:T(8,128)(2,1)S(1)}, bf16[1,2,128,64]{2,3,1,0:T(8,128)(2,1)S(1)}, u32[]{:S(2)}, u32[]{:S(2)}) collective-permute-start(bf16[1,2,128,64]{2,3,1,0:T(8,128)(2,1)S(1)} %get-tuple-element.23), channel_id=1, source_target_pairs={{0,4},{1,5},{2,6},{3,7},{4,0},{5,1},{6,2},{7,3},{8,12},{9,13},{10,... | collective-permute-start | bytes 98312 | tf_op jit(solution)/shard_map/ppermute | solution.py:149
  67.7 7.0 %collective-permute-start.3 = (bf16[1,2,128,64]{2,3,1,0:T(8,128)(2,1)S(1)}, bf16[1,2,128,64]{2,3,1,0:T(8,128)(2,1)S(1)}, u32[]{:S(2)}, u32[]{:S(2)}) collective-permute-start(bf16[1,2,128,64]{2,3,1,0:T(8,128)(2,1)S(1)} %get-tuple-element.23), channel_id=1, source_target_pairs={{0,8},{1,9},{2,10},{3,11},{4,12},{5,13},{6,14},{7,15},{8,0},{9,1},... | collective-permute-start | bytes 98312 | tf_op jit(solution)/shard_map/ppermute | solution.py:149
  74.7 2.4 %collective-permute-start.4 = (bf16[1,2,128,64]{2,3,1,0:T(8,128)(2,1)S(1)}, bf16[1,2,128,64]{2,3,1,0:T(8,128)(2,1)S(1)}, u32[]{:S(2)}, u32[]{:S(2)}) collective-permute-start(bf16[1,2,128,64]{2,3,1,0:T(8,128)(2,1)S(1)} %get-tuple-element.23), channel_id=1, source_target_pairs={{0,12},{1,13},{2,14},{3,15},{4,8},{5,9},{6,10},{7,11},{8,4},{9,5},... | collective-permute-start | bytes 98312 | tf_op jit(solution)/shard_map/ppermute | solution.py:149
  77.7 3.3 %collective-permute-done.3 = bf16[1,2,128,64]{2,3,1,0:T(8,128)(2,1)S(1)} collective-permute-done((bf16[1,2,128,64]{2,3,1,0:T(8,128)(2,1)S(1)}, bf16[1,2,128,64]{2,3,1,0:T(8,128)(2,1)S(1)}, u32[]{:S(2)}, u32[]{:S(2)}) %collective-permute-start.3) | collective-permute-done | bytes 32800 | tf_op jit(solution)/shard_map/ppermute | solution.py:149
  81.1 2.5 %collective-permute-done.4 = bf16[1,2,128,64]{2,3,1,0:T(8,128)(2,1)S(1)} collective-permute-done((bf16[1,2,128,64]{2,3,1,0:T(8,128)(2,1)S(1)}, bf16[1,2,128,64]{2,3,1,0:T(8,128)(2,1)S(1)}, u32[]{:S(2)}, u32[]{:S(2)}) %collective-permute-start.4) | collective-permute-done | bytes 32800 | tf_op jit(solution)/shard_map/ppermute | solution.py:149
  83.6 2.2 %collective-permute-start.5 = (bf16[4,2,128,64]{2,3,1,0:T(8,128)(2,1)S(1)}, bf16[4,2,128,64]{2,3,1,0:T(8,128)(2,1)S(1)}, u32[]{:S(2)}, u32[]{:S(2)}) collective-permute-start(bf16[4,2,128,64]{2,3,1,0:T(8,128)(2,1)S(1)} %pad_maximum_fusion), channel_id=1, source_target_pairs={{0,1},{1,0},{2,3},{3,2},{4,5},{5,4},{6,7},{7,6},{8,9},{9,8},{10,11... | collective-permute-start | bytes 393224 | tf_op jit(solution)/shard_map/ppermute | solution.py:149
  85.8 2.9 %collective-permute-start.6 = (bf16[4,2,128,64]{2,3,1,0:T(8,128)(2,1)S(1)}, bf16[4,2,128,64]{2,3,1,0:T(8,128)(2,1)S(1)}, u32[]{:S(2)}, u32[]{:S(2)}) collective-permute-start(bf16[4,2,128,64]{2,3,1,0:T(8,128)(2,1)S(1)} %pad_maximum_fusion), channel_id=1, source_target_pairs={{0,2},{1,3},{2,0},{3,1},{4,6},{5,7},{6,4},{7,5},{8,10},{9,11},{10,... | collective-permute-start | bytes 393224 | tf_op jit(solution)/shard_map/ppermute | solution.py:149
  88.7 4.2 %collective-permute-start.7 = (bf16[4,2,128,64]{2,3,1,0:T(8,128)(2,1)S(1)}, bf16[4,2,128,64]{2,3,1,0:T(8,128)(2,1)S(1)}, u32[]{:S(2)}, u32[]{:S(2)}) collective-permute-start(bf16[4,2,128,64]{2,3,1,0:T(8,128)(2,1)S(1)} %pad_maximum_fusion), channel_id=1, source_target_pairs={{0,3},{1,2},{2,1},{3,0},{4,7},{5,6},{6,5},{7,4},{8,11},{9,10},{10,... | collective-permute-start | bytes 393224 | tf_op jit(solution)/shard_map/ppermute | solution.py:149
  93.0 3.3 %collective-permute-done.7 = bf16[4,2,128,64]{2,3,1,0:T(8,128)(2,1)S(1)} collective-permute-done((bf16[4,2,128,64]{2,3,1,0:T(8,128)(2,1)S(1)}, bf16[4,2,128,64]{2,3,1,0:T(8,128)(2,1)S(1)}, u32[]{:S(2)}, u32[]{:S(2)}) %collective-permute-start.7) | collective-permute-done | bytes 131104 | tf_op jit(solution)/shard_map/ppermute | solution.py:149
  97.8 7.5 %collective-permute-start.11 = (bf16[1216,76]{1,0:T(8,128)(2,1)S(1)}, bf16[1216,76]{1,0:T(8,128)(2,1)S(1)}, u32[]{:S(2)}, u32[]{:S(2)}) collective-permute-start(bf16[1216,76]{1,0:T(8,128)(2,1)S(1)} %reshape.405), channel_id=1, source_target_pairs={{0,256},{256,0},{1,257},{257,1},{2,258},{258,2},{3,259},{259,3},{4... | collective-permute-start | bytes 554504 | tf_op jit(solution)/shard_map/ppermute | solution.py:15
  105.4 4.6 %collective-permute-start.10 = (bf16[10,128,64]{1,2,0:T(8,128)(2,1)S(1)}, bf16[10,128,64]{1,2,0:T(8,128)(2,1)S(1)}, u32[]{:S(2)}, u32[]{:S(2)}) collective-permute-start(bf16[10,128,64]{1,2,0:T(8,128)(2,1)S(1)} %get-tuple-element.11), channel_id=1, source_target_pairs={{0,48},{1,49},{2,50},{3,51},{4,52},{5,53},{6,54},{7,55},{8,56},{9,... | collective-permute-start | bytes 491528 | tf_op jit(solution)/shard_map/ppermute | solution.py:164
  110.0 1.9 %collective-permute-start.8 = (bf16[10,128,64]{1,2,0:T(8,128)(2,1)S(1)}, bf16[10,128,64]{1,2,0:T(8,128)(2,1)S(1)}, u32[]{:S(2)}, u32[]{:S(2)}) collective-permute-start(bf16[10,128,64]{1,2,0:T(8,128)(2,1)S(1)} %get-tuple-element.10), channel_id=1, source_target_pairs={{0,16},{1,17},{2,18},{3,19},{4,20},{5,21},{6,22},{7,23},{8,24},{9,... | collective-permute-start | bytes 491528 | tf_op jit(solution)/shard_map/ppermute | solution.py:164
  111.9 3.1 %collective-permute-start.9 = (bf16[10,128,64]{1,2,0:T(8,128)(2,1)S(1)}, bf16[10,128,64]{1,2,0:T(8,128)(2,1)S(1)}, u32[]{:S(2)}, u32[]{:S(2)}) collective-permute-start(bf16[10,128,64]{1,2,0:T(8,128)(2,1)S(1)} %get-tuple-element.12), channel_id=1, source_target_pairs={{0,32},{1,33},{2,34},{3,35},{4,36},{5,37},{6,38},{7,39},{8,40},{9,... | collective-permute-start | bytes 491528 | tf_op jit(solution)/shard_map/ppermute | solution.py:164
  116.2 1.1 collective-permute-done.8
  117.3 3.3 %collective-permute-done.9 = bf16[10,128,64]{1,2,0:T(8,128)(2,1)S(1)} collective-permute-done((bf16[10,128,64]{1,2,0:T(8,128)(2,1)S(1)}, bf16[10,128,64]{1,2,0:T(8,128)(2,1)S(1)}, u32[]{:S(2)}, u32[]{:S(2)}) %collective-permute-start.9) | collective-permute-done | bytes 163872 | tf_op jit(solution)/shard_map/ppermute | solution.py:164
  120.6 1.2 fusion.6
  121.8 12.5 %all-to-all-start.2 = ((f32[64,2,76]{2,1,0:T(2,128)}), f32[64,2,76]{2,1,0:T(2,128)S(1)}, u32[]{:S(2)}, u32[]{:S(2)}) async-start(f32[64,2,76]{2,1,0:T(2,128)} %bitcast.40), calls=%async_computation.2 | async-start | bytes 131072 | tf_op jit(solution)/shard_map/all_to_all | solution.py:174
  134.3 13.5 %all-to-all-done.2 = f32[64,2,76]{2,1,0:T(2,128)S(1)} async-done(((f32[64,2,76]{2,1,0:T(2,128)}), f32[64,2,76]{2,1,0:T(2,128)S(1)}, u32[]{:S(2)}, u32[]{:S(2)}) %all-to-all-start.2) | async-done | bytes 38944 | tf_op jit(solution)/shard_map/all_to_all | solution.py:174
  149.9 4.6 %collective-permute-start.12 = (f32[2,2,32]{2,1,0:T(2,128)S(1)}, f32[2,2,32]{2,1,0:T(2,128)S(1)}, u32[]{:S(2)}, u32[]{:S(2)}) collective-permute-start(f32[2,2,32]{2,1,0:T(2,128)S(1)} %constant_dynamic-slice_fusion.1), channel_id=1, source_target_pairs={{0,256},{256,0},{1,257},{257,1},{2,258},{258,2},{3,259},{259,3},{4... | collective-permute-start | bytes 1544 | tf_op jit(solution)/shard_map/ppermute | solution.py:15
  (120 shorter events, 14.5 us)
Async XLA Ops:
  0.0 149.6 %copy-start = (bf16[2432,64]{0,1:T(8,128)(2,1)S(1)}, bf16[2432,64]{0,1:T(8,128)(2,1)}, u32[]{:S(2)}) copy-start(bf16[2432,64]{0,1:T(8,128)(2,1)} %param.29) | copy-start | bytes 933892
  0.0 14.1 %copy-start.1 = (s32[64]{0:T(128)S(1)}, s32[64]{0:T(128)}, u32[]{:S(2)}) copy-start(s32[64]{0:T(128)} %constant.181.clone) | copy-start | bytes 772
  0.0 13.4 %copy-start.7 = (bf16[1,1,2,2,2432]{4,3,2,1,0:T(2,128)(2,1)S(1)}, bf16[1,1,2,2,2432]{4,3,2,1,0:T(2,128)(2,1)}, u32[]{:S(2)}) copy-start(bf16[1,1,2,2,2432]{4,3,2,1,0:T(2,128)(2,1)} %param.19) | copy-start | bytes 58372
  0.0 15.6 %copy-start.4 = (f32[1,6,2432]{2,0,1:T(1,128)S(1)}, f32[1,6,2432]{2,0,1:T(1,128)}, u32[]{:S(2)}) copy-start(f32[1,6,2432]{2,0,1:T(1,128)} %param.27) | copy-start | bytes 175108
  0.8 17.5 %collective-permute-start = (bf16[2,2432]{1,0:T(2,128)(2,1)S(1)}, bf16[2,2432]{1,0:T(2,128)(2,1)S(1)}, u32[]{:S(2)}, u32[]{:S(2)}) collective-permute-start(bf16[2,2432]{1,0:T(2,128)(2,1)S(1)} %slice_bitcast_fusion.2), channel_id=1, source_target_pairs={{0,64},{64,0},{128,192},{192,128},{1,65},{65,1},{129,193},{193,129... | collective-permute-start | bytes 29192 | tf_op jit(solution)/shard_map/ppermute | solution.py:15
  5.5 12.8 %collective-permute-start.1 = (bf16[2,2432]{1,0:T(2,128)(2,1)S(1)}, bf16[2,2432]{1,0:T(2,128)(2,1)S(1)}, u32[]{:S(2)}, u32[]{:S(2)}) collective-permute-start(bf16[2,2432]{1,0:T(2,128)(2,1)S(1)} %slice_bitcast_fusion.1), channel_id=1, source_target_pairs={{0,64},{64,0},{128,192},{192,128},{1,65},{65,1},{129,193},{193,129... | collective-permute-start | bytes 29192 | tf_op jit(solution)/shard_map/ppermute | solution.py:15
  7.5 8.4 %copy-start.2 = (f32[1,6,2,2432]{3,2,1,0:T(2,128)S(1)}, f32[1,6,2,2432]{3,2,1,0:T(2,128)}, u32[]{:S(2)}) copy-start(f32[1,6,2,2432]{3,2,1,0:T(2,128)} %param.28) | copy-start | bytes 350212
  8.5 7.7 %copy-start.5 = (bf16[1,1,2,2,2432]{4,3,2,1,0:T(2,128)(2,1)S(1)}, bf16[1,1,2,2,2432]{4,3,2,1,0:T(2,128)(2,1)}, u32[]{:S(2)}) copy-start(bf16[1,1,2,2,2432]{4,3,2,1,0:T(2,128)(2,1)} %param.21) | copy-start | bytes 58372
  8.6 7.9 %copy-start.3 = (bf16[19,2432]{1,0:T(8,128)(2,1)S(1)}, bf16[19,2432]{1,0:T(8,128)(2,1)}, u32[]{:S(2)}) copy-start(bf16[19,2432]{1,0:T(8,128)(2,1)} %param.26) | copy-start | bytes 277252
  19.7 32.4 %all-to-all-start = ((bf16[64,2,512]{2,1,0:T(2,128)(2,1)}), bf16[64,2,512]{2,1,0:T(2,128)(2,1)S(1)}, u32[]{:S(2)}, u32[]{:S(2)}) async-start(bf16[64,2,512]{2,1,0:T(2,128)(2,1)} %reshape.464), calls=%async_computation | async-start | bytes 262144 | tf_op jit(solution)/shard_map/all_to_all | solution.py:116
  52.1 45.0 %all-to-all-start.1 = ((bf16[64,2,722]{2,1,0:T(2,128)(2,1)}), bf16[64,2,722]{2,1,0:T(2,128)(2,1)S(1)}, u32[]{:S(2)}, u32[]{:S(2)}) async-start(bf16[64,2,722]{2,1,0:T(2,128)(2,1)} %reshape.466), calls=%async_computation.1 | async-start | bytes 393216 | tf_op jit(solution)/shard_map/all_to_all | solution.py:133
  60.8 16.9 %collective-permute-start.2 = (bf16[1,2,128,64]{2,3,1,0:T(8,128)(2,1)S(1)}, bf16[1,2,128,64]{2,3,1,0:T(8,128)(2,1)S(1)}, u32[]{:S(2)}, u32[]{:S(2)}) collective-permute-start(bf16[1,2,128,64]{2,3,1,0:T(8,128)(2,1)S(1)} %get-tuple-element.23), channel_id=1, source_target_pairs={{0,4},{1,5},{2,6},{3,7},{4,0},{5,1},{6,2},{7,3},{8,12},{9,13},{10,... | collective-permute-start | bytes 98312 | tf_op jit(solution)/shard_map/ppermute | solution.py:149
  67.7 13.4 %collective-permute-start.3 = (bf16[1,2,128,64]{2,3,1,0:T(8,128)(2,1)S(1)}, bf16[1,2,128,64]{2,3,1,0:T(8,128)(2,1)S(1)}, u32[]{:S(2)}, u32[]{:S(2)}) collective-permute-start(bf16[1,2,128,64]{2,3,1,0:T(8,128)(2,1)S(1)} %get-tuple-element.23), channel_id=1, source_target_pairs={{0,8},{1,9},{2,10},{3,11},{4,12},{5,13},{6,14},{7,15},{8,0},{9,1},... | collective-permute-start | bytes 98312 | tf_op jit(solution)/shard_map/ppermute | solution.py:149
  74.7 8.9 %collective-permute-start.4 = (bf16[1,2,128,64]{2,3,1,0:T(8,128)(2,1)S(1)}, bf16[1,2,128,64]{2,3,1,0:T(8,128)(2,1)S(1)}, u32[]{:S(2)}, u32[]{:S(2)}) collective-permute-start(bf16[1,2,128,64]{2,3,1,0:T(8,128)(2,1)S(1)} %get-tuple-element.23), channel_id=1, source_target_pairs={{0,12},{1,13},{2,14},{3,15},{4,8},{5,9},{6,10},{7,11},{8,4},{9,5},... | collective-permute-start | bytes 98312 | tf_op jit(solution)/shard_map/ppermute | solution.py:149
  83.6 9.3 %collective-permute-start.5 = (bf16[4,2,128,64]{2,3,1,0:T(8,128)(2,1)S(1)}, bf16[4,2,128,64]{2,3,1,0:T(8,128)(2,1)S(1)}, u32[]{:S(2)}, u32[]{:S(2)}) collective-permute-start(bf16[4,2,128,64]{2,3,1,0:T(8,128)(2,1)S(1)} %pad_maximum_fusion), channel_id=1, source_target_pairs={{0,1},{1,0},{2,3},{3,2},{4,5},{5,4},{6,7},{7,6},{8,9},{9,8},{10,11... | collective-permute-start | bytes 393224 | tf_op jit(solution)/shard_map/ppermute | solution.py:149
  85.8 7.2 %collective-permute-start.6 = (bf16[4,2,128,64]{2,3,1,0:T(8,128)(2,1)S(1)}, bf16[4,2,128,64]{2,3,1,0:T(8,128)(2,1)S(1)}, u32[]{:S(2)}, u32[]{:S(2)}) collective-permute-start(bf16[4,2,128,64]{2,3,1,0:T(8,128)(2,1)S(1)} %pad_maximum_fusion), channel_id=1, source_target_pairs={{0,2},{1,3},{2,0},{3,1},{4,6},{5,7},{6,4},{7,5},{8,10},{9,11},{10,... | collective-permute-start | bytes 393224 | tf_op jit(solution)/shard_map/ppermute | solution.py:149
  88.7 7.6 %collective-permute-start.7 = (bf16[4,2,128,64]{2,3,1,0:T(8,128)(2,1)S(1)}, bf16[4,2,128,64]{2,3,1,0:T(8,128)(2,1)S(1)}, u32[]{:S(2)}, u32[]{:S(2)}) collective-permute-start(bf16[4,2,128,64]{2,3,1,0:T(8,128)(2,1)S(1)} %pad_maximum_fusion), channel_id=1, source_target_pairs={{0,3},{1,2},{2,1},{3,0},{4,7},{5,6},{6,5},{7,4},{8,11},{9,10},{10,... | collective-permute-start | bytes 393224 | tf_op jit(solution)/shard_map/ppermute | solution.py:149
  97.8 17.3 %collective-permute-start.11 = (bf16[1216,76]{1,0:T(8,128)(2,1)S(1)}, bf16[1216,76]{1,0:T(8,128)(2,1)S(1)}, u32[]{:S(2)}, u32[]{:S(2)}) collective-permute-start(bf16[1216,76]{1,0:T(8,128)(2,1)S(1)} %reshape.405), channel_id=1, source_target_pairs={{0,256},{256,0},{1,257},{257,1},{2,258},{258,2},{3,259},{259,3},{4... | collective-permute-start | bytes 554504 | tf_op jit(solution)/shard_map/ppermute | solution.py:15
  105.4 10.9 %collective-permute-start.10 = (bf16[10,128,64]{1,2,0:T(8,128)(2,1)S(1)}, bf16[10,128,64]{1,2,0:T(8,128)(2,1)S(1)}, u32[]{:S(2)}, u32[]{:S(2)}) collective-permute-start(bf16[10,128,64]{1,2,0:T(8,128)(2,1)S(1)} %get-tuple-element.11), channel_id=1, source_target_pairs={{0,48},{1,49},{2,50},{3,51},{4,52},{5,53},{6,54},{7,55},{8,56},{9,... | collective-permute-start | bytes 491528 | tf_op jit(solution)/shard_map/ppermute | solution.py:164
  110.0 7.4 %collective-permute-start.8 = (bf16[10,128,64]{1,2,0:T(8,128)(2,1)S(1)}, bf16[10,128,64]{1,2,0:T(8,128)(2,1)S(1)}, u32[]{:S(2)}, u32[]{:S(2)}) collective-permute-start(bf16[10,128,64]{1,2,0:T(8,128)(2,1)S(1)} %get-tuple-element.10), channel_id=1, source_target_pairs={{0,16},{1,17},{2,18},{3,19},{4,20},{5,21},{6,22},{7,23},{8,24},{9,... | collective-permute-start | bytes 491528 | tf_op jit(solution)/shard_map/ppermute | solution.py:164
  111.9 8.7 %collective-permute-start.9 = (bf16[10,128,64]{1,2,0:T(8,128)(2,1)S(1)}, bf16[10,128,64]{1,2,0:T(8,128)(2,1)S(1)}, u32[]{:S(2)}, u32[]{:S(2)}) collective-permute-start(bf16[10,128,64]{1,2,0:T(8,128)(2,1)S(1)} %get-tuple-element.12), channel_id=1, source_target_pairs={{0,32},{1,33},{2,34},{3,35},{4,36},{5,37},{6,38},{7,39},{8,40},{9,... | collective-permute-start | bytes 491528 | tf_op jit(solution)/shard_map/ppermute | solution.py:164
  116.2 18.1 %copy-start.11 = (s32[32]{0:T(128)S(1)}, s32[32]{0:T(128)}, u32[]{:S(2)}) copy-start(s32[32]{0:T(128)} %constant.216) | copy-start | bytes 388
  116.2 18.1 %copy-start.12 = (s32[32]{0:T(128)S(1)}, s32[32]{0:T(128)}, u32[]{:S(2)}) copy-start(s32[32]{0:T(128)} %constant.217) | copy-start | bytes 388
  116.2 33.1 %copy-start.6 = (bf16[1,1,2,2,2432]{4,3,2,1,0:T(2,128)(2,1)S(1)}, bf16[1,1,2,2,2432]{4,3,2,1,0:T(2,128)(2,1)}, u32[]{:S(2)}) copy-start(bf16[1,1,2,2,2432]{4,3,2,1,0:T(2,128)(2,1)} %param.22) | copy-start | bytes 58372
  121.8 32.7 %copy-start.9 = (f32[6]{0:T(128)S(1)}, f32[6]{0:T(128)}, u32[]{:S(2)}) copy-start(f32[6]{0:T(128)} %param.31) | copy-start | bytes 76
  121.8 32.7 %copy-start.10 = (f32[6]{0:T(128)S(1)}, f32[6]{0:T(128)}, u32[]{:S(2)}) copy-start(f32[6]{0:T(128)} %param.30) | copy-start | bytes 76
  121.8 33.5 %copy-start.8 = (f32[1,2,2,32]{3,2,1,0:T(2,128)S(1)}, f32[1,2,2,32]{3,2,1,0:T(2,128)}, u32[]{:S(2)}) copy-start(f32[1,2,2,32]{3,2,1,0:T(2,128)} %param.23) | copy-start | bytes 1540
  121.8 26.0 %all-to-all-start.2 = ((f32[64,2,76]{2,1,0:T(2,128)}), f32[64,2,76]{2,1,0:T(2,128)S(1)}, u32[]{:S(2)}, u32[]{:S(2)}) async-start(f32[64,2,76]{2,1,0:T(2,128)} %bitcast.40), calls=%async_computation.2 | async-start | bytes 131072 | tf_op jit(solution)/shard_map/all_to_all | solution.py:174
  149.9 5.4 %collective-permute-start.12 = (f32[2,2,32]{2,1,0:T(2,128)S(1)}, f32[2,2,32]{2,1,0:T(2,128)S(1)}, u32[]{:S(2)}, u32[]{:S(2)}) collective-permute-start(f32[2,2,32]{2,1,0:T(2,128)S(1)} %constant_dynamic-slice_fusion.1), channel_id=1, source_target_pairs={{0,256},{256,0},{1,257},{257,1},{2,258},{258,2},{3,259},{259,3},{4... | collective-permute-start | bytes 1544 | tf_op jit(solution)/shard_map/ppermute | solution.py:15

commit v9 on v7

--- a/solution.py
+++ b/solution.py
@@ -85,7 +85,9 @@
     local_values = values[0, 0]
     shard_rows = resident_key_rows.shape[1]
     slot_total = nseq * shard_rows
-    far_keys, far_values = from_partner((resident_key_rows[1], local_values[1]), "grp", 0)
+    far_keys, far_values = from_partner(
+        jnp.stack([resident_key_rows[1], local_values[1]]), "grp", 0
+    )
 
     head_table = head_placement(nseq)
 

time: 149 us -> 146 us (0.980)
    ppermute x4 -> x3, starting transfers between devices: 17.9 us -> 15.7 us  [from_partner(): lax.ppermute(x, axis, [(i, i ^ 1 << apart) for i in range(lax.axis_size(a...]
  transfers between devices with their start and end apart: 15 -> 14, of which waited for: 6 -> 6; matrix products, arithmetic and copies ran while one was open for 9% -> 8% of each run, Pallas kernels for 0% -> 0%
where the time goes in v9:
time: 146 us; the launch traced here: 145 us
  starting transfers between devices  78.1 us (53%)
  waiting for transfers between devices  43.7 us (30%)
  local copies, waits for them, and re-layouts  13.3 us (9%)
  other arithmetic  6.25 us (4%)
  matrix products  2.77 us (2%)
    ppermute x6, starting transfers between devices, shards(): lax.ppermute(gathered, 'seq', [(i, i ^ shift) for i in range(nseq)])  25.5 us
    all_to_all x1, waiting for transfers between devices, shards(): joint = lax.all_to_all(joint, 'seq', 0, 0, tiled=True)  20.7 us
    all_to_all x1, starting transfers between devices, shards(): joint = lax.all_to_all(joint, 'seq', 0, 0, tiled=True)  18.3 us
    ppermute x3, starting transfers between devices, from_partner(): lax.ppermute(x, axis, [(i, i ^ 1 << apart) for i in range(lax.axis_size(a...  15.7 us
    all_to_all x1, waiting for transfers between devices, shards(): received = lax.all_to_all(projected_parts, 'seq', 0, 0, tiled=True)  13.5 us
    ppermute x3, starting transfers between devices, shards(): lax.ppermute(outgoing, 'seq', [(i, i ^ shift) for i in range(nseq)])  10.6 us
    all_to_all x1, starting transfers between devices, shards(): received = lax.all_to_all(projected_parts, 'seq', 0, 0, tiled=True)  7.96 us
    ppermute x6, waiting for transfers between devices, shards(): lax.ppermute(gathered, 'seq', [(i, i ^ shift) for i in range(nseq)])  4.9 us
  transfers between devices with their start and end apart: 14, of which 6 were waited for; matrix products, arithmetic and copies ran while one was open for 8% of the time, Pallas kernels for 0%

profile of v9, /device:TPU:1, one launch (start us, length us, event | category | flops | bytes accessed | tf_op | source)
XLA Modules:
  0.0 145.1 jit_solution(6404242791164553264)
XLA Ops:
  0.0 0.8 slice_bitcast_fusion.1
  0.9 4.0 %collective-permute-start = (bf16[2,2,2432]{2,1,0:T(2,128)(2,1)S(1)}, bf16[2,2,2432]{2,1,0:T(2,128)(2,1)S(1)}, u32[]{:S(2)}, u32[]{:S(2)}) collective-permute-start(bf16[2,2,2432]{2,1,0:T(2,128)(2,1)S(1)} %pad_maximum_fusion.2), channel_id=1, source_target_pairs={{0,64},{64,0},{128,192},{192,128},{1,65},{65,1},{129,193},{193,129... | collective-permute-start | bytes 58376 | tf_op jit(solution)/shard_map/ppermute | solution.py:15
  4.9 0.8 concatenate.97
  5.9 1.3 gather_fusion
  9.4 0.6 iota_compare_fusion.4
  10.1 0.7 iota_compare_fusion.5
  10.8 0.8 gather_fusion.2
  11.7 0.7 fusion.48
  14.9 0.8 reduce.2
  15.7 1.1 reshape.458
  16.8 18.3 %all-to-all-start = ((bf16[64,2,1234]{2,1,0:T(2,128)(2,1)}), bf16[64,2,1234]{2,1,0:T(2,128)(2,1)S(1)}, u32[]{:S(2)}, u32[]{:S(2)}) async-start(bf16[64,2,1234]{2,1,0:T(2,128)(2,1)} %reshape.458), calls=%async_computation | async-start | bytes 655360 | tf_op jit(solution)/shard_map/all_to_all | solution.py:122
  35.6 20.7 %all-to-all-done = bf16[64,2,1234]{2,1,0:T(2,128)(2,1)S(1)} async-done(((bf16[64,2,1234]{2,1,0:T(2,128)(2,1)}), bf16[64,2,1234]{2,1,0:T(2,128)(2,1)S(1)}, u32[]{:S(2)}, u32[]{:S(2)}) %all-to-all-start) | async-done | bytes 315936 | tf_op jit(solution)/shard_map/all_to_all | solution.py:122
  58.5 4.8 %collective-permute-start.1 = (bf16[1,2,128,64]{2,3,1,0:T(8,128)(2,1)S(1)}, bf16[1,2,128,64]{2,3,1,0:T(8,128)(2,1)S(1)}, u32[]{:S(2)}, u32[]{:S(2)}) collective-permute-start(bf16[1,2,128,64]{2,3,1,0:T(8,128)(2,1)S(1)} %get-tuple-element.23), channel_id=1, source_target_pairs={{0,4},{1,5},{2,6},{3,7},{4,0},{5,1},{6,2},{7,3},{8,12},{9,13},{10,... | collective-permute-start | bytes 98312 | tf_op jit(solution)/shard_map/ppermute | solution.py:155
  63.4 6.9 %collective-permute-start.2 = (bf16[1,2,128,64]{2,3,1,0:T(8,128)(2,1)S(1)}, bf16[1,2,128,64]{2,3,1,0:T(8,128)(2,1)S(1)}, u32[]{:S(2)}, u32[]{:S(2)}) collective-permute-start(bf16[1,2,128,64]{2,3,1,0:T(8,128)(2,1)S(1)} %get-tuple-element.23), channel_id=1, source_target_pairs={{0,8},{1,9},{2,10},{3,11},{4,12},{5,13},{6,14},{7,15},{8,0},{9,1},... | collective-permute-start | bytes 98312 | tf_op jit(solution)/shard_map/ppermute | solution.py:155
  70.3 4.5 %collective-permute-start.3 = (bf16[1,2,128,64]{2,3,1,0:T(8,128)(2,1)S(1)}, bf16[1,2,128,64]{2,3,1,0:T(8,128)(2,1)S(1)}, u32[]{:S(2)}, u32[]{:S(2)}) collective-permute-start(bf16[1,2,128,64]{2,3,1,0:T(8,128)(2,1)S(1)} %get-tuple-element.23), channel_id=1, source_target_pairs={{0,12},{1,13},{2,14},{3,15},{4,8},{5,9},{6,10},{7,11},{8,4},{9,5},... | collective-permute-start | bytes 98312 | tf_op jit(solution)/shard_map/ppermute | solution.py:155
  74.8 0.7 fusion.49
  76.0 6.1 %collective-permute-start.10 = (bf16[1216,76]{1,0:T(8,128)(2,1)S(1)}, bf16[1216,76]{1,0:T(8,128)(2,1)S(1)}, u32[]{:S(2)}, u32[]{:S(2)}) collective-permute-start(bf16[1216,76]{1,0:T(8,128)(2,1)S(1)} %reshape.399), channel_id=1, source_target_pairs={{0,256},{256,0},{1,257},{257,1},{2,258},{258,2},{3,259},{259,3},{4... | collective-permute-start | bytes 554504 | tf_op jit(solution)/shard_map/ppermute | solution.py:15
  82.2 2.5 %collective-permute-start.4 = (bf16[4,2,128,64]{2,3,1,0:T(8,128)(2,1)S(1)}, bf16[4,2,128,64]{2,3,1,0:T(8,128)(2,1)S(1)}, u32[]{:S(2)}, u32[]{:S(2)}) collective-permute-start(bf16[4,2,128,64]{2,3,1,0:T(8,128)(2,1)S(1)} %pad_maximum_fusion), channel_id=1, source_target_pairs={{0,1},{1,0},{2,3},{3,2},{4,5},{5,4},{6,7},{7,6},{8,9},{9,8},{10,11... | collective-permute-start | bytes 393224 | tf_op jit(solution)/shard_map/ppermute | solution.py:155
  84.6 2.7 %collective-permute-start.5 = (bf16[4,2,128,64]{2,3,1,0:T(8,128)(2,1)S(1)}, bf16[4,2,128,64]{2,3,1,0:T(8,128)(2,1)S(1)}, u32[]{:S(2)}, u32[]{:S(2)}) collective-permute-start(bf16[4,2,128,64]{2,3,1,0:T(8,128)(2,1)S(1)} %pad_maximum_fusion), channel_id=1, source_target_pairs={{0,2},{1,3},{2,0},{3,1},{4,6},{5,7},{6,4},{7,5},{8,10},{9,11},{10,... | collective-permute-start | bytes 393224 | tf_op jit(solution)/shard_map/ppermute | solution.py:155
  87.3 4.1 %collective-permute-start.6 = (bf16[4,2,128,64]{2,3,1,0:T(8,128)(2,1)S(1)}, bf16[4,2,128,64]{2,3,1,0:T(8,128)(2,1)S(1)}, u32[]{:S(2)}, u32[]{:S(2)}) collective-permute-start(bf16[4,2,128,64]{2,3,1,0:T(8,128)(2,1)S(1)} %pad_maximum_fusion), channel_id=1, source_target_pairs={{0,3},{1,2},{2,1},{3,0},{4,7},{5,6},{6,5},{7,4},{8,11},{9,10},{10,... | collective-permute-start | bytes 393224 | tf_op jit(solution)/shard_map/ppermute | solution.py:155
  91.5 4.9 %collective-permute-done.5 = bf16[4,2,128,64]{2,3,1,0:T(8,128)(2,1)S(1)} collective-permute-done((bf16[4,2,128,64]{2,3,1,0:T(8,128)(2,1)S(1)}, bf16[4,2,128,64]{2,3,1,0:T(8,128)(2,1)S(1)}, u32[]{:S(2)}, u32[]{:S(2)}) %collective-permute-start.5) | collective-permute-done | bytes 131104 | tf_op jit(solution)/shard_map/ppermute | solution.py:155
  97.3 6.2 %collective-permute-start.9 = (bf16[10,128,64]{1,2,0:T(8,128)(2,1)S(1)}, bf16[10,128,64]{1,2,0:T(8,128)(2,1)S(1)}, u32[]{:S(2)}, u32[]{:S(2)}) collective-permute-start(bf16[10,128,64]{1,2,0:T(8,128)(2,1)S(1)} %get-tuple-element.11), channel_id=1, source_target_pairs={{0,48},{1,49},{2,50},{3,51},{4,52},{5,53},{6,54},{7,55},{8,56},{9,... | collective-permute-start | bytes 491528 | tf_op jit(solution)/shard_map/ppermute | solution.py:170
  103.6 1.9 %collective-permute-start.8 = (bf16[10,128,64]{1,2,0:T(8,128)(2,1)S(1)}, bf16[10,128,64]{1,2,0:T(8,128)(2,1)S(1)}, u32[]{:S(2)}, u32[]{:S(2)}) collective-permute-start(bf16[10,128,64]{1,2,0:T(8,128)(2,1)S(1)} %get-tuple-element.12), channel_id=1, source_target_pairs={{0,32},{1,33},{2,34},{3,35},{4,36},{5,37},{6,38},{7,39},{8,40},{9,... | collective-permute-start | bytes 491528 | tf_op jit(solution)/shard_map/ppermute | solution.py:170
  105.5 2.5 %collective-permute-start.7 = (bf16[10,128,64]{1,2,0:T(8,128)(2,1)S(1)}, bf16[10,128,64]{1,2,0:T(8,128)(2,1)S(1)}, u32[]{:S(2)}, u32[]{:S(2)}) collective-permute-start(bf16[10,128,64]{1,2,0:T(8,128)(2,1)S(1)} %get-tuple-element.10), channel_id=1, source_target_pairs={{0,16},{1,17},{2,18},{3,19},{4,20},{5,21},{6,22},{7,23},{8,24},{9,... | collective-permute-start | bytes 491528 | tf_op jit(solution)/shard_map/ppermute | solution.py:170
  108.5 0.7 gather_fusion.3
  109.2 1.9 %collective-permute-done.8 = bf16[10,128,64]{1,2,0:T(8,128)(2,1)S(1)} collective-permute-done((bf16[10,128,64]{1,2,0:T(8,128)(2,1)S(1)}, bf16[10,128,64]{1,2,0:T(8,128)(2,1)S(1)}, u32[]{:S(2)}, u32[]{:S(2)}) %collective-permute-start.8) | collective-permute-done | bytes 163872 | tf_op jit(solution)/shard_map/ppermute | solution.py:170
  111.2 2.0 %collective-permute-done.7 = bf16[10,128,64]{1,2,0:T(8,128)(2,1)S(1)} collective-permute-done((bf16[10,128,64]{1,2,0:T(8,128)(2,1)S(1)}, bf16[10,128,64]{1,2,0:T(8,128)(2,1)S(1)}, u32[]{:S(2)}, u32[]{:S(2)}) %collective-permute-start.7) | collective-permute-done | bytes 163872 | tf_op jit(solution)/shard_map/ppermute | solution.py:170
  113.2 1.1 fusion.6
  114.3 8.0 %all-to-all-start.1 = ((f32[64,2,76]{2,1,0:T(2,128)}), f32[64,2,76]{2,1,0:T(2,128)S(1)}, u32[]{:S(2)}, u32[]{:S(2)}) async-start(f32[64,2,76]{2,1,0:T(2,128)} %bitcast.39), calls=%async_computation.1 | async-start | bytes 131072 | tf_op jit(solution)/shard_map/all_to_all | solution.py:180
  122.4 13.5 %all-to-all-done.1 = f32[64,2,76]{2,1,0:T(2,128)S(1)} async-done(((f32[64,2,76]{2,1,0:T(2,128)}), f32[64,2,76]{2,1,0:T(2,128)S(1)}, u32[]{:S(2)}, u32[]{:S(2)}) %all-to-all-start.1) | async-done | bytes 38944 | tf_op jit(solution)/shard_map/all_to_all | solution.py:180
  138.0 5.6 %collective-permute-start.11 = (f32[2,2,32]{2,1,0:T(2,128)S(1)}, f32[2,2,32]{2,1,0:T(2,128)S(1)}, u32[]{:S(2)}, u32[]{:S(2)}) collective-permute-start(f32[2,2,32]{2,1,0:T(2,128)S(1)} %constant_dynamic-slice_fusion.1), channel_id=1, source_target_pairs={{0,256},{256,0},{1,257},{257,1},{2,258},{258,2},{3,259},{259,3},{4... | collective-permute-start | bytes 1544 | tf_op jit(solution)/shard_map/ppermute | solution.py:15
  144.4 0.7 fusion.43
  (128 shorter events, 12.2 us)
Async XLA Ops:
  0.0 137.6 %copy-start = (bf16[2432,64]{0,1:T(8,128)(2,1)S(1)}, bf16[2432,64]{0,1:T(8,128)(2,1)}, u32[]{:S(2)}) copy-start(bf16[2432,64]{0,1:T(8,128)(2,1)} %param.29) | copy-start | bytes 933892
  0.0 10.8 %copy-start.1 = (s32[64]{0:T(128)S(1)}, s32[64]{0:T(128)}, u32[]{:S(2)}) copy-start(s32[64]{0:T(128)} %constant.181.clone) | copy-start | bytes 772
  0.0 7.3 %copy-start.7 = (bf16[1,1,2,2,2432]{4,3,2,1,0:T(2,128)(2,1)S(1)}, bf16[1,1,2,2,2432]{4,3,2,1,0:T(2,128)(2,1)}, u32[]{:S(2)}) copy-start(bf16[1,1,2,2,2432]{4,3,2,1,0:T(2,128)(2,1)} %param.19) | copy-start | bytes 58372
  0.0 7.5 %copy-start.8 = (s32[4,2]{0,1:T(2,128)S(1)}, s32[4,2]{0,1:T(2,128)}, u32[]{:S(2)}) copy-start(s32[4,2]{0,1:T(2,128)} %param.25) | copy-start | bytes 100
  0.0 7.5 %copy-start.10 = (s32[4,2]{0,1:T(2,128)S(1)}, s32[4,2]{0,1:T(2,128)}, u32[]{:S(2)}) copy-start(s32[4,2]{0,1:T(2,128)} %param.24) | copy-start | bytes 100
  0.8 11.5 %copy-start.5 = (bf16[1,1,2,2,2432]{4,3,2,1,0:T(2,128)(2,1)S(1)}, bf16[1,1,2,2,2432]{4,3,2,1,0:T(2,128)(2,1)}, u32[]{:S(2)}) copy-start(bf16[1,1,2,2,2432]{4,3,2,1,0:T(2,128)(2,1)} %param.21) | copy-start | bytes 58372
  0.9 12.5 %collective-permute-start = (bf16[2,2,2432]{2,1,0:T(2,128)(2,1)S(1)}, bf16[2,2,2432]{2,1,0:T(2,128)(2,1)S(1)}, u32[]{:S(2)}, u32[]{:S(2)}) collective-permute-start(bf16[2,2,2432]{2,1,0:T(2,128)(2,1)S(1)} %pad_maximum_fusion.2), channel_id=1, source_target_pairs={{0,64},{64,0},{128,192},{192,128},{1,65},{65,1},{129,193},{193,129... | collective-permute-start | bytes 58376 | tf_op jit(solution)/shard_map/ppermute | solution.py:15
  5.7 6.7 %copy-start.3 = (bf16[19,2432]{1,0:T(8,128)(2,1)S(1)}, bf16[19,2432]{1,0:T(8,128)(2,1)}, u32[]{:S(2)}) copy-start(bf16[19,2432]{1,0:T(8,128)(2,1)} %param.26) | copy-start | bytes 277252
  15.7 19.4 %copy-start.4 = (f32[1,6,2432]{2,0,1:T(1,128)S(1)}, f32[1,6,2432]{2,0,1:T(1,128)}, u32[]{:S(2)}) copy-start(f32[1,6,2432]{2,0,1:T(1,128)} %param.27) | copy-start | bytes 175108
  15.7 19.7 %copy-start.2 = (f32[1,6,2,2432]{3,2,1,0:T(2,128)S(1)}, f32[1,6,2,2432]{3,2,1,0:T(2,128)}, u32[]{:S(2)}) copy-start(f32[1,6,2,2432]{3,2,1,0:T(2,128)} %param.28) | copy-start | bytes 350212
  16.8 39.6 %all-to-all-start = ((bf16[64,2,1234]{2,1,0:T(2,128)(2,1)}), bf16[64,2,1234]{2,1,0:T(2,128)(2,1)S(1)}, u32[]{:S(2)}, u32[]{:S(2)}) async-start(bf16[64,2,1234]{2,1,0:T(2,128)(2,1)} %reshape.458), calls=%async_computation | async-start | bytes 655360 | tf_op jit(solution)/shard_map/all_to_all | solution.py:122
  58.5 23.5 %collective-permute-start.1 = (bf16[1,2,128,64]{2,3,1,0:T(8,128)(2,1)S(1)}, bf16[1,2,128,64]{2,3,1,0:T(8,128)(2,1)S(1)}, u32[]{:S(2)}, u32[]{:S(2)}) collective-permute-start(bf16[1,2,128,64]{2,3,1,0:T(8,128)(2,1)S(1)} %get-tuple-element.23), channel_id=1, source_target_pairs={{0,4},{1,5},{2,6},{3,7},{4,0},{5,1},{6,2},{7,3},{8,12},{9,13},{10,... | collective-permute-start | bytes 98312 | tf_op jit(solution)/shard_map/ppermute | solution.py:155
  63.4 18.7 %collective-permute-start.2 = (bf16[1,2,128,64]{2,3,1,0:T(8,128)(2,1)S(1)}, bf16[1,2,128,64]{2,3,1,0:T(8,128)(2,1)S(1)}, u32[]{:S(2)}, u32[]{:S(2)}) collective-permute-start(bf16[1,2,128,64]{2,3,1,0:T(8,128)(2,1)S(1)} %get-tuple-element.23), channel_id=1, source_target_pairs={{0,8},{1,9},{2,10},{3,11},{4,12},{5,13},{6,14},{7,15},{8,0},{9,1},... | collective-permute-start | bytes 98312 | tf_op jit(solution)/shard_map/ppermute | solution.py:155
  70.3 11.8 %collective-permute-start.3 = (bf16[1,2,128,64]{2,3,1,0:T(8,128)(2,1)S(1)}, bf16[1,2,128,64]{2,3,1,0:T(8,128)(2,1)S(1)}, u32[]{:S(2)}, u32[]{:S(2)}) collective-permute-start(bf16[1,2,128,64]{2,3,1,0:T(8,128)(2,1)S(1)} %get-tuple-element.23), channel_id=1, source_target_pairs={{0,12},{1,13},{2,14},{3,15},{4,8},{5,9},{6,10},{7,11},{8,4},{9,5},... | collective-permute-start | bytes 98312 | tf_op jit(solution)/shard_map/ppermute | solution.py:155
  76.0 32.0 %collective-permute-start.10 = (bf16[1216,76]{1,0:T(8,128)(2,1)S(1)}, bf16[1216,76]{1,0:T(8,128)(2,1)S(1)}, u32[]{:S(2)}, u32[]{:S(2)}) collective-permute-start(bf16[1216,76]{1,0:T(8,128)(2,1)S(1)} %reshape.399), channel_id=1, source_target_pairs={{0,256},{256,0},{1,257},{257,1},{2,258},{258,2},{3,259},{259,3},{4... | collective-permute-start | bytes 554504 | tf_op jit(solution)/shard_map/ppermute | solution.py:15
  82.2 9.3 %collective-permute-start.4 = (bf16[4,2,128,64]{2,3,1,0:T(8,128)(2,1)S(1)}, bf16[4,2,128,64]{2,3,1,0:T(8,128)(2,1)S(1)}, u32[]{:S(2)}, u32[]{:S(2)}) collective-permute-start(bf16[4,2,128,64]{2,3,1,0:T(8,128)(2,1)S(1)} %pad_maximum_fusion), channel_id=1, source_target_pairs={{0,1},{1,0},{2,3},{3,2},{4,5},{5,4},{6,7},{7,6},{8,9},{9,8},{10,11... | collective-permute-start | bytes 393224 | tf_op jit(solution)/shard_map/ppermute | solution.py:155
  84.6 11.8 %collective-permute-start.5 = (bf16[4,2,128,64]{2,3,1,0:T(8,128)(2,1)S(1)}, bf16[4,2,128,64]{2,3,1,0:T(8,128)(2,1)S(1)}, u32[]{:S(2)}, u32[]{:S(2)}) collective-permute-start(bf16[4,2,128,64]{2,3,1,0:T(8,128)(2,1)S(1)} %pad_maximum_fusion), channel_id=1, source_target_pairs={{0,2},{1,3},{2,0},{3,1},{4,6},{5,7},{6,4},{7,5},{8,10},{9,11},{10,... | collective-permute-start | bytes 393224 | tf_op jit(solution)/shard_map/ppermute | solution.py:155
  87.3 9.1 %collective-permute-start.6 = (bf16[4,2,128,64]{2,3,1,0:T(8,128)(2,1)S(1)}, bf16[4,2,128,64]{2,3,1,0:T(8,128)(2,1)S(1)}, u32[]{:S(2)}, u32[]{:S(2)}) collective-permute-start(bf16[4,2,128,64]{2,3,1,0:T(8,128)(2,1)S(1)} %pad_maximum_fusion), channel_id=1, source_target_pairs={{0,3},{1,2},{2,1},{3,0},{4,7},{5,6},{6,5},{7,4},{8,11},{9,10},{10,... | collective-permute-start | bytes 393224 | tf_op jit(solution)/shard_map/ppermute | solution.py:155
  97.3 11.9 %collective-permute-start.9 = (bf16[10,128,64]{1,2,0:T(8,128)(2,1)S(1)}, bf16[10,128,64]{1,2,0:T(8,128)(2,1)S(1)}, u32[]{:S(2)}, u32[]{:S(2)}) collective-permute-start(bf16[10,128,64]{1,2,0:T(8,128)(2,1)S(1)} %get-tuple-element.11), channel_id=1, source_target_pairs={{0,48},{1,49},{2,50},{3,51},{4,52},{5,53},{6,54},{7,55},{8,56},{9,... | collective-permute-start | bytes 491528 | tf_op jit(solution)/shard_map/ppermute | solution.py:170
  103.6 7.6 %collective-permute-start.8 = (bf16[10,128,64]{1,2,0:T(8,128)(2,1)S(1)}, bf16[10,128,64]{1,2,0:T(8,128)(2,1)S(1)}, u32[]{:S(2)}, u32[]{:S(2)}) collective-permute-start(bf16[10,128,64]{1,2,0:T(8,128)(2,1)S(1)} %get-tuple-element.12), channel_id=1, source_target_pairs={{0,32},{1,33},{2,34},{3,35},{4,36},{5,37},{6,38},{7,39},{8,40},{9,... | collective-permute-start | bytes 491528 | tf_op jit(solution)/shard_map/ppermute | solution.py:170
  105.5 7.7 %collective-permute-start.7 = (bf16[10,128,64]{1,2,0:T(8,128)(2,1)S(1)}, bf16[10,128,64]{1,2,0:T(8,128)(2,1)S(1)}, u32[]{:S(2)}, u32[]{:S(2)}) collective-permute-start(bf16[10,128,64]{1,2,0:T(8,128)(2,1)S(1)} %get-tuple-element.10), channel_id=1, source_target_pairs={{0,16},{1,17},{2,18},{3,19},{4,20},{5,21},{6,22},{7,23},{8,24},{9,... | collective-permute-start | bytes 491528 | tf_op jit(solution)/shard_map/ppermute | solution.py:170
  109.2 13.1 %copy-start.13 = (s32[32]{0:T(128)S(1)}, s32[32]{0:T(128)}, u32[]{:S(2)}) copy-start(s32[32]{0:T(128)} %constant.217) | copy-start | bytes 388
  109.2 13.1 %copy-start.14 = (s32[32]{0:T(128)S(1)}, s32[32]{0:T(128)}, u32[]{:S(2)}) copy-start(s32[32]{0:T(128)} %constant.216) | copy-start | bytes 388
  109.2 28.1 %copy-start.6 = (bf16[1,1,2,2,2432]{4,3,2,1,0:T(2,128)(2,1)S(1)}, bf16[1,1,2,2,2432]{4,3,2,1,0:T(2,128)(2,1)}, u32[]{:S(2)}) copy-start(bf16[1,1,2,2,2432]{4,3,2,1,0:T(2,128)(2,1)} %param.22) | copy-start | bytes 58372
  114.3 29.3 %copy-start.11 = (f32[6]{0:T(128)S(1)}, f32[6]{0:T(128)}, u32[]{:S(2)}) copy-start(f32[6]{0:T(128)} %param.31) | copy-start | bytes 76
  114.3 29.3 %copy-start.12 = (f32[6]{0:T(128)S(1)}, f32[6]{0:T(128)}, u32[]{:S(2)}) copy-start(f32[6]{0:T(128)} %param.30) | copy-start | bytes 76
  114.3 30.1 %copy-start.9 = (f32[1,2,2,32]{3,2,1,0:T(2,128)S(1)}, f32[1,2,2,32]{3,2,1,0:T(2,128)}, u32[]{:S(2)}) copy-start(f32[1,2,2,32]{3,2,1,0:T(2,128)} %param.23) | copy-start | bytes 1540
  114.3 21.5 %all-to-all-start.1 = ((f32[64,2,76]{2,1,0:T(2,128)}), f32[64,2,76]{2,1,0:T(2,128)S(1)}, u32[]{:S(2)}, u32[]{:S(2)}) async-start(f32[64,2,76]{2,1,0:T(2,128)} %bitcast.39), calls=%async_computation.1 | async-start | bytes 131072 | tf_op jit(solution)/shard_map/all_to_all | solution.py:180
  138.0 6.4 %collective-permute-start.11 = (f32[2,2,32]{2,1,0:T(2,128)S(1)}, f32[2,2,32]{2,1,0:T(2,128)S(1)}, u32[]{:S(2)}, u32[]{:S(2)}) collective-permute-start(f32[2,2,32]{2,1,0:T(2,128)S(1)} %constant_dynamic-slice_fusion.1), channel_id=1, source_target_pairs={{0,256},{256,0},{1,257},{257,1},{2,258},{258,2},{3,259},{259,3},{4... | collective-permute-start | bytes 1544 | tf_op jit(solution)/shard_map/ppermute | solution.py:15

commit v10 on v9

--- a/solution.py
+++ b/solution.py
@@ -46,6 +46,16 @@
 def plane_heads(n):
     assert n == 64
     return -(-HEADS // 4)
+
+
+def swap_digits(i):
+    return (i >> 2) | ((i & 3) << 2)
+
+
+def head_of(j):
+    x, z = j >> 4, j & 15
+    head = x * plane_heads(64) + z
+    return jnp.where((z < plane_heads(64)) & (head < HEADS), head, HEADS)
 
 
 def head_placement(n):
@@ -157,10 +167,10 @@
         gathered = jnp.concatenate(parts, 0)
         masks = grown
     plane = len(masks)
-    inverse = [masks.index(z) for z in range(plane)]
+    assert masks == [swap_digits(i) for i in range(len(masks))]
     my_z = me % plane
     my_x = me // plane
-    by_z = jnp.take(gathered, jnp.take(jnp.array(inverse, jnp.int32), jnp.bitwise_xor(my_z, jnp.arange(plane))), axis=0)
+    by_z = jnp.take(gathered, swap_digits(jnp.bitwise_xor(my_z, jnp.arange(plane))), axis=0)
     my_region = my_x % 2
     parts = [lax.dynamic_index_in_dim(by_z, my_region, 1, keepdims=False)]
     sources = [my_x * plane + jnp.arange(plane)]
@@ -170,7 +180,7 @@
         parts.append(lax.ppermute(outgoing, "seq", [(i, i ^ shift) for i in range(nseq)]))
         sources.append(jnp.bitwise_xor(my_x, digit) * plane + jnp.arange(used))
     gathered = jnp.concatenate(parts, 0)
-    source_head = jnp.take(jnp.array(head_table, jnp.int32), jnp.concatenate(sources))
+    source_head = head_of(jnp.concatenate(sources))
     w_heads = jnp.pad(w_cols.reshape(HEADS, HD, col_width), ((0, 1), (0, 0), (0, 0)))
     w_ordered = jnp.take(w_heads, source_head, axis=0)
     projected_cols = jnp.einsum(
@@ -178,12 +188,8 @@
     )
     projected_parts = projected_cols.reshape(nseq, shard_rows, col_width)
     received = lax.all_to_all(projected_parts, "seq", 0, 0, tiled=True)
-    by_region = []
-    for region in range(2):
-        owners = [owner_of(region_of, chunk_of, region, c) for c in range(chunks)]
-        picked = jnp.take(received, jnp.array(owners, jnp.int32), axis=0)
-        by_region.append(picked.transpose(1, 0, 2).reshape(shard_rows, D))
-    projected = jnp.stack(by_region)
+    projected = received.reshape(2, 2, 16, shard_rows, col_width).transpose(1, 3, 0, 2, 4)
+    projected = projected.reshape(2, shard_rows, D)
 
     item_count = guide.shape[0]
     indicator_mask = (jnp.arange(item_count)[None, :] == item_ids[:, None]).astype(jnp.float32)

time: 146 us -> 145 us (level)
    gather x5 -> x1, local copies, waits for them, and re-layouts: 3.96 us -> 0.65 us  [shards(): jnp.take(gathered, swap_digits(jnp.bitwise_xor(my_z, jnp.arange(plane))),...]
  transfers between devices with their start and end apart: 14 -> 14, of which waited for: 6 -> 6; matrix products, arithmetic and copies ran while one was open for 8% -> 9% of each run, Pallas kernels for 0% -> 0%
where the time goes in v10:
time: 145 us; the launch traced here: 144 us
  starting transfers between devices  78.7 us (54%)
  waiting for transfers between devices  42.8 us (30%)
  local copies, waits for them, and re-layouts  12.9 us (9%)
  other arithmetic  6.06 us (4%)
  matrix products  2.77 us (2%)
    ppermute x6, starting transfers between devices, shards(): lax.ppermute(gathered, 'seq', [(i, i ^ shift) for i in range(nseq)])  25.5 us
    all_to_all x1, waiting for transfers between devices, shards(): joint = lax.all_to_all(joint, 'seq', 0, 0, tiled=True)  20.6 us
    all_to_all x1, starting transfers between devices, shards(): joint = lax.all_to_all(joint, 'seq', 0, 0, tiled=True)  18.3 us
    ppermute x3, starting transfers between devices, from_partner(): lax.ppermute(x, axis, [(i, i ^ 1 << apart) for i in range(lax.axis_size(a...  14.9 us
    all_to_all x1, waiting for transfers between devices, shards(): received = lax.all_to_all(projected_parts, 'seq', 0, 0, tiled=True)  12.2 us
    ppermute x3, starting transfers between devices, shards(): lax.ppermute(outgoing, 'seq', [(i, i ^ shift) for i in range(nseq)])  11.3 us
    all_to_all x1, starting transfers between devices, shards(): received = lax.all_to_all(projected_parts, 'seq', 0, 0, tiled=True)  8.73 us
    ppermute x3, waiting for transfers between devices, shards(): lax.ppermute(outgoing, 'seq', [(i, i ^ shift) for i in range(nseq)])  4.84 us
  transfers between devices with their start and end apart: 14, of which 6 were waited for; matrix products, arithmetic and copies ran while one was open for 9% of the time, Pallas kernels for 0%

profile of v10, /device:TPU:1, one launch (start us, length us, event | category | flops | bytes accessed | tf_op | source)
XLA Modules:
  0.0 144.1 jit_solution(5640396400487290578)
XLA Ops:
  0.0 0.8 slice_bitcast_fusion.1
  0.8 4.0 %collective-permute-start = (bf16[2,2,2432]{2,1,0:T(2,128)(2,1)S(1)}, bf16[2,2,2432]{2,1,0:T(2,128)(2,1)S(1)}, u32[]{:S(2)}, u32[]{:S(2)}) collective-permute-start(bf16[2,2,2432]{2,1,0:T(2,128)(2,1)S(1)} %pad_maximum_fusion.2), channel_id=1, source_target_pairs={{0,64},{64,0},{128,192},{192,128},{1,65},{65,1},{129,193},{193,129... | collective-permute-start | bytes 58376 | tf_op jit(solution)/shard_map/ppermute | solution.py:15
  4.9 0.8 concatenate.79
  6.0 0.8 concatenate.78
  6.8 0.8 constant_dynamic-slice_fusion.3
  8.7 1.3 iota_compare_fusion.3
  10.6 0.8 concatenate.81
  11.5 1.4 reshape.292
  14.7 0.8 reduce.2
  15.5 1.1 reshape.319
  16.6 18.3 %all-to-all-start = ((bf16[64,2,1234]{2,1,0:T(2,128)(2,1)}), bf16[64,2,1234]{2,1,0:T(2,128)(2,1)S(1)}, u32[]{:S(2)}, u32[]{:S(2)}) async-start(bf16[64,2,1234]{2,1,0:T(2,128)(2,1)} %reshape.319), calls=%async_computation | async-start | bytes 655360 | tf_op jit(solution)/shard_map/all_to_all | solution.py:132
  35.7 20.6 %all-to-all-done = bf16[64,2,1234]{2,1,0:T(2,128)(2,1)S(1)} async-done(((bf16[64,2,1234]{2,1,0:T(2,128)(2,1)}), bf16[64,2,1234]{2,1,0:T(2,128)(2,1)S(1)}, u32[]{:S(2)}, u32[]{:S(2)}) %all-to-all-start) | async-done | bytes 315936 | tf_op jit(solution)/shard_map/all_to_all | solution.py:132
  58.4 4.8 %collective-permute-start.1 = (bf16[1,2,128,64]{2,3,1,0:T(8,128)(2,1)S(1)}, bf16[1,2,128,64]{2,3,1,0:T(8,128)(2,1)S(1)}, u32[]{:S(2)}, u32[]{:S(2)}) collective-permute-start(bf16[1,2,128,64]{2,3,1,0:T(8,128)(2,1)S(1)} %get-tuple-element.20), channel_id=1, source_target_pairs={{0,4},{1,5},{2,6},{3,7},{4,0},{5,1},{6,2},{7,3},{8,12},{9,13},{10,... | collective-permute-start | bytes 98312 | tf_op jit(solution)/shard_map/ppermute | solution.py:165
  63.2 6.9 %collective-permute-start.2 = (bf16[1,2,128,64]{2,3,1,0:T(8,128)(2,1)S(1)}, bf16[1,2,128,64]{2,3,1,0:T(8,128)(2,1)S(1)}, u32[]{:S(2)}, u32[]{:S(2)}) collective-permute-start(bf16[1,2,128,64]{2,3,1,0:T(8,128)(2,1)S(1)} %get-tuple-element.20), channel_id=1, source_target_pairs={{0,8},{1,9},{2,10},{3,11},{4,12},{5,13},{6,14},{7,15},{8,0},{9,1},... | collective-permute-start | bytes 98312 | tf_op jit(solution)/shard_map/ppermute | solution.py:165
  70.1 4.5 %collective-permute-start.3 = (bf16[1,2,128,64]{2,3,1,0:T(8,128)(2,1)S(1)}, bf16[1,2,128,64]{2,3,1,0:T(8,128)(2,1)S(1)}, u32[]{:S(2)}, u32[]{:S(2)}) collective-permute-start(bf16[1,2,128,64]{2,3,1,0:T(8,128)(2,1)S(1)} %get-tuple-element.20), channel_id=1, source_target_pairs={{0,12},{1,13},{2,14},{3,15},{4,8},{5,9},{6,10},{7,11},{8,4},{9,5},... | collective-permute-start | bytes 98312 | tf_op jit(solution)/shard_map/ppermute | solution.py:165
  75.2 6.1 %collective-permute-start.10 = (bf16[1216,76]{1,0:T(8,128)(2,1)S(1)}, bf16[1216,76]{1,0:T(8,128)(2,1)S(1)}, u32[]{:S(2)}, u32[]{:S(2)}) collective-permute-start(bf16[1216,76]{1,0:T(8,128)(2,1)S(1)} %reshape.294), channel_id=1, source_target_pairs={{0,256},{256,0},{1,257},{257,1},{2,258},{258,2},{3,259},{259,3},{4... | collective-permute-start | bytes 554504 | tf_op jit(solution)/shard_map/ppermute | solution.py:15
  81.4 2.5 %collective-permute-start.4 = (bf16[4,2,128,64]{2,3,1,0:T(8,128)(2,1)S(1)}, bf16[4,2,128,64]{2,3,1,0:T(8,128)(2,1)S(1)}, u32[]{:S(2)}, u32[]{:S(2)}) collective-permute-start(bf16[4,2,128,64]{2,3,1,0:T(8,128)(2,1)S(1)} %pad_maximum_fusion), channel_id=1, source_target_pairs={{0,1},{1,0},{2,3},{3,2},{4,5},{5,4},{6,7},{7,6},{8,9},{9,8},{10,11... | collective-permute-start | bytes 393224 | tf_op jit(solution)/shard_map/ppermute | solution.py:165
  83.9 2.7 %collective-permute-start.5 = (bf16[4,2,128,64]{2,3,1,0:T(8,128)(2,1)S(1)}, bf16[4,2,128,64]{2,3,1,0:T(8,128)(2,1)S(1)}, u32[]{:S(2)}, u32[]{:S(2)}) collective-permute-start(bf16[4,2,128,64]{2,3,1,0:T(8,128)(2,1)S(1)} %pad_maximum_fusion), channel_id=1, source_target_pairs={{0,2},{1,3},{2,0},{3,1},{4,6},{5,7},{6,4},{7,5},{8,10},{9,11},{10,... | collective-permute-start | bytes 393224 | tf_op jit(solution)/shard_map/ppermute | solution.py:165
  86.6 4.1 %collective-permute-start.6 = (bf16[4,2,128,64]{2,3,1,0:T(8,128)(2,1)S(1)}, bf16[4,2,128,64]{2,3,1,0:T(8,128)(2,1)S(1)}, u32[]{:S(2)}, u32[]{:S(2)}) collective-permute-start(bf16[4,2,128,64]{2,3,1,0:T(8,128)(2,1)S(1)} %pad_maximum_fusion), channel_id=1, source_target_pairs={{0,3},{1,2},{2,1},{3,0},{4,7},{5,6},{6,5},{7,4},{8,11},{9,10},{10,... | collective-permute-start | bytes 393224 | tf_op jit(solution)/shard_map/ppermute | solution.py:165
  90.8 4.5 %collective-permute-done.5 = bf16[4,2,128,64]{2,3,1,0:T(8,128)(2,1)S(1)} collective-permute-done((bf16[4,2,128,64]{2,3,1,0:T(8,128)(2,1)S(1)}, bf16[4,2,128,64]{2,3,1,0:T(8,128)(2,1)S(1)}, u32[]{:S(2)}, u32[]{:S(2)}) %collective-permute-start.5) | collective-permute-done | bytes 131104 | tf_op jit(solution)/shard_map/ppermute | solution.py:165
  96.2 3.3 %collective-permute-start.7 = (bf16[10,128,64]{1,2,0:T(8,128)(2,1)S(1)}, bf16[10,128,64]{1,2,0:T(8,128)(2,1)S(1)}, u32[]{:S(2)}, u32[]{:S(2)}) collective-permute-start(bf16[10,128,64]{1,2,0:T(8,128)(2,1)S(1)} %get-tuple-element.7), channel_id=1, source_target_pairs={{0,16},{1,17},{2,18},{3,19},{4,20},{5,21},{6,22},{7,23},{8,24},{9,... | collective-permute-start | bytes 491528 | tf_op jit(solution)/shard_map/ppermute | solution.py:180
  99.5 6.1 %collective-permute-start.8 = (bf16[10,128,64]{1,2,0:T(8,128)(2,1)S(1)}, bf16[10,128,64]{1,2,0:T(8,128)(2,1)S(1)}, u32[]{:S(2)}, u32[]{:S(2)}) collective-permute-start(bf16[10,128,64]{1,2,0:T(8,128)(2,1)S(1)} %get-tuple-element.9), channel_id=1, source_target_pairs={{0,32},{1,33},{2,34},{3,35},{4,36},{5,37},{6,38},{7,39},{8,40},{9,... | collective-permute-start | bytes 491528 | tf_op jit(solution)/shard_map/ppermute | solution.py:180
  105.6 1.9 %collective-permute-start.9 = (bf16[10,128,64]{1,2,0:T(8,128)(2,1)S(1)}, bf16[10,128,64]{1,2,0:T(8,128)(2,1)S(1)}, u32[]{:S(2)}, u32[]{:S(2)}) collective-permute-start(bf16[10,128,64]{1,2,0:T(8,128)(2,1)S(1)} %get-tuple-element.8), channel_id=1, source_target_pairs={{0,48},{1,49},{2,50},{3,51},{4,52},{5,53},{6,54},{7,55},{8,56},{9,... | collective-permute-start | bytes 491528 | tf_op jit(solution)/shard_map/ppermute | solution.py:180
  108.0 0.7 gather_fusion.1
  108.7 0.7 collective-permute-done.8
  109.4 4.2 %collective-permute-done.9 = bf16[10,128,64]{1,2,0:T(8,128)(2,1)S(1)} collective-permute-done((bf16[10,128,64]{1,2,0:T(8,128)(2,1)S(1)}, bf16[10,128,64]{1,2,0:T(8,128)(2,1)S(1)}, u32[]{:S(2)}, u32[]{:S(2)}) %collective-permute-start.9) | collective-permute-done | bytes 163872 | tf_op jit(solution)/shard_map/ppermute | solution.py:180
  113.6 1.1 fusion.6
  114.7 8.7 %all-to-all-start.1 = ((f32[64,2,76]{2,1,0:T(2,128)}), f32[64,2,76]{2,1,0:T(2,128)S(1)}, u32[]{:S(2)}, u32[]{:S(2)}) async-start(f32[64,2,76]{2,1,0:T(2,128)} %bitcast.35), calls=%async_computation.1 | async-start | bytes 131072 | tf_op jit(solution)/shard_map/all_to_all | solution.py:190
  123.5 1.2 fusion.47
  124.7 12.2 %all-to-all-done.1 = f32[64,2,76]{2,1,0:T(2,128)S(1)} async-done(((f32[64,2,76]{2,1,0:T(2,128)}), f32[64,2,76]{2,1,0:T(2,128)S(1)}, u32[]{:S(2)}, u32[]{:S(2)}) %all-to-all-start.1) | async-done | bytes 38944 | tf_op jit(solution)/shard_map/all_to_all | solution.py:190
  137.8 4.8 %collective-permute-start.11 = (f32[2,2,32]{2,1,0:T(2,128)S(1)}, f32[2,2,32]{2,1,0:T(2,128)S(1)}, u32[]{:S(2)}, u32[]{:S(2)}) collective-permute-start(f32[2,2,32]{2,1,0:T(2,128)S(1)} %constant_dynamic-slice_fusion.1), channel_id=1, source_target_pairs={{0,256},{256,0},{1,257},{257,1},{2,258},{258,2},{3,259},{259,3},{4... | collective-permute-start | bytes 1544 | tf_op jit(solution)/shard_map/ppermute | solution.py:15
  143.5 0.7 fusion.42
  (102 shorter events, 10.0 us)
Async XLA Ops:
  0.0 137.5 %copy-start = (bf16[2432,64]{0,1:T(8,128)(2,1)S(1)}, bf16[2432,64]{0,1:T(8,128)(2,1)}, u32[]{:S(2)}) copy-start(bf16[2432,64]{0,1:T(8,128)(2,1)} %param.23) | copy-start | bytes 933892
  0.8 12.4 %collective-permute-start = (bf16[2,2,2432]{2,1,0:T(2,128)(2,1)S(1)}, bf16[2,2,2432]{2,1,0:T(2,128)(2,1)S(1)}, u32[]{:S(2)}, u32[]{:S(2)}) collective-permute-start(bf16[2,2,2432]{2,1,0:T(2,128)(2,1)S(1)} %pad_maximum_fusion.2), channel_id=1, source_target_pairs={{0,64},{64,0},{128,192},{192,128},{1,65},{65,1},{129,193},{193,129... | collective-permute-start | bytes 58376 | tf_op jit(solution)/shard_map/ppermute | solution.py:15
  15.5 19.4 %copy-start.5 = (s32[4,2]{0,1:T(2,128)S(1)}, s32[4,2]{0,1:T(2,128)}, u32[]{:S(2)}) copy-start(s32[4,2]{0,1:T(2,128)} %param.18) | copy-start | bytes 100
  15.5 19.6 %copy-start.2 = (f32[1,6,2432]{2,0,1:T(1,128)S(1)}, f32[1,6,2432]{2,0,1:T(1,128)}, u32[]{:S(2)}) copy-start(f32[1,6,2432]{2,0,1:T(1,128)} %param.21) | copy-start | bytes 175108
  15.5 19.8 %copy-start.1 = (f32[1,6,2,2432]{3,2,1,0:T(2,128)S(1)}, f32[1,6,2,2432]{3,2,1,0:T(2,128)}, u32[]{:S(2)}) copy-start(f32[1,6,2,2432]{3,2,1,0:T(2,128)} %param.22) | copy-start | bytes 350212
  16.6 39.6 %all-to-all-start = ((bf16[64,2,1234]{2,1,0:T(2,128)(2,1)}), bf16[64,2,1234]{2,1,0:T(2,128)(2,1)S(1)}, u32[]{:S(2)}, u32[]{:S(2)}) async-start(bf16[64,2,1234]{2,1,0:T(2,128)(2,1)} %reshape.319), calls=%async_computation | async-start | bytes 655360 | tf_op jit(solution)/shard_map/all_to_all | solution.py:132
  58.4 23.0 %collective-permute-start.1 = (bf16[1,2,128,64]{2,3,1,0:T(8,128)(2,1)S(1)}, bf16[1,2,128,64]{2,3,1,0:T(8,128)(2,1)S(1)}, u32[]{:S(2)}, u32[]{:S(2)}) collective-permute-start(bf16[1,2,128,64]{2,3,1,0:T(8,128)(2,1)S(1)} %get-tuple-element.20), channel_id=1, source_target_pairs={{0,4},{1,5},{2,6},{3,7},{4,0},{5,1},{6,2},{7,3},{8,12},{9,13},{10,... | collective-permute-start | bytes 98312 | tf_op jit(solution)/shard_map/ppermute | solution.py:165
  63.2 18.1 %collective-permute-start.2 = (bf16[1,2,128,64]{2,3,1,0:T(8,128)(2,1)S(1)}, bf16[1,2,128,64]{2,3,1,0:T(8,128)(2,1)S(1)}, u32[]{:S(2)}, u32[]{:S(2)}) collective-permute-start(bf16[1,2,128,64]{2,3,1,0:T(8,128)(2,1)S(1)} %get-tuple-element.20), channel_id=1, source_target_pairs={{0,8},{1,9},{2,10},{3,11},{4,12},{5,13},{6,14},{7,15},{8,0},{9,1},... | collective-permute-start | bytes 98312 | tf_op jit(solution)/shard_map/ppermute | solution.py:165
  70.1 11.2 %collective-permute-start.3 = (bf16[1,2,128,64]{2,3,1,0:T(8,128)(2,1)S(1)}, bf16[1,2,128,64]{2,3,1,0:T(8,128)(2,1)S(1)}, u32[]{:S(2)}, u32[]{:S(2)}) collective-permute-start(bf16[1,2,128,64]{2,3,1,0:T(8,128)(2,1)S(1)} %get-tuple-element.20), channel_id=1, source_target_pairs={{0,12},{1,13},{2,14},{3,15},{4,8},{5,9},{6,10},{7,11},{8,4},{9,5},... | collective-permute-start | bytes 98312 | tf_op jit(solution)/shard_map/ppermute | solution.py:165
  75.2 32.3 %collective-permute-start.10 = (bf16[1216,76]{1,0:T(8,128)(2,1)S(1)}, bf16[1216,76]{1,0:T(8,128)(2,1)S(1)}, u32[]{:S(2)}, u32[]{:S(2)}) collective-permute-start(bf16[1216,76]{1,0:T(8,128)(2,1)S(1)} %reshape.294), channel_id=1, source_target_pairs={{0,256},{256,0},{1,257},{257,1},{2,258},{258,2},{3,259},{259,3},{4... | collective-permute-start | bytes 554504 | tf_op jit(solution)/shard_map/ppermute | solution.py:15
  81.4 9.3 %collective-permute-start.4 = (bf16[4,2,128,64]{2,3,1,0:T(8,128)(2,1)S(1)}, bf16[4,2,128,64]{2,3,1,0:T(8,128)(2,1)S(1)}, u32[]{:S(2)}, u32[]{:S(2)}) collective-permute-start(bf16[4,2,128,64]{2,3,1,0:T(8,128)(2,1)S(1)} %pad_maximum_fusion), channel_id=1, source_target_pairs={{0,1},{1,0},{2,3},{3,2},{4,5},{5,4},{6,7},{7,6},{8,9},{9,8},{10,11... | collective-permute-start | bytes 393224 | tf_op jit(solution)/shard_map/ppermute | solution.py:165
  83.9 11.4 %collective-permute-start.5 = (bf16[4,2,128,64]{2,3,1,0:T(8,128)(2,1)S(1)}, bf16[4,2,128,64]{2,3,1,0:T(8,128)(2,1)S(1)}, u32[]{:S(2)}, u32[]{:S(2)}) collective-permute-start(bf16[4,2,128,64]{2,3,1,0:T(8,128)(2,1)S(1)} %pad_maximum_fusion), channel_id=1, source_target_pairs={{0,2},{1,3},{2,0},{3,1},{4,6},{5,7},{6,4},{7,5},{8,10},{9,11},{10,... | collective-permute-start | bytes 393224 | tf_op jit(solution)/shard_map/ppermute | solution.py:165
  86.6 8.7 %collective-permute-start.6 = (bf16[4,2,128,64]{2,3,1,0:T(8,128)(2,1)S(1)}, bf16[4,2,128,64]{2,3,1,0:T(8,128)(2,1)S(1)}, u32[]{:S(2)}, u32[]{:S(2)}) collective-permute-start(bf16[4,2,128,64]{2,3,1,0:T(8,128)(2,1)S(1)} %pad_maximum_fusion), channel_id=1, source_target_pairs={{0,3},{1,2},{2,1},{3,0},{4,7},{5,6},{6,5},{7,4},{8,11},{9,10},{10,... | collective-permute-start | bytes 393224 | tf_op jit(solution)/shard_map/ppermute | solution.py:165
  96.2 12.5 %collective-permute-start.7 = (bf16[10,128,64]{1,2,0:T(8,128)(2,1)S(1)}, bf16[10,128,64]{1,2,0:T(8,128)(2,1)S(1)}, u32[]{:S(2)}, u32[]{:S(2)}) collective-permute-start(bf16[10,128,64]{1,2,0:T(8,128)(2,1)S(1)} %get-tuple-element.7), channel_id=1, source_target_pairs={{0,16},{1,17},{2,18},{3,19},{4,20},{5,21},{6,22},{7,23},{8,24},{9,... | collective-permute-start | bytes 491528 | tf_op jit(solution)/shard_map/ppermute | solution.py:180
  99.5 9.9 %collective-permute-start.8 = (bf16[10,128,64]{1,2,0:T(8,128)(2,1)S(1)}, bf16[10,128,64]{1,2,0:T(8,128)(2,1)S(1)}, u32[]{:S(2)}, u32[]{:S(2)}) collective-permute-start(bf16[10,128,64]{1,2,0:T(8,128)(2,1)S(1)} %get-tuple-element.9), channel_id=1, source_target_pairs={{0,32},{1,33},{2,34},{3,35},{4,36},{5,37},{6,38},{7,39},{8,40},{9,... | collective-permute-start | bytes 491528 | tf_op jit(solution)/shard_map/ppermute | solution.py:180
  105.6 8.0 %collective-permute-start.9 = (bf16[10,128,64]{1,2,0:T(8,128)(2,1)S(1)}, bf16[10,128,64]{1,2,0:T(8,128)(2,1)S(1)}, u32[]{:S(2)}, u32[]{:S(2)}) collective-permute-start(bf16[10,128,64]{1,2,0:T(8,128)(2,1)S(1)} %get-tuple-element.8), channel_id=1, source_target_pairs={{0,48},{1,49},{2,50},{3,51},{4,52},{5,53},{6,54},{7,55},{8,56},{9,... | collective-permute-start | bytes 491528 | tf_op jit(solution)/shard_map/ppermute | solution.py:180
  108.7 28.4 %copy-start.3 = (bf16[1,1,2,2,2432]{4,3,2,1,0:T(2,128)(2,1)S(1)}, bf16[1,1,2,2,2432]{4,3,2,1,0:T(2,128)(2,1)}, u32[]{:S(2)}) copy-start(bf16[1,1,2,2,2432]{4,3,2,1,0:T(2,128)(2,1)} %param.16) | copy-start | bytes 58372
  114.7 27.9 %copy-start.6 = (f32[6]{0:T(128)S(1)}, f32[6]{0:T(128)}, u32[]{:S(2)}) copy-start(f32[6]{0:T(128)} %param.25) | copy-start | bytes 76
  114.7 27.9 %copy-start.7 = (f32[6]{0:T(128)S(1)}, f32[6]{0:T(128)}, u32[]{:S(2)}) copy-start(f32[6]{0:T(128)} %param.24) | copy-start | bytes 76
  114.7 28.7 %copy-start.4 = (f32[1,2,2,32]{3,2,1,0:T(2,128)S(1)}, f32[1,2,2,32]{3,2,1,0:T(2,128)}, u32[]{:S(2)}) copy-start(f32[1,2,2,32]{3,2,1,0:T(2,128)} %param.17) | copy-start | bytes 1540
  114.7 22.3 %all-to-all-start.1 = ((f32[64,2,76]{2,1,0:T(2,128)}), f32[64,2,76]{2,1,0:T(2,128)S(1)}, u32[]{:S(2)}, u32[]{:S(2)}) async-start(f32[64,2,76]{2,1,0:T(2,128)} %bitcast.35), calls=%async_computation.1 | async-start | bytes 131072 | tf_op jit(solution)/shard_map/all_to_all | solution.py:190
  137.8 5.7 %collective-permute-start.11 = (f32[2,2,32]{2,1,0:T(2,128)S(1)}, f32[2,2,32]{2,1,0:T(2,128)S(1)}, u32[]{:S(2)}, u32[]{:S(2)}) collective-permute-start(f32[2,2,32]{2,1,0:T(2,128)S(1)} %constant_dynamic-slice_fusion.1), channel_id=1, source_target_pairs={{0,256},{256,0},{1,257},{257,1},{2,258},{258,2},{3,259},{259,3},{4... | collective-permute-start | bytes 1544 | tf_op jit(solution)/shard_map/ppermute | solution.py:15

commit v11 on v10

--- a/solution.py
+++ b/solution.py
@@ -116,10 +116,9 @@
     chunks = max(chunk_of) + 1
     block_rows = w_out.shape[0]
     col_width = D // chunks
-    w_parts = w_out.reshape(block_rows, chunks, col_width).transpose(1, 0, 2)
-    w_parts = w_parts.reshape(planes // 2, 1, 16, block_rows, col_width)
-    w_parts = jnp.broadcast_to(w_parts, (planes // 2, 2, 16, block_rows, col_width))
-    w_parts = w_parts.reshape(nseq, block_rows, col_width)
+    half_width = col_width // 2
+    w_parts = w_out.reshape(block_rows, planes // 2, 16, 2, half_width).transpose(1, 3, 2, 0, 4)
+    w_parts = w_parts.reshape(nseq, block_rows, half_width)
     packed = to_heads(
         jnp.concatenate(
             [local_query, resident_key_rows, far_keys[None], local_values, far_values[None]], 0
@@ -127,7 +126,7 @@
     )
     head_width = packed.shape[1] * shard_rows * HD
     joint = jnp.concatenate(
-        [packed.reshape(nseq, head_width), w_parts.reshape(nseq, block_rows * col_width)], 1
+        [packed.reshape(nseq, head_width), w_parts.reshape(nseq, block_rows * half_width)], 1
     )
     joint = lax.all_to_all(joint, "seq", 0, 0, tiled=True)
     head_rows = joint[:, :head_width].reshape(nseq, 8, shard_rows, HD)
@@ -146,9 +145,9 @@
     )
     head_attn = jnp.stack([home_out, shared_out]).astype(jnp.bfloat16)
 
-    w_half = joint[:, head_width:].reshape(nseq * block_rows, col_width)
+    w_half = joint[:, head_width:].reshape(nseq * block_rows, half_width)
     w_other = from_partner(w_half, "cfg", 0)
-    w_cols = jnp.where(
+    w_quarter = jnp.where(
         branch == 0,
         jnp.concatenate([w_half, w_other], 0),
         jnp.concatenate([w_other, w_half], 0),
@@ -177,9 +176,23 @@
     for digit in (1, 2, 3):
         shift = digit * plane
         outgoing = lax.dynamic_index_in_dim(by_z[:used], (my_x ^ digit) % 2, 1, keepdims=False)
-        parts.append(lax.ppermute(outgoing, "seq", [(i, i ^ shift) for i in range(nseq)]))
+        pairs = [(i, i ^ shift) for i in range(nseq)]
+        if digit == 1:
+            block_size = outgoing.size
+            both = lax.ppermute(
+                jnp.concatenate([outgoing.reshape(-1), w_quarter.reshape(-1)]), "seq", pairs
+            )
+            parts.append(both[:block_size].reshape(outgoing.shape))
+            w_partner = both[block_size:].reshape(w_quarter.shape)
+        else:
+            parts.append(lax.ppermute(outgoing, "seq", pairs))
         sources.append(jnp.bitwise_xor(my_x, digit) * plane + jnp.arange(used))
     gathered = jnp.concatenate(parts, 0)
+    w_cols = jnp.where(
+        my_region == 0,
+        jnp.concatenate([w_quarter, w_partner], 1),
+        jnp.concatenate([w_partner, w_quarter], 1),
+    )
     source_head = head_of(jnp.concatenate(sources))
     w_heads = jnp.pad(w_cols.reshape(HEADS, HD, col_width), ((0, 1), (0, 0), (0, 0)))
     w_ordered = jnp.take(w_heads, source_head, axis=0)

time: 145 us -> 143 us (0.986)
  waiting for transfers between devices: 42.8 us -> 34.9 us
  local copies, waits for them, and re-layouts: 12.9 us -> 18 us
    all_to_all x1, waiting for transfers between devices: 20.6 us -> 17.4 us  [shards(): joint = lax.all_to_all(joint, 'seq', 0, 0, tiled=True)]
    ppermute x3, waiting for transfers between devices: 4.84 us -> 2.41 us  [the longest x2 2.41 us: shards(): parts.append(lax.ppermute(outgoing, 'seq', pairs))]
    ppermute x6, waiting for transfers between devices: 4.54 us -> 2.25 us  [shards(): lax.ppermute(gathered, 'seq', [(i, i ^ shift) for i in range(nseq)])]
    concatenate x0 -> x1, local copies, waits for them, and re-layouts: none -> 1.65 us  [shards(): jnp.concatenate([w_quarter, w_partner], 1)]
    select_n x0 -> x2, local copies, waits for them, and re-layouts: none -> 1.63 us  [shards(): jnp.where(branch == 0, jnp.concatenate([w_half, w_other], 0), jnp.concate...]
    reshape x2 -> x7, local copies, waits for them, and re-layouts: 1.79 us -> 2.91 us  [the longest x2 1.85 us: shards(): w_out.reshape(block_rows, planes // 2, 16, 2, half_width)]
  transfers between devices with their start and end apart: 14 -> 14, of which waited for: 6 -> 5; matrix products, arithmetic and copies ran while one was open for 9% -> 12% of each run, Pallas kernels for 0% -> 0%
where the time goes in v11:
time: 143 us; the launch traced here: 142 us
  starting transfers between devices  78.3 us (55%)
  waiting for transfers between devices  34.9 us (24%)
  local copies, waits for them, and re-layouts  18 us (13%)
  other arithmetic  6.58 us (5%)
  matrix products  3.7 us (3%)
    ppermute x6, starting transfers between devices, shards(): lax.ppermute(gathered, 'seq', [(i, i ^ shift) for i in range(nseq)])  25.5 us
    all_to_all x1, starting transfers between devices, shards(): joint = lax.all_to_all(joint, 'seq', 0, 0, tiled=True)  18.3 us
    all_to_all x1, waiting for transfers between devices, shards(): joint = lax.all_to_all(joint, 'seq', 0, 0, tiled=True)  17.4 us
    ppermute x3, starting transfers between devices, from_partner(): lax.ppermute(x, axis, [(i, i ^ 1 << apart) for i in range(lax.axis_size(a...  15.7 us
    all_to_all x1, waiting for transfers between devices, shards(): received = lax.all_to_all(projected_parts, 'seq', 0, 0, tiled=True)  12.2 us
    ppermute x2, starting transfers between devices, shards(): parts.append(lax.ppermute(outgoing, 'seq', pairs))  8.36 us
    all_to_all x1, starting transfers between devices, shards(): received = lax.all_to_all(projected_parts, 'seq', 0, 0, tiled=True)  7.37 us
    ppermute x1, starting transfers between devices, shards(): lax.ppermute(jnp.concatenate([outgoing.reshape(-1), w_quarter.reshape(-1)...  3.19 us
  transfers between devices with their start and end apart: 14, of which 5 were waited for; matrix products, arithmetic and copies ran while one was open for 12% of the time, Pallas kernels for 0%

profile of v11, /device:TPU:1, one launch (start us, length us, event | category | flops | bytes accessed | tf_op | source)
XLA Modules:
  0.0 142.4 jit_solution(3917375984329146740)
XLA Ops:
  0.0 0.8 slice_bitcast_fusion.1
  0.8 4.0 %collective-permute-start = (bf16[2,2,2432]{2,1,0:T(2,128)(2,1)S(1)}, bf16[2,2,2432]{2,1,0:T(2,128)(2,1)S(1)}, u32[]{:S(2)}, u32[]{:S(2)}) collective-permute-start(bf16[2,2,2432]{2,1,0:T(2,128)(2,1)S(1)} %pad_maximum_fusion.3), channel_id=1, source_target_pairs={{0,64},{64,0},{128,192},{192,128},{1,65},{65,1},{129,193},{193,129... | collective-permute-start | bytes 58376 | tf_op jit(solution)/shard_map/ppermute | solution.py:15
  4.9 0.8 concatenate.92
  5.8 0.8 concatenate.91
  6.7 0.8 constant_dynamic-slice_fusion.4
  9.4 1.3 iota_compare_fusion.3
  10.7 0.8 concatenate.94
  11.6 0.9 fusion.44
  12.4 1.6 %reshape.309 = bf16[19,2,16,2,38]{4,3,2,1,0:T(2,128)(2,1)S(1)} reshape(bf16[19,2432]{1,0:T(8,128)(2,1)} %param.20) | data formatting | bytes 184832 | tf_op jit(solution)/shard_map/reshape | solution.py:120
  16.0 0.7 reduce.2
  16.7 0.9 reshape.338
  17.6 18.3 %all-to-all-start = ((bf16[64,2,873]{2,1,0:T(2,128)(2,1)}), bf16[64,2,873]{2,1,0:T(2,128)(2,1)S(1)}, u32[]{:S(2)}, u32[]{:S(2)}) async-start(bf16[64,2,873]{2,1,0:T(2,128)(2,1)} %reshape.338), calls=%async_computation | async-start | bytes 458752 | tf_op jit(solution)/shard_map/all_to_all | solution.py:131
  36.2 17.4 %all-to-all-done = bf16[64,2,873]{2,1,0:T(2,128)(2,1)S(1)} async-done(((bf16[64,2,873]{2,1,0:T(2,128)(2,1)}), bf16[64,2,873]{2,1,0:T(2,128)(2,1)S(1)}, u32[]{:S(2)}, u32[]{:S(2)}) %all-to-all-start) | async-done | bytes 223520 | tf_op jit(solution)/shard_map/all_to_all | solution.py:131
  55.5 4.0 %collective-permute-start.1 = (bf16[1,2,128,64]{2,3,1,0:T(8,128)(2,1)S(1)}, bf16[1,2,128,64]{2,3,1,0:T(8,128)(2,1)S(1)}, u32[]{:S(2)}, u32[]{:S(2)}) collective-permute-start(bf16[1,2,128,64]{2,3,1,0:T(8,128)(2,1)S(1)} %get-tuple-element.20), channel_id=1, source_target_pairs={{0,4},{1,5},{2,6},{3,7},{4,0},{5,1},{6,2},{7,3},{8,12},{9,13},{10,... | collective-permute-start | bytes 98312 | tf_op jit(solution)/shard_map/ppermute | solution.py:164
  59.6 6.9 %collective-permute-start.2 = (bf16[1,2,128,64]{2,3,1,0:T(8,128)(2,1)S(1)}, bf16[1,2,128,64]{2,3,1,0:T(8,128)(2,1)S(1)}, u32[]{:S(2)}, u32[]{:S(2)}) collective-permute-start(bf16[1,2,128,64]{2,3,1,0:T(8,128)(2,1)S(1)} %get-tuple-element.20), channel_id=1, source_target_pairs={{0,8},{1,9},{2,10},{3,11},{4,12},{5,13},{6,14},{7,15},{8,0},{9,1},... | collective-permute-start | bytes 98312 | tf_op jit(solution)/shard_map/ppermute | solution.py:164
  66.5 5.3 %collective-permute-start.3 = (bf16[1,2,128,64]{2,3,1,0:T(8,128)(2,1)S(1)}, bf16[1,2,128,64]{2,3,1,0:T(8,128)(2,1)S(1)}, u32[]{:S(2)}, u32[]{:S(2)}) collective-permute-start(bf16[1,2,128,64]{2,3,1,0:T(8,128)(2,1)S(1)} %get-tuple-element.20), channel_id=1, source_target_pairs={{0,12},{1,13},{2,14},{3,15},{4,8},{5,9},{6,10},{7,11},{8,4},{9,5},... | collective-permute-start | bytes 98312 | tf_op jit(solution)/shard_map/ppermute | solution.py:164
  72.2 5.6 %collective-permute-start.7 = (bf16[1216,38]{1,0:T(8,128)(2,1)S(1)}, bf16[1216,38]{1,0:T(8,128)(2,1)S(1)}, u32[]{:S(2)}, u32[]{:S(2)}) collective-permute-start(bf16[1216,38]{1,0:T(8,128)(2,1)S(1)} %reshape.312), channel_id=1, source_target_pairs={{0,256},{256,0},{1,257},{257,1},{2,258},{258,2},{3,259},{259,3},{4... | collective-permute-start | bytes 277256 | tf_op jit(solution)/shard_map/ppermute | solution.py:15
  78.0 2.6 %collective-permute-start.4 = (bf16[4,2,128,64]{2,3,1,0:T(8,128)(2,1)S(1)}, bf16[4,2,128,64]{2,3,1,0:T(8,128)(2,1)S(1)}, u32[]{:S(2)}, u32[]{:S(2)}) collective-permute-start(bf16[4,2,128,64]{2,3,1,0:T(8,128)(2,1)S(1)} %pad_maximum_fusion.1), channel_id=1, source_target_pairs={{0,1},{1,0},{2,3},{3,2},{4,5},{5,4},{6,7},{7,6},{8,9},{9,8},{10,11... | collective-permute-start | bytes 393224 | tf_op jit(solution)/shard_map/ppermute | solution.py:164
  80.6 3.0 %collective-permute-start.5 = (bf16[4,2,128,64]{2,3,1,0:T(8,128)(2,1)S(1)}, bf16[4,2,128,64]{2,3,1,0:T(8,128)(2,1)S(1)}, u32[]{:S(2)}, u32[]{:S(2)}) collective-permute-start(bf16[4,2,128,64]{2,3,1,0:T(8,128)(2,1)S(1)} %pad_maximum_fusion.1), channel_id=1, source_target_pairs={{0,2},{1,3},{2,0},{3,1},{4,6},{5,7},{6,4},{7,5},{8,10},{9,11},{10,... | collective-permute-start | bytes 393224 | tf_op jit(solution)/shard_map/ppermute | solution.py:164
  83.6 3.7 %collective-permute-start.6 = (bf16[4,2,128,64]{2,3,1,0:T(8,128)(2,1)S(1)}, bf16[4,2,128,64]{2,3,1,0:T(8,128)(2,1)S(1)}, u32[]{:S(2)}, u32[]{:S(2)}) collective-permute-start(bf16[4,2,128,64]{2,3,1,0:T(8,128)(2,1)S(1)} %pad_maximum_fusion.1), channel_id=1, source_target_pairs={{0,3},{1,2},{2,1},{3,0},{4,7},{5,6},{6,5},{7,4},{8,11},{9,10},{10,... | collective-permute-start | bytes 393224 | tf_op jit(solution)/shard_map/ppermute | solution.py:164
  88.1 1.2 select_n.175
  89.4 2.2 %collective-permute-done.6 = bf16[4,2,128,64]{2,3,1,0:T(8,128)(2,1)S(1)} collective-permute-done((bf16[4,2,128,64]{2,3,1,0:T(8,128)(2,1)S(1)}, bf16[4,2,128,64]{2,3,1,0:T(8,128)(2,1)S(1)}, u32[]{:S(2)}, u32[]{:S(2)}) %collective-permute-start.6) | collective-permute-done | bytes 131104 | tf_op jit(solution)/shard_map/ppermute | solution.py:164
  93.0 3.2 %collective-permute-start.8 = (bf16[174336]{0:T(1024)(128)(2,1)S(1)}, bf16[174336]{0:T(1024)(128)(2,1)S(1)}, u32[]{:S(2)}, u32[]{:S(2)}) collective-permute-start(bf16[174336]{0:T(1024)(128)(2,1)S(1)} %pad_maximum_fusion), channel_id=1, source_target_pairs={{0,16},{1,17},{2,18},{3,19},{4,20},{5,21},{6,22},{7,23},{8,24},{9,... | collective-permute-start | bytes 1046024 | tf_op jit(solution)/shard_map/ppermute | solution.py:182
  96.6 5.3 %collective-permute-start.10 = (bf16[10,128,64]{1,2,0:T(8,128)(2,1)S(1)}, bf16[10,128,64]{1,2,0:T(8,128)(2,1)S(1)}, u32[]{:S(2)}, u32[]{:S(2)}) collective-permute-start(bf16[10,128,64]{1,2,0:T(8,128)(2,1)S(1)} %get-tuple-element.8), channel_id=1, source_target_pairs={{0,48},{1,49},{2,50},{3,51},{4,52},{5,53},{6,54},{7,55},{8,56},{9,... | collective-permute-start | bytes 491528 | tf_op jit(solution)/shard_map/ppermute | solution.py:188
  101.9 3.1 %collective-permute-start.9 = (bf16[10,128,64]{1,2,0:T(8,128)(2,1)S(1)}, bf16[10,128,64]{1,2,0:T(8,128)(2,1)}, u32[]{:S(2)}, u32[]{:S(2)}) collective-permute-start(bf16[10,128,64]{1,2,0:T(8,128)(2,1)S(1)} %get-tuple-element.9), channel_id=1, source_target_pairs={{0,32},{1,33},{2,34},{3,35},{4,36},{5,37},{6,38},{7,39},{8,40},{9,... | collective-permute-start | bytes 491528 | tf_op jit(solution)/shard_map/ppermute | solution.py:188
  105.4 1.6 %concatenate.108 = bf16[38,64,38]{2,1,0:T(8,128)(2,1)S(1)} reshape(bf16[92416]{0:T(1024)(128)(2,1)S(1)} %slice.133) | data formatting | bytes 369664 | tf_op jit(solution)/shard_map/concatenate | solution.py:193
  108.6 2.4 %collective-permute-done.9 = bf16[10,128,64]{1,2,0:T(8,128)(2,1)} collective-permute-done((bf16[10,128,64]{1,2,0:T(8,128)(2,1)S(1)}, bf16[10,128,64]{1,2,0:T(8,128)(2,1)}, u32[]{:S(2)}, u32[]{:S(2)}) %collective-permute-start.9) | collective-permute-done | bytes 163872 | tf_op jit(solution)/shard_map/ppermute | solution.py:188
  111.0 2.1 %fusion.6 = f32[128,76,1]{1,0,2:T(8,128)} fusion(bf16[10,128,64]{1,2,0:T(8,128)(2,1)S(1)} %collective-permute-done.10, bf16[10,128,64]{1,2,0:T(8,128)(2,1)} %collective-permute-done.9, bf16[10,128,64]{1,2,0:T(8,128)(2,1)S(1)} %copy.49, bf16[16,128,64]{1,2,0:T(8,128)(2,1)S(1)} %dynamic-slice_bitcast_fusion, bf16[46,64,76]{2,1,0:T(8,128)(2,1)S(1)} %gather_fusion.1, ...), kind=kOutput, calls=%fused_computation.13 | convolution fusion | flops 58632704 | bytes 1240110 | tf_op jit(solution)/shard_map/isd,idc->sc/dot_general | solution.py:199
  113.1 7.4 %all-to-all-start.1 = ((f32[64,2,76]{2,1,0:T(2,128)}), f32[64,2,76]{2,1,0:T(2,128)S(1)}, u32[]{:S(2)}, u32[]{:S(2)}) async-start(f32[64,2,76]{2,1,0:T(2,128)} %bitcast.33), calls=%async_computation.1 | async-start | bytes 131072 | tf_op jit(solution)/shard_map/all_to_all | solution.py:203
  120.5 1.3 fusion.47
  121.8 12.2 %all-to-all-done.1 = f32[64,2,76]{2,1,0:T(2,128)S(1)} async-done(((f32[64,2,76]{2,1,0:T(2,128)}), f32[64,2,76]{2,1,0:T(2,128)S(1)}, u32[]{:S(2)}, u32[]{:S(2)}) %all-to-all-start.1) | async-done | bytes 38944 | tf_op jit(solution)/shard_map/all_to_all | solution.py:203
  134.8 6.1 %collective-permute-start.11 = (f32[2,2,32]{2,1,0:T(2,128)S(1)}, f32[2,2,32]{2,1,0:T(2,128)S(1)}, u32[]{:S(2)}, u32[]{:S(2)}) collective-permute-start(f32[2,2,32]{2,1,0:T(2,128)S(1)} %constant_dynamic-slice_fusion.1), channel_id=1, source_target_pairs={{0,256},{256,0},{1,257},{257,1},{2,258},{258,2},{3,259},{259,3},{4... | collective-permute-start | bytes 1544 | tf_op jit(solution)/shard_map/ppermute | solution.py:15
  (112 shorter events, 13.1 us)
Async XLA Ops:
  0.0 134.5 %copy-start = (bf16[2432,64]{0,1:T(8,128)(2,1)S(1)}, bf16[2432,64]{0,1:T(8,128)(2,1)}, u32[]{:S(2)}) copy-start(bf16[2432,64]{0,1:T(8,128)(2,1)} %param.23) | copy-start | bytes 933892
  0.8 13.7 %collective-permute-start = (bf16[2,2,2432]{2,1,0:T(2,128)(2,1)S(1)}, bf16[2,2,2432]{2,1,0:T(2,128)(2,1)S(1)}, u32[]{:S(2)}, u32[]{:S(2)}) collective-permute-start(bf16[2,2,2432]{2,1,0:T(2,128)(2,1)S(1)} %pad_maximum_fusion.3), channel_id=1, source_target_pairs={{0,64},{64,0},{128,192},{192,128},{1,65},{65,1},{129,193},{193,129... | collective-permute-start | bytes 58376 | tf_op jit(solution)/shard_map/ppermute | solution.py:15
  15.5 20.4 %copy-start.1 = (f32[1,6,2,2432]{3,2,1,0:T(2,128)S(1)}, f32[1,6,2,2432]{3,2,1,0:T(2,128)}, u32[]{:S(2)}) copy-start(f32[1,6,2,2432]{3,2,1,0:T(2,128)} %param.22) | copy-start | bytes 350212
  17.6 36.0 %all-to-all-start = ((bf16[64,2,873]{2,1,0:T(2,128)(2,1)}), bf16[64,2,873]{2,1,0:T(2,128)(2,1)S(1)}, u32[]{:S(2)}, u32[]{:S(2)}) async-start(bf16[64,2,873]{2,1,0:T(2,128)(2,1)} %reshape.338), calls=%async_computation | async-start | bytes 458752 | tf_op jit(solution)/shard_map/all_to_all | solution.py:131
  55.5 22.5 %collective-permute-start.1 = (bf16[1,2,128,64]{2,3,1,0:T(8,128)(2,1)S(1)}, bf16[1,2,128,64]{2,3,1,0:T(8,128)(2,1)S(1)}, u32[]{:S(2)}, u32[]{:S(2)}) collective-permute-start(bf16[1,2,128,64]{2,3,1,0:T(8,128)(2,1)S(1)} %get-tuple-element.20), channel_id=1, source_target_pairs={{0,4},{1,5},{2,6},{3,7},{4,0},{5,1},{6,2},{7,3},{8,12},{9,13},{10,... | collective-permute-start | bytes 98312 | tf_op jit(solution)/shard_map/ppermute | solution.py:164
  59.6 18.4 %collective-permute-start.2 = (bf16[1,2,128,64]{2,3,1,0:T(8,128)(2,1)S(1)}, bf16[1,2,128,64]{2,3,1,0:T(8,128)(2,1)S(1)}, u32[]{:S(2)}, u32[]{:S(2)}) collective-permute-start(bf16[1,2,128,64]{2,3,1,0:T(8,128)(2,1)S(1)} %get-tuple-element.20), channel_id=1, source_target_pairs={{0,8},{1,9},{2,10},{3,11},{4,12},{5,13},{6,14},{7,15},{8,0},{9,1},... | collective-permute-start | bytes 98312 | tf_op jit(solution)/shard_map/ppermute | solution.py:164
  66.5 11.5 %collective-permute-start.3 = (bf16[1,2,128,64]{2,3,1,0:T(8,128)(2,1)S(1)}, bf16[1,2,128,64]{2,3,1,0:T(8,128)(2,1)S(1)}, u32[]{:S(2)}, u32[]{:S(2)}) collective-permute-start(bf16[1,2,128,64]{2,3,1,0:T(8,128)(2,1)S(1)} %get-tuple-element.20), channel_id=1, source_target_pairs={{0,12},{1,13},{2,14},{3,15},{4,8},{5,9},{6,10},{7,11},{8,4},{9,5},... | collective-permute-start | bytes 98312 | tf_op jit(solution)/shard_map/ppermute | solution.py:164
  72.2 15.2 %collective-permute-start.7 = (bf16[1216,38]{1,0:T(8,128)(2,1)S(1)}, bf16[1216,38]{1,0:T(8,128)(2,1)S(1)}, u32[]{:S(2)}, u32[]{:S(2)}) collective-permute-start(bf16[1216,38]{1,0:T(8,128)(2,1)S(1)} %reshape.312), channel_id=1, source_target_pairs={{0,256},{256,0},{1,257},{257,1},{2,258},{258,2},{3,259},{259,3},{4... | collective-permute-start | bytes 277256 | tf_op jit(solution)/shard_map/ppermute | solution.py:15
  78.0 11.3 %collective-permute-start.4 = (bf16[4,2,128,64]{2,3,1,0:T(8,128)(2,1)S(1)}, bf16[4,2,128,64]{2,3,1,0:T(8,128)(2,1)S(1)}, u32[]{:S(2)}, u32[]{:S(2)}) collective-permute-start(bf16[4,2,128,64]{2,3,1,0:T(8,128)(2,1)S(1)} %pad_maximum_fusion.1), channel_id=1, source_target_pairs={{0,1},{1,0},{2,3},{3,2},{4,5},{5,4},{6,7},{7,6},{8,9},{9,8},{10,11... | collective-permute-start | bytes 393224 | tf_op jit(solution)/shard_map/ppermute | solution.py:164
  80.6 8.8 %collective-permute-start.5 = (bf16[4,2,128,64]{2,3,1,0:T(8,128)(2,1)S(1)}, bf16[4,2,128,64]{2,3,1,0:T(8,128)(2,1)S(1)}, u32[]{:S(2)}, u32[]{:S(2)}) collective-permute-start(bf16[4,2,128,64]{2,3,1,0:T(8,128)(2,1)S(1)} %pad_maximum_fusion.1), channel_id=1, source_target_pairs={{0,2},{1,3},{2,0},{3,1},{4,6},{5,7},{6,4},{7,5},{8,10},{9,11},{10,... | collective-permute-start | bytes 393224 | tf_op jit(solution)/shard_map/ppermute | solution.py:164
  83.6 8.1 %collective-permute-start.6 = (bf16[4,2,128,64]{2,3,1,0:T(8,128)(2,1)S(1)}, bf16[4,2,128,64]{2,3,1,0:T(8,128)(2,1)S(1)}, u32[]{:S(2)}, u32[]{:S(2)}) collective-permute-start(bf16[4,2,128,64]{2,3,1,0:T(8,128)(2,1)S(1)} %pad_maximum_fusion.1), channel_id=1, source_target_pairs={{0,3},{1,2},{2,1},{3,0},{4,7},{5,6},{6,5},{7,4},{8,11},{9,10},{10,... | collective-permute-start | bytes 393224 | tf_op jit(solution)/shard_map/ppermute | solution.py:164
  92.6 3.8 %copy-start.2 = (f32[1,6,2432]{2,0,1:T(1,128)S(1)}, f32[1,6,2432]{2,0,1:T(1,128)}, u32[]{:S(2)}) copy-start(f32[1,6,2432]{2,0,1:T(1,128)} %param.21) | copy-start | bytes 175108
  93.0 12.0 %collective-permute-start.8 = (bf16[174336]{0:T(1024)(128)(2,1)S(1)}, bf16[174336]{0:T(1024)(128)(2,1)S(1)}, u32[]{:S(2)}, u32[]{:S(2)}) collective-permute-start(bf16[174336]{0:T(1024)(128)(2,1)S(1)} %pad_maximum_fusion), channel_id=1, source_target_pairs={{0,16},{1,17},{2,18},{3,19},{4,20},{5,21},{6,22},{7,23},{8,24},{9,... | collective-permute-start | bytes 1046024 | tf_op jit(solution)/shard_map/ppermute | solution.py:182
  96.6 12.1 %collective-permute-start.10 = (bf16[10,128,64]{1,2,0:T(8,128)(2,1)S(1)}, bf16[10,128,64]{1,2,0:T(8,128)(2,1)S(1)}, u32[]{:S(2)}, u32[]{:S(2)}) collective-permute-start(bf16[10,128,64]{1,2,0:T(8,128)(2,1)S(1)} %get-tuple-element.8), channel_id=1, source_target_pairs={{0,48},{1,49},{2,50},{3,51},{4,52},{5,53},{6,54},{7,55},{8,56},{9,... | collective-permute-start | bytes 491528 | tf_op jit(solution)/shard_map/ppermute | solution.py:188
  101.9 9.2 %collective-permute-start.9 = (bf16[10,128,64]{1,2,0:T(8,128)(2,1)S(1)}, bf16[10,128,64]{1,2,0:T(8,128)(2,1)}, u32[]{:S(2)}, u32[]{:S(2)}) collective-permute-start(bf16[10,128,64]{1,2,0:T(8,128)(2,1)S(1)} %get-tuple-element.9), channel_id=1, source_target_pairs={{0,32},{1,33},{2,34},{3,35},{4,36},{5,37},{6,38},{7,39},{8,40},{9,... | collective-permute-start | bytes 491528 | tf_op jit(solution)/shard_map/ppermute | solution.py:188
  108.6 25.6 %copy-start.3 = (bf16[1,1,2,2,2432]{4,3,2,1,0:T(2,128)(2,1)S(1)}, bf16[1,1,2,2,2432]{4,3,2,1,0:T(2,128)(2,1)}, u32[]{:S(2)}) copy-start(bf16[1,1,2,2,2432]{4,3,2,1,0:T(2,128)(2,1)} %param.16) | copy-start | bytes 58372
  113.1 27.8 %copy-start.5 = (f32[6]{0:T(128)S(1)}, f32[6]{0:T(128)}, u32[]{:S(2)}) copy-start(f32[6]{0:T(128)} %param.25) | copy-start | bytes 76
  113.1 27.8 %copy-start.6 = (f32[6]{0:T(128)S(1)}, f32[6]{0:T(128)}, u32[]{:S(2)}) copy-start(f32[6]{0:T(128)} %param.24) | copy-start | bytes 76
  113.1 28.6 %copy-start.4 = (f32[1,2,2,32]{3,2,1,0:T(2,128)S(1)}, f32[1,2,2,32]{3,2,1,0:T(2,128)}, u32[]{:S(2)}) copy-start(f32[1,2,2,32]{3,2,1,0:T(2,128)} %param.17) | copy-start | bytes 1540
  113.1 20.9 %all-to-all-start.1 = ((f32[64,2,76]{2,1,0:T(2,128)}), f32[64,2,76]{2,1,0:T(2,128)S(1)}, u32[]{:S(2)}, u32[]{:S(2)}) async-start(f32[64,2,76]{2,1,0:T(2,128)} %bitcast.33), calls=%async_computation.1 | async-start | bytes 131072 | tf_op jit(solution)/shard_map/all_to_all | solution.py:203
  134.8 6.9 %collective-permute-start.11 = (f32[2,2,32]{2,1,0:T(2,128)S(1)}, f32[2,2,32]{2,1,0:T(2,128)S(1)}, u32[]{:S(2)}, u32[]{:S(2)}) collective-permute-start(f32[2,2,32]{2,1,0:T(2,128)S(1)} %constant_dynamic-slice_fusion.1), channel_id=1, source_target_pairs={{0,256},{256,0},{1,257},{257,1},{2,258},{258,2},{3,259},{259,3},{4... | collective-permute-start | bytes 1544 | tf_op jit(solution)/shard_map/ppermute | solution.py:15

commit v12 on v11

--- a/solution.py
+++ b/solution.py
@@ -132,16 +132,17 @@
     head_rows = joint[:, :head_width].reshape(nseq, 8, shard_rows, HD)
     head_rows = head_rows.transpose(1, 0, 2, 3).reshape(8, slot_total, HD)
     head_q, head_k, head_v = head_rows[0:2], head_rows[2:5], head_rows[5:8]
-    slot_ids = jnp.arange(slot_total)
-    live_home = slot_ids < own_lengths[0]
-    live_own = slot_ids < own_lengths[1]
-    live_pair = slot_ids < pair_lengths[1]
+    key_ids = jnp.arange(2 * slot_total)
+    live_home = key_ids[:slot_total] < own_lengths[0]
+    live_shared = key_ids < jnp.where(
+        key_ids < slot_total, own_lengths[1], slot_total + pair_lengths[1]
+    )
     home_out = head_attend(head_q[0], head_k[0], head_v[0], live_home)
     shared_out = head_attend(
         head_q[1],
-        jnp.concatenate([head_k[1], head_k[2]], 0),
-        jnp.concatenate([head_v[1], head_v[2]], 0),
-        jnp.concatenate([live_own, live_pair], 0),
+        head_k[1:3].reshape(2 * slot_total, HD),
+        head_v[1:3].reshape(2 * slot_total, HD),
+        live_shared,
     )
     head_attn = jnp.stack([home_out, shared_out]).astype(jnp.bfloat16)
 

time: 143 us -> 143 us (level)
  no operation moved by 1% of the time
where the time goes in v12:
time: 143 us; the launch traced here: 142 us
  starting transfers between devices  78.3 us (55%)
  waiting for transfers between devices  34.5 us (24%)
  local copies, waits for them, and re-layouts  17.3 us (12%)
  other arithmetic  5.92 us (4%)
  matrix products  4.62 us (3%)
  between operations  1.54 us (1%)
    ppermute x6, starting transfers between devices, shards(): lax.ppermute(gathered, 'seq', [(i, i ^ shift) for i in range(nseq)])  25.5 us
    all_to_all x1, starting transfers between devices, shards(): joint = lax.all_to_all(joint, 'seq', 0, 0, tiled=True)  18.3 us
    all_to_all x1, waiting for transfers between devices, shards(): joint = lax.all_to_all(joint, 'seq', 0, 0, tiled=True)  17 us
    ppermute x3, starting transfers between devices, from_partner(): lax.ppermute(x, axis, [(i, i ^ 1 << apart) for i in range(lax.axis_size(a...  15.6 us
    all_to_all x1, waiting for transfers between devices, shards(): received = lax.all_to_all(projected_parts, 'seq', 0, 0, tiled=True)  12.2 us
    ppermute x2, starting transfers between devices, shards(): parts.append(lax.ppermute(outgoing, 'seq', pairs))  8.36 us
    all_to_all x1, starting transfers between devices, shards(): received = lax.all_to_all(projected_parts, 'seq', 0, 0, tiled=True)  7.37 us
    ppermute x1, starting transfers between devices, shards(): lax.ppermute(jnp.concatenate([outgoing.reshape(-1), w_quarter.reshape(-1)...  3.19 us
  transfers between devices with their start and end apart: 14, of which 5 were waited for; matrix products, arithmetic and copies ran while one was open for 12% of the time, Pallas kernels for 0%

profile of v12, /device:TPU:1, one launch (start us, length us, event | category | flops | bytes accessed | tf_op | source)
XLA Modules:
  0.0 142.2 jit_solution(972290637705086508)
XLA Ops:
  0.0 0.8 slice_bitcast_fusion.1
  0.8 4.0 %collective-permute-start = (bf16[2,2,2432]{2,1,0:T(2,128)(2,1)S(1)}, bf16[2,2,2432]{2,1,0:T(2,128)(2,1)S(1)}, u32[]{:S(2)}, u32[]{:S(2)}) collective-permute-start(bf16[2,2,2432]{2,1,0:T(2,128)(2,1)S(1)} %pad_maximum_fusion.3), channel_id=1, source_target_pairs={{0,64},{64,0},{128,192},{192,128},{1,65},{65,1},{129,193},{193,129... | collective-permute-start | bytes 58376 | tf_op jit(solution)/shard_map/ppermute | solution.py:15
  4.9 0.8 concatenate.83
  5.8 0.8 concatenate.82
  6.7 0.9 fusion.39
  7.6 0.8 constant_dynamic-slice_fusion.4
  9.6 1.2 fusion.18
  12.1 0.8 concatenate.85
  12.9 0.8 reshape.316
  15.7 0.7 reduce.2
  16.4 0.9 reshape.347
  17.3 18.3 %all-to-all-start = ((bf16[64,2,873]{2,1,0:T(2,128)(2,1)}), bf16[64,2,873]{2,1,0:T(2,128)(2,1)S(1)}, u32[]{:S(2)}, u32[]{:S(2)}) async-start(bf16[64,2,873]{2,1,0:T(2,128)(2,1)} %reshape.347), calls=%async_computation | async-start | bytes 458752 | tf_op jit(solution)/shard_map/all_to_all | solution.py:131
  36.3 17.0 %all-to-all-done = bf16[64,2,873]{2,1,0:T(2,128)(2,1)S(1)} async-done(((bf16[64,2,873]{2,1,0:T(2,128)(2,1)}), bf16[64,2,873]{2,1,0:T(2,128)(2,1)S(1)}, u32[]{:S(2)}, u32[]{:S(2)}) %all-to-all-start) | async-done | bytes 223520 | tf_op jit(solution)/shard_map/all_to_all | solution.py:131
  55.4 4.0 %collective-permute-start.1 = (bf16[1,2,128,64]{2,3,1,0:T(8,128)(2,1)S(1)}, bf16[1,2,128,64]{2,3,1,0:T(8,128)(2,1)S(1)}, u32[]{:S(2)}, u32[]{:S(2)}) collective-permute-start(bf16[1,2,128,64]{2,3,1,0:T(8,128)(2,1)S(1)} %get-tuple-element.18), channel_id=1, source_target_pairs={{0,4},{1,5},{2,6},{3,7},{4,0},{5,1},{6,2},{7,3},{8,12},{9,13},{10,... | collective-permute-start | bytes 98312 | tf_op jit(solution)/shard_map/ppermute | solution.py:165
  59.5 6.9 %collective-permute-start.2 = (bf16[1,2,128,64]{2,3,1,0:T(8,128)(2,1)S(1)}, bf16[1,2,128,64]{2,3,1,0:T(8,128)(2,1)S(1)}, u32[]{:S(2)}, u32[]{:S(2)}) collective-permute-start(bf16[1,2,128,64]{2,3,1,0:T(8,128)(2,1)S(1)} %get-tuple-element.18), channel_id=1, source_target_pairs={{0,8},{1,9},{2,10},{3,11},{4,12},{5,13},{6,14},{7,15},{8,0},{9,1},... | collective-permute-start | bytes 98312 | tf_op jit(solution)/shard_map/ppermute | solution.py:165
  66.4 5.3 %collective-permute-start.3 = (bf16[1,2,128,64]{2,3,1,0:T(8,128)(2,1)S(1)}, bf16[1,2,128,64]{2,3,1,0:T(8,128)(2,1)S(1)}, u32[]{:S(2)}, u32[]{:S(2)}) collective-permute-start(bf16[1,2,128,64]{2,3,1,0:T(8,128)(2,1)S(1)} %get-tuple-element.18), channel_id=1, source_target_pairs={{0,12},{1,13},{2,14},{3,15},{4,8},{5,9},{6,10},{7,11},{8,4},{9,5},... | collective-permute-start | bytes 98312 | tf_op jit(solution)/shard_map/ppermute | solution.py:165
  72.1 5.6 %collective-permute-start.7 = (bf16[1216,38]{1,0:T(8,128)(2,1)S(1)}, bf16[1216,38]{1,0:T(8,128)(2,1)S(1)}, u32[]{:S(2)}, u32[]{:S(2)}) collective-permute-start(bf16[1216,38]{1,0:T(8,128)(2,1)S(1)} %reshape.321), channel_id=1, source_target_pairs={{0,256},{256,0},{1,257},{257,1},{2,258},{258,2},{3,259},{259,3},{4... | collective-permute-start | bytes 277256 | tf_op jit(solution)/shard_map/ppermute | solution.py:15
  77.9 2.6 %collective-permute-start.4 = (bf16[4,2,128,64]{2,3,1,0:T(8,128)(2,1)S(1)}, bf16[4,2,128,64]{2,3,1,0:T(8,128)(2,1)S(1)}, u32[]{:S(2)}, u32[]{:S(2)}) collective-permute-start(bf16[4,2,128,64]{2,3,1,0:T(8,128)(2,1)S(1)} %pad_maximum_fusion.1), channel_id=1, source_target_pairs={{0,1},{1,0},{2,3},{3,2},{4,5},{5,4},{6,7},{7,6},{8,9},{9,8},{10,11... | collective-permute-start | bytes 393224 | tf_op jit(solution)/shard_map/ppermute | solution.py:165
  80.5 3.0 %collective-permute-start.5 = (bf16[4,2,128,64]{2,3,1,0:T(8,128)(2,1)S(1)}, bf16[4,2,128,64]{2,3,1,0:T(8,128)(2,1)S(1)}, u32[]{:S(2)}, u32[]{:S(2)}) collective-permute-start(bf16[4,2,128,64]{2,3,1,0:T(8,128)(2,1)S(1)} %pad_maximum_fusion.1), channel_id=1, source_target_pairs={{0,2},{1,3},{2,0},{3,1},{4,6},{5,7},{6,4},{7,5},{8,10},{9,11},{10,... | collective-permute-start | bytes 393224 | tf_op jit(solution)/shard_map/ppermute | solution.py:165
  83.5 3.7 %collective-permute-start.6 = (bf16[4,2,128,64]{2,3,1,0:T(8,128)(2,1)S(1)}, bf16[4,2,128,64]{2,3,1,0:T(8,128)(2,1)S(1)}, u32[]{:S(2)}, u32[]{:S(2)}) collective-permute-start(bf16[4,2,128,64]{2,3,1,0:T(8,128)(2,1)S(1)} %pad_maximum_fusion.1), channel_id=1, source_target_pairs={{0,3},{1,2},{2,1},{3,0},{4,7},{5,6},{6,5},{7,4},{8,11},{9,10},{10,... | collective-permute-start | bytes 393224 | tf_op jit(solution)/shard_map/ppermute | solution.py:165
  88.0 1.2 select_n.184
  89.3 2.2 %collective-permute-done.6 = bf16[4,2,128,64]{2,3,1,0:T(8,128)(2,1)S(1)} collective-permute-done((bf16[4,2,128,64]{2,3,1,0:T(8,128)(2,1)S(1)}, bf16[4,2,128,64]{2,3,1,0:T(8,128)(2,1)S(1)}, u32[]{:S(2)}, u32[]{:S(2)}) %collective-permute-start.6) | collective-permute-done | bytes 131104 | tf_op jit(solution)/shard_map/ppermute | solution.py:165
  92.9 3.2 %collective-permute-start.8 = (bf16[174336]{0:T(1024)(128)(2,1)S(1)}, bf16[174336]{0:T(1024)(128)(2,1)S(1)}, u32[]{:S(2)}, u32[]{:S(2)}) collective-permute-start(bf16[174336]{0:T(1024)(128)(2,1)S(1)} %pad_maximum_fusion), channel_id=1, source_target_pairs={{0,16},{1,17},{2,18},{3,19},{4,20},{5,21},{6,22},{7,23},{8,24},{9,... | collective-permute-start | bytes 1046024 | tf_op jit(solution)/shard_map/ppermute | solution.py:183
  96.5 5.3 %collective-permute-start.10 = (bf16[10,128,64]{1,2,0:T(8,128)(2,1)S(1)}, bf16[10,128,64]{1,2,0:T(8,128)(2,1)S(1)}, u32[]{:S(2)}, u32[]{:S(2)}) collective-permute-start(bf16[10,128,64]{1,2,0:T(8,128)(2,1)S(1)} %get-tuple-element.8), channel_id=1, source_target_pairs={{0,48},{1,49},{2,50},{3,51},{4,52},{5,53},{6,54},{7,55},{8,56},{9,... | collective-permute-start | bytes 491528 | tf_op jit(solution)/shard_map/ppermute | solution.py:189
  101.7 3.1 %collective-permute-start.9 = (bf16[10,128,64]{1,2,0:T(8,128)(2,1)S(1)}, bf16[10,128,64]{1,2,0:T(8,128)(2,1)}, u32[]{:S(2)}, u32[]{:S(2)}) collective-permute-start(bf16[10,128,64]{1,2,0:T(8,128)(2,1)S(1)} %get-tuple-element.9), channel_id=1, source_target_pairs={{0,32},{1,33},{2,34},{3,35},{4,36},{5,37},{6,38},{7,39},{8,40},{9,... | collective-permute-start | bytes 491528 | tf_op jit(solution)/shard_map/ppermute | solution.py:189
  105.3 1.6 %concatenate.96 = bf16[38,64,38]{2,1,0:T(8,128)(2,1)S(1)} reshape(bf16[92416]{0:T(1024)(128)(2,1)S(1)} %slice.123) | data formatting | bytes 369664 | tf_op jit(solution)/shard_map/concatenate | solution.py:194
  108.5 2.4 %collective-permute-done.9 = bf16[10,128,64]{1,2,0:T(8,128)(2,1)} collective-permute-done((bf16[10,128,64]{1,2,0:T(8,128)(2,1)S(1)}, bf16[10,128,64]{1,2,0:T(8,128)(2,1)}, u32[]{:S(2)}, u32[]{:S(2)}) %collective-permute-start.9) | collective-permute-done | bytes 163872 | tf_op jit(solution)/shard_map/ppermute | solution.py:189
  110.9 2.1 %fusion.6 = f32[128,76,1]{1,0,2:T(8,128)} fusion(bf16[10,128,64]{1,2,0:T(8,128)(2,1)S(1)} %collective-permute-done.10, bf16[10,128,64]{1,2,0:T(8,128)(2,1)} %collective-permute-done.9, bf16[10,128,64]{1,2,0:T(8,128)(2,1)S(1)} %copy.52, bf16[16,128,64]{1,2,0:T(8,128)(2,1)S(1)} %dynamic-slice_bitcast_fusion, bf16[46,64,76]{2,1,0:T(8,128)(2,1)S(1)} %gather_fusion.1, ...), kind=kOutput, calls=%fused_computation.13 | convolution fusion | flops 58632704 | bytes 1240110 | tf_op jit(solution)/shard_map/isd,idc->sc/dot_general | solution.py:200
  113.0 7.4 %all-to-all-start.1 = ((f32[64,2,76]{2,1,0:T(2,128)}), f32[64,2,76]{2,1,0:T(2,128)S(1)}, u32[]{:S(2)}, u32[]{:S(2)}) async-start(f32[64,2,76]{2,1,0:T(2,128)} %bitcast.31), calls=%async_computation.1 | async-start | bytes 131072 | tf_op jit(solution)/shard_map/all_to_all | solution.py:204
  120.4 1.3 fusion.42
  121.7 12.2 %all-to-all-done.1 = f32[64,2,76]{2,1,0:T(2,128)S(1)} async-done(((f32[64,2,76]{2,1,0:T(2,128)}), f32[64,2,76]{2,1,0:T(2,128)S(1)}, u32[]{:S(2)}, u32[]{:S(2)}) %all-to-all-start.1) | async-done | bytes 38944 | tf_op jit(solution)/shard_map/all_to_all | solution.py:204
  134.7 6.0 %collective-permute-start.11 = (f32[2,2,32]{2,1,0:T(2,128)S(1)}, f32[2,2,32]{2,1,0:T(2,128)S(1)}, u32[]{:S(2)}, u32[]{:S(2)}) collective-permute-start(f32[2,2,32]{2,1,0:T(2,128)S(1)} %constant_dynamic-slice_fusion.1), channel_id=1, source_target_pairs={{0,256},{256,0},{1,257},{257,1},{2,258},{258,2},{3,259},{259,3},{4... | collective-permute-start | bytes 1544 | tf_op jit(solution)/shard_map/ppermute | solution.py:15
  (114 shorter events, 13.6 us)
Async XLA Ops:
  0.0 134.4 %copy-start = (bf16[2432,64]{0,1:T(8,128)(2,1)S(1)}, bf16[2432,64]{0,1:T(8,128)(2,1)}, u32[]{:S(2)}) copy-start(bf16[2432,64]{0,1:T(8,128)(2,1)} %param.23) | copy-start | bytes 933892
  0.0 12.9 %copy-start.1 = (bf16[19,2432]{1,0:T(8,128)(2,1)S(1)}, bf16[19,2432]{1,0:T(8,128)(2,1)}, u32[]{:S(2)}) copy-start(bf16[19,2432]{1,0:T(8,128)(2,1)} %param.20) | copy-start | bytes 277252
  0.8 13.4 %collective-permute-start = (bf16[2,2,2432]{2,1,0:T(2,128)(2,1)S(1)}, bf16[2,2,2432]{2,1,0:T(2,128)(2,1)S(1)}, u32[]{:S(2)}, u32[]{:S(2)}) collective-permute-start(bf16[2,2,2432]{2,1,0:T(2,128)(2,1)S(1)} %pad_maximum_fusion.3), channel_id=1, source_target_pairs={{0,64},{64,0},{128,192},{192,128},{1,65},{65,1},{129,193},{193,129... | collective-permute-start | bytes 58376 | tf_op jit(solution)/shard_map/ppermute | solution.py:15
  17.3 36.0 %all-to-all-start = ((bf16[64,2,873]{2,1,0:T(2,128)(2,1)}), bf16[64,2,873]{2,1,0:T(2,128)(2,1)S(1)}, u32[]{:S(2)}, u32[]{:S(2)}) async-start(bf16[64,2,873]{2,1,0:T(2,128)(2,1)} %reshape.347), calls=%async_computation | async-start | bytes 458752 | tf_op jit(solution)/shard_map/all_to_all | solution.py:131
  55.4 22.5 %collective-permute-start.1 = (bf16[1,2,128,64]{2,3,1,0:T(8,128)(2,1)S(1)}, bf16[1,2,128,64]{2,3,1,0:T(8,128)(2,1)S(1)}, u32[]{:S(2)}, u32[]{:S(2)}) collective-permute-start(bf16[1,2,128,64]{2,3,1,0:T(8,128)(2,1)S(1)} %get-tuple-element.18), channel_id=1, source_target_pairs={{0,4},{1,5},{2,6},{3,7},{4,0},{5,1},{6,2},{7,3},{8,12},{9,13},{10,... | collective-permute-start | bytes 98312 | tf_op jit(solution)/shard_map/ppermute | solution.py:165
  59.5 18.4 %collective-permute-start.2 = (bf16[1,2,128,64]{2,3,1,0:T(8,128)(2,1)S(1)}, bf16[1,2,128,64]{2,3,1,0:T(8,128)(2,1)S(1)}, u32[]{:S(2)}, u32[]{:S(2)}) collective-permute-start(bf16[1,2,128,64]{2,3,1,0:T(8,128)(2,1)S(1)} %get-tuple-element.18), channel_id=1, source_target_pairs={{0,8},{1,9},{2,10},{3,11},{4,12},{5,13},{6,14},{7,15},{8,0},{9,1},... | collective-permute-start | bytes 98312 | tf_op jit(solution)/shard_map/ppermute | solution.py:165
  66.4 11.5 %collective-permute-start.3 = (bf16[1,2,128,64]{2,3,1,0:T(8,128)(2,1)S(1)}, bf16[1,2,128,64]{2,3,1,0:T(8,128)(2,1)S(1)}, u32[]{:S(2)}, u32[]{:S(2)}) collective-permute-start(bf16[1,2,128,64]{2,3,1,0:T(8,128)(2,1)S(1)} %get-tuple-element.18), channel_id=1, source_target_pairs={{0,12},{1,13},{2,14},{3,15},{4,8},{5,9},{6,10},{7,11},{8,4},{9,5},... | collective-permute-start | bytes 98312 | tf_op jit(solution)/shard_map/ppermute | solution.py:165
  72.1 15.2 %collective-permute-start.7 = (bf16[1216,38]{1,0:T(8,128)(2,1)S(1)}, bf16[1216,38]{1,0:T(8,128)(2,1)S(1)}, u32[]{:S(2)}, u32[]{:S(2)}) collective-permute-start(bf16[1216,38]{1,0:T(8,128)(2,1)S(1)} %reshape.321), channel_id=1, source_target_pairs={{0,256},{256,0},{1,257},{257,1},{2,258},{258,2},{3,259},{259,3},{4... | collective-permute-start | bytes 277256 | tf_op jit(solution)/shard_map/ppermute | solution.py:15
  77.9 11.3 %collective-permute-start.4 = (bf16[4,2,128,64]{2,3,1,0:T(8,128)(2,1)S(1)}, bf16[4,2,128,64]{2,3,1,0:T(8,128)(2,1)S(1)}, u32[]{:S(2)}, u32[]{:S(2)}) collective-permute-start(bf16[4,2,128,64]{2,3,1,0:T(8,128)(2,1)S(1)} %pad_maximum_fusion.1), channel_id=1, source_target_pairs={{0,1},{1,0},{2,3},{3,2},{4,5},{5,4},{6,7},{7,6},{8,9},{9,8},{10,11... | collective-permute-start | bytes 393224 | tf_op jit(solution)/shard_map/ppermute | solution.py:165
  80.5 8.8 %collective-permute-start.5 = (bf16[4,2,128,64]{2,3,1,0:T(8,128)(2,1)S(1)}, bf16[4,2,128,64]{2,3,1,0:T(8,128)(2,1)S(1)}, u32[]{:S(2)}, u32[]{:S(2)}) collective-permute-start(bf16[4,2,128,64]{2,3,1,0:T(8,128)(2,1)S(1)} %pad_maximum_fusion.1), channel_id=1, source_target_pairs={{0,2},{1,3},{2,0},{3,1},{4,6},{5,7},{6,4},{7,5},{8,10},{9,11},{10,... | collective-permute-start | bytes 393224 | tf_op jit(solution)/shard_map/ppermute | solution.py:165
  83.5 8.1 %collective-permute-start.6 = (bf16[4,2,128,64]{2,3,1,0:T(8,128)(2,1)S(1)}, bf16[4,2,128,64]{2,3,1,0:T(8,128)(2,1)S(1)}, u32[]{:S(2)}, u32[]{:S(2)}) collective-permute-start(bf16[4,2,128,64]{2,3,1,0:T(8,128)(2,1)S(1)} %pad_maximum_fusion.1), channel_id=1, source_target_pairs={{0,3},{1,2},{2,1},{3,0},{4,7},{5,6},{6,5},{7,4},{8,11},{9,10},{10,... | collective-permute-start | bytes 393224 | tf_op jit(solution)/shard_map/ppermute | solution.py:165
  92.5 3.8 %copy-start.2 = (f32[1,6,2432]{2,0,1:T(1,128)S(1)}, f32[1,6,2432]{2,0,1:T(1,128)}, u32[]{:S(2)}) copy-start(f32[1,6,2432]{2,0,1:T(1,128)} %param.21) | copy-start | bytes 175108
  92.9 12.0 %collective-permute-start.8 = (bf16[174336]{0:T(1024)(128)(2,1)S(1)}, bf16[174336]{0:T(1024)(128)(2,1)S(1)}, u32[]{:S(2)}, u32[]{:S(2)}) collective-permute-start(bf16[174336]{0:T(1024)(128)(2,1)S(1)} %pad_maximum_fusion), channel_id=1, source_target_pairs={{0,16},{1,17},{2,18},{3,19},{4,20},{5,21},{6,22},{7,23},{8,24},{9,... | collective-permute-start | bytes 1046024 | tf_op jit(solution)/shard_map/ppermute | solution.py:183
  96.5 12.1 %collective-permute-start.10 = (bf16[10,128,64]{1,2,0:T(8,128)(2,1)S(1)}, bf16[10,128,64]{1,2,0:T(8,128)(2,1)S(1)}, u32[]{:S(2)}, u32[]{:S(2)}) collective-permute-start(bf16[10,128,64]{1,2,0:T(8,128)(2,1)S(1)} %get-tuple-element.8), channel_id=1, source_target_pairs={{0,48},{1,49},{2,50},{3,51},{4,52},{5,53},{6,54},{7,55},{8,56},{9,... | collective-permute-start | bytes 491528 | tf_op jit(solution)/shard_map/ppermute | solution.py:189
  101.7 9.2 %collective-permute-start.9 = (bf16[10,128,64]{1,2,0:T(8,128)(2,1)S(1)}, bf16[10,128,64]{1,2,0:T(8,128)(2,1)}, u32[]{:S(2)}, u32[]{:S(2)}) collective-permute-start(bf16[10,128,64]{1,2,0:T(8,128)(2,1)S(1)} %get-tuple-element.9), channel_id=1, source_target_pairs={{0,32},{1,33},{2,34},{3,35},{4,36},{5,37},{6,38},{7,39},{8,40},{9,... | collective-permute-start | bytes 491528 | tf_op jit(solution)/shard_map/ppermute | solution.py:189
  108.5 25.5 %copy-start.3 = (bf16[1,1,2,2,2432]{4,3,2,1,0:T(2,128)(2,1)S(1)}, bf16[1,1,2,2,2432]{4,3,2,1,0:T(2,128)(2,1)}, u32[]{:S(2)}) copy-start(bf16[1,1,2,2,2432]{4,3,2,1,0:T(2,128)(2,1)} %param.16) | copy-start | bytes 58372
  113.0 27.8 %copy-start.5 = (f32[6]{0:T(128)S(1)}, f32[6]{0:T(128)}, u32[]{:S(2)}) copy-start(f32[6]{0:T(128)} %param.25) | copy-start | bytes 76
  113.0 27.8 %copy-start.6 = (f32[6]{0:T(128)S(1)}, f32[6]{0:T(128)}, u32[]{:S(2)}) copy-start(f32[6]{0:T(128)} %param.24) | copy-start | bytes 76
  113.0 28.6 %copy-start.4 = (f32[1,2,2,32]{3,2,1,0:T(2,128)S(1)}, f32[1,2,2,32]{3,2,1,0:T(2,128)}, u32[]{:S(2)}) copy-start(f32[1,2,2,32]{3,2,1,0:T(2,128)} %param.17) | copy-start | bytes 1540
  113.0 20.9 %all-to-all-start.1 = ((f32[64,2,76]{2,1,0:T(2,128)}), f32[64,2,76]{2,1,0:T(2,128)S(1)}, u32[]{:S(2)}, u32[]{:S(2)}) async-start(f32[64,2,76]{2,1,0:T(2,128)} %bitcast.31), calls=%async_computation.1 | async-start | bytes 131072 | tf_op jit(solution)/shard_map/all_to_all | solution.py:204
  134.7 6.9 %collective-permute-start.11 = (f32[2,2,32]{2,1,0:T(2,128)S(1)}, f32[2,2,32]{2,1,0:T(2,128)S(1)}, u32[]{:S(2)}, u32[]{:S(2)}) collective-permute-start(f32[2,2,32]{2,1,0:T(2,128)S(1)} %constant_dynamic-slice_fusion.1), channel_id=1, source_target_pairs={{0,256},{256,0},{1,257},{257,1},{2,258},{258,2},{3,259},{259,3},{4... | collective-permute-start | bytes 1544 | tf_op jit(solution)/shard_map/ppermute | solution.py:15

commit v13 on v12

--- a/solution.py
+++ b/solution.py
@@ -106,11 +106,10 @@
 
     def to_heads(x):
         n = x.shape[0]
-        x = x.reshape(n, shard_rows, HEADS, HD).transpose(2, 0, 1, 3)
-        x = jnp.pad(x, ((0, planes * used - HEADS), (0, 0), (0, 0), (0, 0)))
-        x = x.reshape(planes, used, n, shard_rows, HD)
-        x = jnp.pad(x, ((0, 0), (0, 16 - used), (0, 0), (0, 0), (0, 0)))
-        return x.reshape(nseq, n, shard_rows, HD)
+        x = jnp.pad(x, ((0, 0), (0, 0), (0, (planes * used - HEADS) * HD)))
+        x = x.reshape(n, shard_rows, planes, used, HD)
+        x = jnp.pad(x, ((0, 0), (0, 0), (0, 0), (0, 16 - used), (0, 0)))
+        return x.reshape(n, shard_rows, nseq, HD).transpose(2, 0, 1, 3)
 
     region_of, chunk_of = projection_split(nseq)
     chunks = max(chunk_of) + 1

time: 143 us -> 143 us (level)
    concatenate x6 -> x1, local copies, waits for them, and re-layouts: 2.75 us -> 0.02 us  [shards(): jnp.concatenate([local_query, resident_key_rows, far_keys[None], local_va...]
    unnamed x28 -> x27, local copies, waits for them, and re-layouts: 1.59 us -> 2.93 us
where the time goes in v13:
time: 143 us; the launch traced here: 142 us
  starting transfers between devices  78.3 us (55%)
  waiting for transfers between devices  34.5 us (24%)
  local copies, waits for them, and re-layouts  17 us (12%)
  other arithmetic  5.93 us (4%)
  matrix products  4.61 us (3%)
  between operations  1.53 us (1%)
    ppermute x6, starting transfers between devices, shards(): lax.ppermute(gathered, 'seq', [(i, i ^ shift) for i in range(nseq)])  25.5 us
    all_to_all x1, starting transfers between devices, shards(): joint = lax.all_to_all(joint, 'seq', 0, 0, tiled=True)  18.3 us
    all_to_all x1, waiting for transfers between devices, shards(): joint = lax.all_to_all(joint, 'seq', 0, 0, tiled=True)  17 us
    ppermute x3, starting transfers between devices, from_partner(): lax.ppermute(x, axis, [(i, i ^ 1 << apart) for i in range(lax.axis_size(a...  15.6 us
    all_to_all x1, waiting for transfers between devices, shards(): received = lax.all_to_all(projected_parts, 'seq', 0, 0, tiled=True)  12.2 us
    ppermute x2, starting transfers between devices, shards(): parts.append(lax.ppermute(outgoing, 'seq', pairs))  8.36 us
    all_to_all x1, starting transfers between devices, shards(): received = lax.all_to_all(projected_parts, 'seq', 0, 0, tiled=True)  7.37 us
    ppermute x1, starting transfers between devices, shards(): lax.ppermute(jnp.concatenate([outgoing.reshape(-1), w_quarter.reshape(-1)...  3.18 us
  transfers between devices with their start and end apart: 14, of which 5 were waited for; matrix products, arithmetic and copies ran while one was open for 12% of the time, Pallas kernels for 0%

profile of v13, /device:TPU:1, one launch (start us, length us, event | category | flops | bytes accessed | tf_op | source)
XLA Modules:
  0.0 141.9 jit_solution(5032960533780025282)
XLA Ops:
  0.0 0.8 slice_bitcast_fusion.1
  0.8 4.0 %collective-permute-start = (bf16[2,2,2432]{2,1,0:T(2,128)(2,1)S(1)}, bf16[2,2,2432]{2,1,0:T(2,128)(2,1)S(1)}, u32[]{:S(2)}, u32[]{:S(2)}) collective-permute-start(bf16[2,2,2432]{2,1,0:T(2,128)(2,1)S(1)} %pad_maximum_fusion.3), channel_id=1, source_target_pairs={{0,64},{64,0},{128,192},{192,128},{1,65},{65,1},{129,193},{193,129... | collective-permute-start | bytes 58376 | tf_op jit(solution)/shard_map/ppermute | solution.py:15
  5.0 0.7 constant_dynamic-update-slice_fusion.4
  5.7 0.8 constant_dynamic-update-slice_fusion.3
  6.5 0.9 fusion.39
  7.3 0.8 constant_dynamic-slice_fusion.4
  9.3 1.2 fusion.18
  11.8 1.6 %reshape.315 = bf16[19,2,16,2,38]{4,3,2,1,0:T(2,128)(2,1)S(1)} reshape(bf16[19,2432]{1,0:T(8,128)(2,1)} %param.20) | data formatting | bytes 184832 | tf_op jit(solution)/shard_map/reshape | solution.py:119
  15.4 0.7 reduce.2
  16.1 0.9 reshape.346
  17.0 18.3 %all-to-all-start = ((bf16[64,2,873]{2,1,0:T(2,128)(2,1)}), bf16[64,2,873]{2,1,0:T(2,128)(2,1)S(1)}, u32[]{:S(2)}, u32[]{:S(2)}) async-start(bf16[64,2,873]{2,1,0:T(2,128)(2,1)} %reshape.346), calls=%async_computation | async-start | bytes 458752 | tf_op jit(solution)/shard_map/all_to_all | solution.py:130
  36.0 17.0 %all-to-all-done = bf16[64,2,873]{2,1,0:T(2,128)(2,1)S(1)} async-done(((bf16[64,2,873]{2,1,0:T(2,128)(2,1)}), bf16[64,2,873]{2,1,0:T(2,128)(2,1)S(1)}, u32[]{:S(2)}, u32[]{:S(2)}) %all-to-all-start) | async-done | bytes 223520 | tf_op jit(solution)/shard_map/all_to_all | solution.py:130
  55.1 4.0 %collective-permute-start.1 = (bf16[1,2,128,64]{2,3,1,0:T(8,128)(2,1)S(1)}, bf16[1,2,128,64]{2,3,1,0:T(8,128)(2,1)S(1)}, u32[]{:S(2)}, u32[]{:S(2)}) collective-permute-start(bf16[1,2,128,64]{2,3,1,0:T(8,128)(2,1)S(1)} %get-tuple-element.18), channel_id=1, source_target_pairs={{0,4},{1,5},{2,6},{3,7},{4,0},{5,1},{6,2},{7,3},{8,12},{9,13},{10,... | collective-permute-start | bytes 98312 | tf_op jit(solution)/shard_map/ppermute | solution.py:164
  59.2 6.9 %collective-permute-start.2 = (bf16[1,2,128,64]{2,3,1,0:T(8,128)(2,1)S(1)}, bf16[1,2,128,64]{2,3,1,0:T(8,128)(2,1)S(1)}, u32[]{:S(2)}, u32[]{:S(2)}) collective-permute-start(bf16[1,2,128,64]{2,3,1,0:T(8,128)(2,1)S(1)} %get-tuple-element.18), channel_id=1, source_target_pairs={{0,8},{1,9},{2,10},{3,11},{4,12},{5,13},{6,14},{7,15},{8,0},{9,1},... | collective-permute-start | bytes 98312 | tf_op jit(solution)/shard_map/ppermute | solution.py:164
  66.0 5.3 %collective-permute-start.3 = (bf16[1,2,128,64]{2,3,1,0:T(8,128)(2,1)S(1)}, bf16[1,2,128,64]{2,3,1,0:T(8,128)(2,1)S(1)}, u32[]{:S(2)}, u32[]{:S(2)}) collective-permute-start(bf16[1,2,128,64]{2,3,1,0:T(8,128)(2,1)S(1)} %get-tuple-element.18), channel_id=1, source_target_pairs={{0,12},{1,13},{2,14},{3,15},{4,8},{5,9},{6,10},{7,11},{8,4},{9,5},... | collective-permute-start | bytes 98312 | tf_op jit(solution)/shard_map/ppermute | solution.py:164
  71.8 5.6 %collective-permute-start.7 = (bf16[1216,38]{1,0:T(8,128)(2,1)S(1)}, bf16[1216,38]{1,0:T(8,128)(2,1)S(1)}, u32[]{:S(2)}, u32[]{:S(2)}) collective-permute-start(bf16[1216,38]{1,0:T(8,128)(2,1)S(1)} %reshape.320), channel_id=1, source_target_pairs={{0,256},{256,0},{1,257},{257,1},{2,258},{258,2},{3,259},{259,3},{4... | collective-permute-start | bytes 277256 | tf_op jit(solution)/shard_map/ppermute | solution.py:15
  77.6 2.6 %collective-permute-start.4 = (bf16[4,2,128,64]{2,3,1,0:T(8,128)(2,1)S(1)}, bf16[4,2,128,64]{2,3,1,0:T(8,128)(2,1)S(1)}, u32[]{:S(2)}, u32[]{:S(2)}) collective-permute-start(bf16[4,2,128,64]{2,3,1,0:T(8,128)(2,1)S(1)} %pad_maximum_fusion.1), channel_id=1, source_target_pairs={{0,1},{1,0},{2,3},{3,2},{4,5},{5,4},{6,7},{7,6},{8,9},{9,8},{10,11... | collective-permute-start | bytes 393224 | tf_op jit(solution)/shard_map/ppermute | solution.py:164
  80.2 3.0 %collective-permute-start.5 = (bf16[4,2,128,64]{2,3,1,0:T(8,128)(2,1)S(1)}, bf16[4,2,128,64]{2,3,1,0:T(8,128)(2,1)S(1)}, u32[]{:S(2)}, u32[]{:S(2)}) collective-permute-start(bf16[4,2,128,64]{2,3,1,0:T(8,128)(2,1)S(1)} %pad_maximum_fusion.1), channel_id=1, source_target_pairs={{0,2},{1,3},{2,0},{3,1},{4,6},{5,7},{6,4},{7,5},{8,10},{9,11},{10,... | collective-permute-start | bytes 393224 | tf_op jit(solution)/shard_map/ppermute | solution.py:164
  83.2 3.7 %collective-permute-start.6 = (bf16[4,2,128,64]{2,3,1,0:T(8,128)(2,1)S(1)}, bf16[4,2,128,64]{2,3,1,0:T(8,128)(2,1)S(1)}, u32[]{:S(2)}, u32[]{:S(2)}) collective-permute-start(bf16[4,2,128,64]{2,3,1,0:T(8,128)(2,1)S(1)} %pad_maximum_fusion.1), channel_id=1, source_target_pairs={{0,3},{1,2},{2,1},{3,0},{4,7},{5,6},{6,5},{7,4},{8,11},{9,10},{10,... | collective-permute-start | bytes 393224 | tf_op jit(solution)/shard_map/ppermute | solution.py:164
  87.7 1.2 select_n.184
  89.0 2.2 %collective-permute-done.6 = bf16[4,2,128,64]{2,3,1,0:T(8,128)(2,1)S(1)} collective-permute-done((bf16[4,2,128,64]{2,3,1,0:T(8,128)(2,1)S(1)}, bf16[4,2,128,64]{2,3,1,0:T(8,128)(2,1)S(1)}, u32[]{:S(2)}, u32[]{:S(2)}) %collective-permute-start.6) | collective-permute-done | bytes 131104 | tf_op jit(solution)/shard_map/ppermute | solution.py:164
  92.6 3.2 %collective-permute-start.8 = (bf16[174336]{0:T(1024)(128)(2,1)S(1)}, bf16[174336]{0:T(1024)(128)(2,1)S(1)}, u32[]{:S(2)}, u32[]{:S(2)}) collective-permute-start(bf16[174336]{0:T(1024)(128)(2,1)S(1)} %pad_maximum_fusion), channel_id=1, source_target_pairs={{0,16},{1,17},{2,18},{3,19},{4,20},{5,21},{6,22},{7,23},{8,24},{9,... | collective-permute-start | bytes 1046024 | tf_op jit(solution)/shard_map/ppermute | solution.py:182
  96.2 5.3 %collective-permute-start.10 = (bf16[10,128,64]{1,2,0:T(8,128)(2,1)S(1)}, bf16[10,128,64]{1,2,0:T(8,128)(2,1)S(1)}, u32[]{:S(2)}, u32[]{:S(2)}) collective-permute-start(bf16[10,128,64]{1,2,0:T(8,128)(2,1)S(1)} %get-tuple-element.8), channel_id=1, source_target_pairs={{0,48},{1,49},{2,50},{3,51},{4,52},{5,53},{6,54},{7,55},{8,56},{9,... | collective-permute-start | bytes 491528 | tf_op jit(solution)/shard_map/ppermute | solution.py:188
  101.4 3.1 %collective-permute-start.9 = (bf16[10,128,64]{1,2,0:T(8,128)(2,1)S(1)}, bf16[10,128,64]{1,2,0:T(8,128)(2,1)}, u32[]{:S(2)}, u32[]{:S(2)}) collective-permute-start(bf16[10,128,64]{1,2,0:T(8,128)(2,1)S(1)} %get-tuple-element.9), channel_id=1, source_target_pairs={{0,32},{1,33},{2,34},{3,35},{4,36},{5,37},{6,38},{7,39},{8,40},{9,... | collective-permute-start | bytes 491528 | tf_op jit(solution)/shard_map/ppermute | solution.py:188
  105.0 1.6 %concatenate.80 = bf16[38,64,38]{2,1,0:T(8,128)(2,1)S(1)} reshape(bf16[92416]{0:T(1024)(128)(2,1)S(1)} %slice.123) | data formatting | bytes 369664 | tf_op jit(solution)/shard_map/concatenate | solution.py:193
  107.5 0.7 gather_fusion.1
  108.2 2.4 %collective-permute-done.9 = bf16[10,128,64]{1,2,0:T(8,128)(2,1)} collective-permute-done((bf16[10,128,64]{1,2,0:T(8,128)(2,1)S(1)}, bf16[10,128,64]{1,2,0:T(8,128)(2,1)}, u32[]{:S(2)}, u32[]{:S(2)}) %collective-permute-start.9) | collective-permute-done | bytes 163872 | tf_op jit(solution)/shard_map/ppermute | solution.py:188
  110.6 2.1 %fusion.6 = f32[128,76,1]{1,0,2:T(8,128)} fusion(bf16[10,128,64]{1,2,0:T(8,128)(2,1)S(1)} %collective-permute-done.10, bf16[10,128,64]{1,2,0:T(8,128)(2,1)} %collective-permute-done.9, bf16[10,128,64]{1,2,0:T(8,128)(2,1)S(1)} %copy.52, bf16[16,128,64]{1,2,0:T(8,128)(2,1)S(1)} %dynamic-slice_bitcast_fusion, bf16[46,64,76]{2,1,0:T(8,128)(2,1)S(1)} %gather_fusion.1, ...), kind=kOutput, calls=%fused_computation.13 | convolution fusion | flops 58632704 | bytes 1240110 | tf_op jit(solution)/shard_map/isd,idc->sc/dot_general | solution.py:199
  112.7 7.4 %all-to-all-start.1 = ((f32[64,2,76]{2,1,0:T(2,128)}), f32[64,2,76]{2,1,0:T(2,128)S(1)}, u32[]{:S(2)}, u32[]{:S(2)}) async-start(f32[64,2,76]{2,1,0:T(2,128)} %bitcast.34), calls=%async_computation.1 | async-start | bytes 131072 | tf_op jit(solution)/shard_map/all_to_all | solution.py:203
  120.1 1.3 fusion.42
  121.4 12.2 %all-to-all-done.1 = f32[64,2,76]{2,1,0:T(2,128)S(1)} async-done(((f32[64,2,76]{2,1,0:T(2,128)}), f32[64,2,76]{2,1,0:T(2,128)S(1)}, u32[]{:S(2)}, u32[]{:S(2)}) %all-to-all-start.1) | async-done | bytes 38944 | tf_op jit(solution)/shard_map/all_to_all | solution.py:203
  134.4 6.1 %collective-permute-start.11 = (f32[2,2,32]{2,1,0:T(2,128)S(1)}, f32[2,2,32]{2,1,0:T(2,128)S(1)}, u32[]{:S(2)}, u32[]{:S(2)}) collective-permute-start(f32[2,2,32]{2,1,0:T(2,128)S(1)} %constant_dynamic-slice_fusion.1), channel_id=1, source_target_pairs={{0,256},{256,0},{1,257},{257,1},{2,258},{258,2},{3,259},{259,3},{4... | collective-permute-start | bytes 1544 | tf_op jit(solution)/shard_map/ppermute | solution.py:15
  (109 shorter events, 12.8 us)
Async XLA Ops:
  0.0 134.1 %copy-start = (bf16[2432,64]{0,1:T(8,128)(2,1)S(1)}, bf16[2432,64]{0,1:T(8,128)(2,1)}, u32[]{:S(2)}) copy-start(bf16[2432,64]{0,1:T(8,128)(2,1)} %param.23) | copy-start | bytes 933892
  0.8 13.1 %collective-permute-start = (bf16[2,2,2432]{2,1,0:T(2,128)(2,1)S(1)}, bf16[2,2,2432]{2,1,0:T(2,128)(2,1)S(1)}, u32[]{:S(2)}, u32[]{:S(2)}) collective-permute-start(bf16[2,2,2432]{2,1,0:T(2,128)(2,1)S(1)} %pad_maximum_fusion.3), channel_id=1, source_target_pairs={{0,64},{64,0},{128,192},{192,128},{1,65},{65,1},{129,193},{193,129... | collective-permute-start | bytes 58376 | tf_op jit(solution)/shard_map/ppermute | solution.py:15
  11.8 2.1 %copy-start.3 = (bf16[1,1,2,2,2432]{4,3,2,1,0:T(2,128)(2,1)S(1)}, bf16[1,1,2,2,2432]{4,3,2,1,0:T(2,128)(2,1)}, u32[]{:S(2)}) copy-start(bf16[1,1,2,2,2432]{4,3,2,1,0:T(2,128)(2,1)} %param.15) | copy-start | bytes 58372
  17.0 36.0 %all-to-all-start = ((bf16[64,2,873]{2,1,0:T(2,128)(2,1)}), bf16[64,2,873]{2,1,0:T(2,128)(2,1)S(1)}, u32[]{:S(2)}, u32[]{:S(2)}) async-start(bf16[64,2,873]{2,1,0:T(2,128)(2,1)} %reshape.346), calls=%async_computation | async-start | bytes 458752 | tf_op jit(solution)/shard_map/all_to_all | solution.py:130
  55.1 22.5 %collective-permute-start.1 = (bf16[1,2,128,64]{2,3,1,0:T(8,128)(2,1)S(1)}, bf16[1,2,128,64]{2,3,1,0:T(8,128)(2,1)S(1)}, u32[]{:S(2)}, u32[]{:S(2)}) collective-permute-start(bf16[1,2,128,64]{2,3,1,0:T(8,128)(2,1)S(1)} %get-tuple-element.18), channel_id=1, source_target_pairs={{0,4},{1,5},{2,6},{3,7},{4,0},{5,1},{6,2},{7,3},{8,12},{9,13},{10,... | collective-permute-start | bytes 98312 | tf_op jit(solution)/shard_map/ppermute | solution.py:164
  59.2 18.4 %collective-permute-start.2 = (bf16[1,2,128,64]{2,3,1,0:T(8,128)(2,1)S(1)}, bf16[1,2,128,64]{2,3,1,0:T(8,128)(2,1)S(1)}, u32[]{:S(2)}, u32[]{:S(2)}) collective-permute-start(bf16[1,2,128,64]{2,3,1,0:T(8,128)(2,1)S(1)} %get-tuple-element.18), channel_id=1, source_target_pairs={{0,8},{1,9},{2,10},{3,11},{4,12},{5,13},{6,14},{7,15},{8,0},{9,1},... | collective-permute-start | bytes 98312 | tf_op jit(solution)/shard_map/ppermute | solution.py:164
  66.0 11.5 %collective-permute-start.3 = (bf16[1,2,128,64]{2,3,1,0:T(8,128)(2,1)S(1)}, bf16[1,2,128,64]{2,3,1,0:T(8,128)(2,1)S(1)}, u32[]{:S(2)}, u32[]{:S(2)}) collective-permute-start(bf16[1,2,128,64]{2,3,1,0:T(8,128)(2,1)S(1)} %get-tuple-element.18), channel_id=1, source_target_pairs={{0,12},{1,13},{2,14},{3,15},{4,8},{5,9},{6,10},{7,11},{8,4},{9,5},... | collective-permute-start | bytes 98312 | tf_op jit(solution)/shard_map/ppermute | solution.py:164
  71.8 15.2 %collective-permute-start.7 = (bf16[1216,38]{1,0:T(8,128)(2,1)S(1)}, bf16[1216,38]{1,0:T(8,128)(2,1)S(1)}, u32[]{:S(2)}, u32[]{:S(2)}) collective-permute-start(bf16[1216,38]{1,0:T(8,128)(2,1)S(1)} %reshape.320), channel_id=1, source_target_pairs={{0,256},{256,0},{1,257},{257,1},{2,258},{258,2},{3,259},{259,3},{4... | collective-permute-start | bytes 277256 | tf_op jit(solution)/shard_map/ppermute | solution.py:15
  77.6 11.3 %collective-permute-start.4 = (bf16[4,2,128,64]{2,3,1,0:T(8,128)(2,1)S(1)}, bf16[4,2,128,64]{2,3,1,0:T(8,128)(2,1)S(1)}, u32[]{:S(2)}, u32[]{:S(2)}) collective-permute-start(bf16[4,2,128,64]{2,3,1,0:T(8,128)(2,1)S(1)} %pad_maximum_fusion.1), channel_id=1, source_target_pairs={{0,1},{1,0},{2,3},{3,2},{4,5},{5,4},{6,7},{7,6},{8,9},{9,8},{10,11... | collective-permute-start | bytes 393224 | tf_op jit(solution)/shard_map/ppermute | solution.py:164
  80.2 8.8 %collective-permute-start.5 = (bf16[4,2,128,64]{2,3,1,0:T(8,128)(2,1)S(1)}, bf16[4,2,128,64]{2,3,1,0:T(8,128)(2,1)S(1)}, u32[]{:S(2)}, u32[]{:S(2)}) collective-permute-start(bf16[4,2,128,64]{2,3,1,0:T(8,128)(2,1)S(1)} %pad_maximum_fusion.1), channel_id=1, source_target_pairs={{0,2},{1,3},{2,0},{3,1},{4,6},{5,7},{6,4},{7,5},{8,10},{9,11},{10,... | collective-permute-start | bytes 393224 | tf_op jit(solution)/shard_map/ppermute | solution.py:164
  83.2 8.1 %collective-permute-start.6 = (bf16[4,2,128,64]{2,3,1,0:T(8,128)(2,1)S(1)}, bf16[4,2,128,64]{2,3,1,0:T(8,128)(2,1)S(1)}, u32[]{:S(2)}, u32[]{:S(2)}) collective-permute-start(bf16[4,2,128,64]{2,3,1,0:T(8,128)(2,1)S(1)} %pad_maximum_fusion.1), channel_id=1, source_target_pairs={{0,3},{1,2},{2,1},{3,0},{4,7},{5,6},{6,5},{7,4},{8,11},{9,10},{10,... | collective-permute-start | bytes 393224 | tf_op jit(solution)/shard_map/ppermute | solution.py:164
  92.1 3.8 %copy-start.1 = (f32[1,6,2432]{2,0,1:T(1,128)S(1)}, f32[1,6,2432]{2,0,1:T(1,128)}, u32[]{:S(2)}) copy-start(f32[1,6,2432]{2,0,1:T(1,128)} %param.21) | copy-start | bytes 175108
  92.6 12.0 %collective-permute-start.8 = (bf16[174336]{0:T(1024)(128)(2,1)S(1)}, bf16[174336]{0:T(1024)(128)(2,1)S(1)}, u32[]{:S(2)}, u32[]{:S(2)}) collective-permute-start(bf16[174336]{0:T(1024)(128)(2,1)S(1)} %pad_maximum_fusion), channel_id=1, source_target_pairs={{0,16},{1,17},{2,18},{3,19},{4,20},{5,21},{6,22},{7,23},{8,24},{9,... | collective-permute-start | bytes 1046024 | tf_op jit(solution)/shard_map/ppermute | solution.py:182
  96.2 12.1 %collective-permute-start.10 = (bf16[10,128,64]{1,2,0:T(8,128)(2,1)S(1)}, bf16[10,128,64]{1,2,0:T(8,128)(2,1)S(1)}, u32[]{:S(2)}, u32[]{:S(2)}) collective-permute-start(bf16[10,128,64]{1,2,0:T(8,128)(2,1)S(1)} %get-tuple-element.8), channel_id=1, source_target_pairs={{0,48},{1,49},{2,50},{3,51},{4,52},{5,53},{6,54},{7,55},{8,56},{9,... | collective-permute-start | bytes 491528 | tf_op jit(solution)/shard_map/ppermute | solution.py:188
  101.4 9.2 %collective-permute-start.9 = (bf16[10,128,64]{1,2,0:T(8,128)(2,1)S(1)}, bf16[10,128,64]{1,2,0:T(8,128)(2,1)}, u32[]{:S(2)}, u32[]{:S(2)}) collective-permute-start(bf16[10,128,64]{1,2,0:T(8,128)(2,1)S(1)} %get-tuple-element.9), channel_id=1, source_target_pairs={{0,32},{1,33},{2,34},{3,35},{4,36},{5,37},{6,38},{7,39},{8,40},{9,... | collective-permute-start | bytes 491528 | tf_op jit(solution)/shard_map/ppermute | solution.py:188
  108.2 25.5 %copy-start.2 = (bf16[1,1,2,2,2432]{4,3,2,1,0:T(2,128)(2,1)S(1)}, bf16[1,1,2,2,2432]{4,3,2,1,0:T(2,128)(2,1)}, u32[]{:S(2)}) copy-start(bf16[1,1,2,2,2432]{4,3,2,1,0:T(2,128)(2,1)} %param.16) | copy-start | bytes 58372
  112.7 27.8 %copy-start.5 = (f32[6]{0:T(128)S(1)}, f32[6]{0:T(128)}, u32[]{:S(2)}) copy-start(f32[6]{0:T(128)} %param.25) | copy-start | bytes 76
  112.7 27.8 %copy-start.6 = (f32[6]{0:T(128)S(1)}, f32[6]{0:T(128)}, u32[]{:S(2)}) copy-start(f32[6]{0:T(128)} %param.24) | copy-start | bytes 76
  112.7 28.6 %copy-start.4 = (f32[1,2,2,32]{3,2,1,0:T(2,128)S(1)}, f32[1,2,2,32]{3,2,1,0:T(2,128)}, u32[]{:S(2)}) copy-start(f32[1,2,2,32]{3,2,1,0:T(2,128)} %param.17) | copy-start | bytes 1540
  112.7 20.9 %all-to-all-start.1 = ((f32[64,2,76]{2,1,0:T(2,128)}), f32[64,2,76]{2,1,0:T(2,128)S(1)}, u32[]{:S(2)}, u32[]{:S(2)}) async-start(f32[64,2,76]{2,1,0:T(2,128)} %bitcast.34), calls=%async_computation.1 | async-start | bytes 131072 | tf_op jit(solution)/shard_map/all_to_all | solution.py:203
  134.4 6.9 %collective-permute-start.11 = (f32[2,2,32]{2,1,0:T(2,128)S(1)}, f32[2,2,32]{2,1,0:T(2,128)S(1)}, u32[]{:S(2)}, u32[]{:S(2)}) collective-permute-start(f32[2,2,32]{2,1,0:T(2,128)S(1)} %constant_dynamic-slice_fusion.1), channel_id=1, source_target_pairs={{0,256},{256,0},{1,257},{257,1},{2,258},{258,2},{3,259},{259,3},{4... | collective-permute-start | bytes 1544 | tf_op jit(solution)/shard_map/ppermute | solution.py:15

commit v14 on v13

--- a/solution.py
+++ b/solution.py
@@ -232,10 +232,10 @@
     own_velocity = lax.dynamic_slice_in_dim(velocity, branch * part_width, part_width, 2)
     other_velocity = from_partner(outgoing_velocity, "cfg", 0)
     is_conditional = branch == 0
-    cond_velocity = jnp.where(is_conditional, own_velocity, other_velocity)
-    uncond_velocity = jnp.where(is_conditional, other_velocity, own_velocity)
-    guided = uncond_velocity + weight_now * (cond_velocity - uncond_velocity)
-    updated = latent_part - step_now * guided
+    own_weight = jnp.where(is_conditional, weight_now, 1.0 - weight_now)
+    other_weight = jnp.where(is_conditional, 1.0 - weight_now, weight_now)
+    partial = latent_part - step_now * (own_weight * own_velocity)
+    updated = partial - step_now * (other_weight * other_velocity)
     return updated[None]
 
 

time: 143 us -> 144 us (level)
  no operation moved by 1% of the time
where the time goes in v14:
time: 144 us; the launch traced here: 143 us
  starting transfers between devices  78.3 us (54%)
  waiting for transfers between devices  35.8 us (25%)
  local copies, waits for them, and re-layouts  17.1 us (12%)
  other arithmetic  6.04 us (4%)
  matrix products  4.61 us (3%)
  between operations  1.56 us (1%)
    ppermute x6, starting transfers between devices, shards(): lax.ppermute(gathered, 'seq', [(i, i ^ shift) for i in range(nseq)])  25.5 us
    all_to_all x1, starting transfers between devices, shards(): joint = lax.all_to_all(joint, 'seq', 0, 0, tiled=True)  18.3 us
    all_to_all x1, waiting for transfers between devices, shards(): joint = lax.all_to_all(joint, 'seq', 0, 0, tiled=True)  17 us
    ppermute x3, starting transfers between devices, from_partner(): lax.ppermute(x, axis, [(i, i ^ 1 << apart) for i in range(lax.axis_size(a...  15.6 us
    all_to_all x1, waiting for transfers between devices, shards(): received = lax.all_to_all(projected_parts, 'seq', 0, 0, tiled=True)  13.3 us
    ppermute x2, starting transfers between devices, shards(): parts.append(lax.ppermute(outgoing, 'seq', pairs))  8.36 us
    all_to_all x1, starting transfers between devices, shards(): received = lax.all_to_all(projected_parts, 'seq', 0, 0, tiled=True)  7.37 us
    ppermute x1, starting transfers between devices, shards(): lax.ppermute(jnp.concatenate([outgoing.reshape(-1), w_quarter.reshape(-1)...  3.19 us
  transfers between devices with their start and end apart: 14, of which 5 were waited for; matrix products, arithmetic and copies ran while one was open for 12% of the time, Pallas kernels for 0%

profile of v14, /device:TPU:1, one launch (start us, length us, event | category | flops | bytes accessed | tf_op | source)
XLA Modules:
  0.0 143.3 jit_solution(16770220767037121725)
XLA Ops:
  0.0 0.8 slice_bitcast_fusion.1
  0.8 4.0 %collective-permute-start = (bf16[2,2,2432]{2,1,0:T(2,128)(2,1)S(1)}, bf16[2,2,2432]{2,1,0:T(2,128)(2,1)S(1)}, u32[]{:S(2)}, u32[]{:S(2)}) collective-permute-start(bf16[2,2,2432]{2,1,0:T(2,128)(2,1)S(1)} %pad_maximum_fusion.3), channel_id=1, source_target_pairs={{0,64},{64,0},{128,192},{192,128},{1,65},{65,1},{129,193},{193,129... | collective-permute-start | bytes 58376 | tf_op jit(solution)/shard_map/ppermute | solution.py:15
  5.0 0.7 constant_dynamic-update-slice_fusion.4
  5.7 0.8 constant_dynamic-update-slice_fusion.3
  6.5 0.9 fusion.43
  7.3 0.8 constant_dynamic-slice_fusion.4
  9.4 1.2 fusion.18
  11.2 1.3 fusion.46
  13.2 1.6 %reshape.324 = bf16[19,2,16,2,38]{4,3,2,1,0:T(2,128)(2,1)S(1)} reshape(bf16[19,2432]{1,0:T(8,128)(2,1)} %param.20) | data formatting | bytes 184832 | tf_op jit(solution)/shard_map/reshape | solution.py:119
  16.8 0.7 reduce.2
  17.5 0.9 reshape.355
  18.4 18.3 %all-to-all-start = ((bf16[64,2,873]{2,1,0:T(2,128)(2,1)}), bf16[64,2,873]{2,1,0:T(2,128)(2,1)S(1)}, u32[]{:S(2)}, u32[]{:S(2)}) async-start(bf16[64,2,873]{2,1,0:T(2,128)(2,1)} %reshape.355), calls=%async_computation | async-start | bytes 458752 | tf_op jit(solution)/shard_map/all_to_all | solution.py:130
  37.4 17.0 %all-to-all-done = bf16[64,2,873]{2,1,0:T(2,128)(2,1)S(1)} async-done(((bf16[64,2,873]{2,1,0:T(2,128)(2,1)}), bf16[64,2,873]{2,1,0:T(2,128)(2,1)S(1)}, u32[]{:S(2)}, u32[]{:S(2)}) %all-to-all-start) | async-done | bytes 223520 | tf_op jit(solution)/shard_map/all_to_all | solution.py:130
  56.5 4.0 %collective-permute-start.1 = (bf16[1,2,128,64]{2,3,1,0:T(8,128)(2,1)S(1)}, bf16[1,2,128,64]{2,3,1,0:T(8,128)(2,1)S(1)}, u32[]{:S(2)}, u32[]{:S(2)}) collective-permute-start(bf16[1,2,128,64]{2,3,1,0:T(8,128)(2,1)S(1)} %get-tuple-element.18), channel_id=1, source_target_pairs={{0,4},{1,5},{2,6},{3,7},{4,0},{5,1},{6,2},{7,3},{8,12},{9,13},{10,... | collective-permute-start | bytes 98312 | tf_op jit(solution)/shard_map/ppermute | solution.py:164
  60.6 6.9 %collective-permute-start.2 = (bf16[1,2,128,64]{2,3,1,0:T(8,128)(2,1)S(1)}, bf16[1,2,128,64]{2,3,1,0:T(8,128)(2,1)S(1)}, u32[]{:S(2)}, u32[]{:S(2)}) collective-permute-start(bf16[1,2,128,64]{2,3,1,0:T(8,128)(2,1)S(1)} %get-tuple-element.18), channel_id=1, source_target_pairs={{0,8},{1,9},{2,10},{3,11},{4,12},{5,13},{6,14},{7,15},{8,0},{9,1},... | collective-permute-start | bytes 98312 | tf_op jit(solution)/shard_map/ppermute | solution.py:164
  67.5 5.3 %collective-permute-start.3 = (bf16[1,2,128,64]{2,3,1,0:T(8,128)(2,1)S(1)}, bf16[1,2,128,64]{2,3,1,0:T(8,128)(2,1)S(1)}, u32[]{:S(2)}, u32[]{:S(2)}) collective-permute-start(bf16[1,2,128,64]{2,3,1,0:T(8,128)(2,1)S(1)} %get-tuple-element.18), channel_id=1, source_target_pairs={{0,12},{1,13},{2,14},{3,15},{4,8},{5,9},{6,10},{7,11},{8,4},{9,5},... | collective-permute-start | bytes 98312 | tf_op jit(solution)/shard_map/ppermute | solution.py:164
  73.2 5.6 %collective-permute-start.7 = (bf16[1216,38]{1,0:T(8,128)(2,1)S(1)}, bf16[1216,38]{1,0:T(8,128)(2,1)S(1)}, u32[]{:S(2)}, u32[]{:S(2)}) collective-permute-start(bf16[1216,38]{1,0:T(8,128)(2,1)S(1)} %reshape.329), channel_id=1, source_target_pairs={{0,256},{256,0},{1,257},{257,1},{2,258},{258,2},{3,259},{259,3},{4... | collective-permute-start | bytes 277256 | tf_op jit(solution)/shard_map/ppermute | solution.py:15
  79.0 2.6 %collective-permute-start.4 = (bf16[4,2,128,64]{2,3,1,0:T(8,128)(2,1)S(1)}, bf16[4,2,128,64]{2,3,1,0:T(8,128)(2,1)S(1)}, u32[]{:S(2)}, u32[]{:S(2)}) collective-permute-start(bf16[4,2,128,64]{2,3,1,0:T(8,128)(2,1)S(1)} %pad_maximum_fusion.1), channel_id=1, source_target_pairs={{0,1},{1,0},{2,3},{3,2},{4,5},{5,4},{6,7},{7,6},{8,9},{9,8},{10,11... | collective-permute-start | bytes 393224 | tf_op jit(solution)/shard_map/ppermute | solution.py:164
  81.6 3.0 %collective-permute-start.5 = (bf16[4,2,128,64]{2,3,1,0:T(8,128)(2,1)S(1)}, bf16[4,2,128,64]{2,3,1,0:T(8,128)(2,1)S(1)}, u32[]{:S(2)}, u32[]{:S(2)}) collective-permute-start(bf16[4,2,128,64]{2,3,1,0:T(8,128)(2,1)S(1)} %pad_maximum_fusion.1), channel_id=1, source_target_pairs={{0,2},{1,3},{2,0},{3,1},{4,6},{5,7},{6,4},{7,5},{8,10},{9,11},{10,... | collective-permute-start | bytes 393224 | tf_op jit(solution)/shard_map/ppermute | solution.py:164
  84.6 3.7 %collective-permute-start.6 = (bf16[4,2,128,64]{2,3,1,0:T(8,128)(2,1)S(1)}, bf16[4,2,128,64]{2,3,1,0:T(8,128)(2,1)S(1)}, u32[]{:S(2)}, u32[]{:S(2)}) collective-permute-start(bf16[4,2,128,64]{2,3,1,0:T(8,128)(2,1)S(1)} %pad_maximum_fusion.1), channel_id=1, source_target_pairs={{0,3},{1,2},{2,1},{3,0},{4,7},{5,6},{6,5},{7,4},{8,11},{9,10},{10,... | collective-permute-start | bytes 393224 | tf_op jit(solution)/shard_map/ppermute | solution.py:164
  89.1 1.2 select_n.195
  90.4 2.2 %collective-permute-done.6 = bf16[4,2,128,64]{2,3,1,0:T(8,128)(2,1)S(1)} collective-permute-done((bf16[4,2,128,64]{2,3,1,0:T(8,128)(2,1)S(1)}, bf16[4,2,128,64]{2,3,1,0:T(8,128)(2,1)S(1)}, u32[]{:S(2)}, u32[]{:S(2)}) %collective-permute-start.6) | collective-permute-done | bytes 131104 | tf_op jit(solution)/shard_map/ppermute | solution.py:164
  94.0 3.2 %collective-permute-start.8 = (bf16[174336]{0:T(1024)(128)(2,1)S(1)}, bf16[174336]{0:T(1024)(128)(2,1)S(1)}, u32[]{:S(2)}, u32[]{:S(2)}) collective-permute-start(bf16[174336]{0:T(1024)(128)(2,1)S(1)} %pad_maximum_fusion), channel_id=1, source_target_pairs={{0,16},{1,17},{2,18},{3,19},{4,20},{5,21},{6,22},{7,23},{8,24},{9,... | collective-permute-start | bytes 1046024 | tf_op jit(solution)/shard_map/ppermute | solution.py:182
  97.6 5.3 %collective-permute-start.10 = (bf16[10,128,64]{1,2,0:T(8,128)(2,1)S(1)}, bf16[10,128,64]{1,2,0:T(8,128)(2,1)S(1)}, u32[]{:S(2)}, u32[]{:S(2)}) collective-permute-start(bf16[10,128,64]{1,2,0:T(8,128)(2,1)S(1)} %get-tuple-element.8), channel_id=1, source_target_pairs={{0,48},{1,49},{2,50},{3,51},{4,52},{5,53},{6,54},{7,55},{8,56},{9,... | collective-permute-start | bytes 491528 | tf_op jit(solution)/shard_map/ppermute | solution.py:188
  102.8 3.1 %collective-permute-start.9 = (bf16[10,128,64]{1,2,0:T(8,128)(2,1)S(1)}, bf16[10,128,64]{1,2,0:T(8,128)(2,1)}, u32[]{:S(2)}, u32[]{:S(2)}) collective-permute-start(bf16[10,128,64]{1,2,0:T(8,128)(2,1)S(1)} %get-tuple-element.9), channel_id=1, source_target_pairs={{0,32},{1,33},{2,34},{3,35},{4,36},{5,37},{6,38},{7,39},{8,40},{9,... | collective-permute-start | bytes 491528 | tf_op jit(solution)/shard_map/ppermute | solution.py:188
  106.4 1.6 %concatenate.80 = bf16[38,64,38]{2,1,0:T(8,128)(2,1)S(1)} reshape(bf16[92416]{0:T(1024)(128)(2,1)S(1)} %slice.123) | data formatting | bytes 369664 | tf_op jit(solution)/shard_map/concatenate | solution.py:193
  109.6 2.4 %collective-permute-done.9 = bf16[10,128,64]{1,2,0:T(8,128)(2,1)} collective-permute-done((bf16[10,128,64]{1,2,0:T(8,128)(2,1)S(1)}, bf16[10,128,64]{1,2,0:T(8,128)(2,1)}, u32[]{:S(2)}, u32[]{:S(2)}) %collective-permute-start.9) | collective-permute-done | bytes 163872 | tf_op jit(solution)/shard_map/ppermute | solution.py:188
  112.0 2.1 %fusion.6 = f32[128,76,1]{1,0,2:T(8,128)} fusion(bf16[10,128,64]{1,2,0:T(8,128)(2,1)S(1)} %collective-permute-done.10, bf16[10,128,64]{1,2,0:T(8,128)(2,1)} %collective-permute-done.9, bf16[10,128,64]{1,2,0:T(8,128)(2,1)S(1)} %copy.52, bf16[16,128,64]{1,2,0:T(8,128)(2,1)S(1)} %dynamic-slice_bitcast_fusion, bf16[46,64,76]{2,1,0:T(8,128)(2,1)S(1)} %gather_fusion.1, ...), kind=kOutput, calls=%fused_computation.13 | convolution fusion | flops 58632704 | bytes 1240110 | tf_op jit(solution)/shard_map/isd,idc->sc/dot_general | solution.py:199
  114.1 7.4 %all-to-all-start.1 = ((f32[64,2,76]{2,1,0:T(2,128)}), f32[64,2,76]{2,1,0:T(2,128)S(1)}, u32[]{:S(2)}, u32[]{:S(2)}) async-start(f32[64,2,76]{2,1,0:T(2,128)} %bitcast.34), calls=%async_computation.1 | async-start | bytes 131072 | tf_op jit(solution)/shard_map/all_to_all | solution.py:203
  121.7 13.3 %all-to-all-done.1 = f32[64,2,76]{2,1,0:T(2,128)S(1)} async-done(((f32[64,2,76]{2,1,0:T(2,128)}), f32[64,2,76]{2,1,0:T(2,128)S(1)}, u32[]{:S(2)}, u32[]{:S(2)}) %all-to-all-start.1) | async-done | bytes 38944 | tf_op jit(solution)/shard_map/all_to_all | solution.py:203
  135.8 6.0 %collective-permute-start.11 = (f32[2,2,32]{2,1,0:T(2,128)S(1)}, f32[2,2,32]{2,1,0:T(2,128)S(1)}, u32[]{:S(2)}, u32[]{:S(2)}) collective-permute-start(f32[2,2,32]{2,1,0:T(2,128)S(1)} %constant_dynamic-slice_fusion), channel_id=1, source_target_pairs={{0,256},{256,0},{1,257},{257,1},{2,258},{258,2},{3,259},{259,3},{4... | collective-permute-start | bytes 1544 | tf_op jit(solution)/shard_map/ppermute | solution.py:15
  141.9 0.8 collective-permute-done.11
  (110 shorter events, 13.0 us)
Async XLA Ops:
  0.0 135.5 %copy-start = (bf16[2432,64]{0,1:T(8,128)(2,1)S(1)}, bf16[2432,64]{0,1:T(8,128)(2,1)}, u32[]{:S(2)}) copy-start(bf16[2432,64]{0,1:T(8,128)(2,1)} %param.23) | copy-start | bytes 933892
  0.8 14.5 %collective-permute-start = (bf16[2,2,2432]{2,1,0:T(2,128)(2,1)S(1)}, bf16[2,2,2432]{2,1,0:T(2,128)(2,1)S(1)}, u32[]{:S(2)}, u32[]{:S(2)}) collective-permute-start(bf16[2,2,2432]{2,1,0:T(2,128)(2,1)S(1)} %pad_maximum_fusion.3), channel_id=1, source_target_pairs={{0,64},{64,0},{128,192},{192,128},{1,65},{65,1},{129,193},{193,129... | collective-permute-start | bytes 58376 | tf_op jit(solution)/shard_map/ppermute | solution.py:15
  13.2 2.1 %copy-start.3 = (bf16[1,1,2,2,2432]{4,3,2,1,0:T(2,128)(2,1)S(1)}, bf16[1,1,2,2,2432]{4,3,2,1,0:T(2,128)(2,1)}, u32[]{:S(2)}) copy-start(bf16[1,1,2,2,2432]{4,3,2,1,0:T(2,128)(2,1)} %param.15) | copy-start | bytes 58372
  18.4 36.0 %all-to-all-start = ((bf16[64,2,873]{2,1,0:T(2,128)(2,1)}), bf16[64,2,873]{2,1,0:T(2,128)(2,1)S(1)}, u32[]{:S(2)}, u32[]{:S(2)}) async-start(bf16[64,2,873]{2,1,0:T(2,128)(2,1)} %reshape.355), calls=%async_computation | async-start | bytes 458752 | tf_op jit(solution)/shard_map/all_to_all | solution.py:130
  56.5 22.5 %collective-permute-start.1 = (bf16[1,2,128,64]{2,3,1,0:T(8,128)(2,1)S(1)}, bf16[1,2,128,64]{2,3,1,0:T(8,128)(2,1)S(1)}, u32[]{:S(2)}, u32[]{:S(2)}) collective-permute-start(bf16[1,2,128,64]{2,3,1,0:T(8,128)(2,1)S(1)} %get-tuple-element.18), channel_id=1, source_target_pairs={{0,4},{1,5},{2,6},{3,7},{4,0},{5,1},{6,2},{7,3},{8,12},{9,13},{10,... | collective-permute-start | bytes 98312 | tf_op jit(solution)/shard_map/ppermute | solution.py:164
  60.6 18.4 %collective-permute-start.2 = (bf16[1,2,128,64]{2,3,1,0:T(8,128)(2,1)S(1)}, bf16[1,2,128,64]{2,3,1,0:T(8,128)(2,1)S(1)}, u32[]{:S(2)}, u32[]{:S(2)}) collective-permute-start(bf16[1,2,128,64]{2,3,1,0:T(8,128)(2,1)S(1)} %get-tuple-element.18), channel_id=1, source_target_pairs={{0,8},{1,9},{2,10},{3,11},{4,12},{5,13},{6,14},{7,15},{8,0},{9,1},... | collective-permute-start | bytes 98312 | tf_op jit(solution)/shard_map/ppermute | solution.py:164
  67.5 11.5 %collective-permute-start.3 = (bf16[1,2,128,64]{2,3,1,0:T(8,128)(2,1)S(1)}, bf16[1,2,128,64]{2,3,1,0:T(8,128)(2,1)S(1)}, u32[]{:S(2)}, u32[]{:S(2)}) collective-permute-start(bf16[1,2,128,64]{2,3,1,0:T(8,128)(2,1)S(1)} %get-tuple-element.18), channel_id=1, source_target_pairs={{0,12},{1,13},{2,14},{3,15},{4,8},{5,9},{6,10},{7,11},{8,4},{9,5},... | collective-permute-start | bytes 98312 | tf_op jit(solution)/shard_map/ppermute | solution.py:164
  73.2 15.2 %collective-permute-start.7 = (bf16[1216,38]{1,0:T(8,128)(2,1)S(1)}, bf16[1216,38]{1,0:T(8,128)(2,1)S(1)}, u32[]{:S(2)}, u32[]{:S(2)}) collective-permute-start(bf16[1216,38]{1,0:T(8,128)(2,1)S(1)} %reshape.329), channel_id=1, source_target_pairs={{0,256},{256,0},{1,257},{257,1},{2,258},{258,2},{3,259},{259,3},{4... | collective-permute-start | bytes 277256 | tf_op jit(solution)/shard_map/ppermute | solution.py:15
  79.0 11.3 %collective-permute-start.4 = (bf16[4,2,128,64]{2,3,1,0:T(8,128)(2,1)S(1)}, bf16[4,2,128,64]{2,3,1,0:T(8,128)(2,1)S(1)}, u32[]{:S(2)}, u32[]{:S(2)}) collective-permute-start(bf16[4,2,128,64]{2,3,1,0:T(8,128)(2,1)S(1)} %pad_maximum_fusion.1), channel_id=1, source_target_pairs={{0,1},{1,0},{2,3},{3,2},{4,5},{5,4},{6,7},{7,6},{8,9},{9,8},{10,11... | collective-permute-start | bytes 393224 | tf_op jit(solution)/shard_map/ppermute | solution.py:164
  81.6 8.8 %collective-permute-start.5 = (bf16[4,2,128,64]{2,3,1,0:T(8,128)(2,1)S(1)}, bf16[4,2,128,64]{2,3,1,0:T(8,128)(2,1)S(1)}, u32[]{:S(2)}, u32[]{:S(2)}) collective-permute-start(bf16[4,2,128,64]{2,3,1,0:T(8,128)(2,1)S(1)} %pad_maximum_fusion.1), channel_id=1, source_target_pairs={{0,2},{1,3},{2,0},{3,1},{4,6},{5,7},{6,4},{7,5},{8,10},{9,11},{10,... | collective-permute-start | bytes 393224 | tf_op jit(solution)/shard_map/ppermute | solution.py:164
  84.6 8.1 %collective-permute-start.6 = (bf16[4,2,128,64]{2,3,1,0:T(8,128)(2,1)S(1)}, bf16[4,2,128,64]{2,3,1,0:T(8,128)(2,1)S(1)}, u32[]{:S(2)}, u32[]{:S(2)}) collective-permute-start(bf16[4,2,128,64]{2,3,1,0:T(8,128)(2,1)S(1)} %pad_maximum_fusion.1), channel_id=1, source_target_pairs={{0,3},{1,2},{2,1},{3,0},{4,7},{5,6},{6,5},{7,4},{8,11},{9,10},{10,... | collective-permute-start | bytes 393224 | tf_op jit(solution)/shard_map/ppermute | solution.py:164
  93.5 3.8 %copy-start.1 = (f32[1,6,2432]{2,0,1:T(1,128)S(1)}, f32[1,6,2432]{2,0,1:T(1,128)}, u32[]{:S(2)}) copy-start(f32[1,6,2432]{2,0,1:T(1,128)} %param.21) | copy-start | bytes 175108
  94.0 12.0 %collective-permute-start.8 = (bf16[174336]{0:T(1024)(128)(2,1)S(1)}, bf16[174336]{0:T(1024)(128)(2,1)S(1)}, u32[]{:S(2)}, u32[]{:S(2)}) collective-permute-start(bf16[174336]{0:T(1024)(128)(2,1)S(1)} %pad_maximum_fusion), channel_id=1, source_target_pairs={{0,16},{1,17},{2,18},{3,19},{4,20},{5,21},{6,22},{7,23},{8,24},{9,... | collective-permute-start | bytes 1046024 | tf_op jit(solution)/shard_map/ppermute | solution.py:182
  97.6 12.1 %collective-permute-start.10 = (bf16[10,128,64]{1,2,0:T(8,128)(2,1)S(1)}, bf16[10,128,64]{1,2,0:T(8,128)(2,1)S(1)}, u32[]{:S(2)}, u32[]{:S(2)}) collective-permute-start(bf16[10,128,64]{1,2,0:T(8,128)(2,1)S(1)} %get-tuple-element.8), channel_id=1, source_target_pairs={{0,48},{1,49},{2,50},{3,51},{4,52},{5,53},{6,54},{7,55},{8,56},{9,... | collective-permute-start | bytes 491528 | tf_op jit(solution)/shard_map/ppermute | solution.py:188
  102.8 9.2 %collective-permute-start.9 = (bf16[10,128,64]{1,2,0:T(8,128)(2,1)S(1)}, bf16[10,128,64]{1,2,0:T(8,128)(2,1)}, u32[]{:S(2)}, u32[]{:S(2)}) collective-permute-start(bf16[10,128,64]{1,2,0:T(8,128)(2,1)S(1)} %get-tuple-element.9), channel_id=1, source_target_pairs={{0,32},{1,33},{2,34},{3,35},{4,36},{5,37},{6,38},{7,39},{8,40},{9,... | collective-permute-start | bytes 491528 | tf_op jit(solution)/shard_map/ppermute | solution.py:188
  109.6 11.9 %copy-start.5 = (f32[6]{0:T(128)S(1)}, f32[6]{0:T(128)}, u32[]{:S(2)}) copy-start(f32[6]{0:T(128)} %param.25) | copy-start | bytes 76
  109.6 11.9 %copy-start.6 = (f32[6]{0:T(128)S(1)}, f32[6]{0:T(128)}, u32[]{:S(2)}) copy-start(f32[6]{0:T(128)} %param.24) | copy-start | bytes 76
  109.6 25.5 %copy-start.2 = (bf16[1,1,2,2,2432]{4,3,2,1,0:T(2,128)(2,1)S(1)}, bf16[1,1,2,2,2432]{4,3,2,1,0:T(2,128)(2,1)}, u32[]{:S(2)}) copy-start(bf16[1,1,2,2,2432]{4,3,2,1,0:T(2,128)(2,1)} %param.16) | copy-start | bytes 58372
  114.1 28.6 %copy-start.4 = (f32[1,2,2,32]{3,2,1,0:T(2,128)S(1)}, f32[1,2,2,32]{3,2,1,0:T(2,128)}, u32[]{:S(2)}) copy-start(f32[1,2,2,32]{3,2,1,0:T(2,128)} %param.17) | copy-start | bytes 1540
  114.1 20.9 %all-to-all-start.1 = ((f32[64,2,76]{2,1,0:T(2,128)}), f32[64,2,76]{2,1,0:T(2,128)S(1)}, u32[]{:S(2)}, u32[]{:S(2)}) async-start(f32[64,2,76]{2,1,0:T(2,128)} %bitcast.34), calls=%async_computation.1 | async-start | bytes 131072 | tf_op jit(solution)/shard_map/all_to_all | solution.py:203
  135.8 6.9 %collective-permute-start.11 = (f32[2,2,32]{2,1,0:T(2,128)S(1)}, f32[2,2,32]{2,1,0:T(2,128)S(1)}, u32[]{:S(2)}, u32[]{:S(2)}) collective-permute-start(f32[2,2,32]{2,1,0:T(2,128)S(1)} %constant_dynamic-slice_fusion), channel_id=1, source_target_pairs={{0,256},{256,0},{1,257},{257,1},{2,258},{258,2},{3,259},{259,3},{4... | collective-permute-start | bytes 1544 | tf_op jit(solution)/shard_map/ppermute | solution.py:15
